TPU v7x, 256 devices: a whole 4x4x8 slice. The times are simulated.
256 devices in a mesh: gx: 8 (over z_hi, y), gy: 8 (over x, core), gz: 4 (over z_lo).
Axes of the slice: x: 4, y: 4, z: 8 (z_hi: 2, z_lo: 4; z = z_hi * 4 + z_lo), core: 2. Of those that a mesh axis runs over, the one named last changes fastest.
Arguments:
- pressure: float32 [128, 128, 512], P('gx', 'gy', 'gz'), may hold values from -6 to 6
- velocity: float32 [3, 128, 128, 512], P(None, 'gx', 'gy', 'gz'), may hold values from -6 to 6
- inv_density: float32 [128, 128, 512], P('gx', 'gy', 'gz'), may hold values from 0.5 to 2
- bulk: float32 [128, 128, 512], P('gx', 'gy', 'gz'), may hold values from 0.25 to 1
- node_weight: float32 [8, 8, 256], P('gx', 'gy'), may hold values from 0.2 to 2
- node_patch: int32 [8, 8, 256], P('gx', 'gy'), may hold values from 0 to 8191, as said below
- patch_slot: int32 [8192], replicated, may hold values from 0 to 8191, as said below
- gauge_x: int32 [256], replicated, may hold values from 0 to 127
- gauge_y: int32 [256], replicated, may hold values from 0 to 127
- gauge_misfit: float32 [4, 256], replicated, may hold values from -6 to 6
Outputs:
- pressure_out: float32 [128, 128, 512], P('gx', 'gy', 'gz')
- velocity_out: float32 [3, 128, 128, 512], P(None, 'gx', 'gy', 'gz')
- slip_grad: float32 [8192], P(('gx', 'gy', 'gz'))
Inputs may be any that keep to these rules, and one draw needn't show every extreme that they name: `node_patch`: of the seafloor nodes of one tile, at most 16 map to patches whose slot lies in one owner's range of 128 slots; in every draw one owner receives exactly 16 from every tile. `patch_slot`: A permutation of the patches.
All inputs are finite; a program needn't handle non-finite values.
Results may differ from a plain program's by a relative error of at most 0.00018.
Values sent between devices are 32-bit elements; how exact they have to be, the bound alone decides.
No kernel may reach another device: no remote copies, remote signals or barrier semaphores. Data moves between devices by JAX's collectives and lax.ppermute only.
A program may use at most 64 MiB of HBM per device.

v0:
```python
import jax
import jax.numpy as jnp
from jax import lax
from jax.sharding import PartitionSpec as P

ITERS = 4


time_step = 0.5
margin = 4


def extended(block, sides, width):
    for axis, dim in sides:
        count = lax.axis_size(axis)
        forward = [(i, i + 1) for i in range(count - 1)]
        backward = [(target, source) for source, target in forward]
        low = lax.ppermute(
            lax.slice_in_dim(block, block.shape[dim] - width, None, axis=dim), axis, forward
        )
        high = lax.ppermute(lax.slice_in_dim(block, 0, width, axis=dim), axis, backward)
        block = jnp.concatenate([low, block, high], axis=dim)
    return block


def in_blocks(x, dim, size):
    before, after = (x.shape[:dim], x.shape[dim + 1 :])
    return jnp.moveaxis(x.reshape(*before, size, -1, *after), dim, 0)


def summed_on_arrival(x, axis, dim):
    size = lax.axis_size(axis)
    parts = lax.all_to_all(in_blocks(x, dim, size), axis, 0, 0, tiled=True)
    return jnp.sum(parts, axis=0)


def picked(x, axis, root):
    return lax.dynamic_index_in_dim(lax.all_gather(x, axis), root, 0, keepdims=False)


def depth_weights(levels, first_crust):
    ocean_last = levels == first_crust - 1
    crust_first = levels == first_crust
    weight_above = jnp.where(ocean_last, 0.5, jnp.where(crust_first, 1.0, 0.5)).astype(jnp.float32)
    weight_here = jnp.where(ocean_last, 0.5, jnp.where(crust_first, -1.5, 0.0)).astype(jnp.float32)
    weight_below = jnp.where(ocean_last, -1.0, jnp.where(crust_first, 0.5, -0.5)).astype(
        jnp.float32
    )
    return (weight_above, weight_here, weight_below)


def source_planes(gauge_x, gauge_y, gauge_misfit, start_x, start_y, span_x, span_y):
    local_x = gauge_x - start_x
    local_y = gauge_y - start_y
    inside = (local_x >= 0) & (local_x < span_x) & (local_y >= 0) & (local_y < span_y)
    gauge_cell = jnp.where(inside, local_x * span_y + local_y, -1)
    gauge_table = (
        gauge_cell[:, None] == jnp.arange(span_x * span_y, dtype=jnp.int32)[None, :]
    ).astype(jnp.float32)
    return jnp.dot(gauge_misfit, gauge_table, precision=lax.Precision.HIGHEST).reshape(
        gauge_misfit.shape[0], span_x, span_y
    )


def local_step(pressure, velocity, inv_density, bulk, weights, source_plane, top_mask):
    weight_above, weight_here, weight_below = weights
    padded = jnp.pad(pressure, 1)
    slope_x = 0.5 * (padded[2:, 1:-1, 1:-1] - padded[:-2, 1:-1, 1:-1])
    slope_y = 0.5 * (padded[1:-1, 2:, 1:-1] - padded[1:-1, :-2, 1:-1])
    slope_z = (
        weight_above * padded[1:-1, 1:-1, 2:]
        + weight_here * pressure
        + weight_below * padded[1:-1, 1:-1, :-2]
    )
    velocity = jnp.stack(
        [
            velocity[0] - time_step * inv_density * slope_x,
            velocity[1] - time_step * inv_density * slope_y,
            velocity[2] - time_step * inv_density * slope_z,
        ]
    )
    along_x = jnp.pad(velocity[0], ((1, 1), (0, 0), (0, 0)))
    along_y = jnp.pad(velocity[1], ((0, 0), (1, 1), (0, 0)))
    along_z = jnp.pad(velocity[2], ((0, 0), (0, 0), (1, 1)))
    spread = (
        0.5 * (along_x[2:] - along_x[:-2])
        + 0.5 * (along_y[:, 2:] - along_y[:, :-2])
        + (
            weight_above * along_z[:, :, 2:]
            + weight_here * velocity[2]
            + weight_below * along_z[:, :, :-2]
        )
    )
    pressure = pressure - time_step * bulk * spread
    pressure = pressure + time_step * source_plane[:, :, None] * top_mask[None, None, :]
    return (pressure, velocity)


def local(
    pressure,
    velocity,
    inv_density,
    bulk,
    node_weight,
    node_patch,
    patch_slot,
    gauge_x,
    gauge_y,
    gauge_misfit,
):
    rows_x, rows_y, depth = pressure.shape
    tiles_z = lax.axis_size("gz")
    depth_index = lax.axis_index("gz")
    first_crust = tiles_z // 2 * depth
    seafloor = jnp.zeros((rows_x, rows_y), jnp.float32)
    levels = depth_index * depth - margin + jnp.arange(depth + 2 * margin, dtype=jnp.int32)
    weights = depth_weights(levels, first_crust)
    top_mask = (levels == 0).astype(jnp.float32)
    sources = source_planes(
        gauge_x,
        gauge_y,
        gauge_misfit,
        lax.axis_index("gx") * rows_x - margin,
        lax.axis_index("gy") * rows_y - margin,
        rows_x + 2 * margin,
        rows_y + 2 * margin,
    )
    media = extended(jnp.stack([inv_density, bulk]), (("gx", 1), ("gy", 2), ("gz", 3)), margin)
    fields = jnp.concatenate([pressure[None], velocity], axis=0)
    for group in range(ITERS // 2):
        wide = extended(fields, (("gx", 1), ("gy", 2), ("gz", 3)), margin)
        wide_pressure = wide[0]
        wide_velocity = wide[1:]
        for inner in range(2):
            instant = 2 * group + inner
            seafloor = seafloor + 0.5 * (
                wide_pressure[margin:-margin, margin:-margin, margin - 1]
                + wide_pressure[margin:-margin, margin:-margin, margin]
            )
            wide_pressure, wide_velocity = local_step(
                wide_pressure,
                wide_velocity,
                media[0],
                media[1],
                weights,
                sources[instant],
                top_mask,
            )
        fields = jnp.concatenate([wide_pressure[None], wide_velocity], axis=0)[
            :, margin:-margin, margin:-margin, margin:-margin
        ]
    pressure = fields[0]
    velocity = fields[1:]
    sea_count = rows_x * rows_y
    owners_count = lax.axis_size("gx") * lax.axis_size("gy")
    patch_count = patch_slot.shape[0] // owners_count
    piece_count = patch_count // tiles_z
    root_tile = tiles_z // 2
    sea_values = node_weight[0, 0] * seafloor.reshape(sea_count)
    slots = patch_slot[node_patch[0, 0]]
    partial_slip = jnp.zeros((patch_slot.shape[0],), jnp.float32).at[slots].add(sea_values)
    slip_grad = summed_on_arrival(partial_slip, ("gx", "gy"), 0)
    slip_grad = picked(slip_grad, "gz", root_tile)
    slip_grad = lax.dynamic_slice_in_dim(slip_grad, depth_index * piece_count, piece_count)
    return (pressure, velocity, slip_grad)


def solution(mesh):
    placed = (
        P("gx", "gy", "gz"),
        P(None, "gx", "gy", "gz"),
        P("gx", "gy", "gz"),
        P("gx", "gy", "gz"),
        P("gx", "gy", None),
        P("gx", "gy", None),
        P(),
        P(),
        P(),
        P(),
    )
    return jax.shard_map(
        local,
        mesh=mesh,
        in_specs=placed,
        out_specs=(P("gx", "gy", "gz"), P(None, "gx", "gy", "gz"), P(("gx", "gy", "gz"))),
        check_vma=False,
    )
```

profile of v0, /device:TPU:24, one launch (start us, length us, event | category | flops | bytes accessed | tf_op | source)
XLA Modules:
  0.0 216.5 jit_solution(18107025135920425715)
XLA Ops:
  1.5 8.8 %collective-permute-start.6 = (f32[2,4,16,128]{3,2,1,0:T(8,128)S(1)}, f32[2,4,16,128]{3,2,1,0:T(8,128)S(1)}, u32[]{:S(2)}, u32[]{:S(2)}) collective-permute-start(f32[2,4,16,128]{3,2,1,0:T(8,128)S(1)} %get-tuple-element.38), channel_id=1, source_target_pairs={{0,32},{32,64},{64,96},{96,128},{128,160},{160,192},{192,224},{1,3... | collective-permute-start | bytes 196616 | tf_op jit(solution)/shard_map/ppermute | solution.py:18
  13.1 9.9 %collective-permute-start = (f32[4,4,16,128]{3,2,1,0:T(8,128)S(1)}, f32[4,4,16,128]{3,2,1,0:T(8,128)S(1)}, u32[]{:S(2)}, u32[]{:S(2)}) collective-permute-start(f32[4,4,16,128]{3,2,1,0:T(8,128)S(1)} %get-tuple-element.34), channel_id=1, source_target_pairs={{0,32},{32,64},{64,96},{96,128},{128,160},{160,192},{192,224},{1,3... | collective-permute-start | bytes 393224 | tf_op jit(solution)/shard_map/ppermute | solution.py:18
  32.8 3.3 %collective-permute-done.1 = f32[4,4,16,128]{3,2,1,0:T(8,128)S(1)} collective-permute-done((f32[4,4,16,128]{3,2,1,0:T(8,128)S(1)}, f32[4,4,16,128]{3,2,1,0:T(8,128)S(1)}, u32[]{:S(2)}, u32[]{:S(2)}) %collective-permute-start.1) | collective-permute-done | bytes 131104 | tf_op jit(solution)/shard_map/ppermute | solution.py:21
  45.8 5.4 %pad_maximum_fusion.2 = f32[2,24,24,128]{2,1,3,0:T(8,128)S(1)} fusion(f32[2,24,4,128]{2,1,3,0:T(8,128)} %copy.79, f32[2,24,16,128]{2,1,3,0:T(8,128)} %copy.78, f32[2,24,4,128]{2,1,3,0:T(8,128)} %copy.77), kind=kLoop, calls=%fused_computation.4 | loop fusion | flops 294912 | bytes 1179648 | tf_op jit(solution)/shard_map/concatenate | solution.py:22
  51.9 5.5 %collective-permute-start.10 = (f32[2,24,24,4]{2,1,3,0:T(8,128)}, f32[2,24,24,4]{2,1,3,0:T(8,128)}, u32[]{:S(2)}, u32[]{:S(2)}) collective-permute-start(f32[2,24,24,4]{2,1,3,0:T(8,128)} %get-tuple-element.20), channel_id=1, source_target_pairs={{0,1},{1,2},{2,3},{4,5},{5,6},{6,7},{8,9},{9,10},{10,11},{12,13},{... | collective-permute-start | bytes 55304 | tf_op jit(solution)/shard_map/ppermute | solution.py:18
  58.9 5.0 %copy.70 = f32[4,24,16,128]{2,1,3,0:T(8,128)} copy(f32[4,24,16,128]{3,2,1,0:T(8,128)} %copy-done.4) | data formatting | bytes 1572864 | tf_op jit(solution)/shard_map/concatenate | solution.py:22
  68.2 4.2 %copy.69 = f32[4,24,4,128]{2,1,3,0:T(8,128)} copy(f32[4,24,4,128]{3,1,2,0:T(8,128)S(1)} %collective-permute-done.2) | data formatting | bytes 393216 | tf_op jit(solution)/shard_map/ppermute | solution.py:18
  72.4 5.1 %copy.71 = f32[4,24,4,128]{2,1,3,0:T(8,128)} copy(f32[4,24,4,128]{3,1,2,0:T(8,128)} %collective-permute-done.3) | data formatting | bytes 393216 | tf_op jit(solution)/shard_map/ppermute | solution.py:21
  77.6 8.2 %pad_maximum_fusion = f32[4,24,24,128]{2,1,3,0:T(8,128)S(1)} fusion(f32[4,24,4,128]{2,1,3,0:T(8,128)} %copy.71, f32[4,24,16,128]{2,1,3,0:T(8,128)} %copy.70, f32[4,24,4,128]{2,1,3,0:T(8,128)} %copy.69), kind=kLoop, calls=%fused_computation.2 | loop fusion | flops 589824 | bytes 2359296 | tf_op jit(solution)/shard_map/concatenate | solution.py:22
  85.8 4.6 %collective-permute-start.4 = (f32[4,24,24,4]{2,1,3,0:T(8,128)S(1)}, f32[4,24,24,4]{2,1,3,0:T(8,128)S(1)}, u32[]{:S(2)}, u32[]{:S(2)}) collective-permute-start(f32[4,24,24,4]{2,1,3,0:T(8,128)S(1)} %get-tuple-element.12), channel_id=1, source_target_pairs={{0,1},{1,2},{2,3},{4,5},{5,6},{6,7},{8,9},{9,10},{10,11},{12,13},{... | collective-permute-start | bytes 110600 | tf_op jit(solution)/shard_map/ppermute | solution.py:18
  92.4 4.4 %copy.73 = f32[4,24,24,128]{3,2,1,0:T(8,128)S(1)} copy(f32[4,24,24,128]{2,1,3,0:T(8,128)} %copy-done.2) | data formatting | bytes 2359296 | tf_op jit(solution)/shard_map/concatenate | solution.py:22
  100.7 2.6 %pad_maximum_fusion.3 = f32[4,24,24,136]{3,2,1,0:T(8,128)S(1)} fusion(f32[4,24,24,4]{3,2,1,0:T(8,128)} %copy.74, f32[4,24,24,128]{3,2,1,0:T(8,128)S(1)} %copy.73, f32[4,24,24,4]{3,2,1,0:T(8,128)} %copy.72), kind=kLoop, calls=%fused_computation.5 | loop fusion | flops 626688 | bytes 2506752 | tf_op jit(solution)/shard_map/concatenate | solution.py:22
  106.4 8.6 %collective-permute-start.12 = (f32[4,4,16,128]{3,2,1,0:T(8,128)S(1)}, f32[4,4,16,128]{3,2,1,0:T(8,128)S(1)}, u32[]{:S(2)}, u32[]{:S(2)}) collective-permute-start(f32[4,4,16,128]{3,2,1,0:T(8,128)S(1)} %get-tuple-element.22), channel_id=1, source_target_pairs={{0,32},{32,64},{64,96},{96,128},{128,160},{160,192},{192,224},{1,3... | collective-permute-start | bytes 393224 | tf_op jit(solution)/shard_map/ppermute | solution.py:18
  118.2 10.2 %collective-permute-done.13 = f32[4,4,16,128]{3,2,1,0:T(8,128)S(1)} collective-permute-done((f32[4,4,16,128]{3,2,1,0:T(8,128)S(1)}, f32[4,4,16,128]{3,2,1,0:T(8,128)S(1)}, u32[]{:S(2)}, u32[]{:S(2)}) %collective-permute-start.13) | collective-permute-done | bytes 131104 | tf_op jit(solution)/shard_map/ppermute | solution.py:21
  133.2 4.3 %copy.86 = f32[4,24,16,128]{2,1,3,0:T(8,128)} copy(f32[4,24,16,128]{3,2,1,0:T(8,128)S(1)} %fusion.1) | data formatting | bytes 1572864 | tf_op jit(solution)/shard_map/concatenate | solution.py:22
  137.4 4.2 %copy.85 = f32[4,24,4,128]{2,1,3,0:T(8,128)} copy(f32[4,24,4,128]{3,1,2,0:T(8,128)S(1)} %collective-permute-done.14) | data formatting | bytes 393216 | tf_op jit(solution)/shard_map/ppermute | solution.py:18
  141.6 4.1 %copy.87 = f32[4,24,4,128]{2,1,3,0:T(8,128)} copy(f32[4,24,4,128]{3,1,2,0:T(8,128)S(1)} %collective-permute-done.15) | data formatting | bytes 393216 | tf_op jit(solution)/shard_map/ppermute | solution.py:21
  145.8 8.1 %pad_maximum_fusion.1 = f32[4,24,24,128]{2,1,3,0:T(8,128)S(1)} fusion(f32[4,24,4,128]{2,1,3,0:T(8,128)} %copy.87, f32[4,24,16,128]{2,1,3,0:T(8,128)} %copy.86, f32[4,24,4,128]{2,1,3,0:T(8,128)} %copy.85), kind=kLoop, calls=%fused_computation.3 | loop fusion | flops 589824 | bytes 2359296 | tf_op jit(solution)/shard_map/concatenate | solution.py:22
  153.9 2.6 %copy-done.1 = f32[4,24,24,128]{2,1,3,0:T(8,128)} copy-done((f32[4,24,24,128]{2,1,3,0:T(8,128)}, f32[4,24,24,128]{2,1,3,0:T(8,128)S(1)}, u32[]{:S(2)}) %copy-start.1) | copy-done | bytes 1179672
  156.6 8.4 %collective-permute-start.16 = (f32[4,24,24,4]{2,1,3,0:T(8,128)S(1)}, f32[4,24,24,4]{2,1,3,0:T(8,128)}, u32[]{:S(2)}, u32[]{:S(2)}) collective-permute-start(f32[4,24,24,4]{2,1,3,0:T(8,128)S(1)} %get-tuple-element.10), channel_id=1, source_target_pairs={{0,1},{1,2},{2,3},{4,5},{5,6},{6,7},{8,9},{9,10},{10,11},{12,13},{... | collective-permute-start | bytes 110600 | tf_op jit(solution)/shard_map/ppermute | solution.py:18
  166.7 4.4 %copy.89 = f32[4,24,24,128]{3,2,1,0:T(8,128)S(1)} copy(f32[4,24,24,128]{2,1,3,0:T(8,128)} %copy-done.1) | data formatting | bytes 2359296 | tf_op jit(solution)/shard_map/concatenate | solution.py:22
  186.0 9.3 %all-to-all-start = ((f32[64,1,128]{2,1,0:T(1,128)}), f32[64,1,128]{2,1,0:T(1,128)S(1)}, u32[]{:S(2)}, u32[]{:S(2)}) async-start(f32[64,1,128]{2,1,0:T(1,128)} %bitcast.28), calls=%async_computation | async-start | bytes 65536 | tf_op jit(solution)/shard_map/all_to_all | solution.py:33
  198.9 6.9 %all-to-all-done = f32[64,1,128]{2,1,0:T(1,128)S(1)} async-done(((f32[64,1,128]{2,1,0:T(1,128)}), f32[64,1,128]{2,1,0:T(1,128)S(1)}, u32[]{:S(2)}, u32[]{:S(2)}) %all-to-all-start) | async-done | bytes 32800 | tf_op jit(solution)/shard_map/all_to_all | solution.py:33
  205.8 10.1 %all-gather.1 = f32[4,1,128]{2,1,0:T(1,128)S(1)} all-gather(f32[1,1,128]{2,1,0:T(1,128)S(1)} %bitcast.115), channel_id=2, replica_groups=mesh['gx'=8,'gy'=8,'gz'=4] {'gz'}, dimensions={0}, use_global_device_ids=true | all-gather | bytes 2560 | tf_op jit(solution)/shard_map/all_gather | solution.py:38
  (112 shorter events, 67.0 us)
Async XLA Ops:
  0.6 130.8 %copy-start = (s32[8192]{0:T(1024)S(1)}, s32[8192]{0:T(1024)}, u32[]{:S(2)}) copy-start(s32[8192]{0:T(1024)} %param.16) | copy-start | bytes 98308
  1.5 25.4 %collective-permute-start.6 = (f32[2,4,16,128]{3,2,1,0:T(8,128)S(1)}, f32[2,4,16,128]{3,2,1,0:T(8,128)S(1)}, u32[]{:S(2)}, u32[]{:S(2)}) collective-permute-start(f32[2,4,16,128]{3,2,1,0:T(8,128)S(1)} %get-tuple-element.38), channel_id=1, source_target_pairs={{0,32},{32,64},{64,96},{96,128},{128,160},{160,192},{192,224},{1,3... | collective-permute-start | bytes 196616 | tf_op jit(solution)/shard_map/ppermute | solution.py:18
  10.2 16.6 %collective-permute-start.7 = (f32[2,4,16,128]{3,2,1,0:T(8,128)S(1)}, f32[2,4,16,128]{3,2,1,0:T(8,128)S(1)}, u32[]{:S(2)}, u32[]{:S(2)}) collective-permute-start(f32[2,4,16,128]{3,2,1,0:T(8,128)S(1)} %get-tuple-element.39), channel_id=1, source_target_pairs={{32,0},{64,32},{96,64},{128,96},{160,128},{192,160},{224,192},{33,... | collective-permute-start | bytes 196616 | tf_op jit(solution)/shard_map/ppermute | solution.py:21
  13.1 19.6 %collective-permute-start = (f32[4,4,16,128]{3,2,1,0:T(8,128)S(1)}, f32[4,4,16,128]{3,2,1,0:T(8,128)S(1)}, u32[]{:S(2)}, u32[]{:S(2)}) collective-permute-start(f32[4,4,16,128]{3,2,1,0:T(8,128)S(1)} %get-tuple-element.34), channel_id=1, source_target_pairs={{0,32},{32,64},{64,96},{96,128},{128,160},{160,192},{192,224},{1,3... | collective-permute-start | bytes 393224 | tf_op jit(solution)/shard_map/ppermute | solution.py:18
  23.1 13.0 %collective-permute-start.1 = (f32[4,4,16,128]{3,2,1,0:T(8,128)S(1)}, f32[4,4,16,128]{3,2,1,0:T(8,128)S(1)}, u32[]{:S(2)}, u32[]{:S(2)}) collective-permute-start(f32[4,4,16,128]{3,2,1,0:T(8,128)S(1)} %get-tuple-element.35), channel_id=1, source_target_pairs={{32,0},{64,32},{96,64},{128,96},{160,128},{192,160},{224,192},{33,... | collective-permute-start | bytes 393224 | tf_op jit(solution)/shard_map/ppermute | solution.py:21
  27.9 8.2 %copy-start.7 = (f32[3,16,16,128]{3,2,1,0:T(8,128)S(1)}, f32[3,16,16,128]{3,2,1,0:T(8,128)}, u32[]{:S(2)}) copy-start(f32[3,16,16,128]{3,2,1,0:T(8,128)} %param.11) | copy-start | bytes 1179652
  27.9 8.2 %copy-start.8 = (f32[16,16,128]{2,1,0:T(8,128)S(1)}, f32[16,16,128]{2,1,0:T(8,128)}, u32[]{:S(2)}) copy-start(f32[16,16,128]{2,1,0:T(8,128)} %param.10) | copy-start | bytes 393220
  30.1 11.1 %collective-permute-start.8 = (f32[2,24,4,128]{3,1,2,0:T(8,128)S(1)}, f32[2,24,4,128]{3,1,2,0:T(8,128)S(1)}, u32[]{:S(2)}, u32[]{:S(2)}) collective-permute-start(f32[2,24,4,128]{3,1,2,0:T(8,128)S(1)} %copy.94), channel_id=1, source_target_pairs={{0,4},{4,8},{8,12},{12,16},{16,20},{20,24},{24,28},{1,5},{5,9},{9,... | collective-permute-start | bytes 294920 | tf_op jit(solution)/shard_map/ppermute | solution.py:18
  31.4 12.1 %collective-permute-start.9 = (f32[2,24,4,128]{3,1,2,0:T(8,128)S(1)}, f32[2,24,4,128]{3,1,2,0:T(8,128)S(1)}, u32[]{:S(2)}, u32[]{:S(2)}) collective-permute-start(f32[2,24,4,128]{3,1,2,0:T(8,128)S(1)} %copy.95), channel_id=1, source_target_pairs={{4,0},{8,4},{12,8},{16,12},{20,16},{24,20},{28,24},{5,1},{9,5},{13... | collective-permute-start | bytes 294920 | tf_op jit(solution)/shard_map/ppermute | solution.py:21
  37.8 30.5 %collective-permute-start.2 = (f32[4,24,4,128]{3,1,2,0:T(8,128)}, f32[4,24,4,128]{3,1,2,0:T(8,128)S(1)}, u32[]{:S(2)}, u32[]{:S(2)}) collective-permute-start(f32[4,24,4,128]{3,1,2,0:T(8,128)} %copy.92), channel_id=1, source_target_pairs={{0,4},{4,8},{8,12},{12,16},{16,20},{20,24},{24,28},{1,5},{5,9},{9,... | collective-permute-start | bytes 589832 | tf_op jit(solution)/shard_map/ppermute | solution.py:18
  39.9 32.5 %collective-permute-start.3 = (f32[4,24,4,128]{3,1,2,0:T(8,128)}, f32[4,24,4,128]{3,1,2,0:T(8,128)}, u32[]{:S(2)}, u32[]{:S(2)}) collective-permute-start(f32[4,24,4,128]{3,1,2,0:T(8,128)} %copy.93), channel_id=1, source_target_pairs={{4,0},{8,4},{12,8},{16,12},{20,16},{24,20},{28,24},{5,1},{9,5},{13... | collective-permute-start | bytes 589832 | tf_op jit(solution)/shard_map/ppermute | solution.py:21
  51.9 13.8 %collective-permute-start.10 = (f32[2,24,24,4]{2,1,3,0:T(8,128)}, f32[2,24,24,4]{2,1,3,0:T(8,128)}, u32[]{:S(2)}, u32[]{:S(2)}) collective-permute-start(f32[2,24,24,4]{2,1,3,0:T(8,128)} %get-tuple-element.20), channel_id=1, source_target_pairs={{0,1},{1,2},{2,3},{4,5},{5,6},{6,7},{8,9},{9,10},{10,11},{12,13},{... | collective-permute-start | bytes 55304 | tf_op jit(solution)/shard_map/ppermute | solution.py:18
  57.4 9.6 %collective-permute-start.11 = (f32[2,24,24,4]{2,1,3,0:T(8,128)S(1)}, f32[2,24,24,4]{2,1,3,0:T(8,128)}, u32[]{:S(2)}, u32[]{:S(2)}) collective-permute-start(f32[2,24,24,4]{2,1,3,0:T(8,128)S(1)} %get-tuple-element.21), channel_id=1, source_target_pairs={{1,0},{2,1},{3,2},{5,4},{6,5},{7,6},{9,8},{10,9},{11,10},{13,12},{... | collective-permute-start | bytes 55304 | tf_op jit(solution)/shard_map/ppermute | solution.py:21
  77.6 14.3 %copy-start.6 = (f32[2,24,24,128]{3,2,1,0:T(8,128)S(1)}, f32[2,24,24,128]{3,2,1,0:T(8,128)}, u32[]{:S(2)}) copy-start(f32[2,24,24,128]{3,2,1,0:T(8,128)} %copy.81) | copy-start | bytes 1769476
  85.8 11.0 %collective-permute-start.4 = (f32[4,24,24,4]{2,1,3,0:T(8,128)S(1)}, f32[4,24,24,4]{2,1,3,0:T(8,128)S(1)}, u32[]{:S(2)}, u32[]{:S(2)}) collective-permute-start(f32[4,24,24,4]{2,1,3,0:T(8,128)S(1)} %get-tuple-element.12), channel_id=1, source_target_pairs={{0,1},{1,2},{2,3},{4,5},{5,6},{6,7},{8,9},{9,10},{10,11},{12,13},{... | collective-permute-start | bytes 110600 | tf_op jit(solution)/shard_map/ppermute | solution.py:18
  90.4 8.6 %collective-permute-start.5 = (f32[4,24,24,4]{2,1,3,0:T(8,128)S(1)}, f32[4,24,24,4]{2,1,3,0:T(8,128)S(1)}, u32[]{:S(2)}, u32[]{:S(2)}) collective-permute-start(f32[4,24,24,4]{2,1,3,0:T(8,128)S(1)} %get-tuple-element.13), channel_id=1, source_target_pairs={{1,0},{2,1},{3,2},{5,4},{6,5},{7,6},{9,8},{10,9},{11,10},{13,12},{... | collective-permute-start | bytes 110600 | tf_op jit(solution)/shard_map/ppermute | solution.py:21
  106.4 11.8 %collective-permute-start.12 = (f32[4,4,16,128]{3,2,1,0:T(8,128)S(1)}, f32[4,4,16,128]{3,2,1,0:T(8,128)S(1)}, u32[]{:S(2)}, u32[]{:S(2)}) collective-permute-start(f32[4,4,16,128]{3,2,1,0:T(8,128)S(1)} %get-tuple-element.22), channel_id=1, source_target_pairs={{0,32},{32,64},{64,96},{96,128},{128,160},{160,192},{192,224},{1,3... | collective-permute-start | bytes 393224 | tf_op jit(solution)/shard_map/ppermute | solution.py:18
  114.9 16.5 %copy-start.10 = (s32[1,1,256]{2,1,0:T(1,128)S(1)}, s32[1,1,256]{2,1,0:T(1,128)}, u32[]{:S(2)}) copy-start(s32[1,1,256]{2,1,0:T(1,128)} %param.15) | copy-start | bytes 3076
  114.9 13.5 %collective-permute-start.13 = (f32[4,4,16,128]{3,2,1,0:T(8,128)S(1)}, f32[4,4,16,128]{3,2,1,0:T(8,128)S(1)}, u32[]{:S(2)}, u32[]{:S(2)}) collective-permute-start(f32[4,4,16,128]{3,2,1,0:T(8,128)S(1)} %get-tuple-element.23), channel_id=1, source_target_pairs={{32,0},{64,32},{96,64},{128,96},{160,128},{192,160},{224,192},{33,... | collective-permute-start | bytes 393224 | tf_op jit(solution)/shard_map/ppermute | solution.py:21
  128.7 8.7 %collective-permute-start.14 = (f32[4,24,4,128]{3,1,2,0:T(8,128)S(1)}, f32[4,24,4,128]{3,1,2,0:T(8,128)S(1)}, u32[]{:S(2)}, u32[]{:S(2)}) collective-permute-start(f32[4,24,4,128]{3,1,2,0:T(8,128)S(1)} %copy.96), channel_id=1, source_target_pairs={{0,4},{4,8},{8,12},{12,16},{16,20},{20,24},{24,28},{1,5},{5,9},{9,... | collective-permute-start | bytes 589832 | tf_op jit(solution)/shard_map/ppermute | solution.py:18
  130.1 11.6 %collective-permute-start.15 = (f32[4,24,4,128]{3,1,2,0:T(8,128)S(1)}, f32[4,24,4,128]{3,1,2,0:T(8,128)S(1)}, u32[]{:S(2)}, u32[]{:S(2)}) collective-permute-start(f32[4,24,4,128]{3,1,2,0:T(8,128)S(1)} %copy.97), channel_id=1, source_target_pairs={{4,0},{8,4},{12,8},{16,12},{20,16},{24,20},{28,24},{5,1},{9,5},{13... | collective-permute-start | bytes 589832 | tf_op jit(solution)/shard_map/ppermute | solution.py:21
  156.6 14.5 %collective-permute-start.16 = (f32[4,24,24,4]{2,1,3,0:T(8,128)S(1)}, f32[4,24,24,4]{2,1,3,0:T(8,128)}, u32[]{:S(2)}, u32[]{:S(2)}) collective-permute-start(f32[4,24,24,4]{2,1,3,0:T(8,128)S(1)} %get-tuple-element.10), channel_id=1, source_target_pairs={{0,1},{1,2},{2,3},{4,5},{5,6},{6,7},{8,9},{9,10},{10,11},{12,13},{... | collective-permute-start | bytes 110600 | tf_op jit(solution)/shard_map/ppermute | solution.py:18
  165.0 8.9 %collective-permute-start.17 = (f32[4,24,24,4]{2,1,3,0:T(8,128)S(1)}, f32[4,24,24,4]{2,1,3,0:T(8,128)}, u32[]{:S(2)}, u32[]{:S(2)}) collective-permute-start(f32[4,24,24,4]{2,1,3,0:T(8,128)S(1)} %get-tuple-element.11), channel_id=1, source_target_pairs={{1,0},{2,1},{3,2},{5,4},{6,5},{7,6},{9,8},{10,9},{11,10},{13,12},{... | collective-permute-start | bytes 110600 | tf_op jit(solution)/shard_map/ppermute | solution.py:21
  186.0 19.8 %all-to-all-start = ((f32[64,1,128]{2,1,0:T(1,128)}), f32[64,1,128]{2,1,0:T(1,128)S(1)}, u32[]{:S(2)}, u32[]{:S(2)}) async-start(f32[64,1,128]{2,1,0:T(1,128)} %bitcast.28), calls=%async_computation | async-start | bytes 65536 | tf_op jit(solution)/shard_map/all_to_all | solution.py:33
  (6 other events, 13.2 us)
where the time goes:
time: 218 us; the launch traced here: 217 us
  starting transfers between devices  73 us (33%)
  local copies, waits for them, and re-layouts  64.9 us (30%)
  other arithmetic  43.6 us (20%)
  waiting for transfers between devices  22.6 us (10%)
  blocking collectives  10.1 us (5%)
    ppermute x9, starting transfers between devices, extended(): lax.ppermute(lax.slice_in_dim(block, block.shape[dim] - width, None, axis...  49.8 us
    concatenate x9, other arithmetic, extended(): block = jnp.concatenate([low, block, high], axis=dim)  28.8 us
    concatenate x6, local copies, waits for them, and re-layouts, extended(): block = jnp.concatenate([low, block, high], axis=dim)  22 us
    ppermute x6, local copies, waits for them, and re-layouts, extended(): lax.ppermute(lax.slice_in_dim(block, 0, width, axis=dim), axis, backward)  17 us
    ppermute x6, local copies, waits for them, and re-layouts, extended(): lax.ppermute(lax.slice_in_dim(block, block.shape[dim] - width, None, axis...  16.2 us
    ppermute x9, waiting for transfers between devices, extended(): lax.ppermute(lax.slice_in_dim(block, 0, width, axis=dim), axis, backward)  14.4 us
    ppermute x9, starting transfers between devices, extended(): lax.ppermute(lax.slice_in_dim(block, 0, width, axis=dim), axis, backward)  13.9 us
    all_gather x1, blocking collectives, picked(): lax.all_gather(x, axis)  10.1 us
  transfers between devices with their start and end apart: 19, of which 6 were waited for; matrix products, arithmetic and copies ran while one was open for 27% of the time, Pallas kernels for 0%

commit v1 on v0

--- a/solution.py
+++ b/solution.py
@@ -125,10 +125,18 @@
         rows_x + 2 * margin,
         rows_y + 2 * margin,
     )
-    media = extended(jnp.stack([inv_density, bulk]), (("gx", 1), ("gy", 2), ("gz", 3)), margin)
     fields = jnp.concatenate([pressure[None], velocity], axis=0)
     for group in range(ITERS // 2):
-        wide = extended(fields, (("gx", 1), ("gy", 2), ("gz", 3)), margin)
+        if group == 0:
+            wide = extended(
+                jnp.concatenate([fields, inv_density[None], bulk[None]], axis=0),
+                (("gx", 1), ("gy", 2), ("gz", 3)),
+                margin,
+            )
+            media = wide[4:]
+            wide = wide[:4]
+        else:
+            wide = extended(fields, (("gx", 1), ("gy", 2), ("gz", 3)), margin)
         wide_pressure = wide[0]
         wide_velocity = wide[1:]
         for inner in range(2):
@@ -158,10 +166,9 @@
     root_tile = tiles_z // 2
     sea_values = node_weight[0, 0] * seafloor.reshape(sea_count)
     slots = patch_slot[node_patch[0, 0]]
+    sea_values = jnp.where(depth_index == root_tile, sea_values, 0.0)
     partial_slip = jnp.zeros((patch_slot.shape[0],), jnp.float32).at[slots].add(sea_values)
-    slip_grad = summed_on_arrival(partial_slip, ("gx", "gy"), 0)
-    slip_grad = picked(slip_grad, "gz", root_tile)
-    slip_grad = lax.dynamic_slice_in_dim(slip_grad, depth_index * piece_count, piece_count)
+    slip_grad = lax.psum_scatter(partial_slip, ("gx", "gy", "gz"), scatter_dimension=0, tiled=True)
     return (pressure, velocity, slip_grad)
 
 

time: 218 us -> 242 us (1.11)
  blocking collectives: 10.1 us -> 78.1 us
  starting transfers between devices: 73 us -> 40.9 us
  local copies, waits for them, and re-layouts: 64.9 us -> 58 us
  other arithmetic: 43.6 us -> 38.9 us
    unnamed x0 -> x1, blocking collectives: none -> 78.1 us
    ppermute x9 -> x6, starting transfers between devices: 49.8 us -> 29.7 us  [extended(): lax.ppermute(lax.slice_in_dim(block, block.shape[dim] - width, None, axis...]
    all_gather x1 -> x0, blocking collectives: 10.1 us -> none  [picked(): lax.all_gather(x, axis)]
    all_to_all x1 -> x0, starting transfers between devices: 9.29 us -> none  [summed_on_arrival(): parts = lax.all_to_all(in_blocks(x, dim, size), axis, 0, 0, tiled=True)]
    all_to_all x1 -> x0, waiting for transfers between devices: 6.87 us -> none  [summed_on_arrival(): parts = lax.all_to_all(in_blocks(x, dim, size), axis, 0, 0, tiled=True)]
    ppermute x9 -> x6, waiting for transfers between devices: 14.4 us -> 18.8 us  [extended(): lax.ppermute(lax.slice_in_dim(block, 0, width, axis=dim), axis, backward)]
    ppermute x6 -> x4, local copies, waits for them, and re-layouts: 16.2 us -> 12.4 us  [extended(): lax.ppermute(lax.slice_in_dim(block, block.shape[dim] - width, None, axis...]
    ppermute x6 -> x4, local copies, waits for them, and re-layouts: 17 us -> 13.6 us  [extended(): lax.ppermute(lax.slice_in_dim(block, 0, width, axis=dim), axis, backward)]
  transfers between devices with their start and end apart: 19 -> 12, of which waited for: 6 -> 6; matrix products, arithmetic and copies ran while one was open for 27% -> 16% of each run, Pallas kernels for 0% -> 0%
where the time goes in v1:
time: 242 us; the launch traced here: 239 us
  blocking collectives  78.1 us (32%)
  local copies, waits for them, and re-layouts  58 us (24%)
  starting transfers between devices  40.9 us (17%)
  other arithmetic  38.9 us (16%)
  waiting for transfers between devices  21.4 us (9%)
    unnamed x1, blocking collectives  78.1 us
    ppermute x6, starting transfers between devices, extended(): lax.ppermute(lax.slice_in_dim(block, block.shape[dim] - width, None, axis...  29.7 us
    concatenate x6, other arithmetic, extended(): block = jnp.concatenate([low, block, high], axis=dim)  26.5 us
    concatenate x4, local copies, waits for them, and re-layouts, extended(): block = jnp.concatenate([low, block, high], axis=dim)  21.5 us
    ppermute x6, waiting for transfers between devices, extended(): lax.ppermute(lax.slice_in_dim(block, 0, width, axis=dim), axis, backward)  18.8 us
    ppermute x4, local copies, waits for them, and re-layouts, extended(): lax.ppermute(lax.slice_in_dim(block, 0, width, axis=dim), axis, backward)  13.6 us
    ppermute x4, local copies, waits for them, and re-layouts, extended(): lax.ppermute(lax.slice_in_dim(block, block.shape[dim] - width, None, axis...  12.4 us
    ppermute x6, starting transfers between devices, extended(): lax.ppermute(lax.slice_in_dim(block, 0, width, axis=dim), axis, backward)  11.2 us
  transfers between devices with their start and end apart: 12, of which 6 were waited for; matrix products, arithmetic and copies ran while one was open for 16% of the time, Pallas kernels for 0%

profile of v1, /device:TPU:24, one launch (start us, length us, event | category | flops | bytes accessed | tf_op | source)
XLA Modules:
  0.0 238.8 jit_solution(341130161772616501)
XLA Ops:
  1.7 8.8 %collective-permute-start = (f32[6,4,16,128]{3,2,1,0:T(8,128)S(1)}, f32[6,4,16,128]{3,2,1,0:T(8,128)S(1)}, u32[]{:S(2)}, u32[]{:S(2)}) collective-permute-start(f32[6,4,16,128]{3,2,1,0:T(8,128)S(1)} %get-tuple-element.32), channel_id=1, source_target_pairs={{0,32},{32,64},{64,96},{96,128},{128,160},{160,192},{192,224},{1,3... | collective-permute-start | bytes 589832 | tf_op jit(solution)/shard_map/ppermute | solution.py:18
  14.6 10.2 %collective-permute-done.1 = f32[6,4,16,128]{3,2,1,0:T(8,128)S(1)} collective-permute-done((f32[6,4,16,128]{3,2,1,0:T(8,128)S(1)}, f32[6,4,16,128]{3,2,1,0:T(8,128)S(1)}, u32[]{:S(2)}, u32[]{:S(2)}) %collective-permute-start.1) | collective-permute-done | bytes 196640 | tf_op jit(solution)/shard_map/ppermute | solution.py:21
  29.3 5.5 %copy.38 = f32[6,24,16,128]{2,1,3,0:T(8,128)} copy(f32[6,24,16,128]{3,2,1,0:T(8,128)S(1)} %pad_maximum_fusion.4) | data formatting | bytes 2359296 | tf_op jit(solution)/shard_map/concatenate | solution.py:22
  34.8 5.6 %copy.37 = f32[6,24,4,128]{2,1,3,0:T(8,128)} copy(f32[6,24,4,128]{3,1,2,0:T(8,128)S(1)} %collective-permute-done.2) | data formatting | bytes 589824 | tf_op jit(solution)/shard_map/ppermute | solution.py:18
  40.5 5.7 %copy.39 = f32[6,24,4,128]{2,1,3,0:T(8,128)} copy(f32[6,24,4,128]{3,1,2,0:T(8,128)S(1)} %collective-permute-done.3) | data formatting | bytes 589824 | tf_op jit(solution)/shard_map/ppermute | solution.py:21
  46.1 11.1 %pad_maximum_fusion = f32[6,24,24,128]{2,1,3,0:T(8,128)S(1)} fusion(f32[6,24,4,128]{2,1,3,0:T(8,128)} %copy.39, f32[6,24,16,128]{2,1,3,0:T(8,128)} %copy.38, f32[6,24,4,128]{2,1,3,0:T(8,128)} %copy.37), kind=kLoop, calls=%fused_computation.2 | loop fusion | flops 884736 | bytes 3538944 | tf_op jit(solution)/shard_map/concatenate | solution.py:22
  57.2 3.6 %copy-done.1 = f32[6,24,24,128]{2,1,3,0:T(8,128)} copy-done((f32[6,24,24,128]{2,1,3,0:T(8,128)}, f32[6,24,24,128]{2,1,3,0:T(8,128)S(1)}, u32[]{:S(2)}) %copy-start.1) | copy-done | bytes 1769496
  60.9 7.1 %collective-permute-start.4 = (f32[6,24,24,4]{2,1,3,0:T(8,128)S(1)}, f32[6,24,24,4]{2,1,3,0:T(8,128)S(1)}, u32[]{:S(2)}, u32[]{:S(2)}) collective-permute-start(f32[6,24,24,4]{2,1,3,0:T(8,128)S(1)} %get-tuple-element.10), channel_id=1, source_target_pairs={{0,1},{1,2},{2,3},{4,5},{5,6},{6,7},{8,9},{9,10},{10,11},{12,13},{... | collective-permute-start | bytes 165896 | tf_op jit(solution)/shard_map/ppermute | solution.py:18
  69.4 7.3 %copy.41 = f32[6,24,24,128]{3,2,1,0:T(8,128)} copy(f32[6,24,24,128]{2,1,3,0:T(8,128)} %copy-done.1) | data formatting | bytes 3538944 | tf_op jit(solution)/shard_map/concatenate | solution.py:22
  78.1 2.1 copy.42
  80.2 3.4 %pad_maximum_fusion.2 = f32[6,24,24,136]{3,2,1,0:T(8,128)S(1)} fusion(f32[6,24,24,4]{3,2,1,0:T(8,128)} %copy.42, f32[6,24,24,128]{3,2,1,0:T(8,128)} %copy.41, f32[6,24,24,4]{3,2,1,0:T(8,128)S(1)} %copy.40), kind=kLoop, calls=%fused_computation.4 | loop fusion | flops 940032 | bytes 3760128 | tf_op jit(solution)/shard_map/concatenate | solution.py:22
  88.8 3.9 %collective-permute-start.7 = (f32[4,4,16,128]{3,2,1,0:T(8,128)S(1)}, f32[4,4,16,128]{3,2,1,0:T(8,128)S(1)}, u32[]{:S(2)}, u32[]{:S(2)}) collective-permute-start(f32[4,4,16,128]{3,2,1,0:T(8,128)S(1)} %get-tuple-element.27), channel_id=1, source_target_pairs={{32,0},{64,32},{96,64},{128,96},{160,128},{192,160},{224,192},{33,... | collective-permute-start | bytes 393224 | tf_op jit(solution)/shard_map/ppermute | solution.py:21
  93.9 8.0 %collective-permute-done.7 = f32[4,4,16,128]{3,2,1,0:T(8,128)S(1)} collective-permute-done((f32[4,4,16,128]{3,2,1,0:T(8,128)S(1)}, f32[4,4,16,128]{3,2,1,0:T(8,128)S(1)}, u32[]{:S(2)}, u32[]{:S(2)}) %collective-permute-start.7) | collective-permute-done | bytes 131104 | tf_op jit(solution)/shard_map/ppermute | solution.py:21
  102.2 3.0 %collective-permute-start.8 = (f32[4,24,4,128]{3,1,2,0:T(8,128)S(1)}, f32[4,24,4,128]{3,1,2,0:T(8,128)S(1)}, u32[]{:S(2)}, u32[]{:S(2)}) collective-permute-start(f32[4,24,4,128]{3,1,2,0:T(8,128)S(1)} %copy.53), channel_id=1, source_target_pairs={{0,4},{4,8},{8,12},{12,16},{16,20},{20,24},{24,28},{1,5},{5,9},{9,... | collective-permute-start | bytes 589832 | tf_op jit(solution)/shard_map/ppermute | solution.py:18
  108.5 4.3 %copy.46 = f32[4,24,16,128]{2,1,3,0:T(8,128)} copy(f32[4,24,16,128]{3,2,1,0:T(8,128)S(1)} %fusion.1) | data formatting | bytes 1572864 | tf_op jit(solution)/shard_map/concatenate | solution.py:22
  112.8 4.3 %copy.45 = f32[4,24,4,128]{2,1,3,0:T(8,128)} copy(f32[4,24,4,128]{3,1,2,0:T(8,128)S(1)} %collective-permute-done.8) | data formatting | bytes 393216 | tf_op jit(solution)/shard_map/ppermute | solution.py:18
  117.0 4.1 %copy.47 = f32[4,24,4,128]{2,1,3,0:T(8,128)} copy(f32[4,24,4,128]{3,1,2,0:T(8,128)S(1)} %collective-permute-done.9) | data formatting | bytes 393216 | tf_op jit(solution)/shard_map/ppermute | solution.py:21
  121.2 8.1 %pad_maximum_fusion.1 = f32[4,24,24,128]{2,1,3,0:T(8,128)S(1)} fusion(f32[4,24,4,128]{2,1,3,0:T(8,128)} %copy.47, f32[4,24,16,128]{2,1,3,0:T(8,128)} %copy.46, f32[4,24,4,128]{2,1,3,0:T(8,128)} %copy.45), kind=kLoop, calls=%fused_computation.3 | loop fusion | flops 589824 | bytes 2359296 | tf_op jit(solution)/shard_map/concatenate | solution.py:22
  129.3 2.6 %copy-done.4 = f32[4,24,24,128]{2,1,3,0:T(8,128)} copy-done((f32[4,24,24,128]{2,1,3,0:T(8,128)}, f32[4,24,24,128]{2,1,3,0:T(8,128)S(1)}, u32[]{:S(2)}) %copy-start.4) | copy-done | bytes 1179672
  132.0 7.7 %collective-permute-start.10 = (f32[4,24,24,4]{2,1,3,0:T(8,128)S(1)}, f32[4,24,24,4]{2,1,3,0:T(8,128)}, u32[]{:S(2)}, u32[]{:S(2)}) collective-permute-start(f32[4,24,24,4]{2,1,3,0:T(8,128)S(1)} %get-tuple-element.15), channel_id=1, source_target_pairs={{0,1},{1,2},{2,3},{4,5},{5,6},{6,7},{8,9},{9,10},{10,11},{12,13},{... | collective-permute-start | bytes 110600 | tf_op jit(solution)/shard_map/ppermute | solution.py:18
  141.2 4.4 %copy.49 = f32[4,24,24,128]{3,2,1,0:T(8,128)S(1)} copy(f32[4,24,24,128]{2,1,3,0:T(8,128)} %copy-done.4) | data formatting | bytes 2359296 | tf_op jit(solution)/shard_map/concatenate | solution.py:22
  148.9 2.4 %pad_maximum_fusion.3 = f32[4,24,24,136]{3,2,1,0:T(8,128)S(1)} fusion(f32[4,24,24,4]{3,2,1,0:T(8,128)} %copy.50, f32[4,24,24,128]{3,2,1,0:T(8,128)S(1)} %copy.49, f32[4,24,24,4]{3,2,1,0:T(8,128)S(1)} %copy.48), kind=kLoop, calls=%fused_computation.5 | loop fusion | flops 626688 | bytes 2506752 | tf_op jit(solution)/shard_map/concatenate | solution.py:22
  154.8 2.0 scatter_custom_fusion
  156.7 78.1 %all-reduce.16 = f32[8192]{0:T(1024)S(1)} all-reduce(f32[8192]{0:T(1024)S(1)} %scatter_custom_fusion), channel_id=2, replica_groups=mesh['gx'=8,'gy'=8,'gz'=4] {'gx','gy','gz'}, use_global_device_ids=true, to_apply=%region_1.2.clone | all-reduce | flops 8192 | bytes 65536
  (78 shorter events, 34.3 us)
Async XLA Ops:
  0.6 106.1 %copy-start = (s32[8192]{0:T(1024)S(1)}, s32[8192]{0:T(1024)}, u32[]{:S(2)}) copy-start(s32[8192]{0:T(1024)} %param.16) | copy-start | bytes 98308
  0.6 28.2 %copy-start.8 = (f32[4,256]{1,0:T(4,128)S(1)}, f32[4,256]{1,0:T(4,128)}, u32[]{:S(2)}) copy-start(f32[4,256]{1,0:T(4,128)} %param.19) | copy-start | bytes 12292
  1.7 12.9 %collective-permute-start = (f32[6,4,16,128]{3,2,1,0:T(8,128)S(1)}, f32[6,4,16,128]{3,2,1,0:T(8,128)S(1)}, u32[]{:S(2)}, u32[]{:S(2)}) collective-permute-start(f32[6,4,16,128]{3,2,1,0:T(8,128)S(1)} %get-tuple-element.32), channel_id=1, source_target_pairs={{0,32},{32,64},{64,96},{96,128},{128,160},{160,192},{192,224},{1,3... | collective-permute-start | bytes 589832 | tf_op jit(solution)/shard_map/ppermute | solution.py:18
  10.5 14.4 %collective-permute-start.1 = (f32[6,4,16,128]{3,2,1,0:T(8,128)S(1)}, f32[6,4,16,128]{3,2,1,0:T(8,128)S(1)}, u32[]{:S(2)}, u32[]{:S(2)}) collective-permute-start(f32[6,4,16,128]{3,2,1,0:T(8,128)S(1)} %get-tuple-element.33), channel_id=1, source_target_pairs={{32,0},{64,32},{96,64},{128,96},{160,128},{192,160},{224,192},{33,... | collective-permute-start | bytes 589832 | tf_op jit(solution)/shard_map/ppermute | solution.py:21
  26.2 8.6 %collective-permute-start.2 = (f32[6,24,4,128]{3,1,2,0:T(8,128)S(1)}, f32[6,24,4,128]{3,1,2,0:T(8,128)S(1)}, u32[]{:S(2)}, u32[]{:S(2)}) collective-permute-start(f32[6,24,4,128]{3,1,2,0:T(8,128)S(1)} %copy.51), channel_id=1, source_target_pairs={{0,4},{4,8},{8,12},{12,16},{16,20},{20,24},{24,28},{1,5},{5,9},{9,... | collective-permute-start | bytes 884744 | tf_op jit(solution)/shard_map/ppermute | solution.py:18
  27.6 12.9 %collective-permute-start.3 = (f32[6,24,4,128]{3,1,2,0:T(8,128)S(1)}, f32[6,24,4,128]{3,1,2,0:T(8,128)S(1)}, u32[]{:S(2)}, u32[]{:S(2)}) collective-permute-start(f32[6,24,4,128]{3,1,2,0:T(8,128)S(1)} %copy.52), channel_id=1, source_target_pairs={{4,0},{8,4},{12,8},{16,12},{20,16},{24,20},{28,24},{5,1},{9,5},{13... | collective-permute-start | bytes 884744 | tf_op jit(solution)/shard_map/ppermute | solution.py:21
  57.2 3.7 %copy-start.1 = (f32[6,24,24,128]{2,1,3,0:T(8,128)}, f32[6,24,24,128]{2,1,3,0:T(8,128)S(1)}, u32[]{:S(2)}) copy-start(f32[6,24,24,128]{2,1,3,0:T(8,128)S(1)} %pad_maximum_fusion) | copy-start | bytes 5308420
  60.9 15.9 %collective-permute-start.4 = (f32[6,24,24,4]{2,1,3,0:T(8,128)S(1)}, f32[6,24,24,4]{2,1,3,0:T(8,128)S(1)}, u32[]{:S(2)}, u32[]{:S(2)}) collective-permute-start(f32[6,24,24,4]{2,1,3,0:T(8,128)S(1)} %get-tuple-element.10), channel_id=1, source_target_pairs={{0,1},{1,2},{2,3},{4,5},{5,6},{6,7},{8,9},{9,10},{10,11},{12,13},{... | collective-permute-start | bytes 165896 | tf_op jit(solution)/shard_map/ppermute | solution.py:18
  68.0 10.1 %collective-permute-start.5 = (f32[6,24,24,4]{2,1,3,0:T(8,128)S(1)}, f32[6,24,24,4]{2,1,3,0:T(8,128)S(1)}, u32[]{:S(2)}, u32[]{:S(2)}) collective-permute-start(f32[6,24,24,4]{2,1,3,0:T(8,128)S(1)} %get-tuple-element.11), channel_id=1, source_target_pairs={{1,0},{2,1},{3,2},{5,4},{6,5},{7,6},{9,8},{10,9},{11,10},{13,12},{... | collective-permute-start | bytes 165896 | tf_op jit(solution)/shard_map/ppermute | solution.py:21
  83.7 2.3 copy-start.2
  83.7 1.0 copy-start.5
  86.7 20.0 %copy-start.7 = (s32[1,1,256]{2,1,0:T(1,128)S(1)}, s32[1,1,256]{2,1,0:T(1,128)}, u32[]{:S(2)}) copy-start(s32[1,1,256]{2,1,0:T(1,128)} %param.15) | copy-start | bytes 3076
  86.8 7.0 %collective-permute-start.6 = (f32[4,4,16,128]{3,2,1,0:T(8,128)S(1)}, f32[4,4,16,128]{3,2,1,0:T(8,128)S(1)}, u32[]{:S(2)}, u32[]{:S(2)}) collective-permute-start(f32[4,4,16,128]{3,2,1,0:T(8,128)S(1)} %get-tuple-element.26), channel_id=1, source_target_pairs={{0,32},{32,64},{64,96},{96,128},{128,160},{160,192},{192,224},{1,3... | collective-permute-start | bytes 393224 | tf_op jit(solution)/shard_map/ppermute | solution.py:18
  88.8 13.1 %collective-permute-start.7 = (f32[4,4,16,128]{3,2,1,0:T(8,128)S(1)}, f32[4,4,16,128]{3,2,1,0:T(8,128)S(1)}, u32[]{:S(2)}, u32[]{:S(2)}) collective-permute-start(f32[4,4,16,128]{3,2,1,0:T(8,128)S(1)} %get-tuple-element.27), channel_id=1, source_target_pairs={{32,0},{64,32},{96,64},{128,96},{160,128},{192,160},{224,192},{33,... | collective-permute-start | bytes 393224 | tf_op jit(solution)/shard_map/ppermute | solution.py:21
  102.2 10.5 %collective-permute-start.8 = (f32[4,24,4,128]{3,1,2,0:T(8,128)S(1)}, f32[4,24,4,128]{3,1,2,0:T(8,128)S(1)}, u32[]{:S(2)}, u32[]{:S(2)}) collective-permute-start(f32[4,24,4,128]{3,1,2,0:T(8,128)S(1)} %copy.53), channel_id=1, source_target_pairs={{0,4},{4,8},{8,12},{12,16},{16,20},{20,24},{24,28},{1,5},{5,9},{9,... | collective-permute-start | bytes 589832 | tf_op jit(solution)/shard_map/ppermute | solution.py:18
  105.3 11.8 %collective-permute-start.9 = (f32[4,24,4,128]{3,1,2,0:T(8,128)S(1)}, f32[4,24,4,128]{3,1,2,0:T(8,128)S(1)}, u32[]{:S(2)}, u32[]{:S(2)}) collective-permute-start(f32[4,24,4,128]{3,1,2,0:T(8,128)S(1)} %copy.54), channel_id=1, source_target_pairs={{4,0},{8,4},{12,8},{16,12},{20,16},{24,20},{28,24},{5,1},{9,5},{13... | collective-permute-start | bytes 589832 | tf_op jit(solution)/shard_map/ppermute | solution.py:21
  129.3 2.7 %copy-start.4 = (f32[4,24,24,128]{2,1,3,0:T(8,128)}, f32[4,24,24,128]{2,1,3,0:T(8,128)S(1)}, u32[]{:S(2)}) copy-start(f32[4,24,24,128]{2,1,3,0:T(8,128)S(1)} %pad_maximum_fusion.1) | copy-start | bytes 3538948
  132.0 13.5 %collective-permute-start.10 = (f32[4,24,24,4]{2,1,3,0:T(8,128)S(1)}, f32[4,24,24,4]{2,1,3,0:T(8,128)}, u32[]{:S(2)}, u32[]{:S(2)}) collective-permute-start(f32[4,24,24,4]{2,1,3,0:T(8,128)S(1)} %get-tuple-element.15), channel_id=1, source_target_pairs={{0,1},{1,2},{2,3},{4,5},{5,6},{6,7},{8,9},{9,10},{10,11},{12,13},{... | collective-permute-start | bytes 110600 | tf_op jit(solution)/shard_map/ppermute | solution.py:18
  139.7 7.6 %collective-permute-start.11 = (f32[4,24,24,4]{2,1,3,0:T(8,128)S(1)}, f32[4,24,24,4]{2,1,3,0:T(8,128)S(1)}, u32[]{:S(2)}, u32[]{:S(2)}) collective-permute-start(f32[4,24,24,4]{2,1,3,0:T(8,128)S(1)} %get-tuple-element.16), channel_id=1, source_target_pairs={{1,0},{2,1},{3,2},{5,4},{6,5},{7,6},{9,8},{10,9},{11,10},{13,12},{... | collective-permute-start | bytes 110600 | tf_op jit(solution)/shard_map/ppermute | solution.py:21
  148.9 2.5 %copy-start.3 = (f32[6,24,24,136]{3,2,1,0:T(8,128)S(1)}, f32[6,24,24,136]{3,2,1,0:T(8,128)}, u32[]{:S(2)}) copy-start(f32[6,24,24,136]{3,2,1,0:T(8,128)} %copy-done.2) | copy-start | bytes 5640196
  152.6 2.2 copy-start.6

commit v2 on v0

v2 whole, which is shorter than its diff:
```python
import functools

import jax
import jax.numpy as jnp
from jax import lax
from jax.experimental import pallas as pl
from jax.experimental.pallas import tpu as pltpu
from jax.sharding import PartitionSpec as P

ITERS = 4


time_step = 0.5


def shifted_up(x, axis):
    count = lax.axis_size(axis)
    return lax.ppermute(x, axis, [(i, i + 1) for i in range(count - 1)])


def shifted_down(x, axis):
    count = lax.axis_size(axis)
    return lax.ppermute(x, axis, [(i + 1, i) for i in range(count - 1)])


def in_blocks(x, dim, size):
    before, after = (x.shape[:dim], x.shape[dim + 1 :])
    return jnp.moveaxis(x.reshape(*before, size, -1, *after), dim, 0)


def summed_on_arrival(x, axis, dim):
    size = lax.axis_size(axis)
    parts = lax.all_to_all(in_blocks(x, dim, size), axis, 0, 0, tiled=True)
    return jnp.sum(parts, axis=0)


def picked(x, axis, root):
    return lax.dynamic_index_in_dim(lax.all_gather(x, axis), root, 0, keepdims=False)


def depth_weights(levels, first_crust):
    ocean_last = levels == first_crust - 1
    crust_first = levels == first_crust
    weight_above = jnp.where(ocean_last, 0.5, jnp.where(crust_first, 1.0, 0.5)).astype(jnp.float32)
    weight_here = jnp.where(ocean_last, 0.5, jnp.where(crust_first, -1.5, 0.0)).astype(jnp.float32)
    weight_below = jnp.where(ocean_last, -1.0, jnp.where(crust_first, 0.5, -0.5)).astype(
        jnp.float32
    )
    return (weight_above, weight_here, weight_below)


def source_planes(gauge_x, gauge_y, gauge_misfit, start_x, start_y, span_x, span_y):
    local_x = gauge_x - start_x
    local_y = gauge_y - start_y
    inside = (local_x >= 0) & (local_x < span_x) & (local_y >= 0) & (local_y < span_y)
    gauge_cell = jnp.where(inside, local_x * span_y + local_y, -1)
    gauge_table = (
        gauge_cell[:, None] == jnp.arange(span_x * span_y, dtype=jnp.int32)[None, :]
    ).astype(jnp.float32)
    return jnp.dot(gauge_misfit, gauge_table, precision=lax.Precision.HIGHEST).reshape(
        gauge_misfit.shape[0], span_x, span_y
    )


def pick(a, axis, index):
    where = lax.broadcasted_iota(jnp.int32, a.shape, a.ndim + axis if axis < 0 else axis) == index
    return jnp.sum(jnp.where(where, a, 0.0), axis=axis, keepdims=True)


def pair(lo, hi, shape, axis):
    where = lax.broadcasted_iota(jnp.int32, shape, axis) == 0
    return jnp.where(where, jnp.broadcast_to(lo, shape), jnp.broadcast_to(hi, shape))


def step_kernel(
    scal_ref,
    wint_ref,
    p_ref,
    v_ref,
    idn_ref,
    bulk_ref,
    src_ref,
    sf_ref,
    pxl_ref,
    pxh_ref,
    pyl_ref,
    pyh_ref,
    pzl_ref,
    pzh_ref,
    vx_ref,
    vy_ref,
    vz_ref,
    ix_ref,
    iy_ref,
    iz_ref,
    po_ref,
    vo_ref,
    sfo_ref,
    vxo_ref,
    vyo_ref,
    vzo_ref,
    sxu_ref,
    sxd_ref,
    syu_ref,
    syd_ref,
    szu_ref,
    szd_ref,
):
    X, Y, Z = p_ref.shape
    rows = pyl_ref.shape[1]
    full = (X, Y, Z)
    yi = lax.broadcasted_iota(jnp.int32, full, 1)
    zi = lax.broadcasted_iota(jnp.int32, full, 2)
    wu = wint_ref[0]
    wm = wint_ref[1]
    wl = wint_ref[2]
    wu_lo = scal_ref[0]
    wm_lo = scal_ref[1]
    wl_lo = scal_ref[2]
    wu_hi = scal_ref[3]
    wm_hi = scal_ref[4]
    wl_hi = scal_ref[5]
    f_ocean = scal_ref[6]
    f_crust = scal_ref[7]

    pres = p_ref[...]
    idn = idn_ref[...]

    p_first = pick(pres, -1, 0)
    p_last = pick(pres, -1, Z - 1)
    pzl = pzl_ref[...]
    pzh = pzh_ref[...]
    zl2 = pick(pzl, -1, 0)
    zl1 = pick(pzl, -1, 1)
    zh1 = pick(pzh, -1, 0)
    zh2 = pick(pzh, -1, 1)
    sfo_ref[...] = sf_ref[...] + 0.5 * (f_ocean * (p_last + zh1) + f_crust * (zl1 + p_first))

    pxl = pxl_ref[...]
    pxh = pxh_ref[...]
    above_x = jnp.concatenate([pres[1:], pxh[0:1]], axis=0)
    below_x = jnp.concatenate([pxl[1:2], pres[:-1]], axis=0)
    slope_x = 0.5 * (above_x - below_x)
    v0 = v_ref[0] - time_step * idn * slope_x
    vx = vx_ref[...]
    ix = ix_ref[...]
    v0_lo = vx[0:1] - time_step * ix[0:1] * (0.5 * (pres[0:1] - pxl[0:1]))
    v0_hi = vx[1:2] - time_step * ix[1:2] * (0.5 * (pxh[1:2] - pres[X - 1 : X]))

    pyl = pyl_ref[...]
    pyh = pyh_ref[...]
    yl1 = pick(pyl, 1, rows - 1)
    yl2 = pick(pyl, 1, rows - 2)
    yh1 = pick(pyh, 1, 0)
    yh2 = pick(pyh, 1, 1)
    p_y0 = pick(pres, 1, 0)
    p_yl = pick(pres, 1, Y - 1)
    above_y = jnp.where(yi == Y - 1, jnp.broadcast_to(yh1, full), pltpu.roll(pres, Y - 1, 1))
    below_y = jnp.where(yi == 0, jnp.broadcast_to(yl1, full), pltpu.roll(pres, 1, 1))
    slope_y = 0.5 * (above_y - below_y)
    v1 = v_ref[1] - time_step * idn * slope_y
    vy = vy_ref[...]
    iy = iy_ref[...]
    v1_lo = pick(vy, 1, 0) - time_step * pick(iy, 1, 0) * (0.5 * (p_y0 - yl2))
    v1_hi = pick(vy, 1, 1) - time_step * pick(iy, 1, 1) * (0.5 * (yh2 - p_yl))

    above_z = jnp.where(zi == Z - 1, jnp.broadcast_to(zh1, full), pltpu.roll(pres, Z - 1, 2))
    below_z = jnp.where(zi == 0, jnp.broadcast_to(zl1, full), pltpu.roll(pres, 1, 2))
    slope_z = wu * above_z + wm * pres + wl * below_z
    v2 = v_ref[2] - time_step * idn * slope_z
    vz = vz_ref[...]
    iz = iz_ref[...]
    v2_lo = pick(vz, -1, 0) - time_step * pick(iz, -1, 0) * (wu_lo * p_first + wm_lo * zl1 + wl_lo * zl2)
    v2_hi = pick(vz, -1, 1) - time_step * pick(iz, -1, 1) * (wu_hi * zh2 + wm_hi * zh1 + wl_hi * p_last)

    vo_ref[0] = v0
    vo_ref[1] = v1
    vo_ref[2] = v2
    vxo_ref[0:1] = v0_lo
    vxo_ref[1:2] = v0_hi
    vyo_ref[...] = pair(v1_lo, v1_hi, vyo_ref.shape, 1)
    vzo_ref[...] = pair(v2_lo, v2_hi, vzo_ref.shape, 2)

    up_x = jnp.concatenate([v0[1:], v0_hi], axis=0)
    down_x = jnp.concatenate([v0_lo, v0[:-1]], axis=0)
    up_y = jnp.where(yi == Y - 1, jnp.broadcast_to(v1_hi, full), pltpu.roll(v1, Y - 1, 1))
    down_y = jnp.where(yi == 0, jnp.broadcast_to(v1_lo, full), pltpu.roll(v1, 1, 1))
    up_z = jnp.where(zi == Z - 1, jnp.broadcast_to(v2_hi, full), pltpu.roll(v2, Z - 1, 2))
    down_z = jnp.where(zi == 0, jnp.broadcast_to(v2_lo, full), pltpu.roll(v2, 1, 2))
    spread = (
        0.5 * (up_x - down_x)
        + 0.5 * (up_y - down_y)
        + (wu * up_z + wm * v2 + wl * down_z)
    )
    new_p = pres - time_step * bulk_ref[...] * spread
    new_p = jnp.where(zi == 0, new_p + jnp.broadcast_to(src_ref[...], full), new_p)
    po_ref[...] = new_p

    sxu_ref[...] = new_p[X - 2 :]
    sxd_ref[...] = new_p[0:2]
    syu_ref[...] = new_p[:, Y - rows :]
    syd_ref[...] = new_p[:, 0:rows]
    zshape = szu_ref.shape
    szu_ref[...] = pair(pick(new_p, -1, Z - 2), pick(new_p, -1, Z - 1), zshape, 2)
    szd_ref[...] = pair(pick(new_p, -1, 0), pick(new_p, -1, 1), zshape, 2)


def run_step(scal, wint, pres, vel, idn, bulk, src, sf, halos, tracked, media_halo):
    X, Y, Z = pres.shape
    rows = halos[2].shape[1]
    f32 = jnp.float32
    shapes = (
        jax.ShapeDtypeStruct((X, Y, Z), f32),
        jax.ShapeDtypeStruct((3, X, Y, Z), f32),
        jax.ShapeDtypeStruct((X, Y, 1), f32),
        jax.ShapeDtypeStruct((2, Y, Z), f32),
        jax.ShapeDtypeStruct((X, 2, Z), f32),
        jax.ShapeDtypeStruct((X, Y, 2), f32),
        jax.ShapeDtypeStruct((2, Y, Z), f32),
        jax.ShapeDtypeStruct((2, Y, Z), f32),
        jax.ShapeDtypeStruct((X, rows, Z), f32),
        jax.ShapeDtypeStruct((X, rows, Z), f32),
        jax.ShapeDtypeStruct((X, Y, 2), f32),
        jax.ShapeDtypeStruct((X, Y, 2), f32),
    )
    vmem = pl.BlockSpec(memory_space=pltpu.VMEM)
    in_specs = [pl.BlockSpec(memory_space=pltpu.SMEM)] + [vmem] * 19
    cells = X * Y * Z
    return pl.pallas_call(
        step_kernel,
        out_shape=shapes,
        in_specs=in_specs,
        out_specs=[vmem] * len(shapes),
        cost_estimate=pl.CostEstimate(
            flops=80 * cells, transcendentals=0, bytes_accessed=4 * 4 * 12 * cells // 4
        ),
    )(scal, wint, pres, vel, idn, bulk, src, sf, *halos, *tracked, *media_halo)


def local(
    pressure,
    velocity,
    inv_density,
    bulk,
    node_weight,
    node_patch,
    patch_slot,
    gauge_x,
    gauge_y,
    gauge_misfit,
):
    X, Y, Z = pressure.shape
    rows = 8
    tiles_z = lax.axis_size("gz")
    depth_index = lax.axis_index("gz")
    first_crust = tiles_z // 2 * Z
    levels = depth_index * Z + jnp.arange(Z, dtype=jnp.int32)
    wint = jnp.stack(depth_weights(levels, first_crust)).reshape(3, 1, 1, Z)
    edge_levels = jnp.stack([depth_index * Z - 1, depth_index * Z + Z])
    edge_w = depth_weights(edge_levels, first_crust)
    ocean_flag = (depth_index == first_crust // Z - 1).astype(jnp.float32)
    crust_flag = (depth_index == first_crust // Z).astype(jnp.float32)
    scal = jnp.stack(
        [edge_w[0][0], edge_w[1][0], edge_w[2][0], edge_w[0][1], edge_w[1][1], edge_w[2][1],
         ocean_flag, crust_flag]
    ).astype(jnp.float32)
    top_flag = (depth_index == 0).astype(jnp.float32)
    sources = source_planes(
        gauge_x,
        gauge_y,
        gauge_misfit,
        lax.axis_index("gx") * X,
        lax.axis_index("gy") * Y,
        X,
        Y,
    )
    src_all = (time_step * sources * top_flag)[..., None]

    v0, v1, v2 = velocity[0], velocity[1], velocity[2]
    x_up = jnp.concatenate([pressure[X - 2 :], v0[X - 1 :], inv_density[X - 1 :]], axis=0)
    x_dn = jnp.concatenate([pressure[:2], v0[:1], inv_density[:1]], axis=0)
    y_up = jnp.concatenate(
        [pressure[:, Y - rows :], v1[:, Y - 1 :], inv_density[:, Y - 1 :]], axis=1
    )
    y_dn = jnp.concatenate([pressure[:, :rows], v1[:, :1], inv_density[:, :1]], axis=1)
    z_up = jnp.concatenate(
        [pressure[:, :, Z - 2 :], v2[:, :, Z - 1 :], inv_density[:, :, Z - 1 :]], axis=2
    )
    z_dn = jnp.concatenate([pressure[:, :, :2], v2[:, :, :1], inv_density[:, :, :1]], axis=2)
    rx_lo = shifted_up(x_up, "gx")
    rx_hi = shifted_down(x_dn, "gx")
    ry_lo = shifted_up(y_up, "gy")
    ry_hi = shifted_down(y_dn, "gy")
    rz_lo = shifted_up(z_up, "gz")
    rz_hi = shifted_down(z_dn, "gz")
    halos = (
        rx_lo[:2],
        rx_hi[:2],
        ry_lo[:, :rows],
        ry_hi[:, :rows],
        rz_lo[:, :, :2],
        rz_hi[:, :, :2],
    )
    tracked = (
        jnp.concatenate([rx_lo[2:3], rx_hi[2:3]], axis=0),
        jnp.concatenate([ry_lo[:, rows : rows + 1], ry_hi[:, rows : rows + 1]], axis=1),
        jnp.concatenate([rz_lo[:, :, 2:3], rz_hi[:, :, 2:3]], axis=2),
    )
    media_halo = (
        jnp.concatenate([rx_lo[3:4], rx_hi[3:4]], axis=0),
        jnp.concatenate([ry_lo[:, rows + 1 : rows + 2], ry_hi[:, rows + 1 : rows + 2]], axis=1),
        jnp.concatenate([rz_lo[:, :, 3:4], rz_hi[:, :, 3:4]], axis=2),
    )
    sf = jnp.zeros((X, Y, 1), jnp.float32)
    pres, vel = pressure, velocity
    for instant in range(ITERS):
        if instant > 0:
            halos = (
                shifted_up(sends[0], "gx"),
                shifted_down(sends[1], "gx"),
                shifted_up(sends[2], "gy"),
                shifted_down(sends[3], "gy"),
                shifted_up(sends[4], "gz"),
                shifted_down(sends[5], "gz"),
            )
        outs = run_step(
            scal, wint, pres, vel, inv_density, bulk, src_all[instant], sf, halos, tracked,
            media_halo,
        )
        pres, vel, sf = outs[0], outs[1], outs[2]
        tracked = outs[3:6]
        sends = outs[6:12]
    seafloor = sf[:, :, 0]

    sea_count = X * Y
    owners_count = lax.axis_size("gx") * lax.axis_size("gy")
    patch_count = patch_slot.shape[0] // owners_count
    piece_count = patch_count // tiles_z
    root_tile = first_crust // Z
    sea_values = node_weight[0, 0] * seafloor.reshape(sea_count)
    slots = patch_slot[node_patch[0, 0]]
    partial_slip = jnp.zeros((patch_slot.shape[0],), jnp.float32).at[slots].add(sea_values)
    slip_grad = summed_on_arrival(partial_slip, ("gx", "gy"), 0)
    slip_grad = picked(slip_grad, "gz", root_tile)
    slip_grad = lax.dynamic_slice_in_dim(slip_grad, depth_index * piece_count, piece_count)
    return (pres, vel, slip_grad)


def solution(mesh):
    placed = (
        P("gx", "gy", "gz"),
        P(None, "gx", "gy", "gz"),
        P("gx", "gy", "gz"),
        P("gx", "gy", "gz"),
        P("gx", "gy", None),
        P("gx", "gy", None),
        P(),
        P(),
        P(),
        P(),
    )
    return jax.shard_map(
        local,
        mesh=mesh,
        in_specs=placed,
        out_specs=(P("gx", "gy", "gz"), P(None, "gx", "gy", "gz"), P(("gx", "gy", "gz"))),
        check_vma=False,
    )
```

time: 218 us -> 181 us (0.83)
  local copies, waits for them, and re-layouts: 64.9 us -> 24 us
  other arithmetic: 43.6 us -> 5.86 us
  waiting for transfers between devices: 22.6 us -> 44.3 us
  Pallas kernels: 0 us -> 13.3 us
  starting transfers between devices: 73 us -> 80.3 us
    ppermute x12 -> x0, local copies, waits for them, and re-layouts: 33.2 us -> none  [the longest x6 17 us: extended(): lax.ppermute(lax.slice_in_dim(block, 0, width, axis=dim), axis, backward)]
    concatenate x10 -> x9, other arithmetic: 29.7 us -> 2.19 us  [the longest x1 0.84 us: local(): jnp.concatenate([rz_lo[:, :, 2:3], rz_hi[:, :, 2:3]], axis=2)]
    concatenate x6 -> x2, local copies, waits for them, and re-layouts: 22 us -> 0.35 us  [the longest x1 0.17 us: local(): jnp.concatenate([pressure[:, :, Z - 2:], v2[:, :, Z - 1:], inv_density[:,...]
    ppermute x18 -> x24, waiting for transfers between devices: 15.7 us -> 33.8 us  [the longest x12 30.3 us: shifted_down(): return lax.ppermute(x, axis, [(i + 1, i) for i in range(count - 1)])]
    pallas_call x0 -> x4, Pallas kernels: none -> 13.3 us  [run_step(): pl.pallas_call(step_kernel, out_shape=shapes, in_specs=in_specs, out_spec...]
    slice x6 -> x23, local copies, waits for them, and re-layouts: 0.88 us -> 6.02 us  [the longest x1 0.99 us: local(): v0, v1, v2 = (velocity[0], velocity[1], velocity[2])]
    ppermute x18 -> x24, starting transfers between devices: 63.7 us -> 68.5 us  [the longest x12 47.2 us: shifted_up(): return lax.ppermute(x, axis, [(i, i + 1) for i in range(count - 1)])]
    another operation x0 -> x2, local copies, waits for them, and re-layouts: none -> 4.56 us  [the longest x1 4.48 us: local(): jnp.stack([edge_w[0][0], edge_w[1][0], edge_w[2][0], edge_w[0][1], edge_w...]
  transfers between devices with their start and end apart: 19 -> 25, of which waited for: 6 -> 6; matrix products, arithmetic and copies ran while one was open for 27% -> 9% of each run, Pallas kernels for 0% -> 0%
where the time goes in v2:
time: 181 us; the launch traced here: 180 us
  starting transfers between devices  80.3 us (44%)
  waiting for transfers between devices  44.3 us (24%)
  local copies, waits for them, and re-layouts  24 us (13%)
  Pallas kernels  13.3 us (7%)
  blocking collectives  10.1 us (6%)
  other arithmetic  5.86 us (3%)
    ppermute x12, starting transfers between devices, shifted_up(): return lax.ppermute(x, axis, [(i, i + 1) for i in range(count - 1)])  47.2 us
    ppermute x12, waiting for transfers between devices, shifted_down(): return lax.ppermute(x, axis, [(i + 1, i) for i in range(count - 1)])  30.3 us
    ppermute x12, starting transfers between devices, shifted_down(): return lax.ppermute(x, axis, [(i + 1, i) for i in range(count - 1)])  21.3 us
    pallas_call x4, Pallas kernels, run_step(): pl.pallas_call(step_kernel, out_shape=shapes, in_specs=in_specs, out_spec...  13.3 us
    all_to_all x1, starting transfers between devices, summed_on_arrival(): parts = lax.all_to_all(in_blocks(x, dim, size), axis, 0, 0, tiled=True)  11.8 us
    all_to_all x1, waiting for transfers between devices, summed_on_arrival(): parts = lax.all_to_all(in_blocks(x, dim, size), axis, 0, 0, tiled=True)  10.5 us
    all_gather x1, blocking collectives, picked(): lax.all_gather(x, axis)  10.1 us
    unnamed x71, local copies, waits for them, and re-layouts  6.09 us
  transfers between devices with their start and end apart: 25, of which 6 were waited for; matrix products, arithmetic and copies ran while one was open for 9% of the time, Pallas kernels for 0%

profile of v2, /device:TPU:24, one launch (start us, length us, event | category | flops | bytes accessed | tf_op | source)
XLA Modules:
  0.0 179.5 jit_solution(4346088135513712303)
XLA Ops:
  4.0 3.8 %collective-permute-start.4 = (f32[16,16,4]{2,1,0:T(8,128)S(1)}, f32[16,16,4]{2,1,0:T(8,128)S(1)}, u32[]{:S(2)}, u32[]{:S(2)}) collective-permute-start(f32[16,16,4]{2,1,0:T(8,128)S(1)} %copy.51), channel_id=1, source_target_pairs={{0,1},{1,2},{2,3},{4,5},{5,6},{6,7},{8,9},{9,10},{10,11},{12,13},{... | collective-permute-start | bytes 12296 | tf_op jit(solution)/shard_map/ppermute | solution.py:18
  11.1 3.0 %collective-permute-start.2 = (f32[16,10,128]{2,1,0:T(8,128)S(1)}, f32[16,10,128]{2,1,0:T(8,128)S(1)}, u32[]{:S(2)}, u32[]{:S(2)}) collective-permute-start(f32[16,10,128]{2,1,0:T(8,128)S(1)} %pad_maximum_fusion), channel_id=1, source_target_pairs={{0,4},{4,8},{8,12},{12,16},{16,20},{20,24},{24,28},{1,5},{5,9},{9,... | collective-permute-start | bytes 245768 | tf_op jit(solution)/shard_map/ppermute | solution.py:18
  14.9 7.8 %collective-permute-start = (f32[4,16,128]{2,1,0:T(8,128)S(1)}, f32[4,16,128]{2,1,0:T(8,128)S(1)}, u32[]{:S(2)}, u32[]{:S(2)}) collective-permute-start(f32[4,16,128]{2,1,0:T(8,128)S(1)} %pad_maximum_fusion.4), channel_id=1, source_target_pairs={{0,32},{32,64},{64,96},{96,128},{128,160},{160,192},{192,224},{1,3... | collective-permute-start | bytes 98312 | tf_op jit(solution)/shard_map/ppermute | solution.py:18
  26.6 4.5 %stack.37.scal_ref = f32[8]{0:T(128)} concatenate(f32[1]{0:T(128)} %get-tuple-element.129, f32[1]{0:T(128)} %get-tuple-element.122, f32[1]{0:T(128)} %get-tuple-element.120, f32[1]{0:T(128)} %get-tuple-element.130, f32[1]{0:T(128)} %get-tuple-element.121, f32[1]{0:T(128)} %get-tuple-element.119, f32[1]{0:T(128)} %bitcast.2, f32[1]{0:T(128)} %bitcast.3), dimensions={0} | concatenate | bytes 64 | tf_op jit(solution)/shard_map/stack | solution.py:263
  35.3 7.9 %collective-permute-done.1 = f32[4,16,128]{2,1,0:T(8,128)S(1)} collective-permute-done((f32[4,16,128]{2,1,0:T(8,128)S(1)}, f32[4,16,128]{2,1,0:T(8,128)S(1)}, u32[]{:S(2)}, u32[]{:S(2)}) %collective-permute-start.1) | collective-permute-done | bytes 32800 | tf_op jit(solution)/shard_map/ppermute | solution.py:23
  46.9 3.3 %shard_map.121 = (f32[16,16,128]{2,1,0:T(8,128)}, f32[3,16,16,128]{3,2,1,0:T(8,128)}, f32[16,16,1]{2,1,0:T(8,128)}, f32[2,16,128]{2,1,0:T(8,128)}, f32[16,2,128]...) custom-call(f32[8]{0:T(128)} %stack.37.scal_ref, ...), custom_call_target="tpu_custom_call" | custom-call | flops 2621440 | bytes 1572864 | tf_op jit(solution)/shard_map/pallas_call | solution.py:229
  53.4 2.7 %collective-permute-start.6 = (f32[2,16,128]{2,1,0:T(8,128)}, f32[2,16,128]{2,1,0:T(8,128)S(1)}, u32[]{:S(2)}, u32[]{:S(2)}) collective-permute-start(f32[2,16,128]{2,1,0:T(8,128)} %get-tuple-element.45), channel_id=1, source_target_pairs={{0,32},{32,64},{64,96},{96,128},{128,160},{160,192},{192,224},{1,3... | collective-permute-start | bytes 49160 | tf_op jit(solution)/shard_map/ppermute | solution.py:18
  56.1 3.2 %collective-permute-start.7 = (f32[2,16,128]{2,1,0:T(8,128)}, f32[2,16,128]{2,1,0:T(8,128)S(1)}, u32[]{:S(2)}, u32[]{:S(2)}) collective-permute-start(f32[2,16,128]{2,1,0:T(8,128)} %get-tuple-element.46), channel_id=1, source_target_pairs={{32,0},{64,32},{96,64},{128,96},{160,128},{192,160},{224,192},{33,... | collective-permute-start | bytes 49160 | tf_op jit(solution)/shard_map/ppermute | solution.py:23
  59.3 4.6 %collective-permute-start.10 = (f32[16,16,2]{2,1,0:T(8,128)}, f32[16,16,2]{2,1,0:T(8,128)S(1)}, u32[]{:S(2)}, u32[]{:S(2)}) collective-permute-start(f32[16,16,2]{2,1,0:T(8,128)} %get-tuple-element.49), channel_id=1, source_target_pairs={{0,1},{1,2},{2,3},{4,5},{5,6},{6,7},{8,9},{9,10},{10,11},{12,13},{... | collective-permute-start | bytes 6152 | tf_op jit(solution)/shard_map/ppermute | solution.py:18
  63.9 3.5 %collective-permute-done.10.pzl_ref = f32[16,16,2]{2,1,0:T(8,128)S(1)} collective-permute-done((f32[16,16,2]{2,1,0:T(8,128)}, f32[16,16,2]{2,1,0:T(8,128)S(1)}, u32[]{:S(2)}, u32[]{:S(2)}) %collective-permute-start.10) | collective-permute-done | bytes 2080 | tf_op jit(solution)/shard_map/ppermute | solution.py:18
  69.5 6.5 %collective-permute-done.11.pzh_ref = f32[16,16,2]{2,1,0:T(8,128)S(1)} collective-permute-done((f32[16,16,2]{2,1,0:T(8,128)}, f32[16,16,2]{2,1,0:T(8,128)S(1)}, u32[]{:S(2)}, u32[]{:S(2)}) %collective-permute-start.11) | collective-permute-done | bytes 2080 | tf_op jit(solution)/shard_map/ppermute | solution.py:23
  76.7 3.4 %shard_map.122 = (f32[16,16,128]{2,1,0:T(8,128)}, f32[3,16,16,128]{3,2,1,0:T(8,128)}, f32[16,16,1]{2,1,0:T(8,128)}, f32[2,16,128]{2,1,0:T(8,128)}, f32[16,2,128]...) custom-call(f32[8]{0:T(128)} %stack.37.scal_ref, ...), custom_call_target="tpu_custom_call" | custom-call | flops 2621440 | bytes 1572864 | tf_op jit(solution)/shard_map/pallas_call | solution.py:229
  80.1 3.9 %collective-permute-start.16 = (f32[16,16,2]{2,1,0:T(8,128)}, f32[16,16,2]{2,1,0:T(8,128)S(1)}, u32[]{:S(2)}, u32[]{:S(2)}) collective-permute-start(f32[16,16,2]{2,1,0:T(8,128)} %get-tuple-element.61), channel_id=1, source_target_pairs={{0,1},{1,2},{2,3},{4,5},{5,6},{6,7},{8,9},{9,10},{10,11},{12,13},{... | collective-permute-start | bytes 6152 | tf_op jit(solution)/shard_map/ppermute | solution.py:18
  88.2 8.1 %collective-permute-start.12 = (f32[2,16,128]{2,1,0:T(8,128)}, f32[2,16,128]{2,1,0:T(8,128)S(1)}, u32[]{:S(2)}, u32[]{:S(2)}) collective-permute-start(f32[2,16,128]{2,1,0:T(8,128)} %get-tuple-element.57), channel_id=1, source_target_pairs={{0,32},{32,64},{64,96},{96,128},{128,160},{160,192},{192,224},{1,3... | collective-permute-start | bytes 49160 | tf_op jit(solution)/shard_map/ppermute | solution.py:18
  99.2 9.0 %collective-permute-done.13.pxh_ref = f32[2,16,128]{2,1,0:T(8,128)S(1)} collective-permute-done((f32[2,16,128]{2,1,0:T(8,128)}, f32[2,16,128]{2,1,0:T(8,128)S(1)}, u32[]{:S(2)}, u32[]{:S(2)}) %collective-permute-start.13) | collective-permute-done | bytes 16416 | tf_op jit(solution)/shard_map/ppermute | solution.py:23
  108.9 3.4 %shard_map.123 = (f32[16,16,128]{2,1,0:T(8,128)}, f32[3,16,16,128]{3,2,1,0:T(8,128)}, f32[16,16,1]{2,1,0:T(8,128)}, f32[2,16,128]{2,1,0:T(8,128)}, f32[16,2,128]...) custom-call(f32[8]{0:T(128)} %stack.37.scal_ref, ...), custom_call_target="tpu_custom_call" | custom-call | flops 2621440 | bytes 1572864 | tf_op jit(solution)/shard_map/pallas_call | solution.py:229
  112.2 4.6 %collective-permute-start.22 = (f32[16,16,2]{2,1,0:T(8,128)}, f32[16,16,2]{2,1,0:T(8,128)S(1)}, u32[]{:S(2)}, u32[]{:S(2)}) collective-permute-start(f32[16,16,2]{2,1,0:T(8,128)} %get-tuple-element.73), channel_id=1, source_target_pairs={{0,1},{1,2},{2,3},{4,5},{5,6},{6,7},{8,9},{9,10},{10,11},{12,13},{... | collective-permute-start | bytes 6152 | tf_op jit(solution)/shard_map/ppermute | solution.py:18
  120.0 3.3 %collective-permute-start.20 = (f32[16,8,128]{2,1,0:T(8,128)S(1)}, f32[16,8,128]{2,1,0:T(8,128)S(1)}, u32[]{:S(2)}, u32[]{:S(2)}) collective-permute-start(f32[16,8,128]{2,1,0:T(8,128)S(1)} %copy-done.29), channel_id=1, source_target_pairs={{0,4},{4,8},{8,12},{12,16},{16,20},{20,24},{24,28},{1,5},{5,9},{9,... | collective-permute-start | bytes 196616 | tf_op jit(solution)/shard_map/ppermute | solution.py:18
  126.6 3.9 %collective-permute-start.19 = (f32[2,16,128]{2,1,0:T(8,128)S(1)}, f32[2,16,128]{2,1,0:T(8,128)S(1)}, u32[]{:S(2)}, u32[]{:S(2)}) collective-permute-start(f32[2,16,128]{2,1,0:T(8,128)S(1)} %copy-done.30), channel_id=1, source_target_pairs={{32,0},{64,32},{96,64},{128,96},{160,128},{192,160},{224,192},{33,... | collective-permute-start | bytes 49160 | tf_op jit(solution)/shard_map/ppermute | solution.py:23
  131.4 6.8 %collective-permute-done.19.pxh_ref = f32[2,16,128]{2,1,0:T(8,128)S(1)} collective-permute-done((f32[2,16,128]{2,1,0:T(8,128)S(1)}, f32[2,16,128]{2,1,0:T(8,128)S(1)}, u32[]{:S(2)}, u32[]{:S(2)}) %collective-permute-start.19) | collective-permute-done | bytes 16416 | tf_op jit(solution)/shard_map/ppermute | solution.py:23
  138.9 3.3 %shard_map.124 = (f32[16,16,128]{2,1,0:T(8,128)}, f32[3,16,16,128]{3,2,1,0:T(8,128)}, f32[16,16,1]{2,1,0:T(8,128)}, f32[2,16,128]{2,1,0:T(8,128)}, f32[16,2,128]...) custom-call(f32[8]{0:T(128)} %stack.37.scal_ref, ...), custom_call_target="tpu_custom_call" | custom-call | flops 2621440 | bytes 1572864 | tf_op jit(solution)/shard_map/pallas_call | solution.py:229
  146.5 11.8 %all-to-all-start = ((f32[64,1,128]{2,1,0:T(1,128)}), f32[64,1,128]{2,1,0:T(1,128)S(1)}, u32[]{:S(2)}, u32[]{:S(2)}) async-start(f32[64,1,128]{2,1,0:T(1,128)} %bitcast.14), calls=%async_computation | async-start | bytes 65536 | tf_op jit(solution)/shard_map/all_to_all | solution.py:33
  158.3 10.5 %all-to-all-done = f32[64,1,128]{2,1,0:T(1,128)S(1)} async-done(((f32[64,1,128]{2,1,0:T(1,128)}), f32[64,1,128]{2,1,0:T(1,128)S(1)}, u32[]{:S(2)}, u32[]{:S(2)}) %all-to-all-start) | async-done | bytes 32800 | tf_op jit(solution)/shard_map/all_to_all | solution.py:33
  168.8 10.1 %all-gather.1 = f32[4,1,128]{2,1,0:T(1,128)S(1)} all-gather(f32[1,1,128]{2,1,0:T(1,128)S(1)} %bitcast.33), channel_id=2, replica_groups=mesh['gx'=8,'gy'=8,'gz'=4] {'gz'}, dimensions={0}, use_global_device_ids=true | all-gather | bytes 2560 | tf_op jit(solution)/shard_map/all_gather | solution.py:38
  (161 shorter events, 45.2 us)
Async XLA Ops:
  4.0 27.1 %collective-permute-start.4 = (f32[16,16,4]{2,1,0:T(8,128)S(1)}, f32[16,16,4]{2,1,0:T(8,128)S(1)}, u32[]{:S(2)}, u32[]{:S(2)}) collective-permute-start(f32[16,16,4]{2,1,0:T(8,128)S(1)} %copy.51), channel_id=1, source_target_pairs={{0,1},{1,2},{2,3},{4,5},{5,6},{6,7},{8,9},{9,10},{10,11},{12,13},{... | collective-permute-start | bytes 12296 | tf_op jit(solution)/shard_map/ppermute | solution.py:18
  8.3 24.8 %collective-permute-start.5 = (f32[16,16,4]{2,1,0:T(8,128)S(1)}, f32[16,16,4]{2,1,0:T(8,128)S(1)}, u32[]{:S(2)}, u32[]{:S(2)}) collective-permute-start(f32[16,16,4]{2,1,0:T(8,128)S(1)} %copy.54), channel_id=1, source_target_pairs={{1,0},{2,1},{3,2},{5,4},{6,5},{7,6},{9,8},{10,9},{11,10},{13,12},{... | collective-permute-start | bytes 12296 | tf_op jit(solution)/shard_map/ppermute | solution.py:23
  9.7 34.6 %collective-permute-start.3 = (f32[16,10,128]{2,1,0:T(8,128)S(1)}, f32[16,10,128]{2,1,0:T(8,128)S(1)}, u32[]{:S(2)}, u32[]{:S(2)}) collective-permute-start(f32[16,10,128]{2,1,0:T(8,128)S(1)} %pad_maximum_fusion.1), channel_id=1, source_target_pairs={{4,0},{8,4},{12,8},{16,12},{20,16},{24,20},{28,24},{5,1},{9,5},{13... | collective-permute-start | bytes 245768 | tf_op jit(solution)/shard_map/ppermute | solution.py:23
  11.1 33.3 %collective-permute-start.2 = (f32[16,10,128]{2,1,0:T(8,128)S(1)}, f32[16,10,128]{2,1,0:T(8,128)S(1)}, u32[]{:S(2)}, u32[]{:S(2)}) collective-permute-start(f32[16,10,128]{2,1,0:T(8,128)S(1)} %pad_maximum_fusion), channel_id=1, source_target_pairs={{0,4},{4,8},{8,12},{12,16},{16,20},{20,24},{24,28},{1,5},{5,9},{9,... | collective-permute-start | bytes 245768 | tf_op jit(solution)/shard_map/ppermute | solution.py:18
  14.9 19.8 %collective-permute-start = (f32[4,16,128]{2,1,0:T(8,128)S(1)}, f32[4,16,128]{2,1,0:T(8,128)S(1)}, u32[]{:S(2)}, u32[]{:S(2)}) collective-permute-start(f32[4,16,128]{2,1,0:T(8,128)S(1)} %pad_maximum_fusion.4), channel_id=1, source_target_pairs={{0,32},{32,64},{64,96},{96,128},{128,160},{160,192},{192,224},{1,3... | collective-permute-start | bytes 98312 | tf_op jit(solution)/shard_map/ppermute | solution.py:18
  31.1 12.0 %collective-permute-start.1 = (f32[4,16,128]{2,1,0:T(8,128)S(1)}, f32[4,16,128]{2,1,0:T(8,128)S(1)}, u32[]{:S(2)}, u32[]{:S(2)}) collective-permute-start(f32[4,16,128]{2,1,0:T(8,128)S(1)} %pad_maximum_fusion.5), channel_id=1, source_target_pairs={{32,0},{64,32},{96,64},{128,96},{160,128},{192,160},{224,192},{33,... | collective-permute-start | bytes 98312 | tf_op jit(solution)/shard_map/ppermute | solution.py:23
  50.2 25.8 %collective-permute-start.8 = (f32[16,8,128]{2,1,0:T(8,128)}, f32[16,8,128]{2,1,0:T(8,128)S(1)}, u32[]{:S(2)}, u32[]{:S(2)}) collective-permute-start(f32[16,8,128]{2,1,0:T(8,128)} %get-tuple-element.47), channel_id=1, source_target_pairs={{0,4},{4,8},{8,12},{12,16},{16,20},{20,24},{24,28},{1,5},{5,9},{9,... | collective-permute-start | bytes 196616 | tf_op jit(solution)/shard_map/ppermute | solution.py:18
  52.1 23.9 %collective-permute-start.9 = (f32[16,8,128]{2,1,0:T(8,128)}, f32[16,8,128]{2,1,0:T(8,128)S(1)}, u32[]{:S(2)}, u32[]{:S(2)}) collective-permute-start(f32[16,8,128]{2,1,0:T(8,128)} %get-tuple-element.48), channel_id=1, source_target_pairs={{4,0},{8,4},{12,8},{16,12},{20,16},{24,20},{28,24},{5,1},{9,5},{13... | collective-permute-start | bytes 196616 | tf_op jit(solution)/shard_map/ppermute | solution.py:23
  53.4 22.6 %collective-permute-start.6 = (f32[2,16,128]{2,1,0:T(8,128)}, f32[2,16,128]{2,1,0:T(8,128)S(1)}, u32[]{:S(2)}, u32[]{:S(2)}) collective-permute-start(f32[2,16,128]{2,1,0:T(8,128)} %get-tuple-element.45), channel_id=1, source_target_pairs={{0,32},{32,64},{64,96},{96,128},{128,160},{160,192},{192,224},{1,3... | collective-permute-start | bytes 49160 | tf_op jit(solution)/shard_map/ppermute | solution.py:18
  56.1 19.9 %collective-permute-start.7 = (f32[2,16,128]{2,1,0:T(8,128)}, f32[2,16,128]{2,1,0:T(8,128)S(1)}, u32[]{:S(2)}, u32[]{:S(2)}) collective-permute-start(f32[2,16,128]{2,1,0:T(8,128)} %get-tuple-element.46), channel_id=1, source_target_pairs={{32,0},{64,32},{96,64},{128,96},{160,128},{192,160},{224,192},{33,... | collective-permute-start | bytes 49160 | tf_op jit(solution)/shard_map/ppermute | solution.py:23
  59.3 8.0 %collective-permute-start.10 = (f32[16,16,2]{2,1,0:T(8,128)}, f32[16,16,2]{2,1,0:T(8,128)S(1)}, u32[]{:S(2)}, u32[]{:S(2)}) collective-permute-start(f32[16,16,2]{2,1,0:T(8,128)} %get-tuple-element.49), channel_id=1, source_target_pairs={{0,1},{1,2},{2,3},{4,5},{5,6},{6,7},{8,9},{9,10},{10,11},{12,13},{... | collective-permute-start | bytes 6152 | tf_op jit(solution)/shard_map/ppermute | solution.py:18
  67.3 8.7 %collective-permute-start.11 = (f32[16,16,2]{2,1,0:T(8,128)}, f32[16,16,2]{2,1,0:T(8,128)S(1)}, u32[]{:S(2)}, u32[]{:S(2)}) collective-permute-start(f32[16,16,2]{2,1,0:T(8,128)} %get-tuple-element.50), channel_id=1, source_target_pairs={{1,0},{2,1},{3,2},{5,4},{6,5},{7,6},{9,8},{10,9},{11,10},{13,12},{... | collective-permute-start | bytes 6152 | tf_op jit(solution)/shard_map/ppermute | solution.py:23
  80.1 16.2 %collective-permute-start.16 = (f32[16,16,2]{2,1,0:T(8,128)}, f32[16,16,2]{2,1,0:T(8,128)S(1)}, u32[]{:S(2)}, u32[]{:S(2)}) collective-permute-start(f32[16,16,2]{2,1,0:T(8,128)} %get-tuple-element.61), channel_id=1, source_target_pairs={{0,1},{1,2},{2,3},{4,5},{5,6},{6,7},{8,9},{9,10},{10,11},{12,13},{... | collective-permute-start | bytes 6152 | tf_op jit(solution)/shard_map/ppermute | solution.py:18
  84.0 15.2 %collective-permute-start.17 = (f32[16,16,2]{2,1,0:T(8,128)}, f32[16,16,2]{2,1,0:T(8,128)S(1)}, u32[]{:S(2)}, u32[]{:S(2)}) collective-permute-start(f32[16,16,2]{2,1,0:T(8,128)} %get-tuple-element.62), channel_id=1, source_target_pairs={{1,0},{2,1},{3,2},{5,4},{6,5},{7,6},{9,8},{10,9},{11,10},{13,12},{... | collective-permute-start | bytes 6152 | tf_op jit(solution)/shard_map/ppermute | solution.py:23
  85.3 22.9 %collective-permute-start.14 = (f32[16,8,128]{2,1,0:T(8,128)}, f32[16,8,128]{2,1,0:T(8,128)S(1)}, u32[]{:S(2)}, u32[]{:S(2)}) collective-permute-start(f32[16,8,128]{2,1,0:T(8,128)} %get-tuple-element.59), channel_id=1, source_target_pairs={{0,4},{4,8},{8,12},{12,16},{16,20},{20,24},{24,28},{1,5},{5,9},{9,... | collective-permute-start | bytes 196616 | tf_op jit(solution)/shard_map/ppermute | solution.py:18
  86.9 21.3 %collective-permute-start.15 = (f32[16,8,128]{2,1,0:T(8,128)}, f32[16,8,128]{2,1,0:T(8,128)S(1)}, u32[]{:S(2)}, u32[]{:S(2)}) collective-permute-start(f32[16,8,128]{2,1,0:T(8,128)} %get-tuple-element.60), channel_id=1, source_target_pairs={{4,0},{8,4},{12,8},{16,12},{20,16},{24,20},{28,24},{5,1},{9,5},{13... | collective-permute-start | bytes 196616 | tf_op jit(solution)/shard_map/ppermute | solution.py:23
  88.2 11.0 %collective-permute-start.12 = (f32[2,16,128]{2,1,0:T(8,128)}, f32[2,16,128]{2,1,0:T(8,128)S(1)}, u32[]{:S(2)}, u32[]{:S(2)}) collective-permute-start(f32[2,16,128]{2,1,0:T(8,128)} %get-tuple-element.57), channel_id=1, source_target_pairs={{0,32},{32,64},{64,96},{96,128},{128,160},{160,192},{192,224},{1,3... | collective-permute-start | bytes 49160 | tf_op jit(solution)/shard_map/ppermute | solution.py:18
  96.4 11.9 %collective-permute-start.13 = (f32[2,16,128]{2,1,0:T(8,128)}, f32[2,16,128]{2,1,0:T(8,128)S(1)}, u32[]{:S(2)}, u32[]{:S(2)}) collective-permute-start(f32[2,16,128]{2,1,0:T(8,128)} %get-tuple-element.58), channel_id=1, source_target_pairs={{32,0},{64,32},{96,64},{128,96},{160,128},{192,160},{224,192},{33,... | collective-permute-start | bytes 49160 | tf_op jit(solution)/shard_map/ppermute | solution.py:23
  112.2 14.3 %collective-permute-start.22 = (f32[16,16,2]{2,1,0:T(8,128)}, f32[16,16,2]{2,1,0:T(8,128)S(1)}, u32[]{:S(2)}, u32[]{:S(2)}) collective-permute-start(f32[16,16,2]{2,1,0:T(8,128)} %get-tuple-element.73), channel_id=1, source_target_pairs={{0,1},{1,2},{2,3},{4,5},{5,6},{6,7},{8,9},{9,10},{10,11},{12,13},{... | collective-permute-start | bytes 6152 | tf_op jit(solution)/shard_map/ppermute | solution.py:18
  118.7 12.7 %collective-permute-start.23 = (f32[16,16,2]{2,1,0:T(8,128)S(1)}, f32[16,16,2]{2,1,0:T(8,128)S(1)}, u32[]{:S(2)}, u32[]{:S(2)}) collective-permute-start(f32[16,16,2]{2,1,0:T(8,128)S(1)} %copy-done.27), channel_id=1, source_target_pairs={{1,0},{2,1},{3,2},{5,4},{6,5},{7,6},{9,8},{10,9},{11,10},{13,12},{... | collective-permute-start | bytes 6152 | tf_op jit(solution)/shard_map/ppermute | solution.py:23
  120.0 18.3 %collective-permute-start.20 = (f32[16,8,128]{2,1,0:T(8,128)S(1)}, f32[16,8,128]{2,1,0:T(8,128)S(1)}, u32[]{:S(2)}, u32[]{:S(2)}) collective-permute-start(f32[16,8,128]{2,1,0:T(8,128)S(1)} %copy-done.29), channel_id=1, source_target_pairs={{0,4},{4,8},{8,12},{12,16},{16,20},{20,24},{24,28},{1,5},{5,9},{9,... | collective-permute-start | bytes 196616 | tf_op jit(solution)/shard_map/ppermute | solution.py:18
  123.3 14.9 %collective-permute-start.21 = (f32[16,8,128]{2,1,0:T(8,128)S(1)}, f32[16,8,128]{2,1,0:T(8,128)S(1)}, u32[]{:S(2)}, u32[]{:S(2)}) collective-permute-start(f32[16,8,128]{2,1,0:T(8,128)S(1)} %copy-done.28), channel_id=1, source_target_pairs={{4,0},{8,4},{12,8},{16,12},{20,16},{24,20},{28,24},{5,1},{9,5},{13... | collective-permute-start | bytes 196616 | tf_op jit(solution)/shard_map/ppermute | solution.py:23
  126.6 11.6 %collective-permute-start.19 = (f32[2,16,128]{2,1,0:T(8,128)S(1)}, f32[2,16,128]{2,1,0:T(8,128)S(1)}, u32[]{:S(2)}, u32[]{:S(2)}) collective-permute-start(f32[2,16,128]{2,1,0:T(8,128)S(1)} %copy-done.30), channel_id=1, source_target_pairs={{32,0},{64,32},{96,64},{128,96},{160,128},{192,160},{224,192},{33,... | collective-permute-start | bytes 49160 | tf_op jit(solution)/shard_map/ppermute | solution.py:23
  146.5 22.3 %all-to-all-start = ((f32[64,1,128]{2,1,0:T(1,128)}), f32[64,1,128]{2,1,0:T(1,128)S(1)}, u32[]{:S(2)}, u32[]{:S(2)}) async-start(f32[64,1,128]{2,1,0:T(1,128)} %bitcast.14), calls=%async_computation | async-start | bytes 65536 | tf_op jit(solution)/shard_map/all_to_all | solution.py:33
  (34 other events, 240.3 us)

commit v3 on v2

--- a/solution.py
+++ b/solution.py
@@ -32,10 +32,6 @@
     size = lax.axis_size(axis)
     parts = lax.all_to_all(in_blocks(x, dim, size), axis, 0, 0, tiled=True)
     return jnp.sum(parts, axis=0)
-
-
-def picked(x, axis, root):
-    return lax.dynamic_index_in_dim(lax.all_gather(x, axis), root, 0, keepdims=False)
 
 
 def depth_weights(levels, first_crust):
@@ -134,7 +130,7 @@
     zl1 = pick(pzl, -1, 1)
     zh1 = pick(pzh, -1, 0)
     zh2 = pick(pzh, -1, 1)
-    sfo_ref[...] = sf_ref[...] + 0.5 * (f_ocean * (p_last + zh1) + f_crust * (zl1 + p_first))
+    sfo_ref[...] = sf_ref[...] + 0.5 * (f_ocean * p_last + f_crust * p_first)
 
     pxl = pxl_ref[...]
     pxh = pxh_ref[...]
@@ -195,6 +191,9 @@
     new_p = pres - time_step * bulk_ref[...] * spread
     new_p = jnp.where(zi == 0, new_p + jnp.broadcast_to(src_ref[...], full), new_p)
     po_ref[...] = new_p
+    sfo_ref[...] = sfo_ref[...] + 0.5 * (
+        scal_ref[8] * pick(new_p, -1, Z - 1) + scal_ref[9] * pick(new_p, -1, 0)
+    )
 
     sxu_ref[...] = new_p[X - 2 :]
     sxd_ref[...] = new_p[0:2]
@@ -235,6 +234,13 @@
             flops=80 * cells, transcendentals=0, bytes_accessed=4 * 4 * 12 * cells // 4
         ),
     )(scal, wint, pres, vel, idn, bulk, src, sf, *halos, *tracked, *media_halo)
+
+
+def seafloor_sums(seafloor, node_weight, node_patch, patch_slot):
+    sea_values = node_weight[0, 0] * seafloor.reshape(-1)
+    slots = patch_slot[node_patch[0, 0]]
+    partial_slip = jnp.zeros((patch_slot.shape[0],), jnp.float32).at[slots].add(sea_values)
+    return summed_on_arrival(partial_slip, ("gx", "gy"), 0)
 
 
 def local(
@@ -260,10 +266,13 @@
     edge_w = depth_weights(edge_levels, first_crust)
     ocean_flag = (depth_index == first_crust // Z - 1).astype(jnp.float32)
     crust_flag = (depth_index == first_crust // Z).astype(jnp.float32)
-    scal = jnp.stack(
-        [edge_w[0][0], edge_w[1][0], edge_w[2][0], edge_w[0][1], edge_w[1][1], edge_w[2][1],
-         ocean_flag, crust_flag]
-    ).astype(jnp.float32)
+    def scal_of(instant):
+        before = 1.0 if instant == 0 else 0.0
+        after = 1.0 if instant < ITERS - 1 else 0.0
+        return jnp.stack(
+            [edge_w[0][0], edge_w[1][0], edge_w[2][0], edge_w[0][1], edge_w[1][1], edge_w[2][1],
+             before * ocean_flag, before * crust_flag, after * ocean_flag, after * crust_flag]
+        ).astype(jnp.float32)
     top_flag = (depth_index == 0).astype(jnp.float32)
     sources = source_planes(
         gauge_x,
@@ -324,25 +333,15 @@
                 shifted_down(sends[5], "gz"),
             )
         outs = run_step(
-            scal, wint, pres, vel, inv_density, bulk, src_all[instant], sf, halos, tracked,
+            scal_of(instant), wint, pres, vel, inv_density, bulk, src_all[instant], sf, halos, tracked,
             media_halo,
         )
         pres, vel, sf = outs[0], outs[1], outs[2]
         tracked = outs[3:6]
         sends = outs[6:12]
-    seafloor = sf[:, :, 0]
-
-    sea_count = X * Y
-    owners_count = lax.axis_size("gx") * lax.axis_size("gy")
-    patch_count = patch_slot.shape[0] // owners_count
-    piece_count = patch_count // tiles_z
-    root_tile = first_crust // Z
-    sea_values = node_weight[0, 0] * seafloor.reshape(sea_count)
-    slots = patch_slot[node_patch[0, 0]]
-    partial_slip = jnp.zeros((patch_slot.shape[0],), jnp.float32).at[slots].add(sea_values)
-    slip_grad = summed_on_arrival(partial_slip, ("gx", "gy"), 0)
-    slip_grad = picked(slip_grad, "gz", root_tile)
-    slip_grad = lax.dynamic_slice_in_dim(slip_grad, depth_index * piece_count, piece_count)
+        if instant == ITERS - 2:
+            owner_sums = seafloor_sums(sf[:, :, 0], node_weight, node_patch, patch_slot)
+    slip_grad = summed_on_arrival(owner_sums, "gz", 0)
     return (pres, vel, slip_grad)
 
 

time: 181 us -> 176 us (0.972)
  the two profiles are of different devices: /device:TPU:24 before, /device:TPU:226 now
where the time goes in v3:
time: 176 us; the launch traced here: 174 us
  starting transfers between devices  106 us (60%)
  local copies, waits for them, and re-layouts  33.3 us (19%)
  waiting for transfers between devices  13.8 us (8%)
  Pallas kernels  13.3 us (8%)
  other arithmetic  6.45 us (4%)
    ppermute x12, starting transfers between devices, shifted_down(): return lax.ppermute(x, axis, [(i + 1, i) for i in range(count - 1)])  66.9 us
    ppermute x12, starting transfers between devices, shifted_up(): return lax.ppermute(x, axis, [(i, i + 1) for i in range(count - 1)])  23.7 us
    all_to_all x2, starting transfers between devices, summed_on_arrival(): parts = lax.all_to_all(in_blocks(x, dim, size), axis, 0, 0, tiled=True)  15.3 us
    pallas_call x4, Pallas kernels, run_step(): pl.pallas_call(step_kernel, out_shape=shapes, in_specs=in_specs, out_spec...  13.3 us
    another operation x3, local copies, waits for them, and re-layouts, scal_of(): jnp.stack([edge_w[0][0], edge_w[1][0], edge_w[2][0], edge_w[0][1], edge_w...  13.1 us
    ppermute x12, waiting for transfers between devices, shifted_up(): return lax.ppermute(x, axis, [(i, i + 1) for i in range(count - 1)])  11.9 us
    unnamed x79, local copies, waits for them, and re-layouts  5.07 us
  transfers between devices with their start and end apart: 26, of which 3 were waited for; matrix products, arithmetic and copies ran while one was open for 15% of the time, Pallas kernels for 0%

profile of v3, /device:TPU:226, one launch (start us, length us, event | category | flops | bytes accessed | tf_op | source)
XLA Modules:
  0.0 174.4 jit_solution(11609490367127646174)
XLA Ops:
  2.9 3.5 %collective-permute-start = (f32[4,16,128]{2,1,0:T(8,128)S(1)}, f32[4,16,128]{2,1,0:T(8,128)S(1)}, u32[]{:S(2)}, u32[]{:S(2)}) collective-permute-start(f32[4,16,128]{2,1,0:T(8,128)S(1)} %pad_maximum_fusion.4), channel_id=1, source_target_pairs={{0,32},{32,64},{64,96},{96,128},{128,160},{160,192},{192,224},{1,3... | collective-permute-start | bytes 98312 | tf_op jit(solution)/shard_map/ppermute | solution.py:18
  6.4 8.4 %collective-permute-start.1 = (f32[4,16,128]{2,1,0:T(8,128)S(1)}, f32[4,16,128]{2,1,0:T(8,128)S(1)}, u32[]{:S(2)}, u32[]{:S(2)}) collective-permute-start(f32[4,16,128]{2,1,0:T(8,128)S(1)} %pad_maximum_fusion.5), channel_id=1, source_target_pairs={{32,0},{64,32},{96,64},{128,96},{160,128},{192,160},{224,192},{33,... | collective-permute-start | bytes 98312 | tf_op jit(solution)/shard_map/ppermute | solution.py:23
  17.9 3.6 %collective-permute-start.3 = (f32[16,10,128]{2,1,0:T(8,128)S(1)}, f32[16,10,128]{2,1,0:T(8,128)S(1)}, u32[]{:S(2)}, u32[]{:S(2)}) collective-permute-start(f32[16,10,128]{2,1,0:T(8,128)S(1)} %pad_maximum_fusion.1), channel_id=1, source_target_pairs={{4,0},{8,4},{12,8},{16,12},{20,16},{24,20},{28,24},{5,1},{9,5},{13... | collective-permute-start | bytes 245768 | tf_op jit(solution)/shard_map/ppermute | solution.py:23
  30.1 4.4 %stack.61.scal_ref = f32[10]{0:T(128)} concatenate(f32[1]{0:T(128)} %get-tuple-element.127, f32[1]{0:T(128)} %get-tuple-element.120, f32[1]{0:T(128)} %get-tuple-element.118, f32[1]{0:T(128)} %get-tuple-element.128, f32[1]{0:T(128)} %get-tuple-element.119, f32[1]{0:T(128)} %get-tuple-element.117, f32[1]{0:T(128)} %bitcast.2, f32[1]{0:T(128)} %bitcast.3, f32[1]{0:T(128)} %bitcast.2, ...), dimensions={0} | concatenate | bytes 80 | tf_op jit(solution)/shard_map/stack | solution.py:272
  36.0 5.4 %collective-permute-done.4 = f32[16,16,4]{2,1,0:T(8,128)S(1)} collective-permute-done((f32[16,16,4]{2,1,0:T(8,128)S(1)}, f32[16,16,4]{2,1,0:T(8,128)S(1)}, u32[]{:S(2)}, u32[]{:S(2)}) %collective-permute-start.4) | collective-permute-done | bytes 4128 | tf_op jit(solution)/shard_map/ppermute | solution.py:18
  47.4 3.3 %shard_map.121 = (f32[16,16,128]{2,1,0:T(8,128)}, f32[3,16,16,128]{3,2,1,0:T(8,128)}, f32[16,16,1]{2,1,0:T(8,128)}, f32[2,16,128]{2,1,0:T(8,128)}, f32[16,2,128]...) custom-call(f32[10]{0:T(128)} %stack.61.scal_ref, ...), custom_call_target="tpu_custom_call" | custom-call | flops 2621440 | bytes 1572864 | tf_op jit(solution)/shard_map/pallas_call | solution.py:228
  53.9 9.9 %collective-permute-start.7 = (f32[2,16,128]{2,1,0:T(8,128)}, f32[2,16,128]{2,1,0:T(8,128)S(1)}, u32[]{:S(2)}, u32[]{:S(2)}) collective-permute-start(f32[2,16,128]{2,1,0:T(8,128)} %get-tuple-element.45), channel_id=1, source_target_pairs={{32,0},{64,32},{96,64},{128,96},{160,128},{192,160},{224,192},{33,... | collective-permute-start | bytes 49160 | tf_op jit(solution)/shard_map/ppermute | solution.py:23
  65.8 3.6 %collective-permute-start.9 = (f32[16,8,128]{2,1,0:T(8,128)}, f32[16,8,128]{2,1,0:T(8,128)S(1)}, u32[]{:S(2)}, u32[]{:S(2)}) collective-permute-start(f32[16,8,128]{2,1,0:T(8,128)} %get-tuple-element.47), channel_id=1, source_target_pairs={{4,0},{8,4},{12,8},{16,12},{20,16},{24,20},{28,24},{5,1},{9,5},{13... | collective-permute-start | bytes 196616 | tf_op jit(solution)/shard_map/ppermute | solution.py:23
  69.4 4.6 %collective-permute-start.11 = (f32[16,16,2]{2,1,0:T(8,128)}, f32[16,16,2]{2,1,0:T(8,128)S(1)}, u32[]{:S(2)}, u32[]{:S(2)}) collective-permute-start(f32[16,16,2]{2,1,0:T(8,128)} %get-tuple-element.49), channel_id=1, source_target_pairs={{1,0},{2,1},{3,2},{5,4},{6,5},{7,6},{9,8},{10,9},{11,10},{13,12},{... | collective-permute-start | bytes 6152 | tf_op jit(solution)/shard_map/ppermute | solution.py:23
  74.0 4.4 %stack.60.scal_ref = f32[10]{0:T(128)} concatenate(f32[1]{0:T(128)} %get-tuple-element.127, f32[1]{0:T(128)} %get-tuple-element.120, f32[1]{0:T(128)} %get-tuple-element.118, f32[1]{0:T(128)} %get-tuple-element.128, f32[1]{0:T(128)} %get-tuple-element.119, f32[1]{0:T(128)} %get-tuple-element.117, f32[1]{0:T(128)} %constant.16.clone.1, f32[1]{0:T(128)} %constant.16.clone.1, ...), dimensions={0} | concatenate | bytes 80 | tf_op jit(solution)/shard_map/stack | solution.py:272
  80.0 3.3 %shard_map.122 = (f32[16,16,128]{2,1,0:T(8,128)}, f32[3,16,16,128]{3,2,1,0:T(8,128)}, f32[16,16,1]{2,1,0:T(8,128)}, f32[2,16,128]{2,1,0:T(8,128)}, f32[16,2,128]...) custom-call(f32[10]{0:T(128)} %stack.60.scal_ref, ...), custom_call_target="tpu_custom_call" | custom-call | flops 2621440 | bytes 1572864 | tf_op jit(solution)/shard_map/pallas_call | solution.py:228
  88.4 9.9 %collective-permute-start.13 = (f32[2,16,128]{2,1,0:T(8,128)S(1)}, f32[2,16,128]{2,1,0:T(8,128)S(1)}, u32[]{:S(2)}, u32[]{:S(2)}) collective-permute-start(f32[2,16,128]{2,1,0:T(8,128)S(1)} %copy-done.34), channel_id=1, source_target_pairs={{32,0},{64,32},{96,64},{128,96},{160,128},{192,160},{224,192},{33,... | collective-permute-start | bytes 49160 | tf_op jit(solution)/shard_map/ppermute | solution.py:23
  100.3 3.6 %collective-permute-start.15 = (f32[16,8,128]{2,1,0:T(8,128)S(1)}, f32[16,8,128]{2,1,0:T(8,128)S(1)}, u32[]{:S(2)}, u32[]{:S(2)}) collective-permute-start(f32[16,8,128]{2,1,0:T(8,128)S(1)} %copy-done.30), channel_id=1, source_target_pairs={{4,0},{8,4},{12,8},{16,12},{20,16},{24,20},{28,24},{5,1},{9,5},{13... | collective-permute-start | bytes 196616 | tf_op jit(solution)/shard_map/ppermute | solution.py:23
  103.9 4.6 %collective-permute-start.17 = (f32[16,16,2]{2,1,0:T(8,128)S(1)}, f32[16,16,2]{2,1,0:T(8,128)S(1)}, u32[]{:S(2)}, u32[]{:S(2)}) collective-permute-start(f32[16,16,2]{2,1,0:T(8,128)S(1)} %copy-done.28), channel_id=1, source_target_pairs={{1,0},{2,1},{3,2},{5,4},{6,5},{7,6},{9,8},{10,9},{11,10},{13,12},{... | collective-permute-start | bytes 6152 | tf_op jit(solution)/shard_map/ppermute | solution.py:23
  112.0 3.3 %shard_map.123 = (f32[16,16,128]{2,1,0:T(8,128)}, f32[3,16,16,128]{3,2,1,0:T(8,128)}, f32[16,16,1]{2,1,0:T(8,128)}, f32[2,16,128]{2,1,0:T(8,128)}, f32[16,2,128]...) custom-call(f32[10]{0:T(128)} %stack.60.scal_ref, ...), custom_call_target="tpu_custom_call" | custom-call | flops 2621440 | bytes 1572864 | tf_op jit(solution)/shard_map/pallas_call | solution.py:228
  119.7 10.2 %all-to-all-start = ((f32[64,1,128]{2,1,0:T(1,128)}), f32[64,1,128]{2,1,0:T(1,128)S(1)}, u32[]{:S(2)}, u32[]{:S(2)}) async-start(f32[64,1,128]{2,1,0:T(1,128)} %bitcast.14), calls=%async_computation | async-start | bytes 65536 | tf_op jit(solution)/shard_map/all_to_all | solution.py:33
  131.9 3.5 %collective-permute-start.21 = (f32[16,8,128]{2,1,0:T(8,128)S(1)}, f32[16,8,128]{2,1,0:T(8,128)S(1)}, u32[]{:S(2)}, u32[]{:S(2)}) collective-permute-start(f32[16,8,128]{2,1,0:T(8,128)S(1)} %copy-done.29), channel_id=1, source_target_pairs={{4,0},{8,4},{12,8},{16,12},{20,16},{24,20},{28,24},{5,1},{9,5},{13... | collective-permute-start | bytes 196616 | tf_op jit(solution)/shard_map/ppermute | solution.py:23
  135.4 3.4 %collective-permute-start.18 = (f32[2,16,128]{2,1,0:T(8,128)S(1)}, f32[2,16,128]{2,1,0:T(8,128)S(1)}, u32[]{:S(2)}, u32[]{:S(2)}) collective-permute-start(f32[2,16,128]{2,1,0:T(8,128)S(1)} %copy-done.33), channel_id=1, source_target_pairs={{0,32},{32,64},{64,96},{96,128},{128,160},{160,192},{192,224},{1,3... | collective-permute-start | bytes 49160 | tf_op jit(solution)/shard_map/ppermute | solution.py:18
  138.9 8.4 %collective-permute-start.19 = (f32[2,16,128]{2,1,0:T(8,128)S(1)}, f32[2,16,128]{2,1,0:T(8,128)S(1)}, u32[]{:S(2)}, u32[]{:S(2)}) collective-permute-start(f32[2,16,128]{2,1,0:T(8,128)S(1)} %copy-done.32), channel_id=1, source_target_pairs={{32,0},{64,32},{96,64},{128,96},{160,128},{192,160},{224,192},{33,... | collective-permute-start | bytes 49160 | tf_op jit(solution)/shard_map/ppermute | solution.py:23
  148.6 6.4 %collective-permute-done.22.pzl_ref = f32[16,16,2]{2,1,0:T(8,128)S(1)} collective-permute-done((f32[16,16,2]{2,1,0:T(8,128)}, f32[16,16,2]{2,1,0:T(8,128)S(1)}, u32[]{:S(2)}, u32[]{:S(2)}) %collective-permute-start.22) | collective-permute-done | bytes 2080 | tf_op jit(solution)/shard_map/ppermute | solution.py:18
  155.0 3.7 %collective-permute-start.23 = (f32[16,16,2]{2,1,0:T(8,128)S(1)}, f32[16,16,2]{2,1,0:T(8,128)S(1)}, u32[]{:S(2)}, u32[]{:S(2)}) collective-permute-start(f32[16,16,2]{2,1,0:T(8,128)S(1)} %copy-done.27), channel_id=1, source_target_pairs={{1,0},{2,1},{3,2},{5,4},{6,5},{7,6},{9,8},{10,9},{11,10},{13,12},{... | collective-permute-start | bytes 6152 | tf_op jit(solution)/shard_map/ppermute | solution.py:23
  159.5 5.1 %all-to-all-start.1 = ((f32[4,1,32]{2,1,0:T(1,128)}), f32[4,1,32]{2,1,0:T(1,128)S(1)}, u32[]{:S(2)}, u32[]{:S(2)}) async-start(f32[4,1,32]{2,1,0:T(1,128)} %bitcast.16), calls=%async_computation.1 | async-start | bytes 4096 | tf_op jit(solution)/shard_map/all_to_all | solution.py:33
  164.6 4.4 %stack.54.scal_ref = f32[10]{0:T(128)} concatenate(f32[1]{0:T(128)} %get-tuple-element.127, f32[1]{0:T(128)} %get-tuple-element.120, f32[1]{0:T(128)} %get-tuple-element.118, f32[1]{0:T(128)} %get-tuple-element.128, f32[1]{0:T(128)} %get-tuple-element.119, f32[1]{0:T(128)} %get-tuple-element.117, f32[1]{0:T(128)} %constant.16.clone.1, f32[1]{0:T(128)} %constant.16.clone.1, ...), dimensions={0} | concatenate | bytes 80 | tf_op jit(solution)/shard_map/stack | solution.py:272
  171.1 3.3 %shard_map.124 = (f32[16,16,128]{2,1,0:T(8,128)}, f32[3,16,16,128]{3,2,1,0:T(8,128)}, f32[16,16,1]{2,1,0:T(8,128)}, f32[2,16,128]{2,1,0:T(8,128)}, f32[16,2,128]...) custom-call(f32[10]{0:T(128)} %stack.54.scal_ref, ...), custom_call_target="tpu_custom_call" | custom-call | flops 2621440 | bytes 1572864 | tf_op jit(solution)/shard_map/pallas_call | solution.py:228
  (172 shorter events, 48.5 us)
Async XLA Ops:
  2.9 40.6 %collective-permute-start = (f32[4,16,128]{2,1,0:T(8,128)S(1)}, f32[4,16,128]{2,1,0:T(8,128)S(1)}, u32[]{:S(2)}, u32[]{:S(2)}) collective-permute-start(f32[4,16,128]{2,1,0:T(8,128)S(1)} %pad_maximum_fusion.4), channel_id=1, source_target_pairs={{0,32},{32,64},{64,96},{96,128},{128,160},{160,192},{192,224},{1,3... | collective-permute-start | bytes 98312 | tf_op jit(solution)/shard_map/ppermute | solution.py:18
  6.4 36.5 %collective-permute-start.1 = (f32[4,16,128]{2,1,0:T(8,128)S(1)}, f32[4,16,128]{2,1,0:T(8,128)S(1)}, u32[]{:S(2)}, u32[]{:S(2)}) collective-permute-start(f32[4,16,128]{2,1,0:T(8,128)S(1)} %pad_maximum_fusion.5), channel_id=1, source_target_pairs={{32,0},{64,32},{96,64},{128,96},{160,128},{192,160},{224,192},{33,... | collective-permute-start | bytes 98312 | tf_op jit(solution)/shard_map/ppermute | solution.py:23
  15.9 28.9 %collective-permute-start.2 = (f32[16,10,128]{2,1,0:T(8,128)S(1)}, f32[16,10,128]{2,1,0:T(8,128)S(1)}, u32[]{:S(2)}, u32[]{:S(2)}) collective-permute-start(f32[16,10,128]{2,1,0:T(8,128)S(1)} %pad_maximum_fusion), channel_id=1, source_target_pairs={{0,4},{4,8},{8,12},{12,16},{16,20},{20,24},{24,28},{1,5},{5,9},{9,... | collective-permute-start | bytes 245768 | tf_op jit(solution)/shard_map/ppermute | solution.py:18
  17.9 26.9 %collective-permute-start.3 = (f32[16,10,128]{2,1,0:T(8,128)S(1)}, f32[16,10,128]{2,1,0:T(8,128)S(1)}, u32[]{:S(2)}, u32[]{:S(2)}) collective-permute-start(f32[16,10,128]{2,1,0:T(8,128)S(1)} %pad_maximum_fusion.1), channel_id=1, source_target_pairs={{4,0},{8,4},{12,8},{16,12},{20,16},{24,20},{28,24},{5,1},{9,5},{13... | collective-permute-start | bytes 245768 | tf_op jit(solution)/shard_map/ppermute | solution.py:23
  22.7 11.8 %collective-permute-start.5 = (f32[16,16,4]{2,1,0:T(8,128)S(1)}, f32[16,16,4]{2,1,0:T(8,128)S(1)}, u32[]{:S(2)}, u32[]{:S(2)}) collective-permute-start(f32[16,16,4]{2,1,0:T(8,128)S(1)} %copy.56), channel_id=1, source_target_pairs={{1,0},{2,1},{3,2},{5,4},{6,5},{7,6},{9,8},{10,9},{11,10},{13,12},{... | collective-permute-start | bytes 12296 | tf_op jit(solution)/shard_map/ppermute | solution.py:23
  50.7 18.8 %collective-permute-start.10 = (f32[16,16,2]{2,1,0:T(8,128)}, f32[16,16,2]{2,1,0:T(8,128)S(1)}, u32[]{:S(2)}, u32[]{:S(2)}) collective-permute-start(f32[16,16,2]{2,1,0:T(8,128)} %get-tuple-element.48), channel_id=1, source_target_pairs={{0,1},{1,2},{2,3},{4,5},{5,6},{6,7},{8,9},{9,10},{10,11},{12,13},{... | collective-permute-start | bytes 6152 | tf_op jit(solution)/shard_map/ppermute | solution.py:18
  52.0 27.3 %collective-permute-start.6 = (f32[2,16,128]{2,1,0:T(8,128)}, f32[2,16,128]{2,1,0:T(8,128)S(1)}, u32[]{:S(2)}, u32[]{:S(2)}) collective-permute-start(f32[2,16,128]{2,1,0:T(8,128)} %get-tuple-element.44), channel_id=1, source_target_pairs={{0,32},{32,64},{64,96},{96,128},{128,160},{160,192},{192,224},{1,3... | collective-permute-start | bytes 49160 | tf_op jit(solution)/shard_map/ppermute | solution.py:18
  53.9 25.4 %collective-permute-start.7 = (f32[2,16,128]{2,1,0:T(8,128)}, f32[2,16,128]{2,1,0:T(8,128)S(1)}, u32[]{:S(2)}, u32[]{:S(2)}) collective-permute-start(f32[2,16,128]{2,1,0:T(8,128)} %get-tuple-element.45), channel_id=1, source_target_pairs={{32,0},{64,32},{96,64},{128,96},{160,128},{192,160},{224,192},{33,... | collective-permute-start | bytes 49160 | tf_op jit(solution)/shard_map/ppermute | solution.py:23
  63.8 15.5 %collective-permute-start.8 = (f32[16,8,128]{2,1,0:T(8,128)}, f32[16,8,128]{2,1,0:T(8,128)S(1)}, u32[]{:S(2)}, u32[]{:S(2)}) collective-permute-start(f32[16,8,128]{2,1,0:T(8,128)} %get-tuple-element.46), channel_id=1, source_target_pairs={{0,4},{4,8},{8,12},{12,16},{16,20},{20,24},{24,28},{1,5},{5,9},{9,... | collective-permute-start | bytes 196616 | tf_op jit(solution)/shard_map/ppermute | solution.py:18
  65.8 13.5 %collective-permute-start.9 = (f32[16,8,128]{2,1,0:T(8,128)}, f32[16,8,128]{2,1,0:T(8,128)S(1)}, u32[]{:S(2)}, u32[]{:S(2)}) collective-permute-start(f32[16,8,128]{2,1,0:T(8,128)} %get-tuple-element.47), channel_id=1, source_target_pairs={{4,0},{8,4},{12,8},{16,12},{20,16},{24,20},{28,24},{5,1},{9,5},{13... | collective-permute-start | bytes 196616 | tf_op jit(solution)/shard_map/ppermute | solution.py:23
  69.4 9.8 %collective-permute-start.11 = (f32[16,16,2]{2,1,0:T(8,128)}, f32[16,16,2]{2,1,0:T(8,128)S(1)}, u32[]{:S(2)}, u32[]{:S(2)}) collective-permute-start(f32[16,16,2]{2,1,0:T(8,128)} %get-tuple-element.49), channel_id=1, source_target_pairs={{1,0},{2,1},{3,2},{5,4},{6,5},{7,6},{9,8},{10,9},{11,10},{13,12},{... | collective-permute-start | bytes 6152 | tf_op jit(solution)/shard_map/ppermute | solution.py:23
  83.3 20.6 %collective-permute-start.16 = (f32[16,16,2]{2,1,0:T(8,128)}, f32[16,16,2]{2,1,0:T(8,128)S(1)}, u32[]{:S(2)}, u32[]{:S(2)}) collective-permute-start(f32[16,16,2]{2,1,0:T(8,128)} %get-tuple-element.60), channel_id=1, source_target_pairs={{0,1},{1,2},{2,3},{4,5},{5,6},{6,7},{8,9},{9,10},{10,11},{12,13},{... | collective-permute-start | bytes 6152 | tf_op jit(solution)/shard_map/ppermute | solution.py:18
  86.4 24.8 %collective-permute-start.12 = (f32[2,16,128]{2,1,0:T(8,128)S(1)}, f32[2,16,128]{2,1,0:T(8,128)S(1)}, u32[]{:S(2)}, u32[]{:S(2)}) collective-permute-start(f32[2,16,128]{2,1,0:T(8,128)S(1)} %copy-done.35), channel_id=1, source_target_pairs={{0,32},{32,64},{64,96},{96,128},{128,160},{160,192},{192,224},{1,3... | collective-permute-start | bytes 49160 | tf_op jit(solution)/shard_map/ppermute | solution.py:18
  88.4 22.9 %collective-permute-start.13 = (f32[2,16,128]{2,1,0:T(8,128)S(1)}, f32[2,16,128]{2,1,0:T(8,128)S(1)}, u32[]{:S(2)}, u32[]{:S(2)}) collective-permute-start(f32[2,16,128]{2,1,0:T(8,128)S(1)} %copy-done.34), channel_id=1, source_target_pairs={{32,0},{64,32},{96,64},{128,96},{160,128},{192,160},{224,192},{33,... | collective-permute-start | bytes 49160 | tf_op jit(solution)/shard_map/ppermute | solution.py:23
  98.3 12.9 %collective-permute-start.14 = (f32[16,8,128]{2,1,0:T(8,128)S(1)}, f32[16,8,128]{2,1,0:T(8,128)S(1)}, u32[]{:S(2)}, u32[]{:S(2)}) collective-permute-start(f32[16,8,128]{2,1,0:T(8,128)S(1)} %copy-done.31), channel_id=1, source_target_pairs={{0,4},{4,8},{8,12},{12,16},{16,20},{20,24},{24,28},{1,5},{5,9},{9,... | collective-permute-start | bytes 196616 | tf_op jit(solution)/shard_map/ppermute | solution.py:18
  100.3 11.0 %collective-permute-start.15 = (f32[16,8,128]{2,1,0:T(8,128)S(1)}, f32[16,8,128]{2,1,0:T(8,128)S(1)}, u32[]{:S(2)}, u32[]{:S(2)}) collective-permute-start(f32[16,8,128]{2,1,0:T(8,128)S(1)} %copy-done.30), channel_id=1, source_target_pairs={{4,0},{8,4},{12,8},{16,12},{20,16},{24,20},{28,24},{5,1},{9,5},{13... | collective-permute-start | bytes 196616 | tf_op jit(solution)/shard_map/ppermute | solution.py:23
  119.7 39.1 %all-to-all-start = ((f32[64,1,128]{2,1,0:T(1,128)}), f32[64,1,128]{2,1,0:T(1,128)S(1)}, u32[]{:S(2)}, u32[]{:S(2)}) async-start(f32[64,1,128]{2,1,0:T(1,128)} %bitcast.14), calls=%async_computation | async-start | bytes 65536 | tf_op jit(solution)/shard_map/all_to_all | solution.py:33
  129.9 40.5 %collective-permute-start.20 = (f32[16,8,128]{2,1,0:T(8,128)}, f32[16,8,128]{2,1,0:T(8,128)S(1)}, u32[]{:S(2)}, u32[]{:S(2)}) collective-permute-start(f32[16,8,128]{2,1,0:T(8,128)} %get-tuple-element.70), channel_id=1, source_target_pairs={{0,4},{4,8},{8,12},{12,16},{16,20},{20,24},{24,28},{1,5},{5,9},{9,... | collective-permute-start | bytes 196616 | tf_op jit(solution)/shard_map/ppermute | solution.py:18
  131.9 38.5 %collective-permute-start.21 = (f32[16,8,128]{2,1,0:T(8,128)S(1)}, f32[16,8,128]{2,1,0:T(8,128)S(1)}, u32[]{:S(2)}, u32[]{:S(2)}) collective-permute-start(f32[16,8,128]{2,1,0:T(8,128)S(1)} %copy-done.29), channel_id=1, source_target_pairs={{4,0},{8,4},{12,8},{16,12},{20,16},{24,20},{28,24},{5,1},{9,5},{13... | collective-permute-start | bytes 196616 | tf_op jit(solution)/shard_map/ppermute | solution.py:23
  135.4 34.9 %collective-permute-start.18 = (f32[2,16,128]{2,1,0:T(8,128)S(1)}, f32[2,16,128]{2,1,0:T(8,128)S(1)}, u32[]{:S(2)}, u32[]{:S(2)}) collective-permute-start(f32[2,16,128]{2,1,0:T(8,128)S(1)} %copy-done.33), channel_id=1, source_target_pairs={{0,32},{32,64},{64,96},{96,128},{128,160},{160,192},{192,224},{1,3... | collective-permute-start | bytes 49160 | tf_op jit(solution)/shard_map/ppermute | solution.py:18
  138.9 31.5 %collective-permute-start.19 = (f32[2,16,128]{2,1,0:T(8,128)S(1)}, f32[2,16,128]{2,1,0:T(8,128)S(1)}, u32[]{:S(2)}, u32[]{:S(2)}) collective-permute-start(f32[2,16,128]{2,1,0:T(8,128)S(1)} %copy-done.32), channel_id=1, source_target_pairs={{32,0},{64,32},{96,64},{128,96},{160,128},{192,160},{224,192},{33,... | collective-permute-start | bytes 49160 | tf_op jit(solution)/shard_map/ppermute | solution.py:23
  147.3 7.7 %collective-permute-start.22 = (f32[16,16,2]{2,1,0:T(8,128)}, f32[16,16,2]{2,1,0:T(8,128)S(1)}, u32[]{:S(2)}, u32[]{:S(2)}) collective-permute-start(f32[16,16,2]{2,1,0:T(8,128)} %get-tuple-element.72), channel_id=1, source_target_pairs={{0,1},{1,2},{2,3},{4,5},{5,6},{6,7},{8,9},{9,10},{10,11},{12,13},{... | collective-permute-start | bytes 6152 | tf_op jit(solution)/shard_map/ppermute | solution.py:18
  155.0 15.3 %collective-permute-start.23 = (f32[16,16,2]{2,1,0:T(8,128)S(1)}, f32[16,16,2]{2,1,0:T(8,128)S(1)}, u32[]{:S(2)}, u32[]{:S(2)}) collective-permute-start(f32[16,16,2]{2,1,0:T(8,128)S(1)} %copy-done.27), channel_id=1, source_target_pairs={{1,0},{2,1},{3,2},{5,4},{6,5},{7,6},{9,8},{10,9},{11,10},{13,12},{... | collective-permute-start | bytes 6152 | tf_op jit(solution)/shard_map/ppermute | solution.py:23
  159.5 10.3 %all-to-all-start.1 = ((f32[4,1,32]{2,1,0:T(1,128)}), f32[4,1,32]{2,1,0:T(1,128)S(1)}, u32[]{:S(2)}, u32[]{:S(2)}) async-start(f32[4,1,32]{2,1,0:T(1,128)} %bitcast.16), calls=%async_computation.1 | async-start | bytes 4096 | tf_op jit(solution)/shard_map/all_to_all | solution.py:33
  (39 other events, 313.0 us)

commit v4 on v3

--- a/solution.py
+++ b/solution.py
@@ -69,6 +69,7 @@
 
 
 def step_kernel(
+    instant,
     scal_ref,
     wint_ref,
     p_ref,
@@ -104,20 +105,21 @@
 ):
     X, Y, Z = p_ref.shape
     rows = pyl_ref.shape[1]
+    base = instant * 16
     full = (X, Y, Z)
     yi = lax.broadcasted_iota(jnp.int32, full, 1)
     zi = lax.broadcasted_iota(jnp.int32, full, 2)
     wu = wint_ref[0]
     wm = wint_ref[1]
     wl = wint_ref[2]
-    wu_lo = scal_ref[0]
-    wm_lo = scal_ref[1]
-    wl_lo = scal_ref[2]
-    wu_hi = scal_ref[3]
-    wm_hi = scal_ref[4]
-    wl_hi = scal_ref[5]
-    f_ocean = scal_ref[6]
-    f_crust = scal_ref[7]
+    wu_lo = scal_ref[base + 0]
+    wm_lo = scal_ref[base + 1]
+    wl_lo = scal_ref[base + 2]
+    wu_hi = scal_ref[base + 3]
+    wm_hi = scal_ref[base + 4]
+    wl_hi = scal_ref[base + 5]
+    f_ocean = scal_ref[base + 6]
+    f_crust = scal_ref[base + 7]
 
     pres = p_ref[...]
     idn = idn_ref[...]
@@ -189,10 +191,10 @@
         + (wu * up_z + wm * v2 + wl * down_z)
     )
     new_p = pres - time_step * bulk_ref[...] * spread
-    new_p = jnp.where(zi == 0, new_p + jnp.broadcast_to(src_ref[...], full), new_p)
+    new_p = jnp.where(zi == 0, new_p + jnp.broadcast_to(src_ref[instant], full), new_p)
     po_ref[...] = new_p
     sfo_ref[...] = sfo_ref[...] + 0.5 * (
-        scal_ref[8] * pick(new_p, -1, Z - 1) + scal_ref[9] * pick(new_p, -1, 0)
+        scal_ref[base + 8] * pick(new_p, -1, Z - 1) + scal_ref[base + 9] * pick(new_p, -1, 0)
     )
 
     sxu_ref[...] = new_p[X - 2 :]
@@ -204,7 +206,7 @@
     szd_ref[...] = pair(pick(new_p, -1, 0), pick(new_p, -1, 1), zshape, 2)
 
 
-def run_step(scal, wint, pres, vel, idn, bulk, src, sf, halos, tracked, media_halo):
+def run_step(instant, scal, wint, pres, vel, idn, bulk, src, sf, halos, tracked, media_halo):
     X, Y, Z = pres.shape
     rows = halos[2].shape[1]
     f32 = jnp.float32
@@ -226,7 +228,7 @@
     in_specs = [pl.BlockSpec(memory_space=pltpu.SMEM)] + [vmem] * 19
     cells = X * Y * Z
     return pl.pallas_call(
-        step_kernel,
+        functools.partial(step_kernel, instant),
         out_shape=shapes,
         in_specs=in_specs,
         out_specs=[vmem] * len(shapes),
@@ -262,17 +264,23 @@
     first_crust = tiles_z // 2 * Z
     levels = depth_index * Z + jnp.arange(Z, dtype=jnp.int32)
     wint = jnp.stack(depth_weights(levels, first_crust)).reshape(3, 1, 1, Z)
-    edge_levels = jnp.stack([depth_index * Z - 1, depth_index * Z + Z])
-    edge_w = depth_weights(edge_levels, first_crust)
-    ocean_flag = (depth_index == first_crust // Z - 1).astype(jnp.float32)
-    crust_flag = (depth_index == first_crust // Z).astype(jnp.float32)
-    def scal_of(instant):
-        before = 1.0 if instant == 0 else 0.0
-        after = 1.0 if instant < ITERS - 1 else 0.0
-        return jnp.stack(
-            [edge_w[0][0], edge_w[1][0], edge_w[2][0], edge_w[0][1], edge_w[1][1], edge_w[2][1],
-             before * ocean_flag, before * crust_flag, after * ocean_flag, after * crust_flag]
-        ).astype(jnp.float32)
+    entry = lax.broadcasted_iota(jnp.int32, (ITERS, 16), 1)
+    step_at = lax.broadcasted_iota(jnp.int32, (ITERS, 16), 0)
+    edge_level = depth_index * Z + jnp.where(entry < 3, -1, Z)
+    e_up, e_mid, e_low = depth_weights(edge_level, first_crust)
+    kind = entry % 3
+    edge_value = jnp.where(kind == 0, e_up, jnp.where(kind == 1, e_mid, e_low))
+    ocean = depth_index == first_crust // Z - 1
+    crust = depth_index == first_crust // Z
+    before = step_at == 0
+    after = step_at < ITERS - 1
+    flag_value = jnp.where(
+        entry == 6, before & ocean,
+        jnp.where(entry == 7, before & crust,
+                  jnp.where(entry == 8, after & ocean, after & crust)),
+    ).astype(jnp.float32)
+    scal_all = jnp.where(entry < 6, edge_value, jnp.where(entry < 10, flag_value, 0.0))
+    scal_all = scal_all.astype(jnp.float32).reshape(ITERS * 16)
     top_flag = (depth_index == 0).astype(jnp.float32)
     sources = source_planes(
         gauge_x,
@@ -333,7 +341,7 @@
                 shifted_down(sends[5], "gz"),
             )
         outs = run_step(
-            scal_of(instant), wint, pres, vel, inv_density, bulk, src_all[instant], sf, halos, tracked,
+            instant, scal_all, wint, pres, vel, inv_density, bulk, src_all, sf, halos, tracked,
             media_halo,
         )
         pres, vel, sf = outs[0], outs[1], outs[2]

time: 176 us -> 161 us (0.915)
  the two profiles are of different devices: /device:TPU:226 before, /device:TPU:130 now
where the time goes in v4:
time: 161 us; the launch traced here: 160 us
  starting transfers between devices  105 us (65%)
  local copies, waits for them, and re-layouts  16 us (10%)
  Pallas kernels  13.5 us (8%)
  blocking collectives  11.3 us (7%)
  other arithmetic  6.53 us (4%)
  waiting for transfers between devices  5.81 us (4%)
  between operations  1.61 us (1%)
    ppermute x12, starting transfers between devices, shifted_down(): return lax.ppermute(x, axis, [(i + 1, i) for i in range(count - 1)])  56.6 us
    ppermute x12, starting transfers between devices, shifted_up(): return lax.ppermute(x, axis, [(i, i + 1) for i in range(count - 1)])  35.1 us
    pallas_call x4, Pallas kernels, run_step(): pl.pallas_call(functools.partial(step_kernel, instant), out_shape=shapes,...  13.5 us
    all_to_all x1, starting transfers between devices, summed_on_arrival(): parts = lax.all_to_all(in_blocks(x, dim, size), axis, 0, 0, tiled=True)  13.4 us
    all_to_all x1, blocking collectives, summed_on_arrival(): parts = lax.all_to_all(in_blocks(x, dim, size), axis, 0, 0, tiled=True)  11.3 us
    unnamed x79, local copies, waits for them, and re-layouts  6.07 us
  transfers between devices with their start and end apart: 25, of which 3 were waited for; matrix products, arithmetic and copies ran while one was open for 6% of the time, Pallas kernels for 0%

profile of v4, /device:TPU:130, one launch (start us, length us, event | category | flops | bytes accessed | tf_op | source)
XLA Modules:
  0.0 160.3 jit_solution(7514946825588846675)
XLA Ops:
  4.0 2.9 %collective-permute-start.4 = (f32[16,16,4]{2,1,0:T(8,128)S(1)}, f32[16,16,4]{2,1,0:T(8,128)S(1)}, u32[]{:S(2)}, u32[]{:S(2)}) collective-permute-start(f32[16,16,4]{2,1,0:T(8,128)S(1)} %copy.53), channel_id=1, source_target_pairs={{0,1},{1,2},{2,3},{4,5},{5,6},{6,7},{8,9},{9,10},{10,11},{12,13},{... | collective-permute-start | bytes 12296 | tf_op jit(solution)/shard_map/ppermute | solution.py:18
  8.8 1.9 %collective-permute-start.2 = (f32[16,10,128]{2,1,0:T(8,128)S(1)}, f32[16,10,128]{2,1,0:T(8,128)S(1)}, u32[]{:S(2)}, u32[]{:S(2)}) collective-permute-start(f32[16,10,128]{2,1,0:T(8,128)S(1)} %pad_maximum_fusion), channel_id=1, source_target_pairs={{0,4},{4,8},{8,12},{12,16},{16,20},{20,24},{24,28},{1,5},{5,9},{9,... | collective-permute-start | bytes 245768 | tf_op jit(solution)/shard_map/ppermute | solution.py:18
  10.8 3.6 %collective-permute-start.3 = (f32[16,10,128]{2,1,0:T(8,128)S(1)}, f32[16,10,128]{2,1,0:T(8,128)S(1)}, u32[]{:S(2)}, u32[]{:S(2)}) collective-permute-start(f32[16,10,128]{2,1,0:T(8,128)S(1)} %pad_maximum_fusion.1), channel_id=1, source_target_pairs={{4,0},{8,4},{12,8},{16,12},{20,16},{24,20},{28,24},{5,1},{9,5},{13... | collective-permute-start | bytes 245768 | tf_op jit(solution)/shard_map/ppermute | solution.py:23
  15.2 3.5 %collective-permute-start = (f32[4,16,128]{2,1,0:T(8,128)S(1)}, f32[4,16,128]{2,1,0:T(8,128)S(1)}, u32[]{:S(2)}, u32[]{:S(2)}) collective-permute-start(f32[4,16,128]{2,1,0:T(8,128)S(1)} %pad_maximum_fusion.4), channel_id=1, source_target_pairs={{0,32},{32,64},{64,96},{96,128},{128,160},{160,192},{192,224},{1,3... | collective-permute-start | bytes 98312 | tf_op jit(solution)/shard_map/ppermute | solution.py:18
  22.3 8.4 %collective-permute-start.1 = (f32[4,16,128]{2,1,0:T(8,128)S(1)}, f32[4,16,128]{2,1,0:T(8,128)S(1)}, u32[]{:S(2)}, u32[]{:S(2)}) collective-permute-start(f32[4,16,128]{2,1,0:T(8,128)S(1)} %pad_maximum_fusion.5), channel_id=1, source_target_pairs={{32,0},{64,32},{96,64},{128,96},{160,128},{192,160},{224,192},{33,... | collective-permute-start | bytes 98312 | tf_op jit(solution)/shard_map/ppermute | solution.py:23
  36.8 3.4 %shard_map.121 = (f32[16,16,128]{2,1,0:T(8,128)}, f32[3,16,16,128]{3,2,1,0:T(8,128)}, f32[16,16,1]{2,1,0:T(8,128)}, f32[2,16,128]{2,1,0:T(8,128)}, f32[16,2,128]...) custom-call(f32[64]{0:T(128)} %reshape.160.scal_ref, ...), custom_call_target="tpu_custom_call" | custom-call | flops 2621440 | bytes 1572864 | tf_op jit(solution)/shard_map/pallas_call | solution.py:230
  40.1 4.6 %collective-permute-start.10 = (f32[16,16,2]{2,1,0:T(8,128)}, f32[16,16,2]{2,1,0:T(8,128)S(1)}, u32[]{:S(2)}, u32[]{:S(2)}) collective-permute-start(f32[16,16,2]{2,1,0:T(8,128)} %get-tuple-element.48), channel_id=1, source_target_pairs={{0,1},{1,2},{2,3},{4,5},{5,6},{6,7},{8,9},{9,10},{10,11},{12,13},{... | collective-permute-start | bytes 6152 | tf_op jit(solution)/shard_map/ppermute | solution.py:18
  47.9 3.6 %collective-permute-start.9 = (f32[16,8,128]{2,1,0:T(8,128)}, f32[16,8,128]{2,1,0:T(8,128)S(1)}, u32[]{:S(2)}, u32[]{:S(2)}) collective-permute-start(f32[16,8,128]{2,1,0:T(8,128)} %get-tuple-element.47), channel_id=1, source_target_pairs={{4,0},{8,4},{12,8},{16,12},{20,16},{24,20},{28,24},{5,1},{9,5},{13... | collective-permute-start | bytes 196616 | tf_op jit(solution)/shard_map/ppermute | solution.py:23
  53.5 9.9 %collective-permute-start.7 = (f32[2,16,128]{2,1,0:T(8,128)}, f32[2,16,128]{2,1,0:T(8,128)S(1)}, u32[]{:S(2)}, u32[]{:S(2)}) collective-permute-start(f32[2,16,128]{2,1,0:T(8,128)} %get-tuple-element.45), channel_id=1, source_target_pairs={{32,0},{64,32},{96,64},{128,96},{160,128},{192,160},{224,192},{33,... | collective-permute-start | bytes 49160 | tf_op jit(solution)/shard_map/ppermute | solution.py:23
  65.8 3.4 %shard_map.122 = (f32[16,16,128]{2,1,0:T(8,128)}, f32[3,16,16,128]{3,2,1,0:T(8,128)}, f32[16,16,1]{2,1,0:T(8,128)}, f32[2,16,128]{2,1,0:T(8,128)}, f32[16,2,128]...) custom-call(f32[64]{0:T(128)} %reshape.160.scal_ref, ...), custom_call_target="tpu_custom_call" | custom-call | flops 2621440 | bytes 1572864 | tf_op jit(solution)/shard_map/pallas_call | solution.py:230
  69.2 4.6 %collective-permute-start.16 = (f32[16,16,2]{2,1,0:T(8,128)}, f32[16,16,2]{2,1,0:T(8,128)S(1)}, u32[]{:S(2)}, u32[]{:S(2)}) collective-permute-start(f32[16,16,2]{2,1,0:T(8,128)} %get-tuple-element.60), channel_id=1, source_target_pairs={{0,1},{1,2},{2,3},{4,5},{5,6},{6,7},{8,9},{9,10},{10,11},{12,13},{... | collective-permute-start | bytes 6152 | tf_op jit(solution)/shard_map/ppermute | solution.py:18
  78.8 3.6 %collective-permute-start.15 = (f32[16,8,128]{2,1,0:T(8,128)S(1)}, f32[16,8,128]{2,1,0:T(8,128)S(1)}, u32[]{:S(2)}, u32[]{:S(2)}) collective-permute-start(f32[16,8,128]{2,1,0:T(8,128)S(1)} %copy-done.30), channel_id=1, source_target_pairs={{4,0},{8,4},{12,8},{16,12},{20,16},{24,20},{28,24},{5,1},{9,5},{13... | collective-permute-start | bytes 196616 | tf_op jit(solution)/shard_map/ppermute | solution.py:23
  84.4 10.3 %collective-permute-start.13 = (f32[2,16,128]{2,1,0:T(8,128)S(1)}, f32[2,16,128]{2,1,0:T(8,128)S(1)}, u32[]{:S(2)}, u32[]{:S(2)}) collective-permute-start(f32[2,16,128]{2,1,0:T(8,128)S(1)} %copy-done.34), channel_id=1, source_target_pairs={{32,0},{64,32},{96,64},{128,96},{160,128},{192,160},{224,192},{33,... | collective-permute-start | bytes 49160 | tf_op jit(solution)/shard_map/ppermute | solution.py:23
  96.9 3.4 %shard_map.123 = (f32[16,16,128]{2,1,0:T(8,128)}, f32[3,16,16,128]{3,2,1,0:T(8,128)}, f32[16,16,1]{2,1,0:T(8,128)}, f32[2,16,128]{2,1,0:T(8,128)}, f32[16,2,128]...) custom-call(f32[64]{0:T(128)} %reshape.160.scal_ref, ...), custom_call_target="tpu_custom_call" | custom-call | flops 2621440 | bytes 1572864 | tf_op jit(solution)/shard_map/pallas_call | solution.py:230
  102.1 2.5 %scatter_custom_fusion = f32[8192]{0:T(1024)} fusion(s32[256]{0:T(256)S(1)} %bitcast.29, f32[256]{0:T(256)S(1)} %mul.48, f32[]{:T(128)} %constant.36.clone.1), kind=kCustom, calls=%fused_computation.19 | custom fusion | flops 256 | bytes 32772 | tf_op jit(solution)/shard_map/scatter-add | solution.py:244
  104.6 13.4 %all-to-all-start = ((f32[64,1,128]{2,1,0:T(1,128)}), f32[64,1,128]{2,1,0:T(1,128)S(1)}, u32[]{:S(2)}, u32[]{:S(2)}) async-start(f32[64,1,128]{2,1,0:T(1,128)} %bitcast.10), calls=%async_computation | async-start | bytes 65536 | tf_op jit(solution)/shard_map/all_to_all | solution.py:33
  118.0 2.1 %collective-permute-start.20 = (f32[16,8,128]{2,1,0:T(8,128)}, f32[16,8,128]{2,1,0:T(8,128)S(1)}, u32[]{:S(2)}, u32[]{:S(2)}) collective-permute-start(f32[16,8,128]{2,1,0:T(8,128)} %get-tuple-element.70), channel_id=1, source_target_pairs={{0,4},{4,8},{8,12},{12,16},{16,20},{20,24},{24,28},{1,5},{5,9},{9,... | collective-permute-start | bytes 196616 | tf_op jit(solution)/shard_map/ppermute | solution.py:18
  120.1 3.5 %collective-permute-start.21 = (f32[16,8,128]{2,1,0:T(8,128)S(1)}, f32[16,8,128]{2,1,0:T(8,128)S(1)}, u32[]{:S(2)}, u32[]{:S(2)}) collective-permute-start(f32[16,8,128]{2,1,0:T(8,128)S(1)} %copy-done.29), channel_id=1, source_target_pairs={{4,0},{8,4},{12,8},{16,12},{20,16},{24,20},{28,24},{5,1},{9,5},{13... | collective-permute-start | bytes 196616 | tf_op jit(solution)/shard_map/ppermute | solution.py:23
  123.6 3.4 %collective-permute-start.18 = (f32[2,16,128]{2,1,0:T(8,128)S(1)}, f32[2,16,128]{2,1,0:T(8,128)S(1)}, u32[]{:S(2)}, u32[]{:S(2)}) collective-permute-start(f32[2,16,128]{2,1,0:T(8,128)S(1)} %copy-done.33), channel_id=1, source_target_pairs={{0,32},{32,64},{64,96},{96,128},{128,160},{160,192},{192,224},{1,3... | collective-permute-start | bytes 49160 | tf_op jit(solution)/shard_map/ppermute | solution.py:18
  127.1 8.4 %collective-permute-start.19 = (f32[2,16,128]{2,1,0:T(8,128)S(1)}, f32[2,16,128]{2,1,0:T(8,128)S(1)}, u32[]{:S(2)}, u32[]{:S(2)}) collective-permute-start(f32[2,16,128]{2,1,0:T(8,128)S(1)} %copy-done.32), channel_id=1, source_target_pairs={{32,0},{64,32},{96,64},{128,96},{160,128},{192,160},{224,192},{33,... | collective-permute-start | bytes 49160 | tf_op jit(solution)/shard_map/ppermute | solution.py:23
  135.5 4.6 %collective-permute-start.22 = (f32[16,16,2]{2,1,0:T(8,128)}, f32[16,16,2]{2,1,0:T(8,128)S(1)}, u32[]{:S(2)}, u32[]{:S(2)}) collective-permute-start(f32[16,16,2]{2,1,0:T(8,128)} %get-tuple-element.72), channel_id=1, source_target_pairs={{0,1},{1,2},{2,3},{4,5},{5,6},{6,7},{8,9},{9,10},{10,11},{12,13},{... | collective-permute-start | bytes 6152 | tf_op jit(solution)/shard_map/ppermute | solution.py:18
  140.1 2.8 %collective-permute-done.22.pzl_ref = f32[16,16,2]{2,1,0:T(8,128)S(1)} collective-permute-done((f32[16,16,2]{2,1,0:T(8,128)}, f32[16,16,2]{2,1,0:T(8,128)S(1)}, u32[]{:S(2)}, u32[]{:S(2)}) %collective-permute-start.22) | collective-permute-done | bytes 2080 | tf_op jit(solution)/shard_map/ppermute | solution.py:18
  144.3 11.3 %all_to_all.18 = f32[4,1,32]{2,1,0:T(1,128)S(1)} all-to-all(f32[4,1,32]{2,1,0:T(1,128)S(1)} %bitcast.25), channel_id=1, replica_groups=mesh['gx'=8,'gy'=8,'gz'=4] {'gz'}, dimensions={0} | all-to-all | bytes 1024 | tf_op jit(solution)/shard_map/all_to_all | solution.py:33
  156.9 3.4 %shard_map.124 = (f32[16,16,128]{2,1,0:T(8,128)}, f32[3,16,16,128]{3,2,1,0:T(8,128)}, f32[16,16,1]{2,1,0:T(8,128)}, f32[2,16,128]{2,1,0:T(8,128)}, f32[16,2,128]...) custom-call(f32[64]{0:T(128)} %reshape.160.scal_ref, ...), custom_call_target="tpu_custom_call" | custom-call | flops 2621440 | bytes 1572864 | tf_op jit(solution)/shard_map/pallas_call | solution.py:230
  (171 shorter events, 36.1 us)
Async XLA Ops:
  4.0 18.3 %collective-permute-start.4 = (f32[16,16,4]{2,1,0:T(8,128)S(1)}, f32[16,16,4]{2,1,0:T(8,128)S(1)}, u32[]{:S(2)}, u32[]{:S(2)}) collective-permute-start(f32[16,16,4]{2,1,0:T(8,128)S(1)} %copy.53), channel_id=1, source_target_pairs={{0,1},{1,2},{2,3},{4,5},{5,6},{6,7},{8,9},{9,10},{10,11},{12,13},{... | collective-permute-start | bytes 12296 | tf_op jit(solution)/shard_map/ppermute | solution.py:18
  7.4 23.4 %collective-permute-start.5 = (f32[16,16,4]{2,1,0:T(8,128)S(1)}, f32[16,16,4]{2,1,0:T(8,128)S(1)}, u32[]{:S(2)}, u32[]{:S(2)}) collective-permute-start(f32[16,16,4]{2,1,0:T(8,128)S(1)} %copy.56), channel_id=1, source_target_pairs={{1,0},{2,1},{3,2},{5,4},{6,5},{7,6},{9,8},{10,9},{11,10},{13,12},{... | collective-permute-start | bytes 12296 | tf_op jit(solution)/shard_map/ppermute | solution.py:23
  8.8 25.3 %collective-permute-start.2 = (f32[16,10,128]{2,1,0:T(8,128)S(1)}, f32[16,10,128]{2,1,0:T(8,128)S(1)}, u32[]{:S(2)}, u32[]{:S(2)}) collective-permute-start(f32[16,10,128]{2,1,0:T(8,128)S(1)} %pad_maximum_fusion), channel_id=1, source_target_pairs={{0,4},{4,8},{8,12},{12,16},{16,20},{20,24},{24,28},{1,5},{5,9},{9,... | collective-permute-start | bytes 245768 | tf_op jit(solution)/shard_map/ppermute | solution.py:18
  10.8 23.4 %collective-permute-start.3 = (f32[16,10,128]{2,1,0:T(8,128)S(1)}, f32[16,10,128]{2,1,0:T(8,128)S(1)}, u32[]{:S(2)}, u32[]{:S(2)}) collective-permute-start(f32[16,10,128]{2,1,0:T(8,128)S(1)} %pad_maximum_fusion.1), channel_id=1, source_target_pairs={{4,0},{8,4},{12,8},{16,12},{20,16},{24,20},{28,24},{5,1},{9,5},{13... | collective-permute-start | bytes 245768 | tf_op jit(solution)/shard_map/ppermute | solution.py:23
  15.2 17.1 %collective-permute-start = (f32[4,16,128]{2,1,0:T(8,128)S(1)}, f32[4,16,128]{2,1,0:T(8,128)S(1)}, u32[]{:S(2)}, u32[]{:S(2)}) collective-permute-start(f32[4,16,128]{2,1,0:T(8,128)S(1)} %pad_maximum_fusion.4), channel_id=1, source_target_pairs={{0,32},{32,64},{64,96},{96,128},{128,160},{160,192},{192,224},{1,3... | collective-permute-start | bytes 98312 | tf_op jit(solution)/shard_map/ppermute | solution.py:18
  22.3 10.6 %collective-permute-start.1 = (f32[4,16,128]{2,1,0:T(8,128)S(1)}, f32[4,16,128]{2,1,0:T(8,128)S(1)}, u32[]{:S(2)}, u32[]{:S(2)}) collective-permute-start(f32[4,16,128]{2,1,0:T(8,128)S(1)} %pad_maximum_fusion.5), channel_id=1, source_target_pairs={{32,0},{64,32},{96,64},{128,96},{160,128},{192,160},{224,192},{33,... | collective-permute-start | bytes 98312 | tf_op jit(solution)/shard_map/ppermute | solution.py:23
  40.1 13.4 %collective-permute-start.10 = (f32[16,16,2]{2,1,0:T(8,128)}, f32[16,16,2]{2,1,0:T(8,128)S(1)}, u32[]{:S(2)}, u32[]{:S(2)}) collective-permute-start(f32[16,16,2]{2,1,0:T(8,128)} %get-tuple-element.48), channel_id=1, source_target_pairs={{0,1},{1,2},{2,3},{4,5},{5,6},{6,7},{8,9},{9,10},{10,11},{12,13},{... | collective-permute-start | bytes 6152 | tf_op jit(solution)/shard_map/ppermute | solution.py:18
  44.7 18.8 %collective-permute-start.11 = (f32[16,16,2]{2,1,0:T(8,128)}, f32[16,16,2]{2,1,0:T(8,128)S(1)}, u32[]{:S(2)}, u32[]{:S(2)}) collective-permute-start(f32[16,16,2]{2,1,0:T(8,128)} %get-tuple-element.49), channel_id=1, source_target_pairs={{1,0},{2,1},{3,2},{5,4},{6,5},{7,6},{9,8},{10,9},{11,10},{13,12},{... | collective-permute-start | bytes 6152 | tf_op jit(solution)/shard_map/ppermute | solution.py:23
  46.0 19.1 %collective-permute-start.8 = (f32[16,8,128]{2,1,0:T(8,128)}, f32[16,8,128]{2,1,0:T(8,128)S(1)}, u32[]{:S(2)}, u32[]{:S(2)}) collective-permute-start(f32[16,8,128]{2,1,0:T(8,128)} %get-tuple-element.46), channel_id=1, source_target_pairs={{0,4},{4,8},{8,12},{12,16},{16,20},{20,24},{24,28},{1,5},{5,9},{9,... | collective-permute-start | bytes 196616 | tf_op jit(solution)/shard_map/ppermute | solution.py:18
  47.9 17.2 %collective-permute-start.9 = (f32[16,8,128]{2,1,0:T(8,128)}, f32[16,8,128]{2,1,0:T(8,128)S(1)}, u32[]{:S(2)}, u32[]{:S(2)}) collective-permute-start(f32[16,8,128]{2,1,0:T(8,128)} %get-tuple-element.47), channel_id=1, source_target_pairs={{4,0},{8,4},{12,8},{16,12},{20,16},{24,20},{28,24},{5,1},{9,5},{13... | collective-permute-start | bytes 196616 | tf_op jit(solution)/shard_map/ppermute | solution.py:23
  51.6 11.9 %collective-permute-start.6 = (f32[2,16,128]{2,1,0:T(8,128)}, f32[2,16,128]{2,1,0:T(8,128)S(1)}, u32[]{:S(2)}, u32[]{:S(2)}) collective-permute-start(f32[2,16,128]{2,1,0:T(8,128)} %get-tuple-element.44), channel_id=1, source_target_pairs={{0,32},{32,64},{64,96},{96,128},{128,160},{160,192},{192,224},{1,3... | collective-permute-start | bytes 49160 | tf_op jit(solution)/shard_map/ppermute | solution.py:18
  53.5 11.6 %collective-permute-start.7 = (f32[2,16,128]{2,1,0:T(8,128)}, f32[2,16,128]{2,1,0:T(8,128)S(1)}, u32[]{:S(2)}, u32[]{:S(2)}) collective-permute-start(f32[2,16,128]{2,1,0:T(8,128)} %get-tuple-element.45), channel_id=1, source_target_pairs={{32,0},{64,32},{96,64},{128,96},{160,128},{192,160},{224,192},{33,... | collective-permute-start | bytes 49160 | tf_op jit(solution)/shard_map/ppermute | solution.py:23
  69.2 15.2 %collective-permute-start.16 = (f32[16,16,2]{2,1,0:T(8,128)}, f32[16,16,2]{2,1,0:T(8,128)S(1)}, u32[]{:S(2)}, u32[]{:S(2)}) collective-permute-start(f32[16,16,2]{2,1,0:T(8,128)} %get-tuple-element.60), channel_id=1, source_target_pairs={{0,1},{1,2},{2,3},{4,5},{5,6},{6,7},{8,9},{9,10},{10,11},{12,13},{... | collective-permute-start | bytes 6152 | tf_op jit(solution)/shard_map/ppermute | solution.py:18
  75.6 19.2 %collective-permute-start.17 = (f32[16,16,2]{2,1,0:T(8,128)S(1)}, f32[16,16,2]{2,1,0:T(8,128)S(1)}, u32[]{:S(2)}, u32[]{:S(2)}) collective-permute-start(f32[16,16,2]{2,1,0:T(8,128)S(1)} %copy-done.28), channel_id=1, source_target_pairs={{1,0},{2,1},{3,2},{5,4},{6,5},{7,6},{9,8},{10,9},{11,10},{13,12},{... | collective-permute-start | bytes 6152 | tf_op jit(solution)/shard_map/ppermute | solution.py:23
  76.9 19.3 %collective-permute-start.14 = (f32[16,8,128]{2,1,0:T(8,128)S(1)}, f32[16,8,128]{2,1,0:T(8,128)S(1)}, u32[]{:S(2)}, u32[]{:S(2)}) collective-permute-start(f32[16,8,128]{2,1,0:T(8,128)S(1)} %copy-done.31), channel_id=1, source_target_pairs={{0,4},{4,8},{8,12},{12,16},{16,20},{20,24},{24,28},{1,5},{5,9},{9,... | collective-permute-start | bytes 196616 | tf_op jit(solution)/shard_map/ppermute | solution.py:18
  78.8 17.4 %collective-permute-start.15 = (f32[16,8,128]{2,1,0:T(8,128)S(1)}, f32[16,8,128]{2,1,0:T(8,128)S(1)}, u32[]{:S(2)}, u32[]{:S(2)}) collective-permute-start(f32[16,8,128]{2,1,0:T(8,128)S(1)} %copy-done.30), channel_id=1, source_target_pairs={{4,0},{8,4},{12,8},{16,12},{20,16},{24,20},{28,24},{5,1},{9,5},{13... | collective-permute-start | bytes 196616 | tf_op jit(solution)/shard_map/ppermute | solution.py:23
  82.5 12.3 %collective-permute-start.12 = (f32[2,16,128]{2,1,0:T(8,128)S(1)}, f32[2,16,128]{2,1,0:T(8,128)S(1)}, u32[]{:S(2)}, u32[]{:S(2)}) collective-permute-start(f32[2,16,128]{2,1,0:T(8,128)S(1)} %copy-done.35), channel_id=1, source_target_pairs={{0,32},{32,64},{64,96},{96,128},{128,160},{160,192},{192,224},{1,3... | collective-permute-start | bytes 49160 | tf_op jit(solution)/shard_map/ppermute | solution.py:18
  84.4 11.8 %collective-permute-start.13 = (f32[2,16,128]{2,1,0:T(8,128)S(1)}, f32[2,16,128]{2,1,0:T(8,128)S(1)}, u32[]{:S(2)}, u32[]{:S(2)}) collective-permute-start(f32[2,16,128]{2,1,0:T(8,128)S(1)} %copy-done.34), channel_id=1, source_target_pairs={{32,0},{64,32},{96,64},{128,96},{160,128},{192,160},{224,192},{33,... | collective-permute-start | bytes 49160 | tf_op jit(solution)/shard_map/ppermute | solution.py:23
  104.6 39.6 %all-to-all-start = ((f32[64,1,128]{2,1,0:T(1,128)}), f32[64,1,128]{2,1,0:T(1,128)S(1)}, u32[]{:S(2)}, u32[]{:S(2)}) async-start(f32[64,1,128]{2,1,0:T(1,128)} %bitcast.10), calls=%async_computation | async-start | bytes 65536 | tf_op jit(solution)/shard_map/all_to_all | solution.py:33
  118.0 38.2 %collective-permute-start.20 = (f32[16,8,128]{2,1,0:T(8,128)}, f32[16,8,128]{2,1,0:T(8,128)S(1)}, u32[]{:S(2)}, u32[]{:S(2)}) collective-permute-start(f32[16,8,128]{2,1,0:T(8,128)} %get-tuple-element.70), channel_id=1, source_target_pairs={{0,4},{4,8},{8,12},{12,16},{16,20},{20,24},{24,28},{1,5},{5,9},{9,... | collective-permute-start | bytes 196616 | tf_op jit(solution)/shard_map/ppermute | solution.py:18
  120.1 36.1 %collective-permute-start.21 = (f32[16,8,128]{2,1,0:T(8,128)S(1)}, f32[16,8,128]{2,1,0:T(8,128)S(1)}, u32[]{:S(2)}, u32[]{:S(2)}) collective-permute-start(f32[16,8,128]{2,1,0:T(8,128)S(1)} %copy-done.29), channel_id=1, source_target_pairs={{4,0},{8,4},{12,8},{16,12},{20,16},{24,20},{28,24},{5,1},{9,5},{13... | collective-permute-start | bytes 196616 | tf_op jit(solution)/shard_map/ppermute | solution.py:23
  123.6 32.6 %collective-permute-start.18 = (f32[2,16,128]{2,1,0:T(8,128)S(1)}, f32[2,16,128]{2,1,0:T(8,128)S(1)}, u32[]{:S(2)}, u32[]{:S(2)}) collective-permute-start(f32[2,16,128]{2,1,0:T(8,128)S(1)} %copy-done.33), channel_id=1, source_target_pairs={{0,32},{32,64},{64,96},{96,128},{128,160},{160,192},{192,224},{1,3... | collective-permute-start | bytes 49160 | tf_op jit(solution)/shard_map/ppermute | solution.py:18
  127.1 29.1 %collective-permute-start.19 = (f32[2,16,128]{2,1,0:T(8,128)S(1)}, f32[2,16,128]{2,1,0:T(8,128)S(1)}, u32[]{:S(2)}, u32[]{:S(2)}) collective-permute-start(f32[2,16,128]{2,1,0:T(8,128)S(1)} %copy-done.32), channel_id=1, source_target_pairs={{32,0},{64,32},{96,64},{128,96},{160,128},{192,160},{224,192},{33,... | collective-permute-start | bytes 49160 | tf_op jit(solution)/shard_map/ppermute | solution.py:23
  142.9 13.3 %collective-permute-start.23 = (f32[16,16,2]{2,1,0:T(8,128)S(1)}, f32[16,16,2]{2,1,0:T(8,128)S(1)}, u32[]{:S(2)}, u32[]{:S(2)}) collective-permute-start(f32[16,16,2]{2,1,0:T(8,128)S(1)} %copy-done.27), channel_id=1, source_target_pairs={{1,0},{2,1},{3,2},{5,4},{6,5},{7,6},{9,8},{10,9},{11,10},{13,12},{... | collective-permute-start | bytes 6152 | tf_op jit(solution)/shard_map/ppermute | solution.py:23
  (38 other events, 288.0 us)

commit v5 on v4

--- a/solution.py
+++ b/solution.py
@@ -132,7 +132,7 @@
     zl1 = pick(pzl, -1, 1)
     zh1 = pick(pzh, -1, 0)
     zh2 = pick(pzh, -1, 1)
-    sfo_ref[...] = sf_ref[...] + 0.5 * (f_ocean * p_last + f_crust * p_first)
+    sfo_ref[...] = sf_ref[...] + 0.5 * (f_ocean * (p_last + zh1) + f_crust * (zl1 + p_first))
 
     pxl = pxl_ref[...]
     pxh = pxh_ref[...]
@@ -193,9 +193,6 @@
     new_p = pres - time_step * bulk_ref[...] * spread
     new_p = jnp.where(zi == 0, new_p + jnp.broadcast_to(src_ref[instant], full), new_p)
     po_ref[...] = new_p
-    sfo_ref[...] = sfo_ref[...] + 0.5 * (
-        scal_ref[base + 8] * pick(new_p, -1, Z - 1) + scal_ref[base + 9] * pick(new_p, -1, 0)
-    )
 
     sxu_ref[...] = new_p[X - 2 :]
     sxd_ref[...] = new_p[0:2]
@@ -272,8 +269,8 @@
     edge_value = jnp.where(kind == 0, e_up, jnp.where(kind == 1, e_mid, e_low))
     ocean = depth_index == first_crust // Z - 1
     crust = depth_index == first_crust // Z
-    before = step_at == 0
-    after = step_at < ITERS - 1
+    before = step_at < ITERS - 1
+    after = step_at < 0
     flag_value = jnp.where(
         entry == 6, before & ocean,
         jnp.where(entry == 7, before & crust,
@@ -340,6 +337,14 @@
                 shifted_up(sends[4], "gz"),
                 shifted_down(sends[5], "gz"),
             )
+        if instant == ITERS - 1:
+            ocean = (depth_index == first_crust // Z - 1).astype(jnp.float32)
+            crust = (depth_index == first_crust // Z).astype(jnp.float32)
+            sf_last = sf + 0.5 * (
+                ocean * (sends[4][:, :, 1:2] + halos[5][:, :, 0:1])
+                + crust * (halos[4][:, :, 1:2] + sends[5][:, :, 0:1])
+            )
+            owner_sums = seafloor_sums(sf_last[:, :, 0], node_weight, node_patch, patch_slot)
         outs = run_step(
             instant, scal_all, wint, pres, vel, inv_density, bulk, src_all, sf, halos, tracked,
             media_halo,
@@ -347,9 +352,15 @@
         pres, vel, sf = outs[0], outs[1], outs[2]
         tracked = outs[3:6]
         sends = outs[6:12]
-        if instant == ITERS - 2:
-            owner_sums = seafloor_sums(sf[:, :, 0], node_weight, node_patch, patch_slot)
-    slip_grad = summed_on_arrival(owner_sums, "gz", 0)
+    ocean_plane = first_crust // Z - 1
+    crust_plane = first_crust // Z
+    spread_out = lax.ppermute(
+        owner_sums, "gz", [(ocean_plane, ocean_plane - 1), (crust_plane, crust_plane + 1)]
+    )
+    inner = (depth_index == ocean_plane) | (depth_index == crust_plane)
+    owner_sums = jnp.where(inner, owner_sums, spread_out)
+    piece = owner_sums.shape[0] // tiles_z
+    slip_grad = lax.dynamic_slice_in_dim(owner_sums, depth_index * piece, piece)
     return (pres, vel, slip_grad)
 
 

time: 161 us -> 162 us (level)
  the two profiles are of different devices: /device:TPU:130 before, /device:TPU:24 now
where the time goes in v5:
time: 162 us; the launch traced here: 160 us
  starting transfers between devices  88.6 us (55%)
  waiting for transfers between devices  33.1 us (20%)
  local copies, waits for them, and re-layouts  16.5 us (10%)
  Pallas kernels  13.6 us (8%)
  other arithmetic  6.28 us (4%)
    ppermute x12, starting transfers between devices, shifted_up(): return lax.ppermute(x, axis, [(i, i + 1) for i in range(count - 1)])  56.6 us
    ppermute x12, waiting for transfers between devices, shifted_down(): return lax.ppermute(x, axis, [(i + 1, i) for i in range(count - 1)])  29.1 us
    ppermute x12, starting transfers between devices, shifted_down(): return lax.ppermute(x, axis, [(i + 1, i) for i in range(count - 1)])  18.7 us
    pallas_call x4, Pallas kernels, run_step(): pl.pallas_call(functools.partial(step_kernel, instant), out_shape=shapes,...  13.6 us
    all_to_all x1, starting transfers between devices, summed_on_arrival(): parts = lax.all_to_all(in_blocks(x, dim, size), axis, 0, 0, tiled=True)  12 us
    unnamed x65, local copies, waits for them, and re-layouts  6.08 us
  transfers between devices with their start and end apart: 26, of which 6 were waited for; matrix products, arithmetic and copies ran while one was open for 8% of the time, Pallas kernels for 2%

profile of v5, /device:TPU:24, one launch (start us, length us, event | category | flops | bytes accessed | tf_op | source)
XLA Modules:
  0.0 159.7 jit_solution(17648129113920420423)
XLA Ops:
  4.0 3.8 %collective-permute-start.4 = (f32[16,16,4]{2,1,0:T(8,128)S(1)}, f32[16,16,4]{2,1,0:T(8,128)S(1)}, u32[]{:S(2)}, u32[]{:S(2)}) collective-permute-start(f32[16,16,4]{2,1,0:T(8,128)S(1)} %copy.51), channel_id=1, source_target_pairs={{0,1},{1,2},{2,3},{4,5},{5,6},{6,7},{8,9},{9,10},{10,11},{12,13},{... | collective-permute-start | bytes 12296 | tf_op jit(solution)/shard_map/ppermute | solution.py:18
  13.3 7.8 %collective-permute-start = (f32[4,16,128]{2,1,0:T(8,128)S(1)}, f32[4,16,128]{2,1,0:T(8,128)S(1)}, u32[]{:S(2)}, u32[]{:S(2)}) collective-permute-start(f32[4,16,128]{2,1,0:T(8,128)S(1)} %pad_maximum_fusion.4), channel_id=1, source_target_pairs={{0,32},{32,64},{64,96},{96,128},{128,160},{160,192},{192,224},{1,3... | collective-permute-start | bytes 98312 | tf_op jit(solution)/shard_map/ppermute | solution.py:18
  28.9 7.6 %collective-permute-done.1 = f32[4,16,128]{2,1,0:T(8,128)S(1)} collective-permute-done((f32[4,16,128]{2,1,0:T(8,128)S(1)}, f32[4,16,128]{2,1,0:T(8,128)S(1)}, u32[]{:S(2)}, u32[]{:S(2)}) %collective-permute-start.1) | collective-permute-done | bytes 32800 | tf_op jit(solution)/shard_map/ppermute | solution.py:23
  40.3 3.4 %shard_map.121 = (f32[16,16,128]{2,1,0:T(8,128)}, f32[3,16,16,128]{3,2,1,0:T(8,128)}, f32[16,16,1]{2,1,0:T(8,128)}, f32[2,16,128]{2,1,0:T(8,128)}, f32[16,2,128]...) custom-call(f32[64]{0:T(128)} %reshape.152.scal_ref, ...), custom_call_target="tpu_custom_call" | custom-call | flops 2621440 | bytes 1572864 | tf_op jit(solution)/shard_map/pallas_call | solution.py:227
  43.7 3.2 %collective-permute-start.8 = (f32[16,8,128]{2,1,0:T(8,128)}, f32[16,8,128]{2,1,0:T(8,128)S(1)}, u32[]{:S(2)}, u32[]{:S(2)}) collective-permute-start(f32[16,8,128]{2,1,0:T(8,128)} %get-tuple-element.46), channel_id=1, source_target_pairs={{0,4},{4,8},{8,12},{12,16},{16,20},{20,24},{24,28},{1,5},{5,9},{9,... | collective-permute-start | bytes 196616 | tf_op jit(solution)/shard_map/ppermute | solution.py:18
  48.2 3.2 %collective-permute-start.6 = (f32[2,16,128]{2,1,0:T(8,128)}, f32[2,16,128]{2,1,0:T(8,128)S(1)}, u32[]{:S(2)}, u32[]{:S(2)}) collective-permute-start(f32[2,16,128]{2,1,0:T(8,128)} %get-tuple-element.44), channel_id=1, source_target_pairs={{0,32},{32,64},{64,96},{96,128},{128,160},{160,192},{192,224},{1,3... | collective-permute-start | bytes 49160 | tf_op jit(solution)/shard_map/ppermute | solution.py:18
  51.3 2.7 %collective-permute-start.7 = (f32[2,16,128]{2,1,0:T(8,128)}, f32[2,16,128]{2,1,0:T(8,128)S(1)}, u32[]{:S(2)}, u32[]{:S(2)}) collective-permute-start(f32[2,16,128]{2,1,0:T(8,128)} %get-tuple-element.45), channel_id=1, source_target_pairs={{32,0},{64,32},{96,64},{128,96},{160,128},{192,160},{224,192},{33,... | collective-permute-start | bytes 49160 | tf_op jit(solution)/shard_map/ppermute | solution.py:23
  54.0 4.6 %collective-permute-start.10 = (f32[16,16,2]{2,1,0:T(8,128)}, f32[16,16,2]{2,1,0:T(8,128)S(1)}, u32[]{:S(2)}, u32[]{:S(2)}) collective-permute-start(f32[16,16,2]{2,1,0:T(8,128)} %get-tuple-element.48), channel_id=1, source_target_pairs={{0,1},{1,2},{2,3},{4,5},{5,6},{6,7},{8,9},{9,10},{10,11},{12,13},{... | collective-permute-start | bytes 6152 | tf_op jit(solution)/shard_map/ppermute | solution.py:18
  58.6 2.8 %collective-permute-done.10.pzl_ref = f32[16,16,2]{2,1,0:T(8,128)S(1)} collective-permute-done((f32[16,16,2]{2,1,0:T(8,128)}, f32[16,16,2]{2,1,0:T(8,128)S(1)}, u32[]{:S(2)}, u32[]{:S(2)}) %collective-permute-start.10) | collective-permute-done | bytes 2080 | tf_op jit(solution)/shard_map/ppermute | solution.py:18
  62.7 6.1 %collective-permute-done.11.pzh_ref = f32[16,16,2]{2,1,0:T(8,128)S(1)} collective-permute-done((f32[16,16,2]{2,1,0:T(8,128)}, f32[16,16,2]{2,1,0:T(8,128)S(1)}, u32[]{:S(2)}, u32[]{:S(2)}) %collective-permute-start.11) | collective-permute-done | bytes 2080 | tf_op jit(solution)/shard_map/ppermute | solution.py:23
  69.5 3.4 %shard_map.122 = (f32[16,16,128]{2,1,0:T(8,128)}, f32[3,16,16,128]{3,2,1,0:T(8,128)}, f32[16,16,1]{2,1,0:T(8,128)}, f32[2,16,128]{2,1,0:T(8,128)}, f32[16,2,128]...) custom-call(f32[64]{0:T(128)} %reshape.152.scal_ref, ...), custom_call_target="tpu_custom_call" | custom-call | flops 2621440 | bytes 1572864 | tf_op jit(solution)/shard_map/pallas_call | solution.py:227
  73.0 4.0 %collective-permute-start.16 = (f32[16,16,2]{2,1,0:T(8,128)}, f32[16,16,2]{2,1,0:T(8,128)S(1)}, u32[]{:S(2)}, u32[]{:S(2)}) collective-permute-start(f32[16,16,2]{2,1,0:T(8,128)} %get-tuple-element.60), channel_id=1, source_target_pairs={{0,1},{1,2},{2,3},{4,5},{5,6},{6,7},{8,9},{9,10},{10,11},{12,13},{... | collective-permute-start | bytes 6152 | tf_op jit(solution)/shard_map/ppermute | solution.py:18
  78.3 2.7 %collective-permute-start.14 = (f32[16,8,128]{2,1,0:T(8,128)}, f32[16,8,128]{2,1,0:T(8,128)S(1)}, u32[]{:S(2)}, u32[]{:S(2)}) collective-permute-start(f32[16,8,128]{2,1,0:T(8,128)} %get-tuple-element.58), channel_id=1, source_target_pairs={{0,4},{4,8},{8,12},{12,16},{16,20},{20,24},{24,28},{1,5},{5,9},{9,... | collective-permute-start | bytes 196616 | tf_op jit(solution)/shard_map/ppermute | solution.py:18
  82.4 9.2 %collective-permute-start.12 = (f32[2,16,128]{2,1,0:T(8,128)}, f32[2,16,128]{2,1,0:T(8,128)S(1)}, u32[]{:S(2)}, u32[]{:S(2)}) collective-permute-start(f32[2,16,128]{2,1,0:T(8,128)} %get-tuple-element.56), channel_id=1, source_target_pairs={{0,32},{32,64},{64,96},{96,128},{128,160},{160,192},{192,224},{1,3... | collective-permute-start | bytes 49160 | tf_op jit(solution)/shard_map/ppermute | solution.py:18
  95.4 8.1 %collective-permute-done.13.pxh_ref = f32[2,16,128]{2,1,0:T(8,128)S(1)} collective-permute-done((f32[2,16,128]{2,1,0:T(8,128)}, f32[2,16,128]{2,1,0:T(8,128)S(1)}, u32[]{:S(2)}, u32[]{:S(2)}) %collective-permute-start.13) | collective-permute-done | bytes 16416 | tf_op jit(solution)/shard_map/ppermute | solution.py:23
  104.1 3.4 %shard_map.123 = (f32[16,16,128]{2,1,0:T(8,128)}, f32[3,16,16,128]{3,2,1,0:T(8,128)}, f32[16,16,1]{2,1,0:T(8,128)}, f32[2,16,128]{2,1,0:T(8,128)}, f32[16,2,128]...) custom-call(f32[64]{0:T(128)} %reshape.152.scal_ref, ...), custom_call_target="tpu_custom_call" | custom-call | flops 2621440 | bytes 1572864 | tf_op jit(solution)/shard_map/pallas_call | solution.py:227
  107.5 4.4 %collective-permute-start.22 = (f32[16,16,2]{2,1,0:T(8,128)}, f32[16,16,2]{2,1,0:T(8,128)S(1)}, u32[]{:S(2)}, u32[]{:S(2)}) collective-permute-start(f32[16,16,2]{2,1,0:T(8,128)} %get-tuple-element.72), channel_id=1, source_target_pairs={{0,1},{1,2},{2,3},{4,5},{5,6},{6,7},{8,9},{9,10},{10,11},{12,13},{... | collective-permute-start | bytes 6152 | tf_op jit(solution)/shard_map/ppermute | solution.py:18
  113.3 4.9 %collective-permute-start.20 = (f32[16,8,128]{2,1,0:T(8,128)}, f32[16,8,128]{2,1,0:T(8,128)S(1)}, u32[]{:S(2)}, u32[]{:S(2)}) collective-permute-start(f32[16,8,128]{2,1,0:T(8,128)} %get-tuple-element.70), channel_id=1, source_target_pairs={{0,4},{4,8},{8,12},{12,16},{16,20},{20,24},{24,28},{1,5},{5,9},{9,... | collective-permute-start | bytes 196616 | tf_op jit(solution)/shard_map/ppermute | solution.py:18
  121.6 2.5 %scatter_custom_fusion = f32[8192]{0:T(1024)} fusion(s32[256]{0:T(256)S(1)} %bitcast.27, f32[256]{0:T(256)S(1)} %mul.75, f32[]{:T(128)} %constant.37.clone.1), kind=kCustom, calls=%fused_computation.27 | custom fusion | flops 256 | bytes 32772 | tf_op jit(solution)/shard_map/scatter-add | solution.py:241
  124.1 12.0 %all-to-all-start = ((f32[64,1,128]{2,1,0:T(1,128)}), f32[64,1,128]{2,1,0:T(1,128)S(1)}, u32[]{:S(2)}, u32[]{:S(2)}) async-start(f32[64,1,128]{2,1,0:T(1,128)} %bitcast.10), calls=%async_computation | async-start | bytes 65536 | tf_op jit(solution)/shard_map/all_to_all | solution.py:33
  136.1 7.3 %collective-permute-start.18 = (f32[2,16,128]{2,1,0:T(8,128)S(1)}, f32[2,16,128]{2,1,0:T(8,128)S(1)}, u32[]{:S(2)}, u32[]{:S(2)}) collective-permute-start(f32[2,16,128]{2,1,0:T(8,128)S(1)} %copy-done.28), channel_id=1, source_target_pairs={{0,32},{32,64},{64,96},{96,128},{128,160},{160,192},{192,224},{1,3... | collective-permute-start | bytes 49160 | tf_op jit(solution)/shard_map/ppermute | solution.py:18
  143.4 1.9 %collective-permute-start.19 = (f32[2,16,128]{2,1,0:T(8,128)S(1)}, f32[2,16,128]{2,1,0:T(8,128)S(1)}, u32[]{:S(2)}, u32[]{:S(2)}) collective-permute-start(f32[2,16,128]{2,1,0:T(8,128)S(1)} %copy-done.27), channel_id=1, source_target_pairs={{32,0},{64,32},{96,64},{128,96},{160,128},{192,160},{224,192},{33,... | collective-permute-start | bytes 49160 | tf_op jit(solution)/shard_map/ppermute | solution.py:23
  147.9 7.2 %collective-permute-done.19.pxh_ref = f32[2,16,128]{2,1,0:T(8,128)S(1)} collective-permute-done((f32[2,16,128]{2,1,0:T(8,128)S(1)}, f32[2,16,128]{2,1,0:T(8,128)S(1)}, u32[]{:S(2)}, u32[]{:S(2)}) %collective-permute-start.19) | collective-permute-done | bytes 16416 | tf_op jit(solution)/shard_map/ppermute | solution.py:23
  155.8 3.4 %shard_map.124 = (f32[16,16,128]{2,1,0:T(8,128)}, f32[3,16,16,128]{3,2,1,0:T(8,128)}, f32[16,16,1]{2,1,0:T(8,128)}, f32[2,16,128]{2,1,0:T(8,128)}, f32[16,2,128]...) custom-call(f32[64]{0:T(128)} %reshape.152.scal_ref, ...), custom_call_target="tpu_custom_call" | custom-call | flops 2621440 | bytes 1572864 | tf_op jit(solution)/shard_map/pallas_call | solution.py:227
  (156 shorter events, 38.6 us)
Async XLA Ops:
  4.0 20.7 %collective-permute-start.4 = (f32[16,16,4]{2,1,0:T(8,128)S(1)}, f32[16,16,4]{2,1,0:T(8,128)S(1)}, u32[]{:S(2)}, u32[]{:S(2)}) collective-permute-start(f32[16,16,4]{2,1,0:T(8,128)S(1)} %copy.51), channel_id=1, source_target_pairs={{0,1},{1,2},{2,3},{4,5},{5,6},{6,7},{8,9},{9,10},{10,11},{12,13},{... | collective-permute-start | bytes 12296 | tf_op jit(solution)/shard_map/ppermute | solution.py:18
  8.3 18.4 %collective-permute-start.5 = (f32[16,16,4]{2,1,0:T(8,128)S(1)}, f32[16,16,4]{2,1,0:T(8,128)S(1)}, u32[]{:S(2)}, u32[]{:S(2)}) collective-permute-start(f32[16,16,4]{2,1,0:T(8,128)S(1)} %copy.54), channel_id=1, source_target_pairs={{1,0},{2,1},{3,2},{5,4},{6,5},{7,6},{9,8},{10,9},{11,10},{13,12},{... | collective-permute-start | bytes 12296 | tf_op jit(solution)/shard_map/ppermute | solution.py:23
  9.7 28.0 %collective-permute-start.2 = (f32[16,10,128]{2,1,0:T(8,128)S(1)}, f32[16,10,128]{2,1,0:T(8,128)S(1)}, u32[]{:S(2)}, u32[]{:S(2)}) collective-permute-start(f32[16,10,128]{2,1,0:T(8,128)S(1)} %pad_maximum_fusion), channel_id=1, source_target_pairs={{0,4},{4,8},{8,12},{12,16},{16,20},{20,24},{24,28},{1,5},{5,9},{9,... | collective-permute-start | bytes 245768 | tf_op jit(solution)/shard_map/ppermute | solution.py:18
  11.2 26.5 %collective-permute-start.3 = (f32[16,10,128]{2,1,0:T(8,128)S(1)}, f32[16,10,128]{2,1,0:T(8,128)S(1)}, u32[]{:S(2)}, u32[]{:S(2)}) collective-permute-start(f32[16,10,128]{2,1,0:T(8,128)S(1)} %pad_maximum_fusion.1), channel_id=1, source_target_pairs={{4,0},{8,4},{12,8},{16,12},{20,16},{24,20},{28,24},{5,1},{9,5},{13... | collective-permute-start | bytes 245768 | tf_op jit(solution)/shard_map/ppermute | solution.py:23
  13.3 15.0 %collective-permute-start = (f32[4,16,128]{2,1,0:T(8,128)S(1)}, f32[4,16,128]{2,1,0:T(8,128)S(1)}, u32[]{:S(2)}, u32[]{:S(2)}) collective-permute-start(f32[4,16,128]{2,1,0:T(8,128)S(1)} %pad_maximum_fusion.4), channel_id=1, source_target_pairs={{0,32},{32,64},{64,96},{96,128},{128,160},{160,192},{192,224},{1,3... | collective-permute-start | bytes 98312 | tf_op jit(solution)/shard_map/ppermute | solution.py:18
  24.7 11.8 %collective-permute-start.1 = (f32[4,16,128]{2,1,0:T(8,128)S(1)}, f32[4,16,128]{2,1,0:T(8,128)S(1)}, u32[]{:S(2)}, u32[]{:S(2)}) collective-permute-start(f32[4,16,128]{2,1,0:T(8,128)S(1)} %pad_maximum_fusion.5), channel_id=1, source_target_pairs={{32,0},{64,32},{96,64},{128,96},{160,128},{192,160},{224,192},{33,... | collective-permute-start | bytes 98312 | tf_op jit(solution)/shard_map/ppermute | solution.py:23
  43.7 25.1 %collective-permute-start.8 = (f32[16,8,128]{2,1,0:T(8,128)}, f32[16,8,128]{2,1,0:T(8,128)S(1)}, u32[]{:S(2)}, u32[]{:S(2)}) collective-permute-start(f32[16,8,128]{2,1,0:T(8,128)} %get-tuple-element.46), channel_id=1, source_target_pairs={{0,4},{4,8},{8,12},{12,16},{16,20},{20,24},{24,28},{1,5},{5,9},{9,... | collective-permute-start | bytes 196616 | tf_op jit(solution)/shard_map/ppermute | solution.py:18
  46.9 22.0 %collective-permute-start.9 = (f32[16,8,128]{2,1,0:T(8,128)}, f32[16,8,128]{2,1,0:T(8,128)S(1)}, u32[]{:S(2)}, u32[]{:S(2)}) collective-permute-start(f32[16,8,128]{2,1,0:T(8,128)} %get-tuple-element.47), channel_id=1, source_target_pairs={{4,0},{8,4},{12,8},{16,12},{20,16},{24,20},{28,24},{5,1},{9,5},{13... | collective-permute-start | bytes 196616 | tf_op jit(solution)/shard_map/ppermute | solution.py:23
  48.2 20.6 %collective-permute-start.6 = (f32[2,16,128]{2,1,0:T(8,128)}, f32[2,16,128]{2,1,0:T(8,128)S(1)}, u32[]{:S(2)}, u32[]{:S(2)}) collective-permute-start(f32[2,16,128]{2,1,0:T(8,128)} %get-tuple-element.44), channel_id=1, source_target_pairs={{0,32},{32,64},{64,96},{96,128},{128,160},{160,192},{192,224},{1,3... | collective-permute-start | bytes 49160 | tf_op jit(solution)/shard_map/ppermute | solution.py:18
  51.3 17.5 %collective-permute-start.7 = (f32[2,16,128]{2,1,0:T(8,128)}, f32[2,16,128]{2,1,0:T(8,128)S(1)}, u32[]{:S(2)}, u32[]{:S(2)}) collective-permute-start(f32[2,16,128]{2,1,0:T(8,128)} %get-tuple-element.45), channel_id=1, source_target_pairs={{32,0},{64,32},{96,64},{128,96},{160,128},{192,160},{224,192},{33,... | collective-permute-start | bytes 49160 | tf_op jit(solution)/shard_map/ppermute | solution.py:23
  73.0 18.6 %collective-permute-start.16 = (f32[16,16,2]{2,1,0:T(8,128)}, f32[16,16,2]{2,1,0:T(8,128)S(1)}, u32[]{:S(2)}, u32[]{:S(2)}) collective-permute-start(f32[16,16,2]{2,1,0:T(8,128)} %get-tuple-element.60), channel_id=1, source_target_pairs={{0,1},{1,2},{2,3},{4,5},{5,6},{6,7},{8,9},{9,10},{10,11},{12,13},{... | collective-permute-start | bytes 6152 | tf_op jit(solution)/shard_map/ppermute | solution.py:18
  77.0 18.3 %collective-permute-start.17 = (f32[16,16,2]{2,1,0:T(8,128)}, f32[16,16,2]{2,1,0:T(8,128)S(1)}, u32[]{:S(2)}, u32[]{:S(2)}) collective-permute-start(f32[16,16,2]{2,1,0:T(8,128)} %get-tuple-element.61), channel_id=1, source_target_pairs={{1,0},{2,1},{3,2},{5,4},{6,5},{7,6},{9,8},{10,9},{11,10},{13,12},{... | collective-permute-start | bytes 6152 | tf_op jit(solution)/shard_map/ppermute | solution.py:23
  78.3 25.2 %collective-permute-start.14 = (f32[16,8,128]{2,1,0:T(8,128)}, f32[16,8,128]{2,1,0:T(8,128)S(1)}, u32[]{:S(2)}, u32[]{:S(2)}) collective-permute-start(f32[16,8,128]{2,1,0:T(8,128)} %get-tuple-element.58), channel_id=1, source_target_pairs={{0,4},{4,8},{8,12},{12,16},{16,20},{20,24},{24,28},{1,5},{5,9},{9,... | collective-permute-start | bytes 196616 | tf_op jit(solution)/shard_map/ppermute | solution.py:18
  81.1 22.4 %collective-permute-start.15 = (f32[16,8,128]{2,1,0:T(8,128)}, f32[16,8,128]{2,1,0:T(8,128)S(1)}, u32[]{:S(2)}, u32[]{:S(2)}) collective-permute-start(f32[16,8,128]{2,1,0:T(8,128)} %get-tuple-element.59), channel_id=1, source_target_pairs={{4,0},{8,4},{12,8},{16,12},{20,16},{24,20},{28,24},{5,1},{9,5},{13... | collective-permute-start | bytes 196616 | tf_op jit(solution)/shard_map/ppermute | solution.py:23
  82.4 13.0 %collective-permute-start.12 = (f32[2,16,128]{2,1,0:T(8,128)}, f32[2,16,128]{2,1,0:T(8,128)S(1)}, u32[]{:S(2)}, u32[]{:S(2)}) collective-permute-start(f32[2,16,128]{2,1,0:T(8,128)} %get-tuple-element.56), channel_id=1, source_target_pairs={{0,32},{32,64},{64,96},{96,128},{128,160},{160,192},{192,224},{1,3... | collective-permute-start | bytes 49160 | tf_op jit(solution)/shard_map/ppermute | solution.py:18
  91.6 11.9 %collective-permute-start.13 = (f32[2,16,128]{2,1,0:T(8,128)}, f32[2,16,128]{2,1,0:T(8,128)S(1)}, u32[]{:S(2)}, u32[]{:S(2)}) collective-permute-start(f32[2,16,128]{2,1,0:T(8,128)} %get-tuple-element.57), channel_id=1, source_target_pairs={{32,0},{64,32},{96,64},{128,96},{160,128},{192,160},{224,192},{33,... | collective-permute-start | bytes 49160 | tf_op jit(solution)/shard_map/ppermute | solution.py:23
  107.5 11.9 %collective-permute-start.22 = (f32[16,16,2]{2,1,0:T(8,128)}, f32[16,16,2]{2,1,0:T(8,128)S(1)}, u32[]{:S(2)}, u32[]{:S(2)}) collective-permute-start(f32[16,16,2]{2,1,0:T(8,128)} %get-tuple-element.72), channel_id=1, source_target_pairs={{0,1},{1,2},{2,3},{4,5},{5,6},{6,7},{8,9},{9,10},{10,11},{12,13},{... | collective-permute-start | bytes 6152 | tf_op jit(solution)/shard_map/ppermute | solution.py:18
  111.9 7.5 %collective-permute-start.23 = (f32[16,16,2]{2,1,0:T(8,128)}, f32[16,16,2]{2,1,0:T(8,128)S(1)}, u32[]{:S(2)}, u32[]{:S(2)}) collective-permute-start(f32[16,16,2]{2,1,0:T(8,128)} %get-tuple-element.73), channel_id=1, source_target_pairs={{1,0},{2,1},{3,2},{5,4},{6,5},{7,6},{9,8},{10,9},{11,10},{13,12},{... | collective-permute-start | bytes 6152 | tf_op jit(solution)/shard_map/ppermute | solution.py:23
  113.3 41.8 %collective-permute-start.20 = (f32[16,8,128]{2,1,0:T(8,128)}, f32[16,8,128]{2,1,0:T(8,128)S(1)}, u32[]{:S(2)}, u32[]{:S(2)}) collective-permute-start(f32[16,8,128]{2,1,0:T(8,128)} %get-tuple-element.70), channel_id=1, source_target_pairs={{0,4},{4,8},{8,12},{12,16},{16,20},{20,24},{24,28},{1,5},{5,9},{9,... | collective-permute-start | bytes 196616 | tf_op jit(solution)/shard_map/ppermute | solution.py:18
  118.1 37.0 %collective-permute-start.21 = (f32[16,8,128]{2,1,0:T(8,128)}, f32[16,8,128]{2,1,0:T(8,128)S(1)}, u32[]{:S(2)}, u32[]{:S(2)}) collective-permute-start(f32[16,8,128]{2,1,0:T(8,128)} %get-tuple-element.71), channel_id=1, source_target_pairs={{4,0},{8,4},{12,8},{16,12},{20,16},{24,20},{28,24},{5,1},{9,5},{13... | collective-permute-start | bytes 196616 | tf_op jit(solution)/shard_map/ppermute | solution.py:23
  124.1 22.5 %all-to-all-start = ((f32[64,1,128]{2,1,0:T(1,128)}), f32[64,1,128]{2,1,0:T(1,128)S(1)}, u32[]{:S(2)}, u32[]{:S(2)}) async-start(f32[64,1,128]{2,1,0:T(1,128)} %bitcast.10), calls=%async_computation | async-start | bytes 65536 | tf_op jit(solution)/shard_map/all_to_all | solution.py:33
  136.1 11.8 %collective-permute-start.18 = (f32[2,16,128]{2,1,0:T(8,128)S(1)}, f32[2,16,128]{2,1,0:T(8,128)S(1)}, u32[]{:S(2)}, u32[]{:S(2)}) collective-permute-start(f32[2,16,128]{2,1,0:T(8,128)S(1)} %copy-done.28), channel_id=1, source_target_pairs={{0,32},{32,64},{64,96},{96,128},{128,160},{160,192},{192,224},{1,3... | collective-permute-start | bytes 49160 | tf_op jit(solution)/shard_map/ppermute | solution.py:18
  143.4 11.6 %collective-permute-start.19 = (f32[2,16,128]{2,1,0:T(8,128)S(1)}, f32[2,16,128]{2,1,0:T(8,128)S(1)}, u32[]{:S(2)}, u32[]{:S(2)}) collective-permute-start(f32[2,16,128]{2,1,0:T(8,128)S(1)} %copy-done.27), channel_id=1, source_target_pairs={{32,0},{64,32},{96,64},{128,96},{160,128},{192,160},{224,192},{33,... | collective-permute-start | bytes 49160 | tf_op jit(solution)/shard_map/ppermute | solution.py:23
  146.6 12.5 %collective-permute-start.24 = (f32[128]{0:T(128)S(1)}, f32[128]{0:T(128)S(1)}, u32[]{:S(2)}, u32[]{:S(2)}) collective-permute-start(f32[128]{0:T(128)S(1)} %reduce_sum.9), channel_id=1, source_target_pairs={{1,0},{2,3},{5,4},{6,7},{9,8},{10,11},{13,12},{14,15},{17,16},{18,... | collective-permute-start | bytes 1544 | tf_op jit(solution)/shard_map/ppermute | solution.py:357
  (32 other events, 194.9 us)

commit v6 on v5

--- a/solution.py
+++ b/solution.py
@@ -239,7 +239,10 @@
     sea_values = node_weight[0, 0] * seafloor.reshape(-1)
     slots = patch_slot[node_patch[0, 0]]
     partial_slip = jnp.zeros((patch_slot.shape[0],), jnp.float32).at[slots].add(sea_values)
-    return summed_on_arrival(partial_slip, ("gx", "gy"), 0)
+    rows_x, rows_y = lax.axis_size("gx"), lax.axis_size("gy")
+    by_column = jnp.moveaxis(partial_slip.reshape(rows_x, rows_y, -1), 1, 0)
+    column_sums = summed_on_arrival(by_column.reshape(-1), "gy", 0)
+    return summed_on_arrival(column_sums, "gx", 0)
 
 
 def local(

time: 162 us -> 178 us (1.099)
  the two profiles are of different devices: /device:TPU:24 before, /device:TPU:58 now
where the time goes in v6:
time: 178 us; the launch traced here: 177 us
  starting transfers between devices  83.9 us (47%)
  waiting for transfers between devices  46.2 us (26%)
  local copies, waits for them, and re-layouts  16.5 us (9%)
  Pallas kernels  13.5 us (8%)
  blocking collectives  8.75 us (5%)
  other arithmetic  6.3 us (4%)
    ppermute x12, starting transfers between devices, shifted_up(): return lax.ppermute(x, axis, [(i, i + 1) for i in range(count - 1)])  42.5 us
    ppermute x12, starting transfers between devices, shifted_down(): return lax.ppermute(x, axis, [(i + 1, i) for i in range(count - 1)])  33.8 us
    ppermute x12, waiting for transfers between devices, shifted_down(): return lax.ppermute(x, axis, [(i + 1, i) for i in range(count - 1)])  33 us
    pallas_call x4, Pallas kernels, run_step(): pl.pallas_call(functools.partial(step_kernel, instant), out_shape=shapes,...  13.5 us
    all_to_all x1, blocking collectives, summed_on_arrival(): parts = lax.all_to_all(in_blocks(x, dim, size), axis, 0, 0, tiled=True)  8.75 us
    all_to_all x1, waiting for transfers between devices, summed_on_arrival(): parts = lax.all_to_all(in_blocks(x, dim, size), axis, 0, 0, tiled=True)  7.92 us
    unnamed x69, local copies, waits for them, and re-layouts  6.05 us
    ppermute x12, waiting for transfers between devices, shifted_up(): return lax.ppermute(x, axis, [(i, i + 1) for i in range(count - 1)])  5.36 us
  transfers between devices with their start and end apart: 26, of which 8 were waited for; matrix products, arithmetic and copies ran while one was open for 5% of the time, Pallas kernels for 0%

profile of v6, /device:TPU:58, one launch (start us, length us, event | category | flops | bytes accessed | tf_op | source)
XLA Modules:
  0.0 177.0 jit_solution(3465444136513889888)
XLA Ops:
  4.0 3.8 %collective-permute-start.4 = (f32[16,16,4]{2,1,0:T(8,128)S(1)}, f32[16,16,4]{2,1,0:T(8,128)S(1)}, u32[]{:S(2)}, u32[]{:S(2)}) collective-permute-start(f32[16,16,4]{2,1,0:T(8,128)S(1)} %copy.57), channel_id=1, source_target_pairs={{0,1},{1,2},{2,3},{4,5},{5,6},{6,7},{8,9},{9,10},{10,11},{12,13},{... | collective-permute-start | bytes 12296 | tf_op jit(solution)/shard_map/ppermute | solution.py:18
  12.4 3.6 %collective-permute-start.3 = (f32[16,10,128]{2,1,0:T(8,128)S(1)}, f32[16,10,128]{2,1,0:T(8,128)S(1)}, u32[]{:S(2)}, u32[]{:S(2)}) collective-permute-start(f32[16,10,128]{2,1,0:T(8,128)S(1)} %pad_maximum_fusion.1), channel_id=1, source_target_pairs={{4,0},{8,4},{12,8},{16,12},{20,16},{24,20},{28,24},{5,1},{9,5},{13... | collective-permute-start | bytes 245768 | tf_op jit(solution)/shard_map/ppermute | solution.py:23
  16.8 7.8 %collective-permute-start = (f32[4,16,128]{2,1,0:T(8,128)S(1)}, f32[4,16,128]{2,1,0:T(8,128)S(1)}, u32[]{:S(2)}, u32[]{:S(2)}) collective-permute-start(f32[4,16,128]{2,1,0:T(8,128)S(1)} %pad_maximum_fusion.4), channel_id=1, source_target_pairs={{0,32},{32,64},{64,96},{96,128},{128,160},{160,192},{192,224},{1,3... | collective-permute-start | bytes 98312 | tf_op jit(solution)/shard_map/ppermute | solution.py:18
  32.4 7.7 %collective-permute-done.1 = f32[4,16,128]{2,1,0:T(8,128)S(1)} collective-permute-done((f32[4,16,128]{2,1,0:T(8,128)S(1)}, f32[4,16,128]{2,1,0:T(8,128)S(1)}, u32[]{:S(2)}, u32[]{:S(2)}) %collective-permute-start.1) | collective-permute-done | bytes 32800 | tf_op jit(solution)/shard_map/ppermute | solution.py:23
  43.9 3.4 %shard_map.121 = (f32[16,16,128]{2,1,0:T(8,128)}, f32[3,16,16,128]{3,2,1,0:T(8,128)}, f32[16,16,1]{2,1,0:T(8,128)}, f32[2,16,128]{2,1,0:T(8,128)}, f32[16,2,128]...) custom-call(f32[64]{0:T(128)} %reshape.159.scal_ref, ...), custom_call_target="tpu_custom_call" | custom-call | flops 2621440 | bytes 1572864 | tf_op jit(solution)/shard_map/pallas_call | solution.py:227
  49.2 3.6 %collective-permute-start.9 = (f32[16,8,128]{2,1,0:T(8,128)}, f32[16,8,128]{2,1,0:T(8,128)S(1)}, u32[]{:S(2)}, u32[]{:S(2)}) collective-permute-start(f32[16,8,128]{2,1,0:T(8,128)} %get-tuple-element.47), channel_id=1, source_target_pairs={{4,0},{8,4},{12,8},{16,12},{20,16},{24,20},{28,24},{5,1},{9,5},{13... | collective-permute-start | bytes 196616 | tf_op jit(solution)/shard_map/ppermute | solution.py:23
  55.1 3.6 %collective-permute-start.7 = (f32[2,16,128]{2,1,0:T(8,128)}, f32[2,16,128]{2,1,0:T(8,128)S(1)}, u32[]{:S(2)}, u32[]{:S(2)}) collective-permute-start(f32[2,16,128]{2,1,0:T(8,128)} %get-tuple-element.45), channel_id=1, source_target_pairs={{32,0},{64,32},{96,64},{128,96},{160,128},{192,160},{224,192},{33,... | collective-permute-start | bytes 49160 | tf_op jit(solution)/shard_map/ppermute | solution.py:23
  58.7 2.9 %collective-permute-start.10 = (f32[16,16,2]{2,1,0:T(8,128)}, f32[16,16,2]{2,1,0:T(8,128)S(1)}, u32[]{:S(2)}, u32[]{:S(2)}) collective-permute-start(f32[16,16,2]{2,1,0:T(8,128)} %get-tuple-element.48), channel_id=1, source_target_pairs={{0,1},{1,2},{2,3},{4,5},{5,6},{6,7},{8,9},{9,10},{10,11},{12,13},{... | collective-permute-start | bytes 6152 | tf_op jit(solution)/shard_map/ppermute | solution.py:18
  61.6 4.1 %collective-permute-done.10.pzl_ref = f32[16,16,2]{2,1,0:T(8,128)S(1)} collective-permute-done((f32[16,16,2]{2,1,0:T(8,128)}, f32[16,16,2]{2,1,0:T(8,128)S(1)}, u32[]{:S(2)}, u32[]{:S(2)}) %collective-permute-start.10) | collective-permute-done | bytes 2080 | tf_op jit(solution)/shard_map/ppermute | solution.py:18
  67.7 5.1 %collective-permute-done.11.pzh_ref = f32[16,16,2]{2,1,0:T(8,128)S(1)} collective-permute-done((f32[16,16,2]{2,1,0:T(8,128)}, f32[16,16,2]{2,1,0:T(8,128)S(1)}, u32[]{:S(2)}, u32[]{:S(2)}) %collective-permute-start.11) | collective-permute-done | bytes 2080 | tf_op jit(solution)/shard_map/ppermute | solution.py:23
  73.6 3.4 %shard_map.122 = (f32[16,16,128]{2,1,0:T(8,128)}, f32[3,16,16,128]{3,2,1,0:T(8,128)}, f32[16,16,1]{2,1,0:T(8,128)}, f32[2,16,128]{2,1,0:T(8,128)}, f32[16,2,128]...) custom-call(f32[64]{0:T(128)} %reshape.159.scal_ref, ...), custom_call_target="tpu_custom_call" | custom-call | flops 2621440 | bytes 1572864 | tf_op jit(solution)/shard_map/pallas_call | solution.py:227
  84.8 3.6 %collective-permute-start.15 = (f32[16,8,128]{2,1,0:T(8,128)}, f32[16,8,128]{2,1,0:T(8,128)S(1)}, u32[]{:S(2)}, u32[]{:S(2)}) collective-permute-start(f32[16,8,128]{2,1,0:T(8,128)} %get-tuple-element.59), channel_id=1, source_target_pairs={{4,0},{8,4},{12,8},{16,12},{20,16},{24,20},{28,24},{5,1},{9,5},{13... | collective-permute-start | bytes 196616 | tf_op jit(solution)/shard_map/ppermute | solution.py:23
  88.4 8.3 %collective-permute-start.12 = (f32[2,16,128]{2,1,0:T(8,128)}, f32[2,16,128]{2,1,0:T(8,128)S(1)}, u32[]{:S(2)}, u32[]{:S(2)}) collective-permute-start(f32[2,16,128]{2,1,0:T(8,128)} %get-tuple-element.56), channel_id=1, source_target_pairs={{0,32},{32,64},{64,96},{96,128},{128,160},{160,192},{192,224},{1,3... | collective-permute-start | bytes 49160 | tf_op jit(solution)/shard_map/ppermute | solution.py:18
  100.5 8.3 %collective-permute-done.13.pxh_ref = f32[2,16,128]{2,1,0:T(8,128)S(1)} collective-permute-done((f32[2,16,128]{2,1,0:T(8,128)}, f32[2,16,128]{2,1,0:T(8,128)S(1)}, u32[]{:S(2)}, u32[]{:S(2)}) %collective-permute-start.13) | collective-permute-done | bytes 16416 | tf_op jit(solution)/shard_map/ppermute | solution.py:23
  109.5 3.4 %shard_map.123 = (f32[16,16,128]{2,1,0:T(8,128)}, f32[3,16,16,128]{3,2,1,0:T(8,128)}, f32[16,16,1]{2,1,0:T(8,128)}, f32[2,16,128]{2,1,0:T(8,128)}, f32[16,2,128]...) custom-call(f32[64]{0:T(128)} %reshape.159.scal_ref, ...), custom_call_target="tpu_custom_call" | custom-call | flops 2621440 | bytes 1572864 | tf_op jit(solution)/shard_map/pallas_call | solution.py:227
  115.6 3.1 %collective-permute-start.23 = (f32[16,16,2]{2,1,0:T(8,128)}, f32[16,16,2]{2,1,0:T(8,128)S(1)}, u32[]{:S(2)}, u32[]{:S(2)}) collective-permute-start(f32[16,16,2]{2,1,0:T(8,128)} %get-tuple-element.73), channel_id=1, source_target_pairs={{1,0},{2,1},{3,2},{5,4},{6,5},{7,6},{9,8},{10,9},{11,10},{13,12},{... | collective-permute-start | bytes 6152 | tf_op jit(solution)/shard_map/ppermute | solution.py:23
  126.8 8.7 %all_to_all.18 = f32[8,1,1024]{2,1,0:T(1,128)S(1)} all-to-all(f32[8,1,1024]{2,1,0:T(1,128)S(1)} %copy.65), channel_id=1, replica_groups=mesh['gx'=8,'gy'=8,'gz'=4] {'gy'}, dimensions={0} | all-to-all | bytes 65536 | tf_op jit(solution)/shard_map/all_to_all | solution.py:33
  136.2 4.5 %all-to-all-start.1 = ((f32[8,1,128]{2,1,0:T(1,128)}), f32[8,1,128]{2,1,0:T(1,128)S(1)}, u32[]{:S(2)}, u32[]{:S(2)}) async-start(f32[8,1,128]{2,1,0:T(1,128)} %bitcast.13), calls=%async_computation.1 | async-start | bytes 8192 | tf_op jit(solution)/shard_map/all_to_all | solution.py:33
  140.7 7.9 %all-to-all-done.1 = f32[8,1,128]{2,1,0:T(1,128)S(1)} async-done(((f32[8,1,128]{2,1,0:T(1,128)}), f32[8,1,128]{2,1,0:T(1,128)S(1)}, u32[]{:S(2)}, u32[]{:S(2)}) %all-to-all-start.1) | async-done | bytes 4128 | tf_op jit(solution)/shard_map/all_to_all | solution.py:33
  148.6 3.1 %collective-permute-start.24 = (f32[128]{0:T(128)S(1)}, f32[128]{0:T(128)S(1)}, u32[]{:S(2)}, u32[]{:S(2)}) collective-permute-start(f32[128]{0:T(128)S(1)} %reduce_sum.19), channel_id=1, source_target_pairs={{1,0},{2,3},{5,4},{6,7},{9,8},{10,11},{13,12},{14,15},{17,16},{18,... | collective-permute-start | bytes 1544 | tf_op jit(solution)/shard_map/ppermute | solution.py:360
  153.7 3.6 %collective-permute-start.21 = (f32[16,8,128]{2,1,0:T(8,128)S(1)}, f32[16,8,128]{2,1,0:T(8,128)S(1)}, u32[]{:S(2)}, u32[]{:S(2)}) collective-permute-start(f32[16,8,128]{2,1,0:T(8,128)S(1)} %copy-done.27), channel_id=1, source_target_pairs={{4,0},{8,4},{12,8},{16,12},{20,16},{24,20},{28,24},{5,1},{9,5},{13... | collective-permute-start | bytes 196616 | tf_op jit(solution)/shard_map/ppermute | solution.py:23
  157.3 4.0 %collective-permute-start.18 = (f32[2,16,128]{2,1,0:T(8,128)S(1)}, f32[2,16,128]{2,1,0:T(8,128)S(1)}, u32[]{:S(2)}, u32[]{:S(2)}) collective-permute-start(f32[2,16,128]{2,1,0:T(8,128)S(1)} %copy-done.30), channel_id=1, source_target_pairs={{0,32},{32,64},{64,96},{96,128},{128,160},{160,192},{192,224},{1,3... | collective-permute-start | bytes 49160 | tf_op jit(solution)/shard_map/ppermute | solution.py:18
  163.9 9.1 %collective-permute-done.19.pxh_ref = f32[2,16,128]{2,1,0:T(8,128)S(1)} collective-permute-done((f32[2,16,128]{2,1,0:T(8,128)S(1)}, f32[2,16,128]{2,1,0:T(8,128)S(1)}, u32[]{:S(2)}, u32[]{:S(2)}) %collective-permute-start.19) | collective-permute-done | bytes 16416 | tf_op jit(solution)/shard_map/ppermute | solution.py:23
  173.6 3.4 %shard_map.124 = (f32[16,16,128]{2,1,0:T(8,128)}, f32[3,16,16,128]{3,2,1,0:T(8,128)}, f32[16,16,1]{2,1,0:T(8,128)}, f32[2,16,128]{2,1,0:T(8,128)}, f32[16,2,128]...) custom-call(f32[64]{0:T(128)} %reshape.159.scal_ref, ...), custom_call_target="tpu_custom_call" | custom-call | flops 2621440 | bytes 1572864 | tf_op jit(solution)/shard_map/pallas_call | solution.py:227
  (163 shorter events, 55.2 us)
Async XLA Ops:
  4.0 24.3 %collective-permute-start.4 = (f32[16,16,4]{2,1,0:T(8,128)S(1)}, f32[16,16,4]{2,1,0:T(8,128)S(1)}, u32[]{:S(2)}, u32[]{:S(2)}) collective-permute-start(f32[16,16,4]{2,1,0:T(8,128)S(1)} %copy.57), channel_id=1, source_target_pairs={{0,1},{1,2},{2,3},{4,5},{5,6},{6,7},{8,9},{9,10},{10,11},{12,13},{... | collective-permute-start | bytes 12296 | tf_op jit(solution)/shard_map/ppermute | solution.py:18
  8.3 22.0 %collective-permute-start.5 = (f32[16,16,4]{2,1,0:T(8,128)S(1)}, f32[16,16,4]{2,1,0:T(8,128)S(1)}, u32[]{:S(2)}, u32[]{:S(2)}) collective-permute-start(f32[16,16,4]{2,1,0:T(8,128)S(1)} %copy.60), channel_id=1, source_target_pairs={{1,0},{2,1},{3,2},{5,4},{6,5},{7,6},{9,8},{10,9},{11,10},{13,12},{... | collective-permute-start | bytes 12296 | tf_op jit(solution)/shard_map/ppermute | solution.py:23
  10.5 30.9 %collective-permute-start.2 = (f32[16,10,128]{2,1,0:T(8,128)S(1)}, f32[16,10,128]{2,1,0:T(8,128)S(1)}, u32[]{:S(2)}, u32[]{:S(2)}) collective-permute-start(f32[16,10,128]{2,1,0:T(8,128)S(1)} %pad_maximum_fusion), channel_id=1, source_target_pairs={{0,4},{4,8},{8,12},{12,16},{16,20},{20,24},{24,28},{1,5},{5,9},{9,... | collective-permute-start | bytes 245768 | tf_op jit(solution)/shard_map/ppermute | solution.py:18
  12.4 28.9 %collective-permute-start.3 = (f32[16,10,128]{2,1,0:T(8,128)S(1)}, f32[16,10,128]{2,1,0:T(8,128)S(1)}, u32[]{:S(2)}, u32[]{:S(2)}) collective-permute-start(f32[16,10,128]{2,1,0:T(8,128)S(1)} %pad_maximum_fusion.1), channel_id=1, source_target_pairs={{4,0},{8,4},{12,8},{16,12},{20,16},{24,20},{28,24},{5,1},{9,5},{13... | collective-permute-start | bytes 245768 | tf_op jit(solution)/shard_map/ppermute | solution.py:23
  16.8 15.0 %collective-permute-start = (f32[4,16,128]{2,1,0:T(8,128)S(1)}, f32[4,16,128]{2,1,0:T(8,128)S(1)}, u32[]{:S(2)}, u32[]{:S(2)}) collective-permute-start(f32[4,16,128]{2,1,0:T(8,128)S(1)} %pad_maximum_fusion.4), channel_id=1, source_target_pairs={{0,32},{32,64},{64,96},{96,128},{128,160},{160,192},{192,224},{1,3... | collective-permute-start | bytes 98312 | tf_op jit(solution)/shard_map/ppermute | solution.py:18
  28.3 11.8 %collective-permute-start.1 = (f32[4,16,128]{2,1,0:T(8,128)S(1)}, f32[4,16,128]{2,1,0:T(8,128)S(1)}, u32[]{:S(2)}, u32[]{:S(2)}) collective-permute-start(f32[4,16,128]{2,1,0:T(8,128)S(1)} %pad_maximum_fusion.5), channel_id=1, source_target_pairs={{32,0},{64,32},{96,64},{128,96},{160,128},{192,160},{224,192},{33,... | collective-permute-start | bytes 98312 | tf_op jit(solution)/shard_map/ppermute | solution.py:23
  47.3 25.6 %collective-permute-start.8 = (f32[16,8,128]{2,1,0:T(8,128)}, f32[16,8,128]{2,1,0:T(8,128)S(1)}, u32[]{:S(2)}, u32[]{:S(2)}) collective-permute-start(f32[16,8,128]{2,1,0:T(8,128)} %get-tuple-element.46), channel_id=1, source_target_pairs={{0,4},{4,8},{8,12},{12,16},{16,20},{20,24},{24,28},{1,5},{5,9},{9,... | collective-permute-start | bytes 196616 | tf_op jit(solution)/shard_map/ppermute | solution.py:18
  49.2 23.7 %collective-permute-start.9 = (f32[16,8,128]{2,1,0:T(8,128)}, f32[16,8,128]{2,1,0:T(8,128)S(1)}, u32[]{:S(2)}, u32[]{:S(2)}) collective-permute-start(f32[16,8,128]{2,1,0:T(8,128)} %get-tuple-element.47), channel_id=1, source_target_pairs={{4,0},{8,4},{12,8},{16,12},{20,16},{24,20},{28,24},{5,1},{9,5},{13... | collective-permute-start | bytes 196616 | tf_op jit(solution)/shard_map/ppermute | solution.py:23
  52.9 20.0 %collective-permute-start.6 = (f32[2,16,128]{2,1,0:T(8,128)}, f32[2,16,128]{2,1,0:T(8,128)S(1)}, u32[]{:S(2)}, u32[]{:S(2)}) collective-permute-start(f32[2,16,128]{2,1,0:T(8,128)} %get-tuple-element.44), channel_id=1, source_target_pairs={{0,32},{32,64},{64,96},{96,128},{128,160},{160,192},{192,224},{1,3... | collective-permute-start | bytes 49160 | tf_op jit(solution)/shard_map/ppermute | solution.py:18
  55.1 17.7 %collective-permute-start.7 = (f32[2,16,128]{2,1,0:T(8,128)}, f32[2,16,128]{2,1,0:T(8,128)S(1)}, u32[]{:S(2)}, u32[]{:S(2)}) collective-permute-start(f32[2,16,128]{2,1,0:T(8,128)} %get-tuple-element.45), channel_id=1, source_target_pairs={{32,0},{64,32},{96,64},{128,96},{160,128},{192,160},{224,192},{33,... | collective-permute-start | bytes 49160 | tf_op jit(solution)/shard_map/ppermute | solution.py:23
  58.7 7.1 %collective-permute-start.10 = (f32[16,16,2]{2,1,0:T(8,128)}, f32[16,16,2]{2,1,0:T(8,128)S(1)}, u32[]{:S(2)}, u32[]{:S(2)}) collective-permute-start(f32[16,16,2]{2,1,0:T(8,128)} %get-tuple-element.48), channel_id=1, source_target_pairs={{0,1},{1,2},{2,3},{4,5},{5,6},{6,7},{8,9},{9,10},{10,11},{12,13},{... | collective-permute-start | bytes 6152 | tf_op jit(solution)/shard_map/ppermute | solution.py:18
  77.0 19.8 %collective-permute-start.16 = (f32[16,16,2]{2,1,0:T(8,128)}, f32[16,16,2]{2,1,0:T(8,128)S(1)}, u32[]{:S(2)}, u32[]{:S(2)}) collective-permute-start(f32[16,16,2]{2,1,0:T(8,128)} %get-tuple-element.60), channel_id=1, source_target_pairs={{0,1},{1,2},{2,3},{4,5},{5,6},{6,7},{8,9},{9,10},{10,11},{12,13},{... | collective-permute-start | bytes 6152 | tf_op jit(solution)/shard_map/ppermute | solution.py:18
  79.9 20.5 %collective-permute-start.17 = (f32[16,16,2]{2,1,0:T(8,128)}, f32[16,16,2]{2,1,0:T(8,128)S(1)}, u32[]{:S(2)}, u32[]{:S(2)}) collective-permute-start(f32[16,16,2]{2,1,0:T(8,128)} %get-tuple-element.61), channel_id=1, source_target_pairs={{1,0},{2,1},{3,2},{5,4},{6,5},{7,6},{9,8},{10,9},{11,10},{13,12},{... | collective-permute-start | bytes 6152 | tf_op jit(solution)/shard_map/ppermute | solution.py:23
  82.9 26.0 %collective-permute-start.14 = (f32[16,8,128]{2,1,0:T(8,128)}, f32[16,8,128]{2,1,0:T(8,128)S(1)}, u32[]{:S(2)}, u32[]{:S(2)}) collective-permute-start(f32[16,8,128]{2,1,0:T(8,128)} %get-tuple-element.58), channel_id=1, source_target_pairs={{0,4},{4,8},{8,12},{12,16},{16,20},{20,24},{24,28},{1,5},{5,9},{9,... | collective-permute-start | bytes 196616 | tf_op jit(solution)/shard_map/ppermute | solution.py:18
  84.8 24.0 %collective-permute-start.15 = (f32[16,8,128]{2,1,0:T(8,128)}, f32[16,8,128]{2,1,0:T(8,128)S(1)}, u32[]{:S(2)}, u32[]{:S(2)}) collective-permute-start(f32[16,8,128]{2,1,0:T(8,128)} %get-tuple-element.59), channel_id=1, source_target_pairs={{4,0},{8,4},{12,8},{16,12},{20,16},{24,20},{28,24},{5,1},{9,5},{13... | collective-permute-start | bytes 196616 | tf_op jit(solution)/shard_map/ppermute | solution.py:23
  88.4 12.0 %collective-permute-start.12 = (f32[2,16,128]{2,1,0:T(8,128)}, f32[2,16,128]{2,1,0:T(8,128)S(1)}, u32[]{:S(2)}, u32[]{:S(2)}) collective-permute-start(f32[2,16,128]{2,1,0:T(8,128)} %get-tuple-element.56), channel_id=1, source_target_pairs={{0,32},{32,64},{64,96},{96,128},{128,160},{160,192},{192,224},{1,3... | collective-permute-start | bytes 49160 | tf_op jit(solution)/shard_map/ppermute | solution.py:18
  96.8 12.0 %collective-permute-start.13 = (f32[2,16,128]{2,1,0:T(8,128)}, f32[2,16,128]{2,1,0:T(8,128)S(1)}, u32[]{:S(2)}, u32[]{:S(2)}) collective-permute-start(f32[2,16,128]{2,1,0:T(8,128)} %get-tuple-element.57), channel_id=1, source_target_pairs={{32,0},{64,32},{96,64},{128,96},{160,128},{192,160},{224,192},{33,... | collective-permute-start | bytes 49160 | tf_op jit(solution)/shard_map/ppermute | solution.py:23
  112.9 7.1 %collective-permute-start.22 = (f32[16,16,2]{2,1,0:T(8,128)}, f32[16,16,2]{2,1,0:T(8,128)S(1)}, u32[]{:S(2)}, u32[]{:S(2)}) collective-permute-start(f32[16,16,2]{2,1,0:T(8,128)} %get-tuple-element.72), channel_id=1, source_target_pairs={{0,1},{1,2},{2,3},{4,5},{5,6},{6,7},{8,9},{9,10},{10,11},{12,13},{... | collective-permute-start | bytes 6152 | tf_op jit(solution)/shard_map/ppermute | solution.py:18
  115.6 7.1 %collective-permute-start.23 = (f32[16,16,2]{2,1,0:T(8,128)}, f32[16,16,2]{2,1,0:T(8,128)S(1)}, u32[]{:S(2)}, u32[]{:S(2)}) collective-permute-start(f32[16,16,2]{2,1,0:T(8,128)} %get-tuple-element.73), channel_id=1, source_target_pairs={{1,0},{2,1},{3,2},{5,4},{6,5},{7,6},{9,8},{10,9},{11,10},{13,12},{... | collective-permute-start | bytes 6152 | tf_op jit(solution)/shard_map/ppermute | solution.py:23
  136.2 12.4 %all-to-all-start.1 = ((f32[8,1,128]{2,1,0:T(1,128)}), f32[8,1,128]{2,1,0:T(1,128)S(1)}, u32[]{:S(2)}, u32[]{:S(2)}) async-start(f32[8,1,128]{2,1,0:T(1,128)} %bitcast.13), calls=%async_computation.1 | async-start | bytes 8192 | tf_op jit(solution)/shard_map/all_to_all | solution.py:33
  148.6 14.6 %collective-permute-start.24 = (f32[128]{0:T(128)S(1)}, f32[128]{0:T(128)S(1)}, u32[]{:S(2)}, u32[]{:S(2)}) collective-permute-start(f32[128]{0:T(128)S(1)} %reduce_sum.19), channel_id=1, source_target_pairs={{1,0},{2,3},{5,4},{6,7},{9,8},{10,11},{13,12},{14,15},{17,16},{18,... | collective-permute-start | bytes 1544 | tf_op jit(solution)/shard_map/ppermute | solution.py:360
  151.7 21.2 %collective-permute-start.20 = (f32[16,8,128]{2,1,0:T(8,128)S(1)}, f32[16,8,128]{2,1,0:T(8,128)S(1)}, u32[]{:S(2)}, u32[]{:S(2)}) collective-permute-start(f32[16,8,128]{2,1,0:T(8,128)S(1)} %copy-done.28), channel_id=1, source_target_pairs={{0,4},{4,8},{8,12},{12,16},{16,20},{20,24},{24,28},{1,5},{5,9},{9,... | collective-permute-start | bytes 196616 | tf_op jit(solution)/shard_map/ppermute | solution.py:18
  153.7 19.3 %collective-permute-start.21 = (f32[16,8,128]{2,1,0:T(8,128)S(1)}, f32[16,8,128]{2,1,0:T(8,128)S(1)}, u32[]{:S(2)}, u32[]{:S(2)}) collective-permute-start(f32[16,8,128]{2,1,0:T(8,128)S(1)} %copy-done.27), channel_id=1, source_target_pairs={{4,0},{8,4},{12,8},{16,12},{20,16},{24,20},{28,24},{5,1},{9,5},{13... | collective-permute-start | bytes 196616 | tf_op jit(solution)/shard_map/ppermute | solution.py:23
  161.3 11.6 %collective-permute-start.19 = (f32[2,16,128]{2,1,0:T(8,128)S(1)}, f32[2,16,128]{2,1,0:T(8,128)S(1)}, u32[]{:S(2)}, u32[]{:S(2)}) collective-permute-start(f32[2,16,128]{2,1,0:T(8,128)S(1)} %copy-done.29), channel_id=1, source_target_pairs={{32,0},{64,32},{96,64},{128,96},{160,128},{192,160},{224,192},{33,... | collective-permute-start | bytes 49160 | tf_op jit(solution)/shard_map/ppermute | solution.py:23
  (34 other events, 287.9 us)

commit v7 on v5

--- a/solution.py
+++ b/solution.py
@@ -68,43 +68,20 @@
     return jnp.where(where, jnp.broadcast_to(lo, shape), jnp.broadcast_to(hi, shape))
 
 
-def step_kernel(
-    instant,
-    scal_ref,
-    wint_ref,
-    p_ref,
-    v_ref,
-    idn_ref,
-    bulk_ref,
-    src_ref,
-    sf_ref,
-    pxl_ref,
-    pxh_ref,
-    pyl_ref,
-    pyh_ref,
-    pzl_ref,
-    pzh_ref,
-    vx_ref,
-    vy_ref,
-    vz_ref,
-    ix_ref,
-    iy_ref,
-    iz_ref,
-    po_ref,
-    vo_ref,
-    sfo_ref,
-    vxo_ref,
-    vyo_ref,
-    vzo_ref,
-    sxu_ref,
-    sxd_ref,
-    syu_ref,
-    syd_ref,
-    szu_ref,
-    szd_ref,
-):
+def step_kernel(instant, first, *refs):
+    if first:
+        (scal_ref, wint_ref, p_ref, v_ref, idn_ref, bulk_ref, src_ref,
+         xl_ref, xh_ref, yl_ref, yh_ref, zl_ref, zh_ref) = refs[:13]
+        outs = refs[13:]
+    else:
+        (scal_ref, wint_ref, p_ref, v_ref, idn_ref, bulk_ref, src_ref, sf_ref,
+         xl_ref, xh_ref, yl_ref, yh_ref, zl_ref, zh_ref,
+         vx_ref, vy_ref, vz_ref, ix_ref, iy_ref, iz_ref) = refs[:20]
+        outs = refs[20:]
+    (po_ref, vo_ref, sfo_ref, vxo_ref, vyo_ref, vzo_ref,
+     sxu_ref, sxd_ref, syu_ref, syd_ref, szu_ref, szd_ref) = outs[:12]
     X, Y, Z = p_ref.shape
-    rows = pyl_ref.shape[1]
+    rows = syu_ref.shape[1]
     base = instant * 16
     full = (X, Y, Z)
     yi = lax.broadcasted_iota(jnp.int32, full, 1)
@@ -121,55 +98,70 @@
     f_ocean = scal_ref[base + 6]
     f_crust = scal_ref[base + 7]
 
+    xl = xl_ref[...]
+    xh = xh_ref[...]
+    yl = yl_ref[...]
+    yh = yh_ref[...]
+    zl = zl_ref[...]
+    zh = zh_ref[...]
+    pxl2, pxl1 = xl[0:1], xl[1:2]
+    pxh1, pxh2 = xh[0:1], xh[1:2]
+    yl2, yl1 = pick(yl, 1, rows - 2), pick(yl, 1, rows - 1)
+    yh1, yh2 = pick(yh, 1, 0), pick(yh, 1, 1)
+    zl2, zl1 = pick(zl, -1, 0), pick(zl, -1, 1)
+    zh1, zh2 = pick(zh, -1, 0), pick(zh, -1, 1)
+    if first:
+        vx_lo, vx_hi, ix_lo, ix_hi = xl[2:3], xh[2:3], xl[3:4], xh[3:4]
+        vy_lo, vy_hi = pick(yl, 1, rows), pick(yh, 1, rows)
+        iy_lo, iy_hi = pick(yl, 1, rows + 1), pick(yh, 1, rows + 1)
+        vz_lo, vz_hi, iz_lo, iz_hi = pick(zl, -1, 2), pick(zh, -1, 2), pick(zl, -1, 3), pick(zh, -1, 3)
+        ixo_ref, iyo_ref, izo_ref = outs[12:15]
+        ixo_ref[0:1] = ix_lo
+        ixo_ref[1:2] = ix_hi
+        iyo_ref[...] = pair(iy_lo, iy_hi, iyo_ref.shape, 1)
+        izo_ref[...] = pair(iz_lo, iz_hi, izo_ref.shape, 2)
+    else:
+        vx = vx_ref[...]
+        ix = ix_ref[...]
+        vy = vy_ref[...]
+        iy = iy_ref[...]
+        vz = vz_ref[...]
+        iz = iz_ref[...]
+        vx_lo, vx_hi, ix_lo, ix_hi = vx[0:1], vx[1:2], ix[0:1], ix[1:2]
+        vy_lo, vy_hi = pick(vy, 1, 0), pick(vy, 1, 1)
+        iy_lo, iy_hi = pick(iy, 1, 0), pick(iy, 1, 1)
+        vz_lo, vz_hi, iz_lo, iz_hi = pick(vz, -1, 0), pick(vz, -1, 1), pick(iz, -1, 0), pick(iz, -1, 1)
+
     pres = p_ref[...]
     idn = idn_ref[...]
 
     p_first = pick(pres, -1, 0)
     p_last = pick(pres, -1, Z - 1)
-    pzl = pzl_ref[...]
-    pzh = pzh_ref[...]
-    zl2 = pick(pzl, -1, 0)
-    zl1 = pick(pzl, -1, 1)
-    zh1 = pick(pzh, -1, 0)
-    zh2 = pick(pzh, -1, 1)
-    sfo_ref[...] = sf_ref[...] + 0.5 * (f_ocean * (p_last + zh1) + f_crust * (zl1 + p_first))
-
-    pxl = pxl_ref[...]
-    pxh = pxh_ref[...]
-    above_x = jnp.concatenate([pres[1:], pxh[0:1]], axis=0)
-    below_x = jnp.concatenate([pxl[1:2], pres[:-1]], axis=0)
+    sea = 0.5 * (f_ocean * (p_last + zh1) + f_crust * (zl1 + p_first))
+    sfo_ref[...] = sea if first else sf_ref[...] + sea
+
+    above_x = jnp.concatenate([pres[1:], pxh1], axis=0)
+    below_x = jnp.concatenate([pxl1, pres[:-1]], axis=0)
     slope_x = 0.5 * (above_x - below_x)
     v0 = v_ref[0] - time_step * idn * slope_x
-    vx = vx_ref[...]
-    ix = ix_ref[...]
-    v0_lo = vx[0:1] - time_step * ix[0:1] * (0.5 * (pres[0:1] - pxl[0:1]))
-    v0_hi = vx[1:2] - time_step * ix[1:2] * (0.5 * (pxh[1:2] - pres[X - 1 : X]))
-
-    pyl = pyl_ref[...]
-    pyh = pyh_ref[...]
-    yl1 = pick(pyl, 1, rows - 1)
-    yl2 = pick(pyl, 1, rows - 2)
-    yh1 = pick(pyh, 1, 0)
-    yh2 = pick(pyh, 1, 1)
+    v0_lo = vx_lo - time_step * ix_lo * (0.5 * (pres[0:1] - pxl2))
+    v0_hi = vx_hi - time_step * ix_hi * (0.5 * (pxh2 - pres[X - 1 : X]))
+
     p_y0 = pick(pres, 1, 0)
     p_yl = pick(pres, 1, Y - 1)
     above_y = jnp.where(yi == Y - 1, jnp.broadcast_to(yh1, full), pltpu.roll(pres, Y - 1, 1))
     below_y = jnp.where(yi == 0, jnp.broadcast_to(yl1, full), pltpu.roll(pres, 1, 1))
     slope_y = 0.5 * (above_y - below_y)
     v1 = v_ref[1] - time_step * idn * slope_y
-    vy = vy_ref[...]
-    iy = iy_ref[...]
-    v1_lo = pick(vy, 1, 0) - time_step * pick(iy, 1, 0) * (0.5 * (p_y0 - yl2))
-    v1_hi = pick(vy, 1, 1) - time_step * pick(iy, 1, 1) * (0.5 * (yh2 - p_yl))
+    v1_lo = vy_lo - time_step * iy_lo * (0.5 * (p_y0 - yl2))
+    v1_hi = vy_hi - time_step * iy_hi * (0.5 * (yh2 - p_yl))
 
     above_z = jnp.where(zi == Z - 1, jnp.broadcast_to(zh1, full), pltpu.roll(pres, Z - 1, 2))
     below_z = jnp.where(zi == 0, jnp.broadcast_to(zl1, full), pltpu.roll(pres, 1, 2))
     slope_z = wu * above_z + wm * pres + wl * below_z
     v2 = v_ref[2] - time_step * idn * slope_z
-    vz = vz_ref[...]
-    iz = iz_ref[...]
-    v2_lo = pick(vz, -1, 0) - time_step * pick(iz, -1, 0) * (wu_lo * p_first + wm_lo * zl1 + wl_lo * zl2)
-    v2_hi = pick(vz, -1, 1) - time_step * pick(iz, -1, 1) * (wu_hi * zh2 + wm_hi * zh1 + wl_hi * p_last)
+    v2_lo = vz_lo - time_step * iz_lo * (wu_lo * p_first + wm_lo * zl1 + wl_lo * zl2)
+    v2_hi = vz_hi - time_step * iz_hi * (wu_hi * zh2 + wm_hi * zh1 + wl_hi * p_last)
 
     vo_ref[0] = v0
     vo_ref[1] = v1
@@ -203,11 +195,12 @@
     szd_ref[...] = pair(pick(new_p, -1, 0), pick(new_p, -1, 1), zshape, 2)
 
 
-def run_step(instant, scal, wint, pres, vel, idn, bulk, src, sf, halos, tracked, media_halo):
+def run_step(instant, operands, rows):
+    pres = operands[2]
     X, Y, Z = pres.shape
-    rows = halos[2].shape[1]
+    first = instant == 0
     f32 = jnp.float32
-    shapes = (
+    shapes = [
         jax.ShapeDtypeStruct((X, Y, Z), f32),
         jax.ShapeDtypeStruct((3, X, Y, Z), f32),
         jax.ShapeDtypeStruct((X, Y, 1), f32),
@@ -220,19 +213,21 @@
         jax.ShapeDtypeStruct((X, rows, Z), f32),
         jax.ShapeDtypeStruct((X, Y, 2), f32),
         jax.ShapeDtypeStruct((X, Y, 2), f32),
-    )
+    ]
+    if first:
+        shapes += shapes[3:6]
     vmem = pl.BlockSpec(memory_space=pltpu.VMEM)
-    in_specs = [pl.BlockSpec(memory_space=pltpu.SMEM)] + [vmem] * 19
+    in_specs = [pl.BlockSpec(memory_space=pltpu.SMEM)] + [vmem] * (len(operands) - 1)
     cells = X * Y * Z
     return pl.pallas_call(
-        functools.partial(step_kernel, instant),
-        out_shape=shapes,
+        functools.partial(step_kernel, instant, first),
+        out_shape=tuple(shapes),
         in_specs=in_specs,
         out_specs=[vmem] * len(shapes),
         cost_estimate=pl.CostEstimate(
             flops=80 * cells, transcendentals=0, bytes_accessed=4 * 4 * 12 * cells // 4
         ),
-    )(scal, wint, pres, vel, idn, bulk, src, sf, *halos, *tracked, *media_halo)
+    )(*operands)
 
 
 def seafloor_sums(seafloor, node_weight, node_patch, patch_slot):
@@ -301,31 +296,15 @@
         [pressure[:, :, Z - 2 :], v2[:, :, Z - 1 :], inv_density[:, :, Z - 1 :]], axis=2
     )
     z_dn = jnp.concatenate([pressure[:, :, :2], v2[:, :, :1], inv_density[:, :, :1]], axis=2)
-    rx_lo = shifted_up(x_up, "gx")
-    rx_hi = shifted_down(x_dn, "gx")
-    ry_lo = shifted_up(y_up, "gy")
-    ry_hi = shifted_down(y_dn, "gy")
-    rz_lo = shifted_up(z_up, "gz")
-    rz_hi = shifted_down(z_dn, "gz")
     halos = (
-        rx_lo[:2],
-        rx_hi[:2],
-        ry_lo[:, :rows],
-        ry_hi[:, :rows],
-        rz_lo[:, :, :2],
-        rz_hi[:, :, :2],
-    )
-    tracked = (
-        jnp.concatenate([rx_lo[2:3], rx_hi[2:3]], axis=0),
-        jnp.concatenate([ry_lo[:, rows : rows + 1], ry_hi[:, rows : rows + 1]], axis=1),
-        jnp.concatenate([rz_lo[:, :, 2:3], rz_hi[:, :, 2:3]], axis=2),
-    )
-    media_halo = (
-        jnp.concatenate([rx_lo[3:4], rx_hi[3:4]], axis=0),
-        jnp.concatenate([ry_lo[:, rows + 1 : rows + 2], ry_hi[:, rows + 1 : rows + 2]], axis=1),
-        jnp.concatenate([rz_lo[:, :, 3:4], rz_hi[:, :, 3:4]], axis=2),
-    )
-    sf = jnp.zeros((X, Y, 1), jnp.float32)
+        shifted_up(x_up, "gx"),
+        shifted_down(x_dn, "gx"),
+        shifted_up(y_up, "gy"),
+        shifted_down(y_dn, "gy"),
+        shifted_up(z_up, "gz"),
+        shifted_down(z_dn, "gz"),
+    )
+    common = (scal_all, wint)
     pres, vel = pressure, velocity
     for instant in range(ITERS):
         if instant > 0:
@@ -345,13 +324,16 @@
                 + crust * (halos[4][:, :, 1:2] + sends[5][:, :, 0:1])
             )
             owner_sums = seafloor_sums(sf_last[:, :, 0], node_weight, node_patch, patch_slot)
-        outs = run_step(
-            instant, scal_all, wint, pres, vel, inv_density, bulk, src_all, sf, halos, tracked,
-            media_halo,
-        )
+        if instant == 0:
+            operands = common + (pres, vel, inv_density, bulk, src_all) + halos
+        else:
+            operands = common + (pres, vel, inv_density, bulk, src_all, sf) + halos + tracked + media_halo
+        outs = run_step(instant, operands, rows)
         pres, vel, sf = outs[0], outs[1], outs[2]
         tracked = outs[3:6]
         sends = outs[6:12]
+        if instant == 0:
+            media_halo = outs[12:15]
     ocean_plane = first_crust // Z - 1
     crust_plane = first_crust // Z
     spread_out = lax.ppermute(

time: 162 us -> 157 us (0.969)
  local copies, waits for them, and re-layouts: 16.5 us -> 13.9 us
  other arithmetic: 6.28 us -> 4.17 us
    slice x10 -> x0, local copies, waits for them, and re-layouts: 2.73 us -> none  [the longest x1 0.63 us: local(): ry_lo[:, :rows]]
    concatenate x3 -> x0, other arithmetic: 2.1 us -> none  [the longest x1 0.85 us: local(): jnp.concatenate([rz_lo[:, :, 2:3], rz_hi[:, :, 2:3]], axis=2)]
    unnamed x65 -> x73, local copies, waits for them, and re-layouts: 6.08 us -> 6.85 us
  transfers between devices with their start and end apart: 26 -> 26, of which waited for: 6 -> 6; matrix products, arithmetic and copies ran while one was open for 8% -> 6% of each run, Pallas kernels for 2% -> 2%
where the time goes in v7:
time: 157 us; the launch traced here: 155 us
  starting transfers between devices  88.8 us (57%)
  waiting for transfers between devices  33 us (21%)
  local copies, waits for them, and re-layouts  13.9 us (9%)
  Pallas kernels  13.8 us (9%)
  other arithmetic  4.17 us (3%)
    ppermute x12, starting transfers between devices, shifted_up(): return lax.ppermute(x, axis, [(i, i + 1) for i in range(count - 1)])  56.9 us
    ppermute x12, waiting for transfers between devices, shifted_down(): return lax.ppermute(x, axis, [(i + 1, i) for i in range(count - 1)])  28.9 us
    ppermute x12, starting transfers between devices, shifted_down(): return lax.ppermute(x, axis, [(i + 1, i) for i in range(count - 1)])  18.6 us
    pallas_call x4, Pallas kernels, run_step(): pl.pallas_call(functools.partial(step_kernel, instant, first), out_shape=...  13.8 us
    all_to_all x1, starting transfers between devices, summed_on_arrival(): parts = lax.all_to_all(in_blocks(x, dim, size), axis, 0, 0, tiled=True)  12 us
    unnamed x73, local copies, waits for them, and re-layouts  6.85 us
  transfers between devices with their start and end apart: 26, of which 6 were waited for; matrix products, arithmetic and copies ran while one was open for 6% of the time, Pallas kernels for 2%

profile of v7, /device:TPU:24, one launch (start us, length us, event | category | flops | bytes accessed | tf_op | source)
XLA Modules:
  0.0 155.3 jit_solution(8137997732896854713)
XLA Ops:
  4.0 3.8 %collective-permute-start.4 = (f32[16,16,4]{2,1,0:T(8,128)S(1)}, f32[16,16,4]{2,1,0:T(8,128)S(1)}, u32[]{:S(2)}, u32[]{:S(2)}) collective-permute-start(f32[16,16,4]{2,1,0:T(8,128)S(1)} %copy.42), channel_id=1, source_target_pairs={{0,1},{1,2},{2,3},{4,5},{5,6},{6,7},{8,9},{9,10},{10,11},{12,13},{... | collective-permute-start | bytes 12296 | tf_op jit(solution)/shard_map/ppermute | solution.py:18
  13.3 7.8 %collective-permute-start = (f32[4,16,128]{2,1,0:T(8,128)S(1)}, f32[4,16,128]{2,1,0:T(8,128)S(1)}, u32[]{:S(2)}, u32[]{:S(2)}) collective-permute-start(f32[4,16,128]{2,1,0:T(8,128)S(1)} %pad_maximum_fusion.2), channel_id=1, source_target_pairs={{0,32},{32,64},{64,96},{96,128},{128,160},{160,192},{192,224},{1,3... | collective-permute-start | bytes 98312 | tf_op jit(solution)/shard_map/ppermute | solution.py:18
  22.4 1.9 %collective-permute-start.1 = (f32[4,16,128]{2,1,0:T(8,128)S(1)}, f32[4,16,128]{2,1,0:T(8,128)S(1)}, u32[]{:S(2)}, u32[]{:S(2)}) collective-permute-start(f32[4,16,128]{2,1,0:T(8,128)S(1)} %pad_maximum_fusion.3), channel_id=1, source_target_pairs={{32,0},{64,32},{96,64},{128,96},{160,128},{192,160},{224,192},{33,... | collective-permute-start | bytes 98312 | tf_op jit(solution)/shard_map/ppermute | solution.py:23
  26.7 7.5 %collective-permute-done.1.refs_8_ = f32[4,16,128]{2,1,0:T(8,128)S(1)} collective-permute-done((f32[4,16,128]{2,1,0:T(8,128)S(1)}, f32[4,16,128]{2,1,0:T(8,128)S(1)}, u32[]{:S(2)}, u32[]{:S(2)}) %collective-permute-start.1) | collective-permute-done | bytes 32800 | tf_op jit(solution)/shard_map/ppermute | solution.py:23
  35.5 3.4 %shard_map.121 = (f32[16,16,128]{2,1,0:T(8,128)}, f32[3,16,16,128]{3,2,1,0:T(8,128)}, f32[16,16,1]{2,1,0:T(8,128)}, f32[2,16,128]{2,1,0:T(8,128)}, f32[16,2,128]...) custom-call(f32[64]{0:T(128)} %reshape.152.refs_0_, ...), custom_call_target="tpu_custom_call" | custom-call | flops 2621440 | bytes 1572864 | tf_op jit(solution)/shard_map/pallas_call | solution.py:222
  38.9 3.2 %collective-permute-start.8 = (f32[16,8,128]{2,1,0:T(8,128)}, f32[16,8,128]{2,1,0:T(8,128)S(1)}, u32[]{:S(2)}, u32[]{:S(2)}) collective-permute-start(f32[16,8,128]{2,1,0:T(8,128)} %get-tuple-element.49), channel_id=1, source_target_pairs={{0,4},{4,8},{8,12},{12,16},{16,20},{20,24},{24,28},{1,5},{5,9},{9,... | collective-permute-start | bytes 196616 | tf_op jit(solution)/shard_map/ppermute | solution.py:18
  43.4 3.3 %collective-permute-start.6 = (f32[2,16,128]{2,1,0:T(8,128)}, f32[2,16,128]{2,1,0:T(8,128)S(1)}, u32[]{:S(2)}, u32[]{:S(2)}) collective-permute-start(f32[2,16,128]{2,1,0:T(8,128)} %get-tuple-element.47), channel_id=1, source_target_pairs={{0,32},{32,64},{64,96},{96,128},{128,160},{160,192},{192,224},{1,3... | collective-permute-start | bytes 49160 | tf_op jit(solution)/shard_map/ppermute | solution.py:18
  46.7 2.5 %collective-permute-start.7 = (f32[2,16,128]{2,1,0:T(8,128)}, f32[2,16,128]{2,1,0:T(8,128)S(1)}, u32[]{:S(2)}, u32[]{:S(2)}) collective-permute-start(f32[2,16,128]{2,1,0:T(8,128)} %get-tuple-element.48), channel_id=1, source_target_pairs={{32,0},{64,32},{96,64},{128,96},{160,128},{192,160},{224,192},{33,... | collective-permute-start | bytes 49160 | tf_op jit(solution)/shard_map/ppermute | solution.py:23
  49.2 4.6 %collective-permute-start.10 = (f32[16,16,2]{2,1,0:T(8,128)}, f32[16,16,2]{2,1,0:T(8,128)S(1)}, u32[]{:S(2)}, u32[]{:S(2)}) collective-permute-start(f32[16,16,2]{2,1,0:T(8,128)} %get-tuple-element.51), channel_id=1, source_target_pairs={{0,1},{1,2},{2,3},{4,5},{5,6},{6,7},{8,9},{9,10},{10,11},{12,13},{... | collective-permute-start | bytes 6152 | tf_op jit(solution)/shard_map/ppermute | solution.py:18
  53.8 2.8 %collective-permute-done.10.refs_12_ = f32[16,16,2]{2,1,0:T(8,128)S(1)} collective-permute-done((f32[16,16,2]{2,1,0:T(8,128)}, f32[16,16,2]{2,1,0:T(8,128)S(1)}, u32[]{:S(2)}, u32[]{:S(2)}) %collective-permute-start.10) | collective-permute-done | bytes 2080 | tf_op jit(solution)/shard_map/ppermute | solution.py:18
  57.9 6.1 %collective-permute-done.11.refs_13_ = f32[16,16,2]{2,1,0:T(8,128)S(1)} collective-permute-done((f32[16,16,2]{2,1,0:T(8,128)}, f32[16,16,2]{2,1,0:T(8,128)S(1)}, u32[]{:S(2)}, u32[]{:S(2)}) %collective-permute-start.11) | collective-permute-done | bytes 2080 | tf_op jit(solution)/shard_map/ppermute | solution.py:23
  64.7 3.5 %shard_map.122 = (f32[16,16,128]{2,1,0:T(8,128)}, f32[3,16,16,128]{3,2,1,0:T(8,128)}, f32[16,16,1]{2,1,0:T(8,128)}, f32[2,16,128]{2,1,0:T(8,128)}, f32[16,2,128]...) custom-call(f32[64]{0:T(128)} %reshape.152.refs_0_, ...), custom_call_target="tpu_custom_call" | custom-call | flops 2621440 | bytes 1572864 | tf_op jit(solution)/shard_map/pallas_call | solution.py:222
  68.2 3.9 %collective-permute-start.16 = (f32[16,16,2]{2,1,0:T(8,128)}, f32[16,16,2]{2,1,0:T(8,128)S(1)}, u32[]{:S(2)}, u32[]{:S(2)}) collective-permute-start(f32[16,16,2]{2,1,0:T(8,128)} %get-tuple-element.66), channel_id=1, source_target_pairs={{0,1},{1,2},{2,3},{4,5},{5,6},{6,7},{8,9},{9,10},{10,11},{12,13},{... | collective-permute-start | bytes 6152 | tf_op jit(solution)/shard_map/ppermute | solution.py:18
  73.5 2.9 %collective-permute-start.14 = (f32[16,8,128]{2,1,0:T(8,128)}, f32[16,8,128]{2,1,0:T(8,128)S(1)}, u32[]{:S(2)}, u32[]{:S(2)}) collective-permute-start(f32[16,8,128]{2,1,0:T(8,128)} %get-tuple-element.64), channel_id=1, source_target_pairs={{0,4},{4,8},{8,12},{12,16},{16,20},{20,24},{24,28},{1,5},{5,9},{9,... | collective-permute-start | bytes 196616 | tf_op jit(solution)/shard_map/ppermute | solution.py:18
  77.6 9.4 %collective-permute-start.12 = (f32[2,16,128]{2,1,0:T(8,128)}, f32[2,16,128]{2,1,0:T(8,128)S(1)}, u32[]{:S(2)}, u32[]{:S(2)}) collective-permute-start(f32[2,16,128]{2,1,0:T(8,128)} %get-tuple-element.62), channel_id=1, source_target_pairs={{0,32},{32,64},{64,96},{96,128},{128,160},{160,192},{192,224},{1,3... | collective-permute-start | bytes 49160 | tf_op jit(solution)/shard_map/ppermute | solution.py:18
  90.8 8.1 %collective-permute-done.13.refs_9_ = f32[2,16,128]{2,1,0:T(8,128)S(1)} collective-permute-done((f32[2,16,128]{2,1,0:T(8,128)}, f32[2,16,128]{2,1,0:T(8,128)S(1)}, u32[]{:S(2)}, u32[]{:S(2)}) %collective-permute-start.13) | collective-permute-done | bytes 16416 | tf_op jit(solution)/shard_map/ppermute | solution.py:23
  99.6 3.5 %shard_map.123 = (f32[16,16,128]{2,1,0:T(8,128)}, f32[3,16,16,128]{3,2,1,0:T(8,128)}, f32[16,16,1]{2,1,0:T(8,128)}, f32[2,16,128]{2,1,0:T(8,128)}, f32[16,2,128]...) custom-call(f32[64]{0:T(128)} %reshape.152.refs_0_, ...), custom_call_target="tpu_custom_call" | custom-call | flops 2621440 | bytes 1572864 | tf_op jit(solution)/shard_map/pallas_call | solution.py:222
  103.0 4.4 %collective-permute-start.22 = (f32[16,16,2]{2,1,0:T(8,128)}, f32[16,16,2]{2,1,0:T(8,128)S(1)}, u32[]{:S(2)}, u32[]{:S(2)}) collective-permute-start(f32[16,16,2]{2,1,0:T(8,128)} %get-tuple-element.78), channel_id=1, source_target_pairs={{0,1},{1,2},{2,3},{4,5},{5,6},{6,7},{8,9},{9,10},{10,11},{12,13},{... | collective-permute-start | bytes 6152 | tf_op jit(solution)/shard_map/ppermute | solution.py:18
  108.7 4.9 %collective-permute-start.20 = (f32[16,8,128]{2,1,0:T(8,128)}, f32[16,8,128]{2,1,0:T(8,128)S(1)}, u32[]{:S(2)}, u32[]{:S(2)}) collective-permute-start(f32[16,8,128]{2,1,0:T(8,128)} %get-tuple-element.76), channel_id=1, source_target_pairs={{0,4},{4,8},{8,12},{12,16},{16,20},{20,24},{24,28},{1,5},{5,9},{9,... | collective-permute-start | bytes 196616 | tf_op jit(solution)/shard_map/ppermute | solution.py:18
  117.1 2.5 %scatter_custom_fusion = f32[8192]{0:T(1024)} fusion(s32[256]{0:T(256)S(1)} %bitcast.23, f32[256]{0:T(256)S(1)} %mul.75, f32[]{:T(128)} %constant.37.clone.1), kind=kCustom, calls=%fused_computation.21 | custom fusion | flops 256 | bytes 32772 | tf_op jit(solution)/shard_map/scatter-add | solution.py:236
  119.6 12.0 %all-to-all-start = ((f32[64,1,128]{2,1,0:T(1,128)}), f32[64,1,128]{2,1,0:T(1,128)S(1)}, u32[]{:S(2)}, u32[]{:S(2)}) async-start(f32[64,1,128]{2,1,0:T(1,128)} %bitcast.10), calls=%async_computation | async-start | bytes 65536 | tf_op jit(solution)/shard_map/all_to_all | solution.py:33
  131.6 7.3 %collective-permute-start.18 = (f32[2,16,128]{2,1,0:T(8,128)S(1)}, f32[2,16,128]{2,1,0:T(8,128)S(1)}, u32[]{:S(2)}, u32[]{:S(2)}) collective-permute-start(f32[2,16,128]{2,1,0:T(8,128)S(1)} %copy-done.32), channel_id=1, source_target_pairs={{0,32},{32,64},{64,96},{96,128},{128,160},{160,192},{192,224},{1,3... | collective-permute-start | bytes 49160 | tf_op jit(solution)/shard_map/ppermute | solution.py:18
  143.4 7.2 %collective-permute-done.19.refs_9_ = f32[2,16,128]{2,1,0:T(8,128)S(1)} collective-permute-done((f32[2,16,128]{2,1,0:T(8,128)S(1)}, f32[2,16,128]{2,1,0:T(8,128)S(1)}, u32[]{:S(2)}, u32[]{:S(2)}) %collective-permute-start.19) | collective-permute-done | bytes 16416 | tf_op jit(solution)/shard_map/ppermute | solution.py:23
  151.3 3.4 %shard_map.124 = (f32[16,16,128]{2,1,0:T(8,128)}, f32[3,16,16,128]{3,2,1,0:T(8,128)}, f32[16,16,1]{2,1,0:T(8,128)}, f32[2,16,128]{2,1,0:T(8,128)}, f32[16,2,128]...) custom-call(f32[64]{0:T(128)} %reshape.152.refs_0_, ...), custom_call_target="tpu_custom_call" | custom-call | flops 2621440 | bytes 1572864 | tf_op jit(solution)/shard_map/pallas_call | solution.py:222
  (150 shorter events, 33.9 us)
Async XLA Ops:
  4.0 18.3 %collective-permute-start.4 = (f32[16,16,4]{2,1,0:T(8,128)S(1)}, f32[16,16,4]{2,1,0:T(8,128)S(1)}, u32[]{:S(2)}, u32[]{:S(2)}) collective-permute-start(f32[16,16,4]{2,1,0:T(8,128)S(1)} %copy.42), channel_id=1, source_target_pairs={{0,1},{1,2},{2,3},{4,5},{5,6},{6,7},{8,9},{9,10},{10,11},{12,13},{... | collective-permute-start | bytes 12296 | tf_op jit(solution)/shard_map/ppermute | solution.py:18
  8.3 18.3 %collective-permute-start.5 = (f32[16,16,4]{2,1,0:T(8,128)S(1)}, f32[16,16,4]{2,1,0:T(8,128)S(1)}, u32[]{:S(2)}, u32[]{:S(2)}) collective-permute-start(f32[16,16,4]{2,1,0:T(8,128)S(1)} %copy.45), channel_id=1, source_target_pairs={{1,0},{2,1},{3,2},{5,4},{6,5},{7,6},{9,8},{10,9},{11,10},{13,12},{... | collective-permute-start | bytes 12296 | tf_op jit(solution)/shard_map/ppermute | solution.py:23
  9.7 24.5 %collective-permute-start.2 = (f32[16,10,128]{2,1,0:T(8,128)S(1)}, f32[16,10,128]{2,1,0:T(8,128)S(1)}, u32[]{:S(2)}, u32[]{:S(2)}) collective-permute-start(f32[16,10,128]{2,1,0:T(8,128)S(1)} %pad_maximum_fusion), channel_id=1, source_target_pairs={{0,4},{4,8},{8,12},{12,16},{16,20},{20,24},{24,28},{1,5},{5,9},{9,... | collective-permute-start | bytes 245768 | tf_op jit(solution)/shard_map/ppermute | solution.py:18
  11.2 23.0 %collective-permute-start.3 = (f32[16,10,128]{2,1,0:T(8,128)S(1)}, f32[16,10,128]{2,1,0:T(8,128)S(1)}, u32[]{:S(2)}, u32[]{:S(2)}) collective-permute-start(f32[16,10,128]{2,1,0:T(8,128)S(1)} %pad_maximum_fusion.1), channel_id=1, source_target_pairs={{4,0},{8,4},{12,8},{16,12},{20,16},{24,20},{28,24},{5,1},{9,5},{13... | collective-permute-start | bytes 245768 | tf_op jit(solution)/shard_map/ppermute | solution.py:23
  13.3 13.4 %collective-permute-start = (f32[4,16,128]{2,1,0:T(8,128)S(1)}, f32[4,16,128]{2,1,0:T(8,128)S(1)}, u32[]{:S(2)}, u32[]{:S(2)}) collective-permute-start(f32[4,16,128]{2,1,0:T(8,128)S(1)} %pad_maximum_fusion.2), channel_id=1, source_target_pairs={{0,32},{32,64},{64,96},{96,128},{128,160},{160,192},{192,224},{1,3... | collective-permute-start | bytes 98312 | tf_op jit(solution)/shard_map/ppermute | solution.py:18
  22.4 11.8 %collective-permute-start.1 = (f32[4,16,128]{2,1,0:T(8,128)S(1)}, f32[4,16,128]{2,1,0:T(8,128)S(1)}, u32[]{:S(2)}, u32[]{:S(2)}) collective-permute-start(f32[4,16,128]{2,1,0:T(8,128)S(1)} %pad_maximum_fusion.3), channel_id=1, source_target_pairs={{32,0},{64,32},{96,64},{128,96},{160,128},{192,160},{224,192},{33,... | collective-permute-start | bytes 98312 | tf_op jit(solution)/shard_map/ppermute | solution.py:23
  38.9 25.1 %collective-permute-start.8 = (f32[16,8,128]{2,1,0:T(8,128)}, f32[16,8,128]{2,1,0:T(8,128)S(1)}, u32[]{:S(2)}, u32[]{:S(2)}) collective-permute-start(f32[16,8,128]{2,1,0:T(8,128)} %get-tuple-element.49), channel_id=1, source_target_pairs={{0,4},{4,8},{8,12},{12,16},{16,20},{20,24},{24,28},{1,5},{5,9},{9,... | collective-permute-start | bytes 196616 | tf_op jit(solution)/shard_map/ppermute | solution.py:18
  42.1 22.0 %collective-permute-start.9 = (f32[16,8,128]{2,1,0:T(8,128)}, f32[16,8,128]{2,1,0:T(8,128)S(1)}, u32[]{:S(2)}, u32[]{:S(2)}) collective-permute-start(f32[16,8,128]{2,1,0:T(8,128)} %get-tuple-element.50), channel_id=1, source_target_pairs={{4,0},{8,4},{12,8},{16,12},{20,16},{24,20},{28,24},{5,1},{9,5},{13... | collective-permute-start | bytes 196616 | tf_op jit(solution)/shard_map/ppermute | solution.py:23
  43.4 20.6 %collective-permute-start.6 = (f32[2,16,128]{2,1,0:T(8,128)}, f32[2,16,128]{2,1,0:T(8,128)S(1)}, u32[]{:S(2)}, u32[]{:S(2)}) collective-permute-start(f32[2,16,128]{2,1,0:T(8,128)} %get-tuple-element.47), channel_id=1, source_target_pairs={{0,32},{32,64},{64,96},{96,128},{128,160},{160,192},{192,224},{1,3... | collective-permute-start | bytes 49160 | tf_op jit(solution)/shard_map/ppermute | solution.py:18
  46.7 17.3 %collective-permute-start.7 = (f32[2,16,128]{2,1,0:T(8,128)}, f32[2,16,128]{2,1,0:T(8,128)S(1)}, u32[]{:S(2)}, u32[]{:S(2)}) collective-permute-start(f32[2,16,128]{2,1,0:T(8,128)} %get-tuple-element.48), channel_id=1, source_target_pairs={{32,0},{64,32},{96,64},{128,96},{160,128},{192,160},{224,192},{33,... | collective-permute-start | bytes 49160 | tf_op jit(solution)/shard_map/ppermute | solution.py:23
  68.2 18.8 %collective-permute-start.16 = (f32[16,16,2]{2,1,0:T(8,128)}, f32[16,16,2]{2,1,0:T(8,128)S(1)}, u32[]{:S(2)}, u32[]{:S(2)}) collective-permute-start(f32[16,16,2]{2,1,0:T(8,128)} %get-tuple-element.66), channel_id=1, source_target_pairs={{0,1},{1,2},{2,3},{4,5},{5,6},{6,7},{8,9},{9,10},{10,11},{12,13},{... | collective-permute-start | bytes 6152 | tf_op jit(solution)/shard_map/ppermute | solution.py:18
  72.2 18.6 %collective-permute-start.17 = (f32[16,16,2]{2,1,0:T(8,128)}, f32[16,16,2]{2,1,0:T(8,128)S(1)}, u32[]{:S(2)}, u32[]{:S(2)}) collective-permute-start(f32[16,16,2]{2,1,0:T(8,128)} %get-tuple-element.67), channel_id=1, source_target_pairs={{1,0},{2,1},{3,2},{5,4},{6,5},{7,6},{9,8},{10,9},{11,10},{13,12},{... | collective-permute-start | bytes 6152 | tf_op jit(solution)/shard_map/ppermute | solution.py:23
  73.5 25.4 %collective-permute-start.14 = (f32[16,8,128]{2,1,0:T(8,128)}, f32[16,8,128]{2,1,0:T(8,128)S(1)}, u32[]{:S(2)}, u32[]{:S(2)}) collective-permute-start(f32[16,8,128]{2,1,0:T(8,128)} %get-tuple-element.64), channel_id=1, source_target_pairs={{0,4},{4,8},{8,12},{12,16},{16,20},{20,24},{24,28},{1,5},{5,9},{9,... | collective-permute-start | bytes 196616 | tf_op jit(solution)/shard_map/ppermute | solution.py:18
  76.3 22.6 %collective-permute-start.15 = (f32[16,8,128]{2,1,0:T(8,128)}, f32[16,8,128]{2,1,0:T(8,128)S(1)}, u32[]{:S(2)}, u32[]{:S(2)}) collective-permute-start(f32[16,8,128]{2,1,0:T(8,128)} %get-tuple-element.65), channel_id=1, source_target_pairs={{4,0},{8,4},{12,8},{16,12},{20,16},{24,20},{28,24},{5,1},{9,5},{13... | collective-permute-start | bytes 196616 | tf_op jit(solution)/shard_map/ppermute | solution.py:23
  77.6 13.1 %collective-permute-start.12 = (f32[2,16,128]{2,1,0:T(8,128)}, f32[2,16,128]{2,1,0:T(8,128)S(1)}, u32[]{:S(2)}, u32[]{:S(2)}) collective-permute-start(f32[2,16,128]{2,1,0:T(8,128)} %get-tuple-element.62), channel_id=1, source_target_pairs={{0,32},{32,64},{64,96},{96,128},{128,160},{160,192},{192,224},{1,3... | collective-permute-start | bytes 49160 | tf_op jit(solution)/shard_map/ppermute | solution.py:18
  87.0 11.9 %collective-permute-start.13 = (f32[2,16,128]{2,1,0:T(8,128)}, f32[2,16,128]{2,1,0:T(8,128)S(1)}, u32[]{:S(2)}, u32[]{:S(2)}) collective-permute-start(f32[2,16,128]{2,1,0:T(8,128)} %get-tuple-element.63), channel_id=1, source_target_pairs={{32,0},{64,32},{96,64},{128,96},{160,128},{192,160},{224,192},{33,... | collective-permute-start | bytes 49160 | tf_op jit(solution)/shard_map/ppermute | solution.py:23
  103.0 11.9 %collective-permute-start.22 = (f32[16,16,2]{2,1,0:T(8,128)}, f32[16,16,2]{2,1,0:T(8,128)S(1)}, u32[]{:S(2)}, u32[]{:S(2)}) collective-permute-start(f32[16,16,2]{2,1,0:T(8,128)} %get-tuple-element.78), channel_id=1, source_target_pairs={{0,1},{1,2},{2,3},{4,5},{5,6},{6,7},{8,9},{9,10},{10,11},{12,13},{... | collective-permute-start | bytes 6152 | tf_op jit(solution)/shard_map/ppermute | solution.py:18
  107.4 7.5 %collective-permute-start.23 = (f32[16,16,2]{2,1,0:T(8,128)}, f32[16,16,2]{2,1,0:T(8,128)S(1)}, u32[]{:S(2)}, u32[]{:S(2)}) collective-permute-start(f32[16,16,2]{2,1,0:T(8,128)} %get-tuple-element.79), channel_id=1, source_target_pairs={{1,0},{2,1},{3,2},{5,4},{6,5},{7,6},{9,8},{10,9},{11,10},{13,12},{... | collective-permute-start | bytes 6152 | tf_op jit(solution)/shard_map/ppermute | solution.py:23
  108.7 41.9 %collective-permute-start.20 = (f32[16,8,128]{2,1,0:T(8,128)}, f32[16,8,128]{2,1,0:T(8,128)S(1)}, u32[]{:S(2)}, u32[]{:S(2)}) collective-permute-start(f32[16,8,128]{2,1,0:T(8,128)} %get-tuple-element.76), channel_id=1, source_target_pairs={{0,4},{4,8},{8,12},{12,16},{16,20},{20,24},{24,28},{1,5},{5,9},{9,... | collective-permute-start | bytes 196616 | tf_op jit(solution)/shard_map/ppermute | solution.py:18
  113.6 37.0 %collective-permute-start.21 = (f32[16,8,128]{2,1,0:T(8,128)}, f32[16,8,128]{2,1,0:T(8,128)S(1)}, u32[]{:S(2)}, u32[]{:S(2)}) collective-permute-start(f32[16,8,128]{2,1,0:T(8,128)} %get-tuple-element.77), channel_id=1, source_target_pairs={{4,0},{8,4},{12,8},{16,12},{20,16},{24,20},{28,24},{5,1},{9,5},{13... | collective-permute-start | bytes 196616 | tf_op jit(solution)/shard_map/ppermute | solution.py:23
  119.6 22.5 %all-to-all-start = ((f32[64,1,128]{2,1,0:T(1,128)}), f32[64,1,128]{2,1,0:T(1,128)S(1)}, u32[]{:S(2)}, u32[]{:S(2)}) async-start(f32[64,1,128]{2,1,0:T(1,128)} %bitcast.10), calls=%async_computation | async-start | bytes 65536 | tf_op jit(solution)/shard_map/all_to_all | solution.py:33
  131.6 11.8 %collective-permute-start.18 = (f32[2,16,128]{2,1,0:T(8,128)S(1)}, f32[2,16,128]{2,1,0:T(8,128)S(1)}, u32[]{:S(2)}, u32[]{:S(2)}) collective-permute-start(f32[2,16,128]{2,1,0:T(8,128)S(1)} %copy-done.32), channel_id=1, source_target_pairs={{0,32},{32,64},{64,96},{96,128},{128,160},{160,192},{192,224},{1,3... | collective-permute-start | bytes 49160 | tf_op jit(solution)/shard_map/ppermute | solution.py:18
  138.9 11.6 %collective-permute-start.19 = (f32[2,16,128]{2,1,0:T(8,128)S(1)}, f32[2,16,128]{2,1,0:T(8,128)S(1)}, u32[]{:S(2)}, u32[]{:S(2)}) collective-permute-start(f32[2,16,128]{2,1,0:T(8,128)S(1)} %copy-done.31), channel_id=1, source_target_pairs={{32,0},{64,32},{96,64},{128,96},{160,128},{192,160},{224,192},{33,... | collective-permute-start | bytes 49160 | tf_op jit(solution)/shard_map/ppermute | solution.py:23
  142.1 12.6 %collective-permute-start.24 = (f32[128]{0:T(128)S(1)}, f32[128]{0:T(128)S(1)}, u32[]{:S(2)}, u32[]{:S(2)}) collective-permute-start(f32[128]{0:T(128)S(1)} %reduce_sum.9), channel_id=1, source_target_pairs={{1,0},{2,3},{5,4},{6,7},{9,8},{10,11},{13,12},{14,15},{17,16},{18,... | collective-permute-start | bytes 1544 | tf_op jit(solution)/shard_map/ppermute | solution.py:339
  (36 other events, 208.7 us)

commit v8 on v7

--- a/solution.py
+++ b/solution.py
@@ -59,8 +59,7 @@
 
 
 def pick(a, axis, index):
-    where = lax.broadcasted_iota(jnp.int32, a.shape, a.ndim + axis if axis < 0 else axis) == index
-    return jnp.sum(jnp.where(where, a, 0.0), axis=axis, keepdims=True)
+    return lax.slice_in_dim(a, index, index + 1, axis=axis % a.ndim)
 
 
 def pair(lo, hi, shape, axis):

time: 157 us -> 157 us (level)
  no operation moved by 1% of the time
where the time goes in v8:
time: 157 us; the launch traced here: 155 us
  starting transfers between devices  88.8 us (57%)
  waiting for transfers between devices  33 us (21%)
  local copies, waits for them, and re-layouts  13.9 us (9%)
  Pallas kernels  13.6 us (9%)
  other arithmetic  4.16 us (3%)
    ppermute x12, starting transfers between devices, shifted_up(): return lax.ppermute(x, axis, [(i, i + 1) for i in range(count - 1)])  56.9 us
    ppermute x12, waiting for transfers between devices, shifted_down(): return lax.ppermute(x, axis, [(i + 1, i) for i in range(count - 1)])  29 us
    ppermute x12, starting transfers between devices, shifted_down(): return lax.ppermute(x, axis, [(i + 1, i) for i in range(count - 1)])  18.6 us
    pallas_call x4, Pallas kernels, run_step(): pl.pallas_call(functools.partial(step_kernel, instant, first), out_shape=...  13.6 us
    all_to_all x1, starting transfers between devices, summed_on_arrival(): parts = lax.all_to_all(in_blocks(x, dim, size), axis, 0, 0, tiled=True)  12 us
    unnamed x73, local copies, waits for them, and re-layouts  6.85 us
  transfers between devices with their start and end apart: 26, of which 6 were waited for; matrix products, arithmetic and copies ran while one was open for 6% of the time, Pallas kernels for 2%

profile of v8, /device:TPU:24, one launch (start us, length us, event | category | flops | bytes accessed | tf_op | source)
XLA Modules:
  0.0 155.1 jit_solution(6556886702697935101)
XLA Ops:
  4.0 3.8 %collective-permute-start.4 = (f32[16,16,4]{2,1,0:T(8,128)S(1)}, f32[16,16,4]{2,1,0:T(8,128)S(1)}, u32[]{:S(2)}, u32[]{:S(2)}) collective-permute-start(f32[16,16,4]{2,1,0:T(8,128)S(1)} %copy.42), channel_id=1, source_target_pairs={{0,1},{1,2},{2,3},{4,5},{5,6},{6,7},{8,9},{9,10},{10,11},{12,13},{... | collective-permute-start | bytes 12296 | tf_op jit(solution)/shard_map/ppermute | solution.py:18
  13.3 7.8 %collective-permute-start = (f32[4,16,128]{2,1,0:T(8,128)S(1)}, f32[4,16,128]{2,1,0:T(8,128)S(1)}, u32[]{:S(2)}, u32[]{:S(2)}) collective-permute-start(f32[4,16,128]{2,1,0:T(8,128)S(1)} %pad_maximum_fusion.2), channel_id=1, source_target_pairs={{0,32},{32,64},{64,96},{96,128},{128,160},{160,192},{192,224},{1,3... | collective-permute-start | bytes 98312 | tf_op jit(solution)/shard_map/ppermute | solution.py:18
  22.4 1.9 %collective-permute-start.1 = (f32[4,16,128]{2,1,0:T(8,128)S(1)}, f32[4,16,128]{2,1,0:T(8,128)S(1)}, u32[]{:S(2)}, u32[]{:S(2)}) collective-permute-start(f32[4,16,128]{2,1,0:T(8,128)S(1)} %pad_maximum_fusion.3), channel_id=1, source_target_pairs={{32,0},{64,32},{96,64},{128,96},{160,128},{192,160},{224,192},{33,... | collective-permute-start | bytes 98312 | tf_op jit(solution)/shard_map/ppermute | solution.py:23
  26.7 7.5 %collective-permute-done.1.refs_8_ = f32[4,16,128]{2,1,0:T(8,128)S(1)} collective-permute-done((f32[4,16,128]{2,1,0:T(8,128)S(1)}, f32[4,16,128]{2,1,0:T(8,128)S(1)}, u32[]{:S(2)}, u32[]{:S(2)}) %collective-permute-start.1) | collective-permute-done | bytes 32800 | tf_op jit(solution)/shard_map/ppermute | solution.py:23
  35.5 3.6 %shard_map.121 = (f32[16,16,128]{2,1,0:T(8,128)}, f32[3,16,16,128]{3,2,1,0:T(8,128)}, f32[16,16,1]{2,1,0:T(8,128)}, f32[2,16,128]{2,1,0:T(8,128)}, f32[16,2,128]...) custom-call(f32[64]{0:T(128)} %reshape.152.refs_0_, ...), custom_call_target="tpu_custom_call" | custom-call | flops 2621440 | bytes 1572864 | tf_op jit(solution)/shard_map/pallas_call | solution.py:221
  39.1 3.2 %collective-permute-start.8 = (f32[16,8,128]{2,1,0:T(8,128)}, f32[16,8,128]{2,1,0:T(8,128)S(1)}, u32[]{:S(2)}, u32[]{:S(2)}) collective-permute-start(f32[16,8,128]{2,1,0:T(8,128)} %get-tuple-element.49), channel_id=1, source_target_pairs={{0,4},{4,8},{8,12},{12,16},{16,20},{20,24},{24,28},{1,5},{5,9},{9,... | collective-permute-start | bytes 196616 | tf_op jit(solution)/shard_map/ppermute | solution.py:18
  43.6 3.3 %collective-permute-start.6 = (f32[2,16,128]{2,1,0:T(8,128)}, f32[2,16,128]{2,1,0:T(8,128)S(1)}, u32[]{:S(2)}, u32[]{:S(2)}) collective-permute-start(f32[2,16,128]{2,1,0:T(8,128)} %get-tuple-element.47), channel_id=1, source_target_pairs={{0,32},{32,64},{64,96},{96,128},{128,160},{160,192},{192,224},{1,3... | collective-permute-start | bytes 49160 | tf_op jit(solution)/shard_map/ppermute | solution.py:18
  46.9 2.5 %collective-permute-start.7 = (f32[2,16,128]{2,1,0:T(8,128)}, f32[2,16,128]{2,1,0:T(8,128)S(1)}, u32[]{:S(2)}, u32[]{:S(2)}) collective-permute-start(f32[2,16,128]{2,1,0:T(8,128)} %get-tuple-element.48), channel_id=1, source_target_pairs={{32,0},{64,32},{96,64},{128,96},{160,128},{192,160},{224,192},{33,... | collective-permute-start | bytes 49160 | tf_op jit(solution)/shard_map/ppermute | solution.py:23
  49.4 4.6 %collective-permute-start.10 = (f32[16,16,2]{2,1,0:T(8,128)}, f32[16,16,2]{2,1,0:T(8,128)S(1)}, u32[]{:S(2)}, u32[]{:S(2)}) collective-permute-start(f32[16,16,2]{2,1,0:T(8,128)} %get-tuple-element.51), channel_id=1, source_target_pairs={{0,1},{1,2},{2,3},{4,5},{5,6},{6,7},{8,9},{9,10},{10,11},{12,13},{... | collective-permute-start | bytes 6152 | tf_op jit(solution)/shard_map/ppermute | solution.py:18
  54.0 2.8 %collective-permute-done.10.refs_12_ = f32[16,16,2]{2,1,0:T(8,128)S(1)} collective-permute-done((f32[16,16,2]{2,1,0:T(8,128)}, f32[16,16,2]{2,1,0:T(8,128)S(1)}, u32[]{:S(2)}, u32[]{:S(2)}) %collective-permute-start.10) | collective-permute-done | bytes 2080 | tf_op jit(solution)/shard_map/ppermute | solution.py:18
  58.1 6.1 %collective-permute-done.11.refs_13_ = f32[16,16,2]{2,1,0:T(8,128)S(1)} collective-permute-done((f32[16,16,2]{2,1,0:T(8,128)}, f32[16,16,2]{2,1,0:T(8,128)S(1)}, u32[]{:S(2)}, u32[]{:S(2)}) %collective-permute-start.11) | collective-permute-done | bytes 2080 | tf_op jit(solution)/shard_map/ppermute | solution.py:23
  64.9 3.4 %shard_map.122 = (f32[16,16,128]{2,1,0:T(8,128)}, f32[3,16,16,128]{3,2,1,0:T(8,128)}, f32[16,16,1]{2,1,0:T(8,128)}, f32[2,16,128]{2,1,0:T(8,128)}, f32[16,2,128]...) custom-call(f32[64]{0:T(128)} %reshape.152.refs_0_, ...), custom_call_target="tpu_custom_call" | custom-call | flops 2621440 | bytes 1572864 | tf_op jit(solution)/shard_map/pallas_call | solution.py:221
  68.3 3.9 %collective-permute-start.16 = (f32[16,16,2]{2,1,0:T(8,128)}, f32[16,16,2]{2,1,0:T(8,128)S(1)}, u32[]{:S(2)}, u32[]{:S(2)}) collective-permute-start(f32[16,16,2]{2,1,0:T(8,128)} %get-tuple-element.66), channel_id=1, source_target_pairs={{0,1},{1,2},{2,3},{4,5},{5,6},{6,7},{8,9},{9,10},{10,11},{12,13},{... | collective-permute-start | bytes 6152 | tf_op jit(solution)/shard_map/ppermute | solution.py:18
  73.5 2.9 %collective-permute-start.14 = (f32[16,8,128]{2,1,0:T(8,128)}, f32[16,8,128]{2,1,0:T(8,128)S(1)}, u32[]{:S(2)}, u32[]{:S(2)}) collective-permute-start(f32[16,8,128]{2,1,0:T(8,128)} %get-tuple-element.64), channel_id=1, source_target_pairs={{0,4},{4,8},{8,12},{12,16},{16,20},{20,24},{24,28},{1,5},{5,9},{9,... | collective-permute-start | bytes 196616 | tf_op jit(solution)/shard_map/ppermute | solution.py:18
  77.7 9.4 %collective-permute-start.12 = (f32[2,16,128]{2,1,0:T(8,128)}, f32[2,16,128]{2,1,0:T(8,128)S(1)}, u32[]{:S(2)}, u32[]{:S(2)}) collective-permute-start(f32[2,16,128]{2,1,0:T(8,128)} %get-tuple-element.62), channel_id=1, source_target_pairs={{0,32},{32,64},{64,96},{96,128},{128,160},{160,192},{192,224},{1,3... | collective-permute-start | bytes 49160 | tf_op jit(solution)/shard_map/ppermute | solution.py:18
  90.9 8.1 %collective-permute-done.13.refs_9_ = f32[2,16,128]{2,1,0:T(8,128)S(1)} collective-permute-done((f32[2,16,128]{2,1,0:T(8,128)}, f32[2,16,128]{2,1,0:T(8,128)S(1)}, u32[]{:S(2)}, u32[]{:S(2)}) %collective-permute-start.13) | collective-permute-done | bytes 16416 | tf_op jit(solution)/shard_map/ppermute | solution.py:23
  99.6 3.3 %shard_map.123 = (f32[16,16,128]{2,1,0:T(8,128)}, f32[3,16,16,128]{3,2,1,0:T(8,128)}, f32[16,16,1]{2,1,0:T(8,128)}, f32[2,16,128]{2,1,0:T(8,128)}, f32[16,2,128]...) custom-call(f32[64]{0:T(128)} %reshape.152.refs_0_, ...), custom_call_target="tpu_custom_call" | custom-call | flops 2621440 | bytes 1572864 | tf_op jit(solution)/shard_map/pallas_call | solution.py:221
  103.0 4.4 %collective-permute-start.22 = (f32[16,16,2]{2,1,0:T(8,128)}, f32[16,16,2]{2,1,0:T(8,128)S(1)}, u32[]{:S(2)}, u32[]{:S(2)}) collective-permute-start(f32[16,16,2]{2,1,0:T(8,128)} %get-tuple-element.78), channel_id=1, source_target_pairs={{0,1},{1,2},{2,3},{4,5},{5,6},{6,7},{8,9},{9,10},{10,11},{12,13},{... | collective-permute-start | bytes 6152 | tf_op jit(solution)/shard_map/ppermute | solution.py:18
  108.7 4.9 %collective-permute-start.20 = (f32[16,8,128]{2,1,0:T(8,128)}, f32[16,8,128]{2,1,0:T(8,128)S(1)}, u32[]{:S(2)}, u32[]{:S(2)}) collective-permute-start(f32[16,8,128]{2,1,0:T(8,128)} %get-tuple-element.76), channel_id=1, source_target_pairs={{0,4},{4,8},{8,12},{12,16},{16,20},{20,24},{24,28},{1,5},{5,9},{9,... | collective-permute-start | bytes 196616 | tf_op jit(solution)/shard_map/ppermute | solution.py:18
  117.0 2.5 %scatter_custom_fusion = f32[8192]{0:T(1024)} fusion(s32[256]{0:T(256)S(1)} %bitcast.23, f32[256]{0:T(256)S(1)} %mul.75, f32[]{:T(128)} %constant.37.clone.1), kind=kCustom, calls=%fused_computation.21 | custom fusion | flops 256 | bytes 32772 | tf_op jit(solution)/shard_map/scatter-add | solution.py:235
  119.5 12.0 %all-to-all-start = ((f32[64,1,128]{2,1,0:T(1,128)}), f32[64,1,128]{2,1,0:T(1,128)S(1)}, u32[]{:S(2)}, u32[]{:S(2)}) async-start(f32[64,1,128]{2,1,0:T(1,128)} %bitcast.10), calls=%async_computation | async-start | bytes 65536 | tf_op jit(solution)/shard_map/all_to_all | solution.py:33
  131.5 7.3 %collective-permute-start.18 = (f32[2,16,128]{2,1,0:T(8,128)S(1)}, f32[2,16,128]{2,1,0:T(8,128)S(1)}, u32[]{:S(2)}, u32[]{:S(2)}) collective-permute-start(f32[2,16,128]{2,1,0:T(8,128)S(1)} %copy-done.32), channel_id=1, source_target_pairs={{0,32},{32,64},{64,96},{96,128},{128,160},{160,192},{192,224},{1,3... | collective-permute-start | bytes 49160 | tf_op jit(solution)/shard_map/ppermute | solution.py:18
  143.3 7.2 %collective-permute-done.19.refs_9_ = f32[2,16,128]{2,1,0:T(8,128)S(1)} collective-permute-done((f32[2,16,128]{2,1,0:T(8,128)S(1)}, f32[2,16,128]{2,1,0:T(8,128)S(1)}, u32[]{:S(2)}, u32[]{:S(2)}) %collective-permute-start.19) | collective-permute-done | bytes 16416 | tf_op jit(solution)/shard_map/ppermute | solution.py:23
  151.2 3.3 %shard_map.124 = (f32[16,16,128]{2,1,0:T(8,128)}, f32[3,16,16,128]{3,2,1,0:T(8,128)}, f32[16,16,1]{2,1,0:T(8,128)}, f32[2,16,128]{2,1,0:T(8,128)}, f32[16,2,128]...) custom-call(f32[64]{0:T(128)} %reshape.152.refs_0_, ...), custom_call_target="tpu_custom_call" | custom-call | flops 2621440 | bytes 1572864 | tf_op jit(solution)/shard_map/pallas_call | solution.py:221
  (150 shorter events, 33.9 us)
Async XLA Ops:
  4.0 18.3 %collective-permute-start.4 = (f32[16,16,4]{2,1,0:T(8,128)S(1)}, f32[16,16,4]{2,1,0:T(8,128)S(1)}, u32[]{:S(2)}, u32[]{:S(2)}) collective-permute-start(f32[16,16,4]{2,1,0:T(8,128)S(1)} %copy.42), channel_id=1, source_target_pairs={{0,1},{1,2},{2,3},{4,5},{5,6},{6,7},{8,9},{9,10},{10,11},{12,13},{... | collective-permute-start | bytes 12296 | tf_op jit(solution)/shard_map/ppermute | solution.py:18
  8.3 18.3 %collective-permute-start.5 = (f32[16,16,4]{2,1,0:T(8,128)S(1)}, f32[16,16,4]{2,1,0:T(8,128)S(1)}, u32[]{:S(2)}, u32[]{:S(2)}) collective-permute-start(f32[16,16,4]{2,1,0:T(8,128)S(1)} %copy.45), channel_id=1, source_target_pairs={{1,0},{2,1},{3,2},{5,4},{6,5},{7,6},{9,8},{10,9},{11,10},{13,12},{... | collective-permute-start | bytes 12296 | tf_op jit(solution)/shard_map/ppermute | solution.py:23
  9.7 24.5 %collective-permute-start.2 = (f32[16,10,128]{2,1,0:T(8,128)S(1)}, f32[16,10,128]{2,1,0:T(8,128)S(1)}, u32[]{:S(2)}, u32[]{:S(2)}) collective-permute-start(f32[16,10,128]{2,1,0:T(8,128)S(1)} %pad_maximum_fusion), channel_id=1, source_target_pairs={{0,4},{4,8},{8,12},{12,16},{16,20},{20,24},{24,28},{1,5},{5,9},{9,... | collective-permute-start | bytes 245768 | tf_op jit(solution)/shard_map/ppermute | solution.py:18
  11.2 23.0 %collective-permute-start.3 = (f32[16,10,128]{2,1,0:T(8,128)S(1)}, f32[16,10,128]{2,1,0:T(8,128)S(1)}, u32[]{:S(2)}, u32[]{:S(2)}) collective-permute-start(f32[16,10,128]{2,1,0:T(8,128)S(1)} %pad_maximum_fusion.1), channel_id=1, source_target_pairs={{4,0},{8,4},{12,8},{16,12},{20,16},{24,20},{28,24},{5,1},{9,5},{13... | collective-permute-start | bytes 245768 | tf_op jit(solution)/shard_map/ppermute | solution.py:23
  13.3 13.4 %collective-permute-start = (f32[4,16,128]{2,1,0:T(8,128)S(1)}, f32[4,16,128]{2,1,0:T(8,128)S(1)}, u32[]{:S(2)}, u32[]{:S(2)}) collective-permute-start(f32[4,16,128]{2,1,0:T(8,128)S(1)} %pad_maximum_fusion.2), channel_id=1, source_target_pairs={{0,32},{32,64},{64,96},{96,128},{128,160},{160,192},{192,224},{1,3... | collective-permute-start | bytes 98312 | tf_op jit(solution)/shard_map/ppermute | solution.py:18
  22.4 11.8 %collective-permute-start.1 = (f32[4,16,128]{2,1,0:T(8,128)S(1)}, f32[4,16,128]{2,1,0:T(8,128)S(1)}, u32[]{:S(2)}, u32[]{:S(2)}) collective-permute-start(f32[4,16,128]{2,1,0:T(8,128)S(1)} %pad_maximum_fusion.3), channel_id=1, source_target_pairs={{32,0},{64,32},{96,64},{128,96},{160,128},{192,160},{224,192},{33,... | collective-permute-start | bytes 98312 | tf_op jit(solution)/shard_map/ppermute | solution.py:23
  39.1 25.1 %collective-permute-start.8 = (f32[16,8,128]{2,1,0:T(8,128)}, f32[16,8,128]{2,1,0:T(8,128)S(1)}, u32[]{:S(2)}, u32[]{:S(2)}) collective-permute-start(f32[16,8,128]{2,1,0:T(8,128)} %get-tuple-element.49), channel_id=1, source_target_pairs={{0,4},{4,8},{8,12},{12,16},{16,20},{20,24},{24,28},{1,5},{5,9},{9,... | collective-permute-start | bytes 196616 | tf_op jit(solution)/shard_map/ppermute | solution.py:18
  42.3 22.0 %collective-permute-start.9 = (f32[16,8,128]{2,1,0:T(8,128)}, f32[16,8,128]{2,1,0:T(8,128)S(1)}, u32[]{:S(2)}, u32[]{:S(2)}) collective-permute-start(f32[16,8,128]{2,1,0:T(8,128)} %get-tuple-element.50), channel_id=1, source_target_pairs={{4,0},{8,4},{12,8},{16,12},{20,16},{24,20},{28,24},{5,1},{9,5},{13... | collective-permute-start | bytes 196616 | tf_op jit(solution)/shard_map/ppermute | solution.py:23
  43.6 20.6 %collective-permute-start.6 = (f32[2,16,128]{2,1,0:T(8,128)}, f32[2,16,128]{2,1,0:T(8,128)S(1)}, u32[]{:S(2)}, u32[]{:S(2)}) collective-permute-start(f32[2,16,128]{2,1,0:T(8,128)} %get-tuple-element.47), channel_id=1, source_target_pairs={{0,32},{32,64},{64,96},{96,128},{128,160},{160,192},{192,224},{1,3... | collective-permute-start | bytes 49160 | tf_op jit(solution)/shard_map/ppermute | solution.py:18
  46.9 17.3 %collective-permute-start.7 = (f32[2,16,128]{2,1,0:T(8,128)}, f32[2,16,128]{2,1,0:T(8,128)S(1)}, u32[]{:S(2)}, u32[]{:S(2)}) collective-permute-start(f32[2,16,128]{2,1,0:T(8,128)} %get-tuple-element.48), channel_id=1, source_target_pairs={{32,0},{64,32},{96,64},{128,96},{160,128},{192,160},{224,192},{33,... | collective-permute-start | bytes 49160 | tf_op jit(solution)/shard_map/ppermute | solution.py:23
  68.3 18.8 %collective-permute-start.16 = (f32[16,16,2]{2,1,0:T(8,128)}, f32[16,16,2]{2,1,0:T(8,128)S(1)}, u32[]{:S(2)}, u32[]{:S(2)}) collective-permute-start(f32[16,16,2]{2,1,0:T(8,128)} %get-tuple-element.66), channel_id=1, source_target_pairs={{0,1},{1,2},{2,3},{4,5},{5,6},{6,7},{8,9},{9,10},{10,11},{12,13},{... | collective-permute-start | bytes 6152 | tf_op jit(solution)/shard_map/ppermute | solution.py:18
  72.2 18.6 %collective-permute-start.17 = (f32[16,16,2]{2,1,0:T(8,128)}, f32[16,16,2]{2,1,0:T(8,128)S(1)}, u32[]{:S(2)}, u32[]{:S(2)}) collective-permute-start(f32[16,16,2]{2,1,0:T(8,128)} %get-tuple-element.67), channel_id=1, source_target_pairs={{1,0},{2,1},{3,2},{5,4},{6,5},{7,6},{9,8},{10,9},{11,10},{13,12},{... | collective-permute-start | bytes 6152 | tf_op jit(solution)/shard_map/ppermute | solution.py:23
  73.5 25.4 %collective-permute-start.14 = (f32[16,8,128]{2,1,0:T(8,128)}, f32[16,8,128]{2,1,0:T(8,128)S(1)}, u32[]{:S(2)}, u32[]{:S(2)}) collective-permute-start(f32[16,8,128]{2,1,0:T(8,128)} %get-tuple-element.64), channel_id=1, source_target_pairs={{0,4},{4,8},{8,12},{12,16},{16,20},{20,24},{24,28},{1,5},{5,9},{9,... | collective-permute-start | bytes 196616 | tf_op jit(solution)/shard_map/ppermute | solution.py:18
  76.4 22.6 %collective-permute-start.15 = (f32[16,8,128]{2,1,0:T(8,128)}, f32[16,8,128]{2,1,0:T(8,128)S(1)}, u32[]{:S(2)}, u32[]{:S(2)}) collective-permute-start(f32[16,8,128]{2,1,0:T(8,128)} %get-tuple-element.65), channel_id=1, source_target_pairs={{4,0},{8,4},{12,8},{16,12},{20,16},{24,20},{28,24},{5,1},{9,5},{13... | collective-permute-start | bytes 196616 | tf_op jit(solution)/shard_map/ppermute | solution.py:23
  77.7 13.1 %collective-permute-start.12 = (f32[2,16,128]{2,1,0:T(8,128)}, f32[2,16,128]{2,1,0:T(8,128)S(1)}, u32[]{:S(2)}, u32[]{:S(2)}) collective-permute-start(f32[2,16,128]{2,1,0:T(8,128)} %get-tuple-element.62), channel_id=1, source_target_pairs={{0,32},{32,64},{64,96},{96,128},{128,160},{160,192},{192,224},{1,3... | collective-permute-start | bytes 49160 | tf_op jit(solution)/shard_map/ppermute | solution.py:18
  87.1 11.9 %collective-permute-start.13 = (f32[2,16,128]{2,1,0:T(8,128)}, f32[2,16,128]{2,1,0:T(8,128)S(1)}, u32[]{:S(2)}, u32[]{:S(2)}) collective-permute-start(f32[2,16,128]{2,1,0:T(8,128)} %get-tuple-element.63), channel_id=1, source_target_pairs={{32,0},{64,32},{96,64},{128,96},{160,128},{192,160},{224,192},{33,... | collective-permute-start | bytes 49160 | tf_op jit(solution)/shard_map/ppermute | solution.py:23
  103.0 11.9 %collective-permute-start.22 = (f32[16,16,2]{2,1,0:T(8,128)}, f32[16,16,2]{2,1,0:T(8,128)S(1)}, u32[]{:S(2)}, u32[]{:S(2)}) collective-permute-start(f32[16,16,2]{2,1,0:T(8,128)} %get-tuple-element.78), channel_id=1, source_target_pairs={{0,1},{1,2},{2,3},{4,5},{5,6},{6,7},{8,9},{9,10},{10,11},{12,13},{... | collective-permute-start | bytes 6152 | tf_op jit(solution)/shard_map/ppermute | solution.py:18
  107.4 7.5 %collective-permute-start.23 = (f32[16,16,2]{2,1,0:T(8,128)}, f32[16,16,2]{2,1,0:T(8,128)S(1)}, u32[]{:S(2)}, u32[]{:S(2)}) collective-permute-start(f32[16,16,2]{2,1,0:T(8,128)} %get-tuple-element.79), channel_id=1, source_target_pairs={{1,0},{2,1},{3,2},{5,4},{6,5},{7,6},{9,8},{10,9},{11,10},{13,12},{... | collective-permute-start | bytes 6152 | tf_op jit(solution)/shard_map/ppermute | solution.py:23
  108.7 41.9 %collective-permute-start.20 = (f32[16,8,128]{2,1,0:T(8,128)}, f32[16,8,128]{2,1,0:T(8,128)S(1)}, u32[]{:S(2)}, u32[]{:S(2)}) collective-permute-start(f32[16,8,128]{2,1,0:T(8,128)} %get-tuple-element.76), channel_id=1, source_target_pairs={{0,4},{4,8},{8,12},{12,16},{16,20},{20,24},{24,28},{1,5},{5,9},{9,... | collective-permute-start | bytes 196616 | tf_op jit(solution)/shard_map/ppermute | solution.py:18
  113.6 37.0 %collective-permute-start.21 = (f32[16,8,128]{2,1,0:T(8,128)}, f32[16,8,128]{2,1,0:T(8,128)S(1)}, u32[]{:S(2)}, u32[]{:S(2)}) collective-permute-start(f32[16,8,128]{2,1,0:T(8,128)} %get-tuple-element.77), channel_id=1, source_target_pairs={{4,0},{8,4},{12,8},{16,12},{20,16},{24,20},{28,24},{5,1},{9,5},{13... | collective-permute-start | bytes 196616 | tf_op jit(solution)/shard_map/ppermute | solution.py:23
  119.5 22.5 %all-to-all-start = ((f32[64,1,128]{2,1,0:T(1,128)}), f32[64,1,128]{2,1,0:T(1,128)S(1)}, u32[]{:S(2)}, u32[]{:S(2)}) async-start(f32[64,1,128]{2,1,0:T(1,128)} %bitcast.10), calls=%async_computation | async-start | bytes 65536 | tf_op jit(solution)/shard_map/all_to_all | solution.py:33
  131.5 11.8 %collective-permute-start.18 = (f32[2,16,128]{2,1,0:T(8,128)S(1)}, f32[2,16,128]{2,1,0:T(8,128)S(1)}, u32[]{:S(2)}, u32[]{:S(2)}) collective-permute-start(f32[2,16,128]{2,1,0:T(8,128)S(1)} %copy-done.32), channel_id=1, source_target_pairs={{0,32},{32,64},{64,96},{96,128},{128,160},{160,192},{192,224},{1,3... | collective-permute-start | bytes 49160 | tf_op jit(solution)/shard_map/ppermute | solution.py:18
  138.9 11.6 %collective-permute-start.19 = (f32[2,16,128]{2,1,0:T(8,128)S(1)}, f32[2,16,128]{2,1,0:T(8,128)S(1)}, u32[]{:S(2)}, u32[]{:S(2)}) collective-permute-start(f32[2,16,128]{2,1,0:T(8,128)S(1)} %copy-done.31), channel_id=1, source_target_pairs={{32,0},{64,32},{96,64},{128,96},{160,128},{192,160},{224,192},{33,... | collective-permute-start | bytes 49160 | tf_op jit(solution)/shard_map/ppermute | solution.py:23
  142.0 12.5 %collective-permute-start.24 = (f32[128]{0:T(128)S(1)}, f32[128]{0:T(128)S(1)}, u32[]{:S(2)}, u32[]{:S(2)}) collective-permute-start(f32[128]{0:T(128)S(1)} %reduce_sum.9), channel_id=1, source_target_pairs={{1,0},{2,3},{5,4},{6,7},{9,8},{10,11},{13,12},{14,15},{17,16},{18,... | collective-permute-start | bytes 1544 | tf_op jit(solution)/shard_map/ppermute | solution.py:338
  (36 other events, 208.8 us)

commit v9 on v8

--- a/solution.py
+++ b/solution.py
@@ -103,7 +103,7 @@
     yh = yh_ref[...]
     zl = zl_ref[...]
     zh = zh_ref[...]
-    pxl2, pxl1 = xl[0:1], xl[1:2]
+    pxl2, pxl1 = (xl[0:1], xl[1:2]) if first else (xl[-2:-1], xl[-1:])
     pxh1, pxh2 = xh[0:1], xh[1:2]
     yl2, yl1 = pick(yl, 1, rows - 2), pick(yl, 1, rows - 1)
     yh1, yh2 = pick(yh, 1, 0), pick(yh, 1, 1)
@@ -185,8 +185,8 @@
     new_p = jnp.where(zi == 0, new_p + jnp.broadcast_to(src_ref[instant], full), new_p)
     po_ref[...] = new_p
 
-    sxu_ref[...] = new_p[X - 2 :]
-    sxd_ref[...] = new_p[0:2]
+    sxu_ref[...] = new_p[X - sxu_ref.shape[0] :]
+    sxd_ref[...] = new_p[0 : sxd_ref.shape[0]]
     syu_ref[...] = new_p[:, Y - rows :]
     syd_ref[...] = new_p[:, 0:rows]
     zshape = szu_ref.shape
@@ -206,8 +206,8 @@
         jax.ShapeDtypeStruct((2, Y, Z), f32),
         jax.ShapeDtypeStruct((X, 2, Z), f32),
         jax.ShapeDtypeStruct((X, Y, 2), f32),
-        jax.ShapeDtypeStruct((2, Y, Z), f32),
-        jax.ShapeDtypeStruct((2, Y, Z), f32),
+        jax.ShapeDtypeStruct((rows, Y, Z), f32),
+        jax.ShapeDtypeStruct((rows, Y, Z), f32),
         jax.ShapeDtypeStruct((X, rows, Z), f32),
         jax.ShapeDtypeStruct((X, rows, Z), f32),
         jax.ShapeDtypeStruct((X, Y, 2), f32),

time: 157 us -> 161 us (1.025)
  the two profiles are of different devices: /device:TPU:24 before, /device:TPU:1 now
where the time goes in v9:
time: 161 us; the launch traced here: 160 us
  starting transfers between devices  104 us (65%)
  waiting for transfers between devices  22 us (14%)
  local copies, waits for them, and re-layouts  13.9 us (9%)
  Pallas kernels  13.7 us (9%)
  other arithmetic  4.13 us (3%)
    ppermute x12, starting transfers between devices, shifted_up(): return lax.ppermute(x, axis, [(i, i + 1) for i in range(count - 1)])  59.1 us
    all_to_all x1, starting transfers between devices, summed_on_arrival(): parts = lax.all_to_all(in_blocks(x, dim, size), axis, 0, 0, tiled=True)  25.8 us
    ppermute x12, starting transfers between devices, shifted_down(): return lax.ppermute(x, axis, [(i + 1, i) for i in range(count - 1)])  18 us
    pallas_call x4, Pallas kernels, run_step(): pl.pallas_call(functools.partial(step_kernel, instant, first), out_shape=...  13.7 us
    all_to_all x1, waiting for transfers between devices, summed_on_arrival(): parts = lax.all_to_all(in_blocks(x, dim, size), axis, 0, 0, tiled=True)  11.7 us
    ppermute x12, waiting for transfers between devices, shifted_down(): return lax.ppermute(x, axis, [(i + 1, i) for i in range(count - 1)])  8 us
    unnamed x69, local copies, waits for them, and re-layouts  6.89 us
  transfers between devices with their start and end apart: 26, of which 5 were waited for; matrix products, arithmetic and copies ran while one was open for 6% of the time, Pallas kernels for 2%

profile of v9, /device:TPU:1, one launch (start us, length us, event | category | flops | bytes accessed | tf_op | source)
XLA Modules:
  0.0 159.6 jit_solution(15954762317540145449)
XLA Ops:
  4.0 4.4 %collective-permute-start.4 = (f32[16,16,4]{2,1,0:T(8,128)S(1)}, f32[16,16,4]{2,1,0:T(8,128)S(1)}, u32[]{:S(2)}, u32[]{:S(2)}) collective-permute-start(f32[16,16,4]{2,1,0:T(8,128)S(1)} %copy.42), channel_id=1, source_target_pairs={{0,1},{1,2},{2,3},{4,5},{5,6},{6,7},{8,9},{9,10},{10,11},{12,13},{... | collective-permute-start | bytes 12296 | tf_op jit(solution)/shard_map/ppermute | solution.py:18
  10.3 4.0 %collective-permute-start.2 = (f32[16,10,128]{2,1,0:T(8,128)S(1)}, f32[16,10,128]{2,1,0:T(8,128)S(1)}, u32[]{:S(2)}, u32[]{:S(2)}) collective-permute-start(f32[16,10,128]{2,1,0:T(8,128)S(1)} %pad_maximum_fusion), channel_id=1, source_target_pairs={{0,4},{4,8},{8,12},{12,16},{16,20},{20,24},{24,28},{1,5},{5,9},{9,... | collective-permute-start | bytes 245768 | tf_op jit(solution)/shard_map/ppermute | solution.py:18
  14.3 1.9 %collective-permute-start.3 = (f32[16,10,128]{2,1,0:T(8,128)S(1)}, f32[16,10,128]{2,1,0:T(8,128)S(1)}, u32[]{:S(2)}, u32[]{:S(2)}) collective-permute-start(f32[16,10,128]{2,1,0:T(8,128)S(1)} %pad_maximum_fusion.1), channel_id=1, source_target_pairs={{4,0},{8,4},{12,8},{16,12},{20,16},{24,20},{28,24},{5,1},{9,5},{13... | collective-permute-start | bytes 245768 | tf_op jit(solution)/shard_map/ppermute | solution.py:23
  17.0 3.2 %collective-permute-start = (f32[4,16,128]{2,1,0:T(8,128)S(1)}, f32[4,16,128]{2,1,0:T(8,128)S(1)}, u32[]{:S(2)}, u32[]{:S(2)}) collective-permute-start(f32[4,16,128]{2,1,0:T(8,128)S(1)} %pad_maximum_fusion.2), channel_id=1, source_target_pairs={{0,32},{32,64},{64,96},{96,128},{128,160},{160,192},{192,224},{1,3... | collective-permute-start | bytes 98312 | tf_op jit(solution)/shard_map/ppermute | solution.py:18
  27.3 3.6 %shard_map.121 = (f32[16,16,128]{2,1,0:T(8,128)}, f32[3,16,16,128]{3,2,1,0:T(8,128)}, f32[16,16,1]{2,1,0:T(8,128)}, f32[2,16,128]{2,1,0:T(8,128)}, f32[16,2,128]...) custom-call(f32[64]{0:T(128)} %reshape.152.refs_0_, ...), custom_call_target="tpu_custom_call" | custom-call | flops 2621440 | bytes 1572864 | tf_op jit(solution)/shard_map/pallas_call | solution.py:221
  31.0 3.2 %collective-permute-start.6 = (f32[8,16,128]{2,1,0:T(8,128)}, f32[8,16,128]{2,1,0:T(8,128)S(1)}, u32[]{:S(2)}, u32[]{:S(2)}) collective-permute-start(f32[8,16,128]{2,1,0:T(8,128)} %get-tuple-element.47), channel_id=1, source_target_pairs={{0,32},{32,64},{64,96},{96,128},{128,160},{160,192},{192,224},{1,3... | collective-permute-start | bytes 196616 | tf_op jit(solution)/shard_map/ppermute | solution.py:18
  35.5 5.4 %collective-permute-start.8 = (f32[16,8,128]{2,1,0:T(8,128)}, f32[16,8,128]{2,1,0:T(8,128)S(1)}, u32[]{:S(2)}, u32[]{:S(2)}) collective-permute-start(f32[16,8,128]{2,1,0:T(8,128)} %get-tuple-element.49), channel_id=1, source_target_pairs={{0,4},{4,8},{8,12},{12,16},{16,20},{20,24},{24,28},{1,5},{5,9},{9,... | collective-permute-start | bytes 196616 | tf_op jit(solution)/shard_map/ppermute | solution.py:18
  40.9 1.9 %collective-permute-start.9 = (f32[16,8,128]{2,1,0:T(8,128)}, f32[16,8,128]{2,1,0:T(8,128)S(1)}, u32[]{:S(2)}, u32[]{:S(2)}) collective-permute-start(f32[16,8,128]{2,1,0:T(8,128)} %get-tuple-element.50), channel_id=1, source_target_pairs={{4,0},{8,4},{12,8},{16,12},{20,16},{24,20},{28,24},{5,1},{9,5},{13... | collective-permute-start | bytes 196616 | tf_op jit(solution)/shard_map/ppermute | solution.py:23
  42.8 4.3 %collective-permute-start.10 = (f32[16,16,2]{2,1,0:T(8,128)}, f32[16,16,2]{2,1,0:T(8,128)S(1)}, u32[]{:S(2)}, u32[]{:S(2)}) collective-permute-start(f32[16,16,2]{2,1,0:T(8,128)} %get-tuple-element.51), channel_id=1, source_target_pairs={{0,1},{1,2},{2,3},{4,5},{5,6},{6,7},{8,9},{9,10},{10,11},{12,13},{... | collective-permute-start | bytes 6152 | tf_op jit(solution)/shard_map/ppermute | solution.py:18
  47.1 2.2 %collective-permute-done.10.refs_12_ = f32[16,16,2]{2,1,0:T(8,128)S(1)} collective-permute-done((f32[16,16,2]{2,1,0:T(8,128)}, f32[16,16,2]{2,1,0:T(8,128)S(1)}, u32[]{:S(2)}, u32[]{:S(2)}) %collective-permute-start.10) | collective-permute-done | bytes 2080 | tf_op jit(solution)/shard_map/ppermute | solution.py:18
  50.6 4.9 %collective-permute-done.11.refs_13_ = f32[16,16,2]{2,1,0:T(8,128)S(1)} collective-permute-done((f32[16,16,2]{2,1,0:T(8,128)}, f32[16,16,2]{2,1,0:T(8,128)S(1)}, u32[]{:S(2)}, u32[]{:S(2)}) %collective-permute-start.11) | collective-permute-done | bytes 2080 | tf_op jit(solution)/shard_map/ppermute | solution.py:23
  56.3 3.4 %shard_map.122 = (f32[16,16,128]{2,1,0:T(8,128)}, f32[3,16,16,128]{3,2,1,0:T(8,128)}, f32[16,16,1]{2,1,0:T(8,128)}, f32[2,16,128]{2,1,0:T(8,128)}, f32[16,2,128]...) custom-call(f32[64]{0:T(128)} %reshape.152.refs_0_, ...), custom_call_target="tpu_custom_call" | custom-call | flops 2621440 | bytes 1572864 | tf_op jit(solution)/shard_map/pallas_call | solution.py:221
  59.7 4.3 %collective-permute-start.16 = (f32[16,16,2]{2,1,0:T(8,128)}, f32[16,16,2]{2,1,0:T(8,128)S(1)}, u32[]{:S(2)}, u32[]{:S(2)}) collective-permute-start(f32[16,16,2]{2,1,0:T(8,128)} %get-tuple-element.66), channel_id=1, source_target_pairs={{0,1},{1,2},{2,3},{4,5},{5,6},{6,7},{8,9},{9,10},{10,11},{12,13},{... | collective-permute-start | bytes 6152 | tf_op jit(solution)/shard_map/ppermute | solution.py:18
  65.3 6.6 %collective-permute-start.12 = (f32[8,16,128]{2,1,0:T(8,128)}, f32[8,16,128]{2,1,0:T(8,128)S(1)}, u32[]{:S(2)}, u32[]{:S(2)}) collective-permute-start(f32[8,16,128]{2,1,0:T(8,128)} %get-tuple-element.62), channel_id=1, source_target_pairs={{0,32},{32,64},{64,96},{96,128},{128,160},{160,192},{192,224},{1,3... | collective-permute-start | bytes 196616 | tf_op jit(solution)/shard_map/ppermute | solution.py:18
  73.2 6.8 %collective-permute-start.14 = (f32[16,8,128]{2,1,0:T(8,128)}, f32[16,8,128]{2,1,0:T(8,128)S(1)}, u32[]{:S(2)}, u32[]{:S(2)}) collective-permute-start(f32[16,8,128]{2,1,0:T(8,128)} %get-tuple-element.64), channel_id=1, source_target_pairs={{0,4},{4,8},{8,12},{12,16},{16,20},{20,24},{24,28},{1,5},{5,9},{9,... | collective-permute-start | bytes 196616 | tf_op jit(solution)/shard_map/ppermute | solution.py:18
  83.8 2.0 %collective-permute-done.15.refs_11_ = f32[16,8,128]{2,1,0:T(8,128)S(1)} collective-permute-done((f32[16,8,128]{2,1,0:T(8,128)}, f32[16,8,128]{2,1,0:T(8,128)S(1)}, u32[]{:S(2)}, u32[]{:S(2)}) %collective-permute-start.15) | collective-permute-done | bytes 65568 | tf_op jit(solution)/shard_map/ppermute | solution.py:23
  86.4 3.4 %shard_map.123 = (f32[16,16,128]{2,1,0:T(8,128)}, f32[3,16,16,128]{3,2,1,0:T(8,128)}, f32[16,16,1]{2,1,0:T(8,128)}, f32[2,16,128]{2,1,0:T(8,128)}, f32[16,2,128]...) custom-call(f32[64]{0:T(128)} %reshape.152.refs_0_, ...), custom_call_target="tpu_custom_call" | custom-call | flops 2621440 | bytes 1572864 | tf_op jit(solution)/shard_map/pallas_call | solution.py:221
  89.8 4.3 %collective-permute-start.22 = (f32[16,16,2]{2,1,0:T(8,128)}, f32[16,16,2]{2,1,0:T(8,128)S(1)}, u32[]{:S(2)}, u32[]{:S(2)}) collective-permute-start(f32[16,16,2]{2,1,0:T(8,128)} %get-tuple-element.78), channel_id=1, source_target_pairs={{0,1},{1,2},{2,3},{4,5},{5,6},{6,7},{8,9},{9,10},{10,11},{12,13},{... | collective-permute-start | bytes 6152 | tf_op jit(solution)/shard_map/ppermute | solution.py:18
  95.4 10.3 %collective-permute-start.18 = (f32[8,16,128]{2,1,0:T(8,128)}, f32[8,16,128]{2,1,0:T(8,128)S(1)}, u32[]{:S(2)}, u32[]{:S(2)}) collective-permute-start(f32[8,16,128]{2,1,0:T(8,128)} %get-tuple-element.74), channel_id=1, source_target_pairs={{0,32},{32,64},{64,96},{96,128},{128,160},{160,192},{192,224},{1,3... | collective-permute-start | bytes 196616 | tf_op jit(solution)/shard_map/ppermute | solution.py:18
  107.0 2.5 %collective-permute-start.20 = (f32[16,8,128]{2,1,0:T(8,128)}, f32[16,8,128]{2,1,0:T(8,128)S(1)}, u32[]{:S(2)}, u32[]{:S(2)}) collective-permute-start(f32[16,8,128]{2,1,0:T(8,128)} %get-tuple-element.76), channel_id=1, source_target_pairs={{0,4},{4,8},{8,12},{12,16},{16,20},{20,24},{24,28},{1,5},{5,9},{9,... | collective-permute-start | bytes 196616 | tf_op jit(solution)/shard_map/ppermute | solution.py:18
  113.6 2.5 %scatter_custom_fusion = f32[8192]{0:T(1024)} fusion(s32[256]{0:T(256)S(1)} %bitcast.23, f32[256]{0:T(256)S(1)} %mul.75, f32[]{:T(128)} %constant.37.clone.1), kind=kCustom, calls=%fused_computation.21 | custom fusion | flops 256 | bytes 32772 | tf_op jit(solution)/shard_map/scatter-add | solution.py:235
  116.1 25.8 %all-to-all-start = ((f32[64,1,128]{2,1,0:T(1,128)}), f32[64,1,128]{2,1,0:T(1,128)S(1)}, u32[]{:S(2)}, u32[]{:S(2)}) async-start(f32[64,1,128]{2,1,0:T(1,128)} %bitcast.10), calls=%async_computation | async-start | bytes 65536 | tf_op jit(solution)/shard_map/all_to_all | solution.py:33
  141.9 11.7 %all-to-all-done = f32[64,1,128]{2,1,0:T(1,128)S(1)} async-done(((f32[64,1,128]{2,1,0:T(1,128)}), f32[64,1,128]{2,1,0:T(1,128)S(1)}, u32[]{:S(2)}, u32[]{:S(2)}) %all-to-all-start) | async-done | bytes 32800 | tf_op jit(solution)/shard_map/all_to_all | solution.py:33
  155.6 3.3 %shard_map.124 = (f32[16,16,128]{2,1,0:T(8,128)}, f32[3,16,16,128]{3,2,1,0:T(8,128)}, f32[16,16,1]{2,1,0:T(8,128)}, f32[2,16,128]{2,1,0:T(8,128)}, f32[16,2,128]...) custom-call(f32[64]{0:T(128)} %reshape.152.refs_0_, ...), custom_call_target="tpu_custom_call" | custom-call | flops 2621440 | bytes 1572864 | tf_op jit(solution)/shard_map/pallas_call | solution.py:221
  (146 shorter events, 32.2 us)
Async XLA Ops:
  4.0 17.4 %collective-permute-start.4 = (f32[16,16,4]{2,1,0:T(8,128)S(1)}, f32[16,16,4]{2,1,0:T(8,128)S(1)}, u32[]{:S(2)}, u32[]{:S(2)}) collective-permute-start(f32[16,16,4]{2,1,0:T(8,128)S(1)} %copy.42), channel_id=1, source_target_pairs={{0,1},{1,2},{2,3},{4,5},{5,6},{6,7},{8,9},{9,10},{10,11},{12,13},{... | collective-permute-start | bytes 12296 | tf_op jit(solution)/shard_map/ppermute | solution.py:18
  8.9 16.1 %collective-permute-start.5 = (f32[16,16,4]{2,1,0:T(8,128)S(1)}, f32[16,16,4]{2,1,0:T(8,128)S(1)}, u32[]{:S(2)}, u32[]{:S(2)}) collective-permute-start(f32[16,16,4]{2,1,0:T(8,128)S(1)} %copy.45), channel_id=1, source_target_pairs={{1,0},{2,1},{3,2},{5,4},{6,5},{7,6},{9,8},{10,9},{11,10},{13,12},{... | collective-permute-start | bytes 12296 | tf_op jit(solution)/shard_map/ppermute | solution.py:23
  10.3 15.8 %collective-permute-start.2 = (f32[16,10,128]{2,1,0:T(8,128)S(1)}, f32[16,10,128]{2,1,0:T(8,128)S(1)}, u32[]{:S(2)}, u32[]{:S(2)}) collective-permute-start(f32[16,10,128]{2,1,0:T(8,128)S(1)} %pad_maximum_fusion), channel_id=1, source_target_pairs={{0,4},{4,8},{8,12},{12,16},{16,20},{20,24},{24,28},{1,5},{5,9},{9,... | collective-permute-start | bytes 245768 | tf_op jit(solution)/shard_map/ppermute | solution.py:18
  14.3 11.8 %collective-permute-start.3 = (f32[16,10,128]{2,1,0:T(8,128)S(1)}, f32[16,10,128]{2,1,0:T(8,128)S(1)}, u32[]{:S(2)}, u32[]{:S(2)}) collective-permute-start(f32[16,10,128]{2,1,0:T(8,128)S(1)} %pad_maximum_fusion.1), channel_id=1, source_target_pairs={{4,0},{8,4},{12,8},{16,12},{20,16},{24,20},{28,24},{5,1},{9,5},{13... | collective-permute-start | bytes 245768 | tf_op jit(solution)/shard_map/ppermute | solution.py:23
  17.0 8.0 %collective-permute-start = (f32[4,16,128]{2,1,0:T(8,128)S(1)}, f32[4,16,128]{2,1,0:T(8,128)S(1)}, u32[]{:S(2)}, u32[]{:S(2)}) collective-permute-start(f32[4,16,128]{2,1,0:T(8,128)S(1)} %pad_maximum_fusion.2), channel_id=1, source_target_pairs={{0,32},{32,64},{64,96},{96,128},{128,160},{160,192},{192,224},{1,3... | collective-permute-start | bytes 98312 | tf_op jit(solution)/shard_map/ppermute | solution.py:18
  31.0 24.5 %collective-permute-start.6 = (f32[8,16,128]{2,1,0:T(8,128)}, f32[8,16,128]{2,1,0:T(8,128)S(1)}, u32[]{:S(2)}, u32[]{:S(2)}) collective-permute-start(f32[8,16,128]{2,1,0:T(8,128)} %get-tuple-element.47), channel_id=1, source_target_pairs={{0,32},{32,64},{64,96},{96,128},{128,160},{160,192},{192,224},{1,3... | collective-permute-start | bytes 196616 | tf_op jit(solution)/shard_map/ppermute | solution.py:18
  34.2 21.3 %collective-permute-start.7 = (f32[8,16,128]{2,1,0:T(8,128)}, f32[8,16,128]{2,1,0:T(8,128)S(1)}, u32[]{:S(2)}, u32[]{:S(2)}) collective-permute-start(f32[8,16,128]{2,1,0:T(8,128)} %get-tuple-element.48), channel_id=1, source_target_pairs={{32,0},{64,32},{96,64},{128,96},{160,128},{192,160},{224,192},{33,... | collective-permute-start | bytes 196616 | tf_op jit(solution)/shard_map/ppermute | solution.py:23
  35.5 20.1 %collective-permute-start.8 = (f32[16,8,128]{2,1,0:T(8,128)}, f32[16,8,128]{2,1,0:T(8,128)S(1)}, u32[]{:S(2)}, u32[]{:S(2)}) collective-permute-start(f32[16,8,128]{2,1,0:T(8,128)} %get-tuple-element.49), channel_id=1, source_target_pairs={{0,4},{4,8},{8,12},{12,16},{16,20},{20,24},{24,28},{1,5},{5,9},{9,... | collective-permute-start | bytes 196616 | tf_op jit(solution)/shard_map/ppermute | solution.py:18
  40.9 14.7 %collective-permute-start.9 = (f32[16,8,128]{2,1,0:T(8,128)}, f32[16,8,128]{2,1,0:T(8,128)S(1)}, u32[]{:S(2)}, u32[]{:S(2)}) collective-permute-start(f32[16,8,128]{2,1,0:T(8,128)} %get-tuple-element.50), channel_id=1, source_target_pairs={{4,0},{8,4},{12,8},{16,12},{20,16},{24,20},{28,24},{5,1},{9,5},{13... | collective-permute-start | bytes 196616 | tf_op jit(solution)/shard_map/ppermute | solution.py:23
  42.8 6.5 %collective-permute-start.10 = (f32[16,16,2]{2,1,0:T(8,128)}, f32[16,16,2]{2,1,0:T(8,128)S(1)}, u32[]{:S(2)}, u32[]{:S(2)}) collective-permute-start(f32[16,16,2]{2,1,0:T(8,128)} %get-tuple-element.51), channel_id=1, source_target_pairs={{0,1},{1,2},{2,3},{4,5},{5,6},{6,7},{8,9},{9,10},{10,11},{12,13},{... | collective-permute-start | bytes 6152 | tf_op jit(solution)/shard_map/ppermute | solution.py:18
  49.3 6.2 %collective-permute-start.11 = (f32[16,16,2]{2,1,0:T(8,128)}, f32[16,16,2]{2,1,0:T(8,128)S(1)}, u32[]{:S(2)}, u32[]{:S(2)}) collective-permute-start(f32[16,16,2]{2,1,0:T(8,128)} %get-tuple-element.52), channel_id=1, source_target_pairs={{1,0},{2,1},{3,2},{5,4},{6,5},{7,6},{9,8},{10,9},{11,10},{13,12},{... | collective-permute-start | bytes 6152 | tf_op jit(solution)/shard_map/ppermute | solution.py:23
  59.7 20.3 %collective-permute-start.16 = (f32[16,16,2]{2,1,0:T(8,128)}, f32[16,16,2]{2,1,0:T(8,128)S(1)}, u32[]{:S(2)}, u32[]{:S(2)}) collective-permute-start(f32[16,16,2]{2,1,0:T(8,128)} %get-tuple-element.66), channel_id=1, source_target_pairs={{0,1},{1,2},{2,3},{4,5},{5,6},{6,7},{8,9},{9,10},{10,11},{12,13},{... | collective-permute-start | bytes 6152 | tf_op jit(solution)/shard_map/ppermute | solution.py:18
  64.0 19.7 %collective-permute-start.17 = (f32[16,16,2]{2,1,0:T(8,128)}, f32[16,16,2]{2,1,0:T(8,128)S(1)}, u32[]{:S(2)}, u32[]{:S(2)}) collective-permute-start(f32[16,16,2]{2,1,0:T(8,128)} %get-tuple-element.67), channel_id=1, source_target_pairs={{1,0},{2,1},{3,2},{5,4},{6,5},{7,6},{9,8},{10,9},{11,10},{13,12},{... | collective-permute-start | bytes 6152 | tf_op jit(solution)/shard_map/ppermute | solution.py:23
  65.3 18.4 %collective-permute-start.12 = (f32[8,16,128]{2,1,0:T(8,128)}, f32[8,16,128]{2,1,0:T(8,128)S(1)}, u32[]{:S(2)}, u32[]{:S(2)}) collective-permute-start(f32[8,16,128]{2,1,0:T(8,128)} %get-tuple-element.62), channel_id=1, source_target_pairs={{0,32},{32,64},{64,96},{96,128},{128,160},{160,192},{192,224},{1,3... | collective-permute-start | bytes 196616 | tf_op jit(solution)/shard_map/ppermute | solution.py:18
  71.9 11.9 %collective-permute-start.13 = (f32[8,16,128]{2,1,0:T(8,128)}, f32[8,16,128]{2,1,0:T(8,128)S(1)}, u32[]{:S(2)}, u32[]{:S(2)}) collective-permute-start(f32[8,16,128]{2,1,0:T(8,128)} %get-tuple-element.63), channel_id=1, source_target_pairs={{32,0},{64,32},{96,64},{128,96},{160,128},{192,160},{224,192},{33,... | collective-permute-start | bytes 196616 | tf_op jit(solution)/shard_map/ppermute | solution.py:23
  73.2 10.6 %collective-permute-start.14 = (f32[16,8,128]{2,1,0:T(8,128)}, f32[16,8,128]{2,1,0:T(8,128)S(1)}, u32[]{:S(2)}, u32[]{:S(2)}) collective-permute-start(f32[16,8,128]{2,1,0:T(8,128)} %get-tuple-element.64), channel_id=1, source_target_pairs={{0,4},{4,8},{8,12},{12,16},{16,20},{20,24},{24,28},{1,5},{5,9},{9,... | collective-permute-start | bytes 196616 | tf_op jit(solution)/shard_map/ppermute | solution.py:18
  80.0 5.8 %collective-permute-start.15 = (f32[16,8,128]{2,1,0:T(8,128)}, f32[16,8,128]{2,1,0:T(8,128)S(1)}, u32[]{:S(2)}, u32[]{:S(2)}) collective-permute-start(f32[16,8,128]{2,1,0:T(8,128)} %get-tuple-element.65), channel_id=1, source_target_pairs={{4,0},{8,4},{12,8},{16,12},{20,16},{24,20},{28,24},{5,1},{9,5},{13... | collective-permute-start | bytes 196616 | tf_op jit(solution)/shard_map/ppermute | solution.py:23
  89.8 19.7 %collective-permute-start.22 = (f32[16,16,2]{2,1,0:T(8,128)}, f32[16,16,2]{2,1,0:T(8,128)S(1)}, u32[]{:S(2)}, u32[]{:S(2)}) collective-permute-start(f32[16,16,2]{2,1,0:T(8,128)} %get-tuple-element.78), channel_id=1, source_target_pairs={{0,1},{1,2},{2,3},{4,5},{5,6},{6,7},{8,9},{9,10},{10,11},{12,13},{... | collective-permute-start | bytes 6152 | tf_op jit(solution)/shard_map/ppermute | solution.py:18
  94.1 17.4 %collective-permute-start.23 = (f32[16,16,2]{2,1,0:T(8,128)}, f32[16,16,2]{2,1,0:T(8,128)S(1)}, u32[]{:S(2)}, u32[]{:S(2)}) collective-permute-start(f32[16,16,2]{2,1,0:T(8,128)} %get-tuple-element.79), channel_id=1, source_target_pairs={{1,0},{2,1},{3,2},{5,4},{6,5},{7,6},{9,8},{10,9},{11,10},{13,12},{... | collective-permute-start | bytes 6152 | tf_op jit(solution)/shard_map/ppermute | solution.py:23
  95.4 59.5 %collective-permute-start.18 = (f32[8,16,128]{2,1,0:T(8,128)}, f32[8,16,128]{2,1,0:T(8,128)S(1)}, u32[]{:S(2)}, u32[]{:S(2)}) collective-permute-start(f32[8,16,128]{2,1,0:T(8,128)} %get-tuple-element.74), channel_id=1, source_target_pairs={{0,32},{32,64},{64,96},{96,128},{128,160},{160,192},{192,224},{1,3... | collective-permute-start | bytes 196616 | tf_op jit(solution)/shard_map/ppermute | solution.py:18
  105.7 49.3 %collective-permute-start.19 = (f32[8,16,128]{2,1,0:T(8,128)}, f32[8,16,128]{2,1,0:T(8,128)S(1)}, u32[]{:S(2)}, u32[]{:S(2)}) collective-permute-start(f32[8,16,128]{2,1,0:T(8,128)} %get-tuple-element.75), channel_id=1, source_target_pairs={{32,0},{64,32},{96,64},{128,96},{160,128},{192,160},{224,192},{33,... | collective-permute-start | bytes 196616 | tf_op jit(solution)/shard_map/ppermute | solution.py:23
  107.0 48.0 %collective-permute-start.20 = (f32[16,8,128]{2,1,0:T(8,128)}, f32[16,8,128]{2,1,0:T(8,128)S(1)}, u32[]{:S(2)}, u32[]{:S(2)}) collective-permute-start(f32[16,8,128]{2,1,0:T(8,128)} %get-tuple-element.76), channel_id=1, source_target_pairs={{0,4},{4,8},{8,12},{12,16},{16,20},{20,24},{24,28},{1,5},{5,9},{9,... | collective-permute-start | bytes 196616 | tf_op jit(solution)/shard_map/ppermute | solution.py:18
  109.5 45.4 %collective-permute-start.21 = (f32[16,8,128]{2,1,0:T(8,128)}, f32[16,8,128]{2,1,0:T(8,128)S(1)}, u32[]{:S(2)}, u32[]{:S(2)}) collective-permute-start(f32[16,8,128]{2,1,0:T(8,128)} %get-tuple-element.77), channel_id=1, source_target_pairs={{4,0},{8,4},{12,8},{16,12},{20,16},{24,20},{28,24},{5,1},{9,5},{13... | collective-permute-start | bytes 196616 | tf_op jit(solution)/shard_map/ppermute | solution.py:23
  116.1 37.5 %all-to-all-start = ((f32[64,1,128]{2,1,0:T(1,128)}), f32[64,1,128]{2,1,0:T(1,128)S(1)}, u32[]{:S(2)}, u32[]{:S(2)}) async-start(f32[64,1,128]{2,1,0:T(1,128)} %bitcast.10), calls=%async_computation | async-start | bytes 65536 | tf_op jit(solution)/shard_map/all_to_all | solution.py:33
  (34 other events, 137.2 us)

commit v10 on v8

--- a/solution.py
+++ b/solution.py
@@ -232,7 +232,14 @@
 def seafloor_sums(seafloor, node_weight, node_patch, patch_slot):
     sea_values = node_weight[0, 0] * seafloor.reshape(-1)
     slots = patch_slot[node_patch[0, 0]]
-    partial_slip = jnp.zeros((patch_slot.shape[0],), jnp.float32).at[slots].add(sea_values)
+    owners = lax.axis_size("gx") * lax.axis_size("gy")
+    per_owner = patch_slot.shape[0] // owners
+    owner_hot = slots[None, :] // per_owner == jnp.arange(owners, dtype=jnp.int32)[:, None]
+    within_hot = (
+        slots[:, None] % per_owner == jnp.arange(per_owner, dtype=jnp.int32)[None, :]
+    ).astype(jnp.float32)
+    weighted = jnp.where(owner_hot, sea_values[None, :], 0.0)
+    partial_slip = jnp.dot(weighted, within_hot, precision=lax.Precision.HIGHEST).reshape(-1)
     return summed_on_arrival(partial_slip, ("gx", "gy"), 0)
 
 
@@ -254,9 +261,12 @@
     depth_index = lax.axis_index("gz")
     first_crust = tiles_z // 2 * Z
     levels = depth_index * Z + jnp.arange(Z, dtype=jnp.int32)
-    wint = jnp.stack(depth_weights(levels, first_crust)).reshape(3, 1, 1, Z)
-    entry = lax.broadcasted_iota(jnp.int32, (ITERS, 16), 1)
-    step_at = lax.broadcasted_iota(jnp.int32, (ITERS, 16), 0)
+    level_grid = depth_index * Z + lax.broadcasted_iota(jnp.int32, (3, 1, 1, Z), 3)
+    w_up, w_mid, w_low = depth_weights(level_grid, first_crust)
+    which = lax.broadcasted_iota(jnp.int32, (3, 1, 1, Z), 0)
+    wint = jnp.where(which == 0, w_up, jnp.where(which == 1, w_mid, w_low))
+    entry = lax.broadcasted_iota(jnp.int32, (ITERS * 16,), 0) % 16
+    step_at = lax.broadcasted_iota(jnp.int32, (ITERS * 16,), 0) // 16
     edge_level = depth_index * Z + jnp.where(entry < 3, -1, Z)
     e_up, e_mid, e_low = depth_weights(edge_level, first_crust)
     kind = entry % 3
@@ -271,7 +281,7 @@
                   jnp.where(entry == 8, after & ocean, after & crust)),
     ).astype(jnp.float32)
     scal_all = jnp.where(entry < 6, edge_value, jnp.where(entry < 10, flag_value, 0.0))
-    scal_all = scal_all.astype(jnp.float32).reshape(ITERS * 16)
+    scal_all = scal_all.astype(jnp.float32)
     top_flag = (depth_index == 0).astype(jnp.float32)
     sources = source_planes(
         gauge_x,

time: 157 us -> 155 us (0.987)
    scatter-add x1 -> x0, other arithmetic: 2.51 us -> none  [seafloor_sums(): jnp.zeros((patch_slot.shape[0],), jnp.float32).at[slots].add(sea_values)]
  transfers between devices with their start and end apart: 26 -> 26, of which waited for: 6 -> 6; matrix products, arithmetic and copies ran while one was open for 6% -> 5% of each run, Pallas kernels for 2% -> 2%
where the time goes in v10:
time: 155 us; the launch traced here: 153 us
  starting transfers between devices  88.1 us (57%)
  waiting for transfers between devices  33.6 us (22%)
  Pallas kernels  13.5 us (9%)
  local copies, waits for them, and re-layouts  12.7 us (8%)
  other arithmetic  2.79 us (2%)
    ppermute x12, starting transfers between devices, shifted_up(): return lax.ppermute(x, axis, [(i, i + 1) for i in range(count - 1)])  55.7 us
    ppermute x12, waiting for transfers between devices, shifted_down(): return lax.ppermute(x, axis, [(i + 1, i) for i in range(count - 1)])  29.6 us
    ppermute x12, starting transfers between devices, shifted_down(): return lax.ppermute(x, axis, [(i + 1, i) for i in range(count - 1)])  19.3 us
    pallas_call x4, Pallas kernels, run_step(): pl.pallas_call(functools.partial(step_kernel, instant, first), out_shape=...  13.5 us
    all_to_all x1, starting transfers between devices, summed_on_arrival(): parts = lax.all_to_all(in_blocks(x, dim, size), axis, 0, 0, tiled=True)  11.8 us
    unnamed x73, local copies, waits for them, and re-layouts  6.87 us
  transfers between devices with their start and end apart: 26, of which 6 were waited for; matrix products, arithmetic and copies ran while one was open for 5% of the time, Pallas kernels for 2%

profile of v10, /device:TPU:24, one launch (start us, length us, event | category | flops | bytes accessed | tf_op | source)
XLA Modules:
  0.0 153.3 jit_solution(8920373376512601762)
XLA Ops:
  4.0 3.8 %collective-permute-start.4 = (f32[16,16,4]{2,1,0:T(8,128)S(1)}, f32[16,16,4]{2,1,0:T(8,128)S(1)}, u32[]{:S(2)}, u32[]{:S(2)}) collective-permute-start(f32[16,16,4]{2,1,0:T(8,128)S(1)} %copy.20), channel_id=1, source_target_pairs={{0,1},{1,2},{2,3},{4,5},{5,6},{6,7},{8,9},{9,10},{10,11},{12,13},{... | collective-permute-start | bytes 12296 | tf_op jit(solution)/shard_map/ppermute | solution.py:18
  13.3 7.8 %collective-permute-start = (f32[4,16,128]{2,1,0:T(8,128)S(1)}, f32[4,16,128]{2,1,0:T(8,128)S(1)}, u32[]{:S(2)}, u32[]{:S(2)}) collective-permute-start(f32[4,16,128]{2,1,0:T(8,128)S(1)} %pad_maximum_fusion.2), channel_id=1, source_target_pairs={{0,32},{32,64},{64,96},{96,128},{128,160},{160,192},{192,224},{1,3... | collective-permute-start | bytes 98312 | tf_op jit(solution)/shard_map/ppermute | solution.py:18
  22.9 1.9 %collective-permute-start.1 = (f32[4,16,128]{2,1,0:T(8,128)S(1)}, f32[4,16,128]{2,1,0:T(8,128)S(1)}, u32[]{:S(2)}, u32[]{:S(2)}) collective-permute-start(f32[4,16,128]{2,1,0:T(8,128)S(1)} %pad_maximum_fusion.3), channel_id=1, source_target_pairs={{32,0},{64,32},{96,64},{128,96},{160,128},{192,160},{224,192},{33,... | collective-permute-start | bytes 98312 | tf_op jit(solution)/shard_map/ppermute | solution.py:23
  26.5 8.2 %collective-permute-done.1.refs_8_ = f32[4,16,128]{2,1,0:T(8,128)S(1)} collective-permute-done((f32[4,16,128]{2,1,0:T(8,128)S(1)}, f32[4,16,128]{2,1,0:T(8,128)S(1)}, u32[]{:S(2)}, u32[]{:S(2)}) %collective-permute-start.1) | collective-permute-done | bytes 32800 | tf_op jit(solution)/shard_map/ppermute | solution.py:23
  36.0 3.6 %shard_map.121 = (f32[16,16,128]{2,1,0:T(8,128)}, f32[3,16,16,128]{3,2,1,0:T(8,128)}, f32[16,16,1]{2,1,0:T(8,128)}, f32[2,16,128]{2,1,0:T(8,128)}, f32[16,2,128]...) custom-call(f32[64]{0:T(128)} %compare_select_fusion.5.refs_0_, ...), custom_call_target="tpu_custom_call" | custom-call | flops 2621440 | bytes 1572864 | tf_op jit(solution)/shard_map/pallas_call | solution.py:221
  39.6 3.2 %collective-permute-start.8 = (f32[16,8,128]{2,1,0:T(8,128)}, f32[16,8,128]{2,1,0:T(8,128)S(1)}, u32[]{:S(2)}, u32[]{:S(2)}) collective-permute-start(f32[16,8,128]{2,1,0:T(8,128)} %get-tuple-element.49), channel_id=1, source_target_pairs={{0,4},{4,8},{8,12},{12,16},{16,20},{20,24},{24,28},{1,5},{5,9},{9,... | collective-permute-start | bytes 196616 | tf_op jit(solution)/shard_map/ppermute | solution.py:18
  44.1 2.6 %collective-permute-start.6 = (f32[2,16,128]{2,1,0:T(8,128)}, f32[2,16,128]{2,1,0:T(8,128)S(1)}, u32[]{:S(2)}, u32[]{:S(2)}) collective-permute-start(f32[2,16,128]{2,1,0:T(8,128)} %get-tuple-element.47), channel_id=1, source_target_pairs={{0,32},{32,64},{64,96},{96,128},{128,160},{160,192},{192,224},{1,3... | collective-permute-start | bytes 49160 | tf_op jit(solution)/shard_map/ppermute | solution.py:18
  46.7 3.2 %collective-permute-start.7 = (f32[2,16,128]{2,1,0:T(8,128)}, f32[2,16,128]{2,1,0:T(8,128)S(1)}, u32[]{:S(2)}, u32[]{:S(2)}) collective-permute-start(f32[2,16,128]{2,1,0:T(8,128)} %get-tuple-element.48), channel_id=1, source_target_pairs={{32,0},{64,32},{96,64},{128,96},{160,128},{192,160},{224,192},{33,... | collective-permute-start | bytes 49160 | tf_op jit(solution)/shard_map/ppermute | solution.py:23
  49.9 4.6 %collective-permute-start.10 = (f32[16,16,2]{2,1,0:T(8,128)}, f32[16,16,2]{2,1,0:T(8,128)S(1)}, u32[]{:S(2)}, u32[]{:S(2)}) collective-permute-start(f32[16,16,2]{2,1,0:T(8,128)} %get-tuple-element.51), channel_id=1, source_target_pairs={{0,1},{1,2},{2,3},{4,5},{5,6},{6,7},{8,9},{9,10},{10,11},{12,13},{... | collective-permute-start | bytes 6152 | tf_op jit(solution)/shard_map/ppermute | solution.py:18
  54.5 2.8 %collective-permute-done.10.refs_12_ = f32[16,16,2]{2,1,0:T(8,128)S(1)} collective-permute-done((f32[16,16,2]{2,1,0:T(8,128)}, f32[16,16,2]{2,1,0:T(8,128)S(1)}, u32[]{:S(2)}, u32[]{:S(2)}) %collective-permute-start.10) | collective-permute-done | bytes 2080 | tf_op jit(solution)/shard_map/ppermute | solution.py:18
  58.6 6.1 %collective-permute-done.11.refs_13_ = f32[16,16,2]{2,1,0:T(8,128)S(1)} collective-permute-done((f32[16,16,2]{2,1,0:T(8,128)}, f32[16,16,2]{2,1,0:T(8,128)S(1)}, u32[]{:S(2)}, u32[]{:S(2)}) %collective-permute-start.11) | collective-permute-done | bytes 2080 | tf_op jit(solution)/shard_map/ppermute | solution.py:23
  65.4 3.3 %shard_map.122 = (f32[16,16,128]{2,1,0:T(8,128)}, f32[3,16,16,128]{3,2,1,0:T(8,128)}, f32[16,16,1]{2,1,0:T(8,128)}, f32[2,16,128]{2,1,0:T(8,128)}, f32[16,2,128]...) custom-call(f32[64]{0:T(128)} %compare_select_fusion.5.refs_0_, ...), custom_call_target="tpu_custom_call" | custom-call | flops 2621440 | bytes 1572864 | tf_op jit(solution)/shard_map/pallas_call | solution.py:221
  68.8 4.2 %collective-permute-start.16 = (f32[16,16,2]{2,1,0:T(8,128)}, f32[16,16,2]{2,1,0:T(8,128)S(1)}, u32[]{:S(2)}, u32[]{:S(2)}) collective-permute-start(f32[16,16,2]{2,1,0:T(8,128)} %get-tuple-element.66), channel_id=1, source_target_pairs={{0,1},{1,2},{2,3},{4,5},{5,6},{6,7},{8,9},{9,10},{10,11},{12,13},{... | collective-permute-start | bytes 6152 | tf_op jit(solution)/shard_map/ppermute | solution.py:18
  74.3 2.6 %collective-permute-start.14 = (f32[16,8,128]{2,1,0:T(8,128)}, f32[16,8,128]{2,1,0:T(8,128)S(1)}, u32[]{:S(2)}, u32[]{:S(2)}) collective-permute-start(f32[16,8,128]{2,1,0:T(8,128)} %get-tuple-element.64), channel_id=1, source_target_pairs={{0,4},{4,8},{8,12},{12,16},{16,20},{20,24},{24,28},{1,5},{5,9},{9,... | collective-permute-start | bytes 196616 | tf_op jit(solution)/shard_map/ppermute | solution.py:18
  78.2 8.7 %collective-permute-start.12 = (f32[2,16,128]{2,1,0:T(8,128)}, f32[2,16,128]{2,1,0:T(8,128)S(1)}, u32[]{:S(2)}, u32[]{:S(2)}) collective-permute-start(f32[2,16,128]{2,1,0:T(8,128)} %get-tuple-element.62), channel_id=1, source_target_pairs={{0,32},{32,64},{64,96},{96,128},{128,160},{160,192},{192,224},{1,3... | collective-permute-start | bytes 49160 | tf_op jit(solution)/shard_map/ppermute | solution.py:18
  90.6 8.1 %collective-permute-done.13.refs_9_ = f32[2,16,128]{2,1,0:T(8,128)S(1)} collective-permute-done((f32[2,16,128]{2,1,0:T(8,128)}, f32[2,16,128]{2,1,0:T(8,128)S(1)}, u32[]{:S(2)}, u32[]{:S(2)}) %collective-permute-start.13) | collective-permute-done | bytes 16416 | tf_op jit(solution)/shard_map/ppermute | solution.py:23
  99.4 3.3 %shard_map.123 = (f32[16,16,128]{2,1,0:T(8,128)}, f32[3,16,16,128]{3,2,1,0:T(8,128)}, f32[16,16,1]{2,1,0:T(8,128)}, f32[2,16,128]{2,1,0:T(8,128)}, f32[16,2,128]...) custom-call(f32[64]{0:T(128)} %compare_select_fusion.5.refs_0_, ...), custom_call_target="tpu_custom_call" | custom-call | flops 2621440 | bytes 1572864 | tf_op jit(solution)/shard_map/pallas_call | solution.py:221
  102.7 4.5 %collective-permute-start.22 = (f32[16,16,2]{2,1,0:T(8,128)}, f32[16,16,2]{2,1,0:T(8,128)S(1)}, u32[]{:S(2)}, u32[]{:S(2)}) collective-permute-start(f32[16,16,2]{2,1,0:T(8,128)} %get-tuple-element.78), channel_id=1, source_target_pairs={{0,1},{1,2},{2,3},{4,5},{5,6},{6,7},{8,9},{9,10},{10,11},{12,13},{... | collective-permute-start | bytes 6152 | tf_op jit(solution)/shard_map/ppermute | solution.py:18
  108.5 5.0 %collective-permute-start.20 = (f32[16,8,128]{2,1,0:T(8,128)}, f32[16,8,128]{2,1,0:T(8,128)S(1)}, u32[]{:S(2)}, u32[]{:S(2)}) collective-permute-start(f32[16,8,128]{2,1,0:T(8,128)} %get-tuple-element.76), channel_id=1, source_target_pairs={{0,4},{4,8},{8,12},{12,16},{16,20},{20,24},{24,28},{1,5},{5,9},{9,... | collective-permute-start | bytes 196616 | tf_op jit(solution)/shard_map/ppermute | solution.py:18
  117.8 11.8 %all-to-all-start = ((f32[64,1,128]{2,1,0:T(1,128)}), f32[64,1,128]{2,1,0:T(1,128)S(1)}, u32[]{:S(2)}, u32[]{:S(2)}) async-start(f32[64,1,128]{2,1,0:T(1,128)} %bitcast.9), calls=%async_computation | async-start | bytes 65536 | tf_op jit(solution)/shard_map/all_to_all | solution.py:33
  129.7 7.3 %collective-permute-start.18 = (f32[2,16,128]{2,1,0:T(8,128)S(1)}, f32[2,16,128]{2,1,0:T(8,128)S(1)}, u32[]{:S(2)}, u32[]{:S(2)}) collective-permute-start(f32[2,16,128]{2,1,0:T(8,128)S(1)} %copy-done.32), channel_id=1, source_target_pairs={{0,32},{32,64},{64,96},{96,128},{128,160},{160,192},{192,224},{1,3... | collective-permute-start | bytes 49160 | tf_op jit(solution)/shard_map/ppermute | solution.py:18
  137.1 1.9 %collective-permute-start.19 = (f32[2,16,128]{2,1,0:T(8,128)S(1)}, f32[2,16,128]{2,1,0:T(8,128)S(1)}, u32[]{:S(2)}, u32[]{:S(2)}) collective-permute-start(f32[2,16,128]{2,1,0:T(8,128)S(1)} %copy-done.31), channel_id=1, source_target_pairs={{32,0},{64,32},{96,64},{128,96},{160,128},{192,160},{224,192},{33,... | collective-permute-start | bytes 49160 | tf_op jit(solution)/shard_map/ppermute | solution.py:23
  141.5 7.2 %collective-permute-done.19.refs_9_ = f32[2,16,128]{2,1,0:T(8,128)S(1)} collective-permute-done((f32[2,16,128]{2,1,0:T(8,128)S(1)}, f32[2,16,128]{2,1,0:T(8,128)S(1)}, u32[]{:S(2)}, u32[]{:S(2)}) %collective-permute-start.19) | collective-permute-done | bytes 16416 | tf_op jit(solution)/shard_map/ppermute | solution.py:23
  149.4 3.3 %shard_map.124 = (f32[16,16,128]{2,1,0:T(8,128)}, f32[3,16,16,128]{3,2,1,0:T(8,128)}, f32[16,16,1]{2,1,0:T(8,128)}, f32[2,16,128]{2,1,0:T(8,128)}, f32[16,2,128]...) custom-call(f32[64]{0:T(128)} %compare_select_fusion.5.refs_0_, ...), custom_call_target="tpu_custom_call" | custom-call | flops 2621440 | bytes 1572864 | tf_op jit(solution)/shard_map/pallas_call | solution.py:221
  (143 shorter events, 32.8 us)
Async XLA Ops:
  4.0 18.9 %collective-permute-start.4 = (f32[16,16,4]{2,1,0:T(8,128)S(1)}, f32[16,16,4]{2,1,0:T(8,128)S(1)}, u32[]{:S(2)}, u32[]{:S(2)}) collective-permute-start(f32[16,16,4]{2,1,0:T(8,128)S(1)} %copy.20), channel_id=1, source_target_pairs={{0,1},{1,2},{2,3},{4,5},{5,6},{6,7},{8,9},{9,10},{10,11},{12,13},{... | collective-permute-start | bytes 12296 | tf_op jit(solution)/shard_map/ppermute | solution.py:18
  8.3 18.1 %collective-permute-start.5 = (f32[16,16,4]{2,1,0:T(8,128)S(1)}, f32[16,16,4]{2,1,0:T(8,128)S(1)}, u32[]{:S(2)}, u32[]{:S(2)}) collective-permute-start(f32[16,16,4]{2,1,0:T(8,128)S(1)} %copy.23), channel_id=1, source_target_pairs={{1,0},{2,1},{3,2},{5,4},{6,5},{7,6},{9,8},{10,9},{11,10},{13,12},{... | collective-permute-start | bytes 12296 | tf_op jit(solution)/shard_map/ppermute | solution.py:23
  9.7 25.0 %collective-permute-start.2 = (f32[16,10,128]{2,1,0:T(8,128)S(1)}, f32[16,10,128]{2,1,0:T(8,128)S(1)}, u32[]{:S(2)}, u32[]{:S(2)}) collective-permute-start(f32[16,10,128]{2,1,0:T(8,128)S(1)} %pad_maximum_fusion), channel_id=1, source_target_pairs={{0,4},{4,8},{8,12},{12,16},{16,20},{20,24},{24,28},{1,5},{5,9},{9,... | collective-permute-start | bytes 245768 | tf_op jit(solution)/shard_map/ppermute | solution.py:18
  11.2 23.5 %collective-permute-start.3 = (f32[16,10,128]{2,1,0:T(8,128)S(1)}, f32[16,10,128]{2,1,0:T(8,128)S(1)}, u32[]{:S(2)}, u32[]{:S(2)}) collective-permute-start(f32[16,10,128]{2,1,0:T(8,128)S(1)} %pad_maximum_fusion.1), channel_id=1, source_target_pairs={{4,0},{8,4},{12,8},{16,12},{20,16},{24,20},{28,24},{5,1},{9,5},{13... | collective-permute-start | bytes 245768 | tf_op jit(solution)/shard_map/ppermute | solution.py:23
  13.3 13.2 %collective-permute-start = (f32[4,16,128]{2,1,0:T(8,128)S(1)}, f32[4,16,128]{2,1,0:T(8,128)S(1)}, u32[]{:S(2)}, u32[]{:S(2)}) collective-permute-start(f32[4,16,128]{2,1,0:T(8,128)S(1)} %pad_maximum_fusion.2), channel_id=1, source_target_pairs={{0,32},{32,64},{64,96},{96,128},{128,160},{160,192},{192,224},{1,3... | collective-permute-start | bytes 98312 | tf_op jit(solution)/shard_map/ppermute | solution.py:18
  22.9 11.8 %collective-permute-start.1 = (f32[4,16,128]{2,1,0:T(8,128)S(1)}, f32[4,16,128]{2,1,0:T(8,128)S(1)}, u32[]{:S(2)}, u32[]{:S(2)}) collective-permute-start(f32[4,16,128]{2,1,0:T(8,128)S(1)} %pad_maximum_fusion.3), channel_id=1, source_target_pairs={{32,0},{64,32},{96,64},{128,96},{160,128},{192,160},{224,192},{33,... | collective-permute-start | bytes 98312 | tf_op jit(solution)/shard_map/ppermute | solution.py:23
  39.6 25.1 %collective-permute-start.8 = (f32[16,8,128]{2,1,0:T(8,128)}, f32[16,8,128]{2,1,0:T(8,128)S(1)}, u32[]{:S(2)}, u32[]{:S(2)}) collective-permute-start(f32[16,8,128]{2,1,0:T(8,128)} %get-tuple-element.49), channel_id=1, source_target_pairs={{0,4},{4,8},{8,12},{12,16},{16,20},{20,24},{24,28},{1,5},{5,9},{9,... | collective-permute-start | bytes 196616 | tf_op jit(solution)/shard_map/ppermute | solution.py:18
  42.8 22.0 %collective-permute-start.9 = (f32[16,8,128]{2,1,0:T(8,128)}, f32[16,8,128]{2,1,0:T(8,128)S(1)}, u32[]{:S(2)}, u32[]{:S(2)}) collective-permute-start(f32[16,8,128]{2,1,0:T(8,128)} %get-tuple-element.50), channel_id=1, source_target_pairs={{4,0},{8,4},{12,8},{16,12},{20,16},{24,20},{28,24},{5,1},{9,5},{13... | collective-permute-start | bytes 196616 | tf_op jit(solution)/shard_map/ppermute | solution.py:23
  44.1 20.6 %collective-permute-start.6 = (f32[2,16,128]{2,1,0:T(8,128)}, f32[2,16,128]{2,1,0:T(8,128)S(1)}, u32[]{:S(2)}, u32[]{:S(2)}) collective-permute-start(f32[2,16,128]{2,1,0:T(8,128)} %get-tuple-element.47), channel_id=1, source_target_pairs={{0,32},{32,64},{64,96},{96,128},{128,160},{160,192},{192,224},{1,3... | collective-permute-start | bytes 49160 | tf_op jit(solution)/shard_map/ppermute | solution.py:18
  46.7 18.0 %collective-permute-start.7 = (f32[2,16,128]{2,1,0:T(8,128)}, f32[2,16,128]{2,1,0:T(8,128)S(1)}, u32[]{:S(2)}, u32[]{:S(2)}) collective-permute-start(f32[2,16,128]{2,1,0:T(8,128)} %get-tuple-element.48), channel_id=1, source_target_pairs={{32,0},{64,32},{96,64},{128,96},{160,128},{192,160},{224,192},{33,... | collective-permute-start | bytes 49160 | tf_op jit(solution)/shard_map/ppermute | solution.py:23
  68.8 18.1 %collective-permute-start.16 = (f32[16,16,2]{2,1,0:T(8,128)}, f32[16,16,2]{2,1,0:T(8,128)S(1)}, u32[]{:S(2)}, u32[]{:S(2)}) collective-permute-start(f32[16,16,2]{2,1,0:T(8,128)} %get-tuple-element.66), channel_id=1, source_target_pairs={{0,1},{1,2},{2,3},{4,5},{5,6},{6,7},{8,9},{9,10},{10,11},{12,13},{... | collective-permute-start | bytes 6152 | tf_op jit(solution)/shard_map/ppermute | solution.py:18
  73.0 17.6 %collective-permute-start.17 = (f32[16,16,2]{2,1,0:T(8,128)}, f32[16,16,2]{2,1,0:T(8,128)S(1)}, u32[]{:S(2)}, u32[]{:S(2)}) collective-permute-start(f32[16,16,2]{2,1,0:T(8,128)} %get-tuple-element.67), channel_id=1, source_target_pairs={{1,0},{2,1},{3,2},{5,4},{6,5},{7,6},{9,8},{10,9},{11,10},{13,12},{... | collective-permute-start | bytes 6152 | tf_op jit(solution)/shard_map/ppermute | solution.py:23
  74.3 24.4 %collective-permute-start.14 = (f32[16,8,128]{2,1,0:T(8,128)}, f32[16,8,128]{2,1,0:T(8,128)S(1)}, u32[]{:S(2)}, u32[]{:S(2)}) collective-permute-start(f32[16,8,128]{2,1,0:T(8,128)} %get-tuple-element.64), channel_id=1, source_target_pairs={{0,4},{4,8},{8,12},{12,16},{16,20},{20,24},{24,28},{1,5},{5,9},{9,... | collective-permute-start | bytes 196616 | tf_op jit(solution)/shard_map/ppermute | solution.py:18
  76.9 21.9 %collective-permute-start.15 = (f32[16,8,128]{2,1,0:T(8,128)}, f32[16,8,128]{2,1,0:T(8,128)S(1)}, u32[]{:S(2)}, u32[]{:S(2)}) collective-permute-start(f32[16,8,128]{2,1,0:T(8,128)} %get-tuple-element.65), channel_id=1, source_target_pairs={{4,0},{8,4},{12,8},{16,12},{20,16},{24,20},{28,24},{5,1},{9,5},{13... | collective-permute-start | bytes 196616 | tf_op jit(solution)/shard_map/ppermute | solution.py:23
  78.2 12.4 %collective-permute-start.12 = (f32[2,16,128]{2,1,0:T(8,128)}, f32[2,16,128]{2,1,0:T(8,128)S(1)}, u32[]{:S(2)}, u32[]{:S(2)}) collective-permute-start(f32[2,16,128]{2,1,0:T(8,128)} %get-tuple-element.62), channel_id=1, source_target_pairs={{0,32},{32,64},{64,96},{96,128},{128,160},{160,192},{192,224},{1,3... | collective-permute-start | bytes 49160 | tf_op jit(solution)/shard_map/ppermute | solution.py:18
  86.9 11.9 %collective-permute-start.13 = (f32[2,16,128]{2,1,0:T(8,128)}, f32[2,16,128]{2,1,0:T(8,128)S(1)}, u32[]{:S(2)}, u32[]{:S(2)}) collective-permute-start(f32[2,16,128]{2,1,0:T(8,128)} %get-tuple-element.63), channel_id=1, source_target_pairs={{32,0},{64,32},{96,64},{128,96},{160,128},{192,160},{224,192},{33,... | collective-permute-start | bytes 49160 | tf_op jit(solution)/shard_map/ppermute | solution.py:23
  102.7 12.1 %collective-permute-start.22 = (f32[16,16,2]{2,1,0:T(8,128)}, f32[16,16,2]{2,1,0:T(8,128)S(1)}, u32[]{:S(2)}, u32[]{:S(2)}) collective-permute-start(f32[16,16,2]{2,1,0:T(8,128)} %get-tuple-element.78), channel_id=1, source_target_pairs={{0,1},{1,2},{2,3},{4,5},{5,6},{6,7},{8,9},{9,10},{10,11},{12,13},{... | collective-permute-start | bytes 6152 | tf_op jit(solution)/shard_map/ppermute | solution.py:18
  107.2 7.6 %collective-permute-start.23 = (f32[16,16,2]{2,1,0:T(8,128)}, f32[16,16,2]{2,1,0:T(8,128)S(1)}, u32[]{:S(2)}, u32[]{:S(2)}) collective-permute-start(f32[16,16,2]{2,1,0:T(8,128)} %get-tuple-element.79), channel_id=1, source_target_pairs={{1,0},{2,1},{3,2},{5,4},{6,5},{7,6},{9,8},{10,9},{11,10},{13,12},{... | collective-permute-start | bytes 6152 | tf_op jit(solution)/shard_map/ppermute | solution.py:23
  108.5 40.2 %collective-permute-start.20 = (f32[16,8,128]{2,1,0:T(8,128)}, f32[16,8,128]{2,1,0:T(8,128)S(1)}, u32[]{:S(2)}, u32[]{:S(2)}) collective-permute-start(f32[16,8,128]{2,1,0:T(8,128)} %get-tuple-element.76), channel_id=1, source_target_pairs={{0,4},{4,8},{8,12},{12,16},{16,20},{20,24},{24,28},{1,5},{5,9},{9,... | collective-permute-start | bytes 196616 | tf_op jit(solution)/shard_map/ppermute | solution.py:18
  113.5 35.2 %collective-permute-start.21 = (f32[16,8,128]{2,1,0:T(8,128)}, f32[16,8,128]{2,1,0:T(8,128)S(1)}, u32[]{:S(2)}, u32[]{:S(2)}) collective-permute-start(f32[16,8,128]{2,1,0:T(8,128)} %get-tuple-element.77), channel_id=1, source_target_pairs={{4,0},{8,4},{12,8},{16,12},{20,16},{24,20},{28,24},{5,1},{9,5},{13... | collective-permute-start | bytes 196616 | tf_op jit(solution)/shard_map/ppermute | solution.py:23
  117.8 22.3 %all-to-all-start = ((f32[64,1,128]{2,1,0:T(1,128)}), f32[64,1,128]{2,1,0:T(1,128)S(1)}, u32[]{:S(2)}, u32[]{:S(2)}) async-start(f32[64,1,128]{2,1,0:T(1,128)} %bitcast.9), calls=%async_computation | async-start | bytes 65536 | tf_op jit(solution)/shard_map/all_to_all | solution.py:33
  129.7 11.8 %collective-permute-start.18 = (f32[2,16,128]{2,1,0:T(8,128)S(1)}, f32[2,16,128]{2,1,0:T(8,128)S(1)}, u32[]{:S(2)}, u32[]{:S(2)}) collective-permute-start(f32[2,16,128]{2,1,0:T(8,128)S(1)} %copy-done.32), channel_id=1, source_target_pairs={{0,32},{32,64},{64,96},{96,128},{128,160},{160,192},{192,224},{1,3... | collective-permute-start | bytes 49160 | tf_op jit(solution)/shard_map/ppermute | solution.py:18
  137.1 11.6 %collective-permute-start.19 = (f32[2,16,128]{2,1,0:T(8,128)S(1)}, f32[2,16,128]{2,1,0:T(8,128)S(1)}, u32[]{:S(2)}, u32[]{:S(2)}) collective-permute-start(f32[2,16,128]{2,1,0:T(8,128)S(1)} %copy-done.31), channel_id=1, source_target_pairs={{32,0},{64,32},{96,64},{128,96},{160,128},{192,160},{224,192},{33,... | collective-permute-start | bytes 49160 | tf_op jit(solution)/shard_map/ppermute | solution.py:23
  140.2 12.5 %collective-permute-start.24 = (f32[128]{0:T(128)S(1)}, f32[128]{0:T(128)S(1)}, u32[]{:S(2)}, u32[]{:S(2)}) collective-permute-start(f32[128]{0:T(128)S(1)} %reduce_sum.9), channel_id=1, source_target_pairs={{1,0},{2,3},{5,4},{6,7},{9,8},{10,11},{13,12},{14,15},{17,16},{18,... | collective-permute-start | bytes 1544 | tf_op jit(solution)/shard_map/ppermute | solution.py:348
  (36 other events, 209.3 us)

commit v11 on v10

--- a/solution.py
+++ b/solution.py
@@ -67,6 +67,14 @@
     return jnp.where(where, jnp.broadcast_to(lo, shape), jnp.broadcast_to(hi, shape))
 
 
+def quad(parts, shape):
+    lane = lax.broadcasted_iota(jnp.int32, shape, len(shape) - 1)
+    out = jnp.broadcast_to(parts[-1], shape)
+    for index in range(len(parts) - 2, -1, -1):
+        out = jnp.where(lane == index, jnp.broadcast_to(parts[index], shape), out)
+    return out
+
+
 def step_kernel(instant, first, *refs):
     if first:
         (scal_ref, wint_ref, p_ref, v_ref, idn_ref, bulk_ref, src_ref,
@@ -75,10 +83,10 @@
     else:
         (scal_ref, wint_ref, p_ref, v_ref, idn_ref, bulk_ref, src_ref, sf_ref,
          xl_ref, xh_ref, yl_ref, yh_ref, zl_ref, zh_ref,
-         vx_ref, vy_ref, vz_ref, ix_ref, iy_ref, iz_ref) = refs[:20]
-        outs = refs[20:]
-    (po_ref, vo_ref, sfo_ref, vxo_ref, vyo_ref, vzo_ref,
-     sxu_ref, sxd_ref, syu_ref, syd_ref, szu_ref, szd_ref) = outs[:12]
+         vx_ref, vy_ref, ix_ref, iy_ref) = refs[:18]
+        outs = refs[18:]
+    (po_ref, vo_ref, sfo_ref, vxo_ref, vyo_ref,
+     sxu_ref, sxd_ref, syu_ref, syd_ref, szu_ref, szd_ref) = outs[:11]
     X, Y, Z = p_ref.shape
     rows = syu_ref.shape[1]
     base = instant * 16
@@ -109,27 +117,23 @@
     yh1, yh2 = pick(yh, 1, 0), pick(yh, 1, 1)
     zl2, zl1 = pick(zl, -1, 0), pick(zl, -1, 1)
     zh1, zh2 = pick(zh, -1, 0), pick(zh, -1, 1)
+    vz_lo, vz_hi, iz_lo, iz_hi = pick(zl, -1, 2), pick(zh, -1, 2), pick(zl, -1, 3), pick(zh, -1, 3)
     if first:
         vx_lo, vx_hi, ix_lo, ix_hi = xl[2:3], xh[2:3], xl[3:4], xh[3:4]
         vy_lo, vy_hi = pick(yl, 1, rows), pick(yh, 1, rows)
         iy_lo, iy_hi = pick(yl, 1, rows + 1), pick(yh, 1, rows + 1)
-        vz_lo, vz_hi, iz_lo, iz_hi = pick(zl, -1, 2), pick(zh, -1, 2), pick(zl, -1, 3), pick(zh, -1, 3)
-        ixo_ref, iyo_ref, izo_ref = outs[12:15]
+        ixo_ref, iyo_ref = outs[11:13]
         ixo_ref[0:1] = ix_lo
         ixo_ref[1:2] = ix_hi
         iyo_ref[...] = pair(iy_lo, iy_hi, iyo_ref.shape, 1)
-        izo_ref[...] = pair(iz_lo, iz_hi, izo_ref.shape, 2)
     else:
         vx = vx_ref[...]
         ix = ix_ref[...]
         vy = vy_ref[...]
         iy = iy_ref[...]
-        vz = vz_ref[...]
-        iz = iz_ref[...]
         vx_lo, vx_hi, ix_lo, ix_hi = vx[0:1], vx[1:2], ix[0:1], ix[1:2]
         vy_lo, vy_hi = pick(vy, 1, 0), pick(vy, 1, 1)
         iy_lo, iy_hi = pick(iy, 1, 0), pick(iy, 1, 1)
-        vz_lo, vz_hi, iz_lo, iz_hi = pick(vz, -1, 0), pick(vz, -1, 1), pick(iz, -1, 0), pick(iz, -1, 1)
 
     pres = p_ref[...]
     idn = idn_ref[...]
@@ -168,7 +172,6 @@
     vxo_ref[0:1] = v0_lo
     vxo_ref[1:2] = v0_hi
     vyo_ref[...] = pair(v1_lo, v1_hi, vyo_ref.shape, 1)
-    vzo_ref[...] = pair(v2_lo, v2_hi, vzo_ref.shape, 2)
 
     up_x = jnp.concatenate([v0[1:], v0_hi], axis=0)
     down_x = jnp.concatenate([v0_lo, v0[:-1]], axis=0)
@@ -182,7 +185,7 @@
         + (wu * up_z + wm * v2 + wl * down_z)
     )
     new_p = pres - time_step * bulk_ref[...] * spread
-    new_p = jnp.where(zi == 0, new_p + jnp.broadcast_to(src_ref[instant], full), new_p)
+    new_p = jnp.where(zi == 0, new_p + jnp.broadcast_to(src_ref[...], full), new_p)
     po_ref[...] = new_p
 
     sxu_ref[...] = new_p[X - 2 :]
@@ -190,8 +193,10 @@
     syu_ref[...] = new_p[:, Y - rows :]
     syd_ref[...] = new_p[:, 0:rows]
     zshape = szu_ref.shape
-    szu_ref[...] = pair(pick(new_p, -1, Z - 2), pick(new_p, -1, Z - 1), zshape, 2)
-    szd_ref[...] = pair(pick(new_p, -1, 0), pick(new_p, -1, 1), zshape, 2)
+    szu_ref[...] = quad(
+        (pick(new_p, -1, Z - 2), pick(new_p, -1, Z - 1), pick(v2, -1, Z - 1), pick(idn, -1, Z - 1)), zshape
+    )
+    szd_ref[...] = quad((pick(new_p, -1, 0), pick(new_p, -1, 1), pick(v2, -1, 0), pick(idn, -1, 0)), zshape)
 
 
 def run_step(instant, operands, rows):
@@ -205,22 +210,23 @@
         jax.ShapeDtypeStruct((X, Y, 1), f32),
         jax.ShapeDtypeStruct((2, Y, Z), f32),
         jax.ShapeDtypeStruct((X, 2, Z), f32),
-        jax.ShapeDtypeStruct((X, Y, 2), f32),
         jax.ShapeDtypeStruct((2, Y, Z), f32),
         jax.ShapeDtypeStruct((2, Y, Z), f32),
         jax.ShapeDtypeStruct((X, rows, Z), f32),
         jax.ShapeDtypeStruct((X, rows, Z), f32),
-        jax.ShapeDtypeStruct((X, Y, 2), f32),
-        jax.ShapeDtypeStruct((X, Y, 2), f32),
+        jax.ShapeDtypeStruct((X, Y, 4), f32),
+        jax.ShapeDtypeStruct((X, Y, 4), f32),
     ]
     if first:
-        shapes += shapes[3:6]
+        shapes += shapes[3:5]
     vmem = pl.BlockSpec(memory_space=pltpu.VMEM)
     in_specs = [pl.BlockSpec(memory_space=pltpu.SMEM)] + [vmem] * (len(operands) - 1)
+    in_specs[6] = pl.BlockSpec((None, X, Y, 1), lambda i: (instant, 0, 0, 0))
     cells = X * Y * Z
     return pl.pallas_call(
         functools.partial(step_kernel, instant, first),
         out_shape=tuple(shapes),
+        grid=(1,),
         in_specs=in_specs,
         out_specs=[vmem] * len(shapes),
         cost_estimate=pl.CostEstimate(
@@ -339,10 +345,10 @@
             operands = common + (pres, vel, inv_density, bulk, src_all, sf) + halos + tracked + media_halo
         outs = run_step(instant, operands, rows)
         pres, vel, sf = outs[0], outs[1], outs[2]
-        tracked = outs[3:6]
-        sends = outs[6:12]
+        tracked = outs[3:5]
+        sends = outs[5:11]
         if instant == 0:
-            media_halo = outs[12:15]
+            media_halo = outs[11:13]
     ocean_plane = first_crust // Z - 1
     crust_plane = first_crust // Z
     spread_out = lax.ppermute(

time: 155 us -> 155 us (level)
  no operation moved by 1% of the time
where the time goes in v11:
time: 155 us; the launch traced here: 153 us
  starting transfers between devices  88.1 us (57%)
  waiting for transfers between devices  33.6 us (22%)
  Pallas kernels  13.5 us (9%)
  local copies, waits for them, and re-layouts  12.7 us (8%)
  other arithmetic  2.77 us (2%)
    ppermute x12, starting transfers between devices, shifted_up(): return lax.ppermute(x, axis, [(i, i + 1) for i in range(count - 1)])  55.7 us
    ppermute x12, waiting for transfers between devices, shifted_down(): return lax.ppermute(x, axis, [(i + 1, i) for i in range(count - 1)])  29.6 us
    ppermute x12, starting transfers between devices, shifted_down(): return lax.ppermute(x, axis, [(i + 1, i) for i in range(count - 1)])  19.3 us
    pallas_call x4, Pallas kernels, run_step(): pl.pallas_call(functools.partial(step_kernel, instant, first), out_shape=...  13.5 us
    all_to_all x1, starting transfers between devices, summed_on_arrival(): parts = lax.all_to_all(in_blocks(x, dim, size), axis, 0, 0, tiled=True)  11.9 us
    unnamed x73, local copies, waits for them, and re-layouts  6.91 us
  transfers between devices with their start and end apart: 26, of which 6 were waited for; matrix products, arithmetic and copies ran while one was open for 5% of the time, Pallas kernels for 2%

profile of v11, /device:TPU:24, one launch (start us, length us, event | category | flops | bytes accessed | tf_op | source)
XLA Modules:
  0.0 153.3 jit_solution(7336838855784844546)
XLA Ops:
  4.0 3.8 %collective-permute-start.4 = (f32[16,16,4]{2,1,0:T(8,128)S(1)}, f32[16,16,4]{2,1,0:T(8,128)S(1)}, u32[]{:S(2)}, u32[]{:S(2)}) collective-permute-start(f32[16,16,4]{2,1,0:T(8,128)S(1)} %copy.20), channel_id=1, source_target_pairs={{0,1},{1,2},{2,3},{4,5},{5,6},{6,7},{8,9},{9,10},{10,11},{12,13},{... | collective-permute-start | bytes 12296 | tf_op jit(solution)/shard_map/ppermute | solution.py:18
  13.3 7.8 %collective-permute-start = (f32[4,16,128]{2,1,0:T(8,128)S(1)}, f32[4,16,128]{2,1,0:T(8,128)S(1)}, u32[]{:S(2)}, u32[]{:S(2)}) collective-permute-start(f32[4,16,128]{2,1,0:T(8,128)S(1)} %pad_maximum_fusion.2), channel_id=1, source_target_pairs={{0,32},{32,64},{64,96},{96,128},{128,160},{160,192},{192,224},{1,3... | collective-permute-start | bytes 98312 | tf_op jit(solution)/shard_map/ppermute | solution.py:18
  22.8 1.9 %collective-permute-start.1 = (f32[4,16,128]{2,1,0:T(8,128)S(1)}, f32[4,16,128]{2,1,0:T(8,128)S(1)}, u32[]{:S(2)}, u32[]{:S(2)}) collective-permute-start(f32[4,16,128]{2,1,0:T(8,128)S(1)} %pad_maximum_fusion.3), channel_id=1, source_target_pairs={{32,0},{64,32},{96,64},{128,96},{160,128},{192,160},{224,192},{33,... | collective-permute-start | bytes 98312 | tf_op jit(solution)/shard_map/ppermute | solution.py:23
  26.5 8.2 %collective-permute-done.1.refs_8_ = f32[4,16,128]{2,1,0:T(8,128)S(1)} collective-permute-done((f32[4,16,128]{2,1,0:T(8,128)S(1)}, f32[4,16,128]{2,1,0:T(8,128)S(1)}, u32[]{:S(2)}, u32[]{:S(2)}) %collective-permute-start.1) | collective-permute-done | bytes 32800 | tf_op jit(solution)/shard_map/ppermute | solution.py:23
  36.0 3.4 %shard_map.121 = (f32[16,16,128]{2,1,0:T(8,128)}, f32[3,16,16,128]{3,2,1,0:T(8,128)}, f32[16,16,1]{2,1,0:T(8,128)}, f32[2,16,128]{2,1,0:T(8,128)}, f32[16,2,128]...) custom-call(f32[64]{0:T(128)} %compare_select_fusion.5.refs_0_, ...), custom_call_target="tpu_custom_call" | custom-call | flops 2621440 | bytes 1572864 | tf_op jit(solution)/shard_map/pallas_call | solution.py:226
  39.4 3.2 %collective-permute-start.8 = (f32[16,8,128]{2,1,0:T(8,128)}, f32[16,8,128]{2,1,0:T(8,128)S(1)}, u32[]{:S(2)}, u32[]{:S(2)}) collective-permute-start(f32[16,8,128]{2,1,0:T(8,128)} %get-tuple-element.45), channel_id=1, source_target_pairs={{0,4},{4,8},{8,12},{12,16},{16,20},{20,24},{24,28},{1,5},{5,9},{9,... | collective-permute-start | bytes 196616 | tf_op jit(solution)/shard_map/ppermute | solution.py:18
  43.8 2.6 %collective-permute-start.6 = (f32[2,16,128]{2,1,0:T(8,128)}, f32[2,16,128]{2,1,0:T(8,128)S(1)}, u32[]{:S(2)}, u32[]{:S(2)}) collective-permute-start(f32[2,16,128]{2,1,0:T(8,128)} %get-tuple-element.43), channel_id=1, source_target_pairs={{0,32},{32,64},{64,96},{96,128},{128,160},{160,192},{192,224},{1,3... | collective-permute-start | bytes 49160 | tf_op jit(solution)/shard_map/ppermute | solution.py:18
  46.5 3.2 %collective-permute-start.7 = (f32[2,16,128]{2,1,0:T(8,128)}, f32[2,16,128]{2,1,0:T(8,128)S(1)}, u32[]{:S(2)}, u32[]{:S(2)}) collective-permute-start(f32[2,16,128]{2,1,0:T(8,128)} %get-tuple-element.44), channel_id=1, source_target_pairs={{32,0},{64,32},{96,64},{128,96},{160,128},{192,160},{224,192},{33,... | collective-permute-start | bytes 49160 | tf_op jit(solution)/shard_map/ppermute | solution.py:23
  49.7 4.6 %collective-permute-start.10 = (f32[16,16,4]{2,1,0:T(8,128)}, f32[16,16,4]{2,1,0:T(8,128)S(1)}, u32[]{:S(2)}, u32[]{:S(2)}) collective-permute-start(f32[16,16,4]{2,1,0:T(8,128)} %get-tuple-element.47), channel_id=1, source_target_pairs={{0,1},{1,2},{2,3},{4,5},{5,6},{6,7},{8,9},{9,10},{10,11},{12,13},{... | collective-permute-start | bytes 12296 | tf_op jit(solution)/shard_map/ppermute | solution.py:18
  54.2 2.8 %collective-permute-done.10.refs_12_ = f32[16,16,4]{2,1,0:T(8,128)S(1)} collective-permute-done((f32[16,16,4]{2,1,0:T(8,128)}, f32[16,16,4]{2,1,0:T(8,128)S(1)}, u32[]{:S(2)}, u32[]{:S(2)}) %collective-permute-start.10) | collective-permute-done | bytes 4128 | tf_op jit(solution)/shard_map/ppermute | solution.py:18
  58.3 6.1 %collective-permute-done.11.refs_13_ = f32[16,16,4]{2,1,0:T(8,128)S(1)} collective-permute-done((f32[16,16,4]{2,1,0:T(8,128)}, f32[16,16,4]{2,1,0:T(8,128)S(1)}, u32[]{:S(2)}, u32[]{:S(2)}) %collective-permute-start.11) | collective-permute-done | bytes 4128 | tf_op jit(solution)/shard_map/ppermute | solution.py:23
  65.2 3.4 %shard_map.122 = (f32[16,16,128]{2,1,0:T(8,128)}, f32[3,16,16,128]{3,2,1,0:T(8,128)}, f32[16,16,1]{2,1,0:T(8,128)}, f32[2,16,128]{2,1,0:T(8,128)}, f32[16,2,128]...) custom-call(f32[64]{0:T(128)} %compare_select_fusion.5.refs_0_, ...), custom_call_target="tpu_custom_call" | custom-call | flops 2621440 | bytes 1572864 | tf_op jit(solution)/shard_map/pallas_call | solution.py:226
  68.6 4.2 %collective-permute-start.16 = (f32[16,16,4]{2,1,0:T(8,128)}, f32[16,16,4]{2,1,0:T(8,128)S(1)}, u32[]{:S(2)}, u32[]{:S(2)}) collective-permute-start(f32[16,16,4]{2,1,0:T(8,128)} %get-tuple-element.60), channel_id=1, source_target_pairs={{0,1},{1,2},{2,3},{4,5},{5,6},{6,7},{8,9},{9,10},{10,11},{12,13},{... | collective-permute-start | bytes 12296 | tf_op jit(solution)/shard_map/ppermute | solution.py:18
  74.1 2.6 %collective-permute-start.14 = (f32[16,8,128]{2,1,0:T(8,128)}, f32[16,8,128]{2,1,0:T(8,128)S(1)}, u32[]{:S(2)}, u32[]{:S(2)}) collective-permute-start(f32[16,8,128]{2,1,0:T(8,128)} %get-tuple-element.58), channel_id=1, source_target_pairs={{0,4},{4,8},{8,12},{12,16},{16,20},{20,24},{24,28},{1,5},{5,9},{9,... | collective-permute-start | bytes 196616 | tf_op jit(solution)/shard_map/ppermute | solution.py:18
  78.0 8.7 %collective-permute-start.12 = (f32[2,16,128]{2,1,0:T(8,128)}, f32[2,16,128]{2,1,0:T(8,128)S(1)}, u32[]{:S(2)}, u32[]{:S(2)}) collective-permute-start(f32[2,16,128]{2,1,0:T(8,128)} %get-tuple-element.56), channel_id=1, source_target_pairs={{0,32},{32,64},{64,96},{96,128},{128,160},{160,192},{192,224},{1,3... | collective-permute-start | bytes 49160 | tf_op jit(solution)/shard_map/ppermute | solution.py:18
  90.4 8.1 %collective-permute-done.13.refs_9_ = f32[2,16,128]{2,1,0:T(8,128)S(1)} collective-permute-done((f32[2,16,128]{2,1,0:T(8,128)}, f32[2,16,128]{2,1,0:T(8,128)S(1)}, u32[]{:S(2)}, u32[]{:S(2)}) %collective-permute-start.13) | collective-permute-done | bytes 16416 | tf_op jit(solution)/shard_map/ppermute | solution.py:23
  99.2 3.4 %shard_map.123 = (f32[16,16,128]{2,1,0:T(8,128)}, f32[3,16,16,128]{3,2,1,0:T(8,128)}, f32[16,16,1]{2,1,0:T(8,128)}, f32[2,16,128]{2,1,0:T(8,128)}, f32[16,2,128]...) custom-call(f32[64]{0:T(128)} %compare_select_fusion.5.refs_0_, ...), custom_call_target="tpu_custom_call" | custom-call | flops 2621440 | bytes 1572864 | tf_op jit(solution)/shard_map/pallas_call | solution.py:226
  102.6 4.4 %collective-permute-start.22 = (f32[16,16,4]{2,1,0:T(8,128)}, f32[16,16,4]{2,1,0:T(8,128)S(1)}, u32[]{:S(2)}, u32[]{:S(2)}) collective-permute-start(f32[16,16,4]{2,1,0:T(8,128)} %get-tuple-element.71), channel_id=1, source_target_pairs={{0,1},{1,2},{2,3},{4,5},{5,6},{6,7},{8,9},{9,10},{10,11},{12,13},{... | collective-permute-start | bytes 12296 | tf_op jit(solution)/shard_map/ppermute | solution.py:18
  108.3 5.1 %collective-permute-start.20 = (f32[16,8,128]{2,1,0:T(8,128)}, f32[16,8,128]{2,1,0:T(8,128)S(1)}, u32[]{:S(2)}, u32[]{:S(2)}) collective-permute-start(f32[16,8,128]{2,1,0:T(8,128)} %get-tuple-element.69), channel_id=1, source_target_pairs={{0,4},{4,8},{8,12},{12,16},{16,20},{20,24},{24,28},{1,5},{5,9},{9,... | collective-permute-start | bytes 196616 | tf_op jit(solution)/shard_map/ppermute | solution.py:18
  117.8 11.9 %all-to-all-start = ((f32[64,1,128]{2,1,0:T(1,128)}), f32[64,1,128]{2,1,0:T(1,128)S(1)}, u32[]{:S(2)}, u32[]{:S(2)}) async-start(f32[64,1,128]{2,1,0:T(1,128)} %bitcast.9), calls=%async_computation | async-start | bytes 65536 | tf_op jit(solution)/shard_map/all_to_all | solution.py:33
  129.6 7.3 %collective-permute-start.18 = (f32[2,16,128]{2,1,0:T(8,128)S(1)}, f32[2,16,128]{2,1,0:T(8,128)S(1)}, u32[]{:S(2)}, u32[]{:S(2)}) collective-permute-start(f32[2,16,128]{2,1,0:T(8,128)S(1)} %copy-done.32), channel_id=1, source_target_pairs={{0,32},{32,64},{64,96},{96,128},{128,160},{160,192},{192,224},{1,3... | collective-permute-start | bytes 49160 | tf_op jit(solution)/shard_map/ppermute | solution.py:18
  137.0 1.9 %collective-permute-start.19 = (f32[2,16,128]{2,1,0:T(8,128)S(1)}, f32[2,16,128]{2,1,0:T(8,128)S(1)}, u32[]{:S(2)}, u32[]{:S(2)}) collective-permute-start(f32[2,16,128]{2,1,0:T(8,128)S(1)} %copy-done.31), channel_id=1, source_target_pairs={{32,0},{64,32},{96,64},{128,96},{160,128},{192,160},{224,192},{33,... | collective-permute-start | bytes 49160 | tf_op jit(solution)/shard_map/ppermute | solution.py:23
  141.4 7.2 %collective-permute-done.19.refs_9_ = f32[2,16,128]{2,1,0:T(8,128)S(1)} collective-permute-done((f32[2,16,128]{2,1,0:T(8,128)S(1)}, f32[2,16,128]{2,1,0:T(8,128)S(1)}, u32[]{:S(2)}, u32[]{:S(2)}) %collective-permute-start.19) | collective-permute-done | bytes 16416 | tf_op jit(solution)/shard_map/ppermute | solution.py:23
  149.3 3.4 %shard_map.124 = (f32[16,16,128]{2,1,0:T(8,128)}, f32[3,16,16,128]{3,2,1,0:T(8,128)}, f32[16,16,1]{2,1,0:T(8,128)}, f32[2,16,128]{2,1,0:T(8,128)}, f32[16,2,128]...) custom-call(f32[64]{0:T(128)} %compare_select_fusion.5.refs_0_, ...), custom_call_target="tpu_custom_call" | custom-call | flops 2621440 | bytes 1572864 | tf_op jit(solution)/shard_map/pallas_call | solution.py:226
  (143 shorter events, 32.8 us)
Async XLA Ops:
  4.0 18.8 %collective-permute-start.4 = (f32[16,16,4]{2,1,0:T(8,128)S(1)}, f32[16,16,4]{2,1,0:T(8,128)S(1)}, u32[]{:S(2)}, u32[]{:S(2)}) collective-permute-start(f32[16,16,4]{2,1,0:T(8,128)S(1)} %copy.20), channel_id=1, source_target_pairs={{0,1},{1,2},{2,3},{4,5},{5,6},{6,7},{8,9},{9,10},{10,11},{12,13},{... | collective-permute-start | bytes 12296 | tf_op jit(solution)/shard_map/ppermute | solution.py:18
  8.3 18.1 %collective-permute-start.5 = (f32[16,16,4]{2,1,0:T(8,128)S(1)}, f32[16,16,4]{2,1,0:T(8,128)S(1)}, u32[]{:S(2)}, u32[]{:S(2)}) collective-permute-start(f32[16,16,4]{2,1,0:T(8,128)S(1)} %copy.23), channel_id=1, source_target_pairs={{1,0},{2,1},{3,2},{5,4},{6,5},{7,6},{9,8},{10,9},{11,10},{13,12},{... | collective-permute-start | bytes 12296 | tf_op jit(solution)/shard_map/ppermute | solution.py:23
  9.7 24.9 %collective-permute-start.2 = (f32[16,10,128]{2,1,0:T(8,128)S(1)}, f32[16,10,128]{2,1,0:T(8,128)S(1)}, u32[]{:S(2)}, u32[]{:S(2)}) collective-permute-start(f32[16,10,128]{2,1,0:T(8,128)S(1)} %pad_maximum_fusion), channel_id=1, source_target_pairs={{0,4},{4,8},{8,12},{12,16},{16,20},{20,24},{24,28},{1,5},{5,9},{9,... | collective-permute-start | bytes 245768 | tf_op jit(solution)/shard_map/ppermute | solution.py:18
  11.2 23.4 %collective-permute-start.3 = (f32[16,10,128]{2,1,0:T(8,128)S(1)}, f32[16,10,128]{2,1,0:T(8,128)S(1)}, u32[]{:S(2)}, u32[]{:S(2)}) collective-permute-start(f32[16,10,128]{2,1,0:T(8,128)S(1)} %pad_maximum_fusion.1), channel_id=1, source_target_pairs={{4,0},{8,4},{12,8},{16,12},{20,16},{24,20},{28,24},{5,1},{9,5},{13... | collective-permute-start | bytes 245768 | tf_op jit(solution)/shard_map/ppermute | solution.py:23
  13.3 13.2 %collective-permute-start = (f32[4,16,128]{2,1,0:T(8,128)S(1)}, f32[4,16,128]{2,1,0:T(8,128)S(1)}, u32[]{:S(2)}, u32[]{:S(2)}) collective-permute-start(f32[4,16,128]{2,1,0:T(8,128)S(1)} %pad_maximum_fusion.2), channel_id=1, source_target_pairs={{0,32},{32,64},{64,96},{96,128},{128,160},{160,192},{192,224},{1,3... | collective-permute-start | bytes 98312 | tf_op jit(solution)/shard_map/ppermute | solution.py:18
  22.8 11.8 %collective-permute-start.1 = (f32[4,16,128]{2,1,0:T(8,128)S(1)}, f32[4,16,128]{2,1,0:T(8,128)S(1)}, u32[]{:S(2)}, u32[]{:S(2)}) collective-permute-start(f32[4,16,128]{2,1,0:T(8,128)S(1)} %pad_maximum_fusion.3), channel_id=1, source_target_pairs={{32,0},{64,32},{96,64},{128,96},{160,128},{192,160},{224,192},{33,... | collective-permute-start | bytes 98312 | tf_op jit(solution)/shard_map/ppermute | solution.py:23
  39.4 25.1 %collective-permute-start.8 = (f32[16,8,128]{2,1,0:T(8,128)}, f32[16,8,128]{2,1,0:T(8,128)S(1)}, u32[]{:S(2)}, u32[]{:S(2)}) collective-permute-start(f32[16,8,128]{2,1,0:T(8,128)} %get-tuple-element.45), channel_id=1, source_target_pairs={{0,4},{4,8},{8,12},{12,16},{16,20},{20,24},{24,28},{1,5},{5,9},{9,... | collective-permute-start | bytes 196616 | tf_op jit(solution)/shard_map/ppermute | solution.py:18
  42.5 22.0 %collective-permute-start.9 = (f32[16,8,128]{2,1,0:T(8,128)}, f32[16,8,128]{2,1,0:T(8,128)S(1)}, u32[]{:S(2)}, u32[]{:S(2)}) collective-permute-start(f32[16,8,128]{2,1,0:T(8,128)} %get-tuple-element.46), channel_id=1, source_target_pairs={{4,0},{8,4},{12,8},{16,12},{20,16},{24,20},{28,24},{5,1},{9,5},{13... | collective-permute-start | bytes 196616 | tf_op jit(solution)/shard_map/ppermute | solution.py:23
  43.8 20.6 %collective-permute-start.6 = (f32[2,16,128]{2,1,0:T(8,128)}, f32[2,16,128]{2,1,0:T(8,128)S(1)}, u32[]{:S(2)}, u32[]{:S(2)}) collective-permute-start(f32[2,16,128]{2,1,0:T(8,128)} %get-tuple-element.43), channel_id=1, source_target_pairs={{0,32},{32,64},{64,96},{96,128},{128,160},{160,192},{192,224},{1,3... | collective-permute-start | bytes 49160 | tf_op jit(solution)/shard_map/ppermute | solution.py:18
  46.5 18.0 %collective-permute-start.7 = (f32[2,16,128]{2,1,0:T(8,128)}, f32[2,16,128]{2,1,0:T(8,128)S(1)}, u32[]{:S(2)}, u32[]{:S(2)}) collective-permute-start(f32[2,16,128]{2,1,0:T(8,128)} %get-tuple-element.44), channel_id=1, source_target_pairs={{32,0},{64,32},{96,64},{128,96},{160,128},{192,160},{224,192},{33,... | collective-permute-start | bytes 49160 | tf_op jit(solution)/shard_map/ppermute | solution.py:23
  68.6 18.1 %collective-permute-start.16 = (f32[16,16,4]{2,1,0:T(8,128)}, f32[16,16,4]{2,1,0:T(8,128)S(1)}, u32[]{:S(2)}, u32[]{:S(2)}) collective-permute-start(f32[16,16,4]{2,1,0:T(8,128)} %get-tuple-element.60), channel_id=1, source_target_pairs={{0,1},{1,2},{2,3},{4,5},{5,6},{6,7},{8,9},{9,10},{10,11},{12,13},{... | collective-permute-start | bytes 12296 | tf_op jit(solution)/shard_map/ppermute | solution.py:18
  72.8 17.6 %collective-permute-start.17 = (f32[16,16,4]{2,1,0:T(8,128)}, f32[16,16,4]{2,1,0:T(8,128)S(1)}, u32[]{:S(2)}, u32[]{:S(2)}) collective-permute-start(f32[16,16,4]{2,1,0:T(8,128)} %get-tuple-element.61), channel_id=1, source_target_pairs={{1,0},{2,1},{3,2},{5,4},{6,5},{7,6},{9,8},{10,9},{11,10},{13,12},{... | collective-permute-start | bytes 12296 | tf_op jit(solution)/shard_map/ppermute | solution.py:23
  74.1 24.4 %collective-permute-start.14 = (f32[16,8,128]{2,1,0:T(8,128)}, f32[16,8,128]{2,1,0:T(8,128)S(1)}, u32[]{:S(2)}, u32[]{:S(2)}) collective-permute-start(f32[16,8,128]{2,1,0:T(8,128)} %get-tuple-element.58), channel_id=1, source_target_pairs={{0,4},{4,8},{8,12},{12,16},{16,20},{20,24},{24,28},{1,5},{5,9},{9,... | collective-permute-start | bytes 196616 | tf_op jit(solution)/shard_map/ppermute | solution.py:18
  76.7 21.9 %collective-permute-start.15 = (f32[16,8,128]{2,1,0:T(8,128)}, f32[16,8,128]{2,1,0:T(8,128)S(1)}, u32[]{:S(2)}, u32[]{:S(2)}) collective-permute-start(f32[16,8,128]{2,1,0:T(8,128)} %get-tuple-element.59), channel_id=1, source_target_pairs={{4,0},{8,4},{12,8},{16,12},{20,16},{24,20},{28,24},{5,1},{9,5},{13... | collective-permute-start | bytes 196616 | tf_op jit(solution)/shard_map/ppermute | solution.py:23
  78.0 12.4 %collective-permute-start.12 = (f32[2,16,128]{2,1,0:T(8,128)}, f32[2,16,128]{2,1,0:T(8,128)S(1)}, u32[]{:S(2)}, u32[]{:S(2)}) collective-permute-start(f32[2,16,128]{2,1,0:T(8,128)} %get-tuple-element.56), channel_id=1, source_target_pairs={{0,32},{32,64},{64,96},{96,128},{128,160},{160,192},{192,224},{1,3... | collective-permute-start | bytes 49160 | tf_op jit(solution)/shard_map/ppermute | solution.py:18
  86.7 11.9 %collective-permute-start.13 = (f32[2,16,128]{2,1,0:T(8,128)}, f32[2,16,128]{2,1,0:T(8,128)S(1)}, u32[]{:S(2)}, u32[]{:S(2)}) collective-permute-start(f32[2,16,128]{2,1,0:T(8,128)} %get-tuple-element.57), channel_id=1, source_target_pairs={{32,0},{64,32},{96,64},{128,96},{160,128},{192,160},{224,192},{33,... | collective-permute-start | bytes 49160 | tf_op jit(solution)/shard_map/ppermute | solution.py:23
  102.6 12.1 %collective-permute-start.22 = (f32[16,16,4]{2,1,0:T(8,128)}, f32[16,16,4]{2,1,0:T(8,128)S(1)}, u32[]{:S(2)}, u32[]{:S(2)}) collective-permute-start(f32[16,16,4]{2,1,0:T(8,128)} %get-tuple-element.71), channel_id=1, source_target_pairs={{0,1},{1,2},{2,3},{4,5},{5,6},{6,7},{8,9},{9,10},{10,11},{12,13},{... | collective-permute-start | bytes 12296 | tf_op jit(solution)/shard_map/ppermute | solution.py:18
  107.0 7.7 %collective-permute-start.23 = (f32[16,16,4]{2,1,0:T(8,128)}, f32[16,16,4]{2,1,0:T(8,128)S(1)}, u32[]{:S(2)}, u32[]{:S(2)}) collective-permute-start(f32[16,16,4]{2,1,0:T(8,128)} %get-tuple-element.72), channel_id=1, source_target_pairs={{1,0},{2,1},{3,2},{5,4},{6,5},{7,6},{9,8},{10,9},{11,10},{13,12},{... | collective-permute-start | bytes 12296 | tf_op jit(solution)/shard_map/ppermute | solution.py:23
  108.3 40.3 %collective-permute-start.20 = (f32[16,8,128]{2,1,0:T(8,128)}, f32[16,8,128]{2,1,0:T(8,128)S(1)}, u32[]{:S(2)}, u32[]{:S(2)}) collective-permute-start(f32[16,8,128]{2,1,0:T(8,128)} %get-tuple-element.69), channel_id=1, source_target_pairs={{0,4},{4,8},{8,12},{12,16},{16,20},{20,24},{24,28},{1,5},{5,9},{9,... | collective-permute-start | bytes 196616 | tf_op jit(solution)/shard_map/ppermute | solution.py:18
  113.4 35.2 %collective-permute-start.21 = (f32[16,8,128]{2,1,0:T(8,128)}, f32[16,8,128]{2,1,0:T(8,128)S(1)}, u32[]{:S(2)}, u32[]{:S(2)}) collective-permute-start(f32[16,8,128]{2,1,0:T(8,128)} %get-tuple-element.70), channel_id=1, source_target_pairs={{4,0},{8,4},{12,8},{16,12},{20,16},{24,20},{28,24},{5,1},{9,5},{13... | collective-permute-start | bytes 196616 | tf_op jit(solution)/shard_map/ppermute | solution.py:23
  117.8 22.3 %all-to-all-start = ((f32[64,1,128]{2,1,0:T(1,128)}), f32[64,1,128]{2,1,0:T(1,128)S(1)}, u32[]{:S(2)}, u32[]{:S(2)}) async-start(f32[64,1,128]{2,1,0:T(1,128)} %bitcast.9), calls=%async_computation | async-start | bytes 65536 | tf_op jit(solution)/shard_map/all_to_all | solution.py:33
  129.6 11.8 %collective-permute-start.18 = (f32[2,16,128]{2,1,0:T(8,128)S(1)}, f32[2,16,128]{2,1,0:T(8,128)S(1)}, u32[]{:S(2)}, u32[]{:S(2)}) collective-permute-start(f32[2,16,128]{2,1,0:T(8,128)S(1)} %copy-done.32), channel_id=1, source_target_pairs={{0,32},{32,64},{64,96},{96,128},{128,160},{160,192},{192,224},{1,3... | collective-permute-start | bytes 49160 | tf_op jit(solution)/shard_map/ppermute | solution.py:18
  137.0 11.6 %collective-permute-start.19 = (f32[2,16,128]{2,1,0:T(8,128)S(1)}, f32[2,16,128]{2,1,0:T(8,128)S(1)}, u32[]{:S(2)}, u32[]{:S(2)}) collective-permute-start(f32[2,16,128]{2,1,0:T(8,128)S(1)} %copy-done.31), channel_id=1, source_target_pairs={{32,0},{64,32},{96,64},{128,96},{160,128},{192,160},{224,192},{33,... | collective-permute-start | bytes 49160 | tf_op jit(solution)/shard_map/ppermute | solution.py:23
  140.1 12.6 %collective-permute-start.24 = (f32[128]{0:T(128)S(1)}, f32[128]{0:T(128)S(1)}, u32[]{:S(2)}, u32[]{:S(2)}) collective-permute-start(f32[128]{0:T(128)S(1)} %reduce_sum.9), channel_id=1, source_target_pairs={{1,0},{2,3},{5,4},{6,7},{9,8},{10,11},{13,12},{14,15},{17,16},{18,... | collective-permute-start | bytes 1544 | tf_op jit(solution)/shard_map/ppermute | solution.py:354
  (36 other events, 209.2 us)

commit v12 on v11

--- a/solution.py
+++ b/solution.py
@@ -140,7 +140,7 @@
 
     p_first = pick(pres, -1, 0)
     p_last = pick(pres, -1, Z - 1)
-    sea = 0.5 * (f_ocean * (p_last + zh1) + f_crust * (zl1 + p_first))
+    sea = 0.5 * (f_ocean * p_last + f_crust * p_first)
     sfo_ref[...] = sea if first else sf_ref[...] + sea
 
     above_x = jnp.concatenate([pres[1:], pxh1], axis=0)
@@ -187,6 +187,9 @@
     new_p = pres - time_step * bulk_ref[...] * spread
     new_p = jnp.where(zi == 0, new_p + jnp.broadcast_to(src_ref[...], full), new_p)
     po_ref[...] = new_p
+    sfo_ref[...] = sfo_ref[...] + 0.5 * (
+        scal_ref[base + 8] * pick(new_p, -1, Z - 1) + scal_ref[base + 9] * pick(new_p, -1, 0)
+    )
 
     sxu_ref[...] = new_p[X - 2 :]
     sxd_ref[...] = new_p[0:2]
@@ -280,7 +283,7 @@
     ocean = depth_index == first_crust // Z - 1
     crust = depth_index == first_crust // Z
     before = step_at < ITERS - 1
-    after = step_at < 0
+    after = step_at == ITERS - 2
     flag_value = jnp.where(
         entry == 6, before & ocean,
         jnp.where(entry == 7, before & crust,
@@ -331,14 +334,6 @@
                 shifted_up(sends[4], "gz"),
                 shifted_down(sends[5], "gz"),
             )
-        if instant == ITERS - 1:
-            ocean = (depth_index == first_crust // Z - 1).astype(jnp.float32)
-            crust = (depth_index == first_crust // Z).astype(jnp.float32)
-            sf_last = sf + 0.5 * (
-                ocean * (sends[4][:, :, 1:2] + halos[5][:, :, 0:1])
-                + crust * (halos[4][:, :, 1:2] + sends[5][:, :, 0:1])
-            )
-            owner_sums = seafloor_sums(sf_last[:, :, 0], node_weight, node_patch, patch_slot)
         if instant == 0:
             operands = common + (pres, vel, inv_density, bulk, src_all) + halos
         else:
@@ -349,13 +344,16 @@
         sends = outs[5:11]
         if instant == 0:
             media_halo = outs[11:13]
+        if instant == ITERS - 2:
+            owner_sums = seafloor_sums(sf[:, :, 0], node_weight, node_patch, patch_slot)
     ocean_plane = first_crust // Z - 1
     crust_plane = first_crust // Z
-    spread_out = lax.ppermute(
-        owner_sums, "gz", [(ocean_plane, ocean_plane - 1), (crust_plane, crust_plane + 1)]
-    )
+    below, above = ocean_plane - 1, crust_plane + 1
+    near = lax.ppermute(owner_sums, "gz", [(ocean_plane, below), (crust_plane, above)])
+    far = lax.ppermute(owner_sums, "gz", [(crust_plane, below), (ocean_plane, above)])
+    across = lax.ppermute(owner_sums, "gz", [(ocean_plane, crust_plane), (crust_plane, ocean_plane)])
     inner = (depth_index == ocean_plane) | (depth_index == crust_plane)
-    owner_sums = jnp.where(inner, owner_sums, spread_out)
+    owner_sums = jnp.where(inner, owner_sums + across, near + far)
     piece = owner_sums.shape[0] // tiles_z
     slip_grad = lax.dynamic_slice_in_dim(owner_sums, depth_index * piece, piece)
     return (pres, vel, slip_grad)

time: 155 us -> 158 us (1.019)
  the two profiles are of different devices: /device:TPU:24 before, /device:TPU:90 now
where the time goes in v12:
time: 158 us; the launch traced here: 156 us
  starting transfers between devices  85.2 us (54%)
  waiting for transfers between devices  39.5 us (25%)
  Pallas kernels  13.8 us (9%)
  local copies, waits for them, and re-layouts  12.7 us (8%)
  other arithmetic  2.56 us (2%)
  between operations  1.58 us (1%)
    ppermute x12, starting transfers between devices, shifted_down(): return lax.ppermute(x, axis, [(i + 1, i) for i in range(count - 1)])  37.1 us
    ppermute x12, starting transfers between devices, shifted_up(): return lax.ppermute(x, axis, [(i, i + 1) for i in range(count - 1)])  34.9 us
    ppermute x12, waiting for transfers between devices, shifted_down(): return lax.ppermute(x, axis, [(i + 1, i) for i in range(count - 1)])  32.9 us
    pallas_call x4, Pallas kernels, run_step(): pl.pallas_call(functools.partial(step_kernel, instant, first), out_shape=...  13.8 us
    all_to_all x1, starting transfers between devices, summed_on_arrival(): parts = lax.all_to_all(in_blocks(x, dim, size), axis, 0, 0, tiled=True)  7.59 us
    unnamed x89, local copies, waits for them, and re-layouts  6.83 us
    all_to_all x1, waiting for transfers between devices, summed_on_arrival(): parts = lax.all_to_all(in_blocks(x, dim, size), axis, 0, 0, tiled=True)  6.56 us
  transfers between devices with their start and end apart: 28, of which 5 were waited for; matrix products, arithmetic and copies ran while one was open for 4% of the time, Pallas kernels for 0%

profile of v12, /device:TPU:90, one launch (start us, length us, event | category | flops | bytes accessed | tf_op | source)
XLA Modules:
  0.0 156.4 jit_solution(9271604994822209957)
XLA Ops:
  4.0 3.8 %collective-permute-start.4 = (f32[16,16,4]{2,1,0:T(8,128)S(1)}, f32[16,16,4]{2,1,0:T(8,128)S(1)}, u32[]{:S(2)}, u32[]{:S(2)}) collective-permute-start(f32[16,16,4]{2,1,0:T(8,128)S(1)} %copy.20), channel_id=1, source_target_pairs={{0,1},{1,2},{2,3},{4,5},{5,6},{6,7},{8,9},{9,10},{10,11},{12,13},{... | collective-permute-start | bytes 12296 | tf_op jit(solution)/shard_map/ppermute | solution.py:18
  12.4 3.6 %collective-permute-start.3 = (f32[16,10,128]{2,1,0:T(8,128)S(1)}, f32[16,10,128]{2,1,0:T(8,128)S(1)}, u32[]{:S(2)}, u32[]{:S(2)}) collective-permute-start(f32[16,10,128]{2,1,0:T(8,128)S(1)} %pad_maximum_fusion.1), channel_id=1, source_target_pairs={{4,0},{8,4},{12,8},{16,12},{20,16},{24,20},{28,24},{5,1},{9,5},{13... | collective-permute-start | bytes 245768 | tf_op jit(solution)/shard_map/ppermute | solution.py:23
  16.8 7.0 %collective-permute-start = (f32[4,16,128]{2,1,0:T(8,128)S(1)}, f32[4,16,128]{2,1,0:T(8,128)S(1)}, u32[]{:S(2)}, u32[]{:S(2)}) collective-permute-start(f32[4,16,128]{2,1,0:T(8,128)S(1)} %pad_maximum_fusion.2), channel_id=1, source_target_pairs={{0,32},{32,64},{64,96},{96,128},{128,160},{160,192},{192,224},{1,3... | collective-permute-start | bytes 98312 | tf_op jit(solution)/shard_map/ppermute | solution.py:18
  29.2 8.2 %collective-permute-done.1.refs_8_ = f32[4,16,128]{2,1,0:T(8,128)S(1)} collective-permute-done((f32[4,16,128]{2,1,0:T(8,128)S(1)}, f32[4,16,128]{2,1,0:T(8,128)S(1)}, u32[]{:S(2)}, u32[]{:S(2)}) %collective-permute-start.1) | collective-permute-done | bytes 32800 | tf_op jit(solution)/shard_map/ppermute | solution.py:23
  38.7 3.4 %shard_map.121 = (f32[16,16,128]{2,1,0:T(8,128)}, f32[3,16,16,128]{3,2,1,0:T(8,128)}, f32[16,16,1]{2,1,0:T(8,128)}, f32[2,16,128]{2,1,0:T(8,128)}, f32[16,2,128]...) custom-call(f32[64]{0:T(128)} %compare_select_fusion.5.refs_0_, ...), custom_call_target="tpu_custom_call" | custom-call | flops 2621440 | bytes 1572864 | tf_op jit(solution)/shard_map/pallas_call | solution.py:229
  42.2 2.8 %collective-permute-start.10 = (f32[16,16,4]{2,1,0:T(8,128)}, f32[16,16,4]{2,1,0:T(8,128)S(1)}, u32[]{:S(2)}, u32[]{:S(2)}) collective-permute-start(f32[16,16,4]{2,1,0:T(8,128)} %get-tuple-element.47), channel_id=1, source_target_pairs={{0,1},{1,2},{2,3},{4,5},{5,6},{6,7},{8,9},{9,10},{10,11},{12,13},{... | collective-permute-start | bytes 12296 | tf_op jit(solution)/shard_map/ppermute | solution.py:18
  45.0 3.0 %collective-permute-start.11 = (f32[16,16,4]{2,1,0:T(8,128)}, f32[16,16,4]{2,1,0:T(8,128)S(1)}, u32[]{:S(2)}, u32[]{:S(2)}) collective-permute-start(f32[16,16,4]{2,1,0:T(8,128)} %get-tuple-element.48), channel_id=1, source_target_pairs={{1,0},{2,1},{3,2},{5,4},{6,5},{7,6},{9,8},{10,9},{11,10},{13,12},{... | collective-permute-start | bytes 12296 | tf_op jit(solution)/shard_map/ppermute | solution.py:23
  50.0 3.6 %collective-permute-start.9 = (f32[16,8,128]{2,1,0:T(8,128)}, f32[16,8,128]{2,1,0:T(8,128)S(1)}, u32[]{:S(2)}, u32[]{:S(2)}) collective-permute-start(f32[16,8,128]{2,1,0:T(8,128)} %get-tuple-element.46), channel_id=1, source_target_pairs={{4,0},{8,4},{12,8},{16,12},{20,16},{24,20},{28,24},{5,1},{9,5},{13... | collective-permute-start | bytes 196616 | tf_op jit(solution)/shard_map/ppermute | solution.py:23
  55.6 3.9 %collective-permute-start.7 = (f32[2,16,128]{2,1,0:T(8,128)}, f32[2,16,128]{2,1,0:T(8,128)S(1)}, u32[]{:S(2)}, u32[]{:S(2)}) collective-permute-start(f32[2,16,128]{2,1,0:T(8,128)} %get-tuple-element.44), channel_id=1, source_target_pairs={{32,0},{64,32},{96,64},{128,96},{160,128},{192,160},{224,192},{33,... | collective-permute-start | bytes 49160 | tf_op jit(solution)/shard_map/ppermute | solution.py:23
  59.6 7.9 %collective-permute-done.7.refs_9_ = f32[2,16,128]{2,1,0:T(8,128)S(1)} collective-permute-done((f32[2,16,128]{2,1,0:T(8,128)}, f32[2,16,128]{2,1,0:T(8,128)S(1)}, u32[]{:S(2)}, u32[]{:S(2)}) %collective-permute-start.7) | collective-permute-done | bytes 16416 | tf_op jit(solution)/shard_map/ppermute | solution.py:23
  68.1 3.5 %shard_map.122 = (f32[16,16,128]{2,1,0:T(8,128)}, f32[3,16,16,128]{3,2,1,0:T(8,128)}, f32[16,16,1]{2,1,0:T(8,128)}, f32[2,16,128]{2,1,0:T(8,128)}, f32[16,2,128]...) custom-call(f32[64]{0:T(128)} %compare_select_fusion.5.refs_0_, ...), custom_call_target="tpu_custom_call" | custom-call | flops 2621440 | bytes 1572864 | tf_op jit(solution)/shard_map/pallas_call | solution.py:229
  76.2 3.0 %collective-permute-start.17 = (f32[16,16,4]{2,1,0:T(8,128)S(1)}, f32[16,16,4]{2,1,0:T(8,128)S(1)}, u32[]{:S(2)}, u32[]{:S(2)}) collective-permute-start(f32[16,16,4]{2,1,0:T(8,128)S(1)} %copy-done.33), channel_id=1, source_target_pairs={{1,0},{2,1},{3,2},{5,4},{6,5},{7,6},{9,8},{10,9},{11,10},{13,12},{... | collective-permute-start | bytes 12296 | tf_op jit(solution)/shard_map/ppermute | solution.py:23
  81.2 3.6 %collective-permute-start.15 = (f32[16,8,128]{2,1,0:T(8,128)S(1)}, f32[16,8,128]{2,1,0:T(8,128)S(1)}, u32[]{:S(2)}, u32[]{:S(2)}) collective-permute-start(f32[16,8,128]{2,1,0:T(8,128)S(1)} %copy-done.35), channel_id=1, source_target_pairs={{4,0},{8,4},{12,8},{16,12},{20,16},{24,20},{28,24},{5,1},{9,5},{13... | collective-permute-start | bytes 196616 | tf_op jit(solution)/shard_map/ppermute | solution.py:23
  86.8 3.9 %collective-permute-start.13 = (f32[2,16,128]{2,1,0:T(8,128)S(1)}, f32[2,16,128]{2,1,0:T(8,128)S(1)}, u32[]{:S(2)}, u32[]{:S(2)}) collective-permute-start(f32[2,16,128]{2,1,0:T(8,128)S(1)} %copy-done.39), channel_id=1, source_target_pairs={{32,0},{64,32},{96,64},{128,96},{160,128},{192,160},{224,192},{33,... | collective-permute-start | bytes 49160 | tf_op jit(solution)/shard_map/ppermute | solution.py:23
  90.8 7.7 %collective-permute-done.13.refs_9_ = f32[2,16,128]{2,1,0:T(8,128)S(1)} collective-permute-done((f32[2,16,128]{2,1,0:T(8,128)S(1)}, f32[2,16,128]{2,1,0:T(8,128)S(1)}, u32[]{:S(2)}, u32[]{:S(2)}) %collective-permute-start.13) | collective-permute-done | bytes 16416 | tf_op jit(solution)/shard_map/ppermute | solution.py:23
  99.1 3.4 %shard_map.123 = (f32[16,16,128]{2,1,0:T(8,128)}, f32[3,16,16,128]{3,2,1,0:T(8,128)}, f32[16,16,1]{2,1,0:T(8,128)}, f32[2,16,128]{2,1,0:T(8,128)}, f32[16,2,128]...) custom-call(f32[64]{0:T(128)} %compare_select_fusion.5.refs_0_, ...), custom_call_target="tpu_custom_call" | custom-call | flops 2621440 | bytes 1572864 | tf_op jit(solution)/shard_map/pallas_call | solution.py:229
  105.3 7.6 %all-to-all-start = ((f32[64,1,128]{2,1,0:T(1,128)}), f32[64,1,128]{2,1,0:T(1,128)S(1)}, u32[]{:S(2)}, u32[]{:S(2)}) async-start(f32[64,1,128]{2,1,0:T(1,128)} %bitcast.9), calls=%async_computation | async-start | bytes 65536 | tf_op jit(solution)/shard_map/all_to_all | solution.py:33
  112.9 2.9 %collective-permute-start.22 = (f32[16,16,4]{2,1,0:T(8,128)S(1)}, f32[16,16,4]{2,1,0:T(8,128)S(1)}, u32[]{:S(2)}, u32[]{:S(2)}) collective-permute-start(f32[16,16,4]{2,1,0:T(8,128)S(1)} %copy-done.32), channel_id=1, source_target_pairs={{0,1},{1,2},{2,3},{4,5},{5,6},{6,7},{8,9},{9,10},{10,11},{12,13},{... | collective-permute-start | bytes 12296 | tf_op jit(solution)/shard_map/ppermute | solution.py:18
  115.8 6.6 %all-to-all-done = f32[64,1,128]{2,1,0:T(1,128)S(1)} async-done(((f32[64,1,128]{2,1,0:T(1,128)}), f32[64,1,128]{2,1,0:T(1,128)S(1)}, u32[]{:S(2)}, u32[]{:S(2)}) %all-to-all-start) | async-done | bytes 32800 | tf_op jit(solution)/shard_map/all_to_all | solution.py:33
  122.5 3.0 %collective-permute-start.24 = (f32[128]{0:T(128)S(1)}, f32[128]{0:T(128)S(1)}, u32[]{:S(2)}, u32[]{:S(2)}) collective-permute-start(f32[128]{0:T(128)S(1)} %reduce_sum.9), channel_id=1, source_target_pairs={{1,2},{2,1},{5,6},{6,5},{9,10},{10,9},{13,14},{14,13},{17,18},{18,... | collective-permute-start | bytes 1544 | tf_op jit(solution)/shard_map/ppermute | solution.py:354
  132.9 3.6 %collective-permute-start.21 = (f32[16,8,128]{2,1,0:T(8,128)S(1)}, f32[16,8,128]{2,1,0:T(8,128)S(1)}, u32[]{:S(2)}, u32[]{:S(2)}) collective-permute-start(f32[16,8,128]{2,1,0:T(8,128)S(1)} %copy-done.34), channel_id=1, source_target_pairs={{4,0},{8,4},{12,8},{16,12},{20,16},{24,20},{28,24},{5,1},{9,5},{13... | collective-permute-start | bytes 196616 | tf_op jit(solution)/shard_map/ppermute | solution.py:23
  136.6 4.0 %collective-permute-start.18 = (f32[2,16,128]{2,1,0:T(8,128)S(1)}, f32[2,16,128]{2,1,0:T(8,128)S(1)}, u32[]{:S(2)}, u32[]{:S(2)}) collective-permute-start(f32[2,16,128]{2,1,0:T(8,128)S(1)} %copy-done.38), channel_id=1, source_target_pairs={{0,32},{32,64},{64,96},{96,128},{128,160},{160,192},{192,224},{1,3... | collective-permute-start | bytes 49160 | tf_op jit(solution)/shard_map/ppermute | solution.py:18
  143.2 9.1 %collective-permute-done.19.refs_9_ = f32[2,16,128]{2,1,0:T(8,128)S(1)} collective-permute-done((f32[2,16,128]{2,1,0:T(8,128)S(1)}, f32[2,16,128]{2,1,0:T(8,128)S(1)}, u32[]{:S(2)}, u32[]{:S(2)}) %collective-permute-start.19) | collective-permute-done | bytes 16416 | tf_op jit(solution)/shard_map/ppermute | solution.py:23
  152.9 3.5 %shard_map.124 = (f32[16,16,128]{2,1,0:T(8,128)}, f32[3,16,16,128]{3,2,1,0:T(8,128)}, f32[16,16,1]{2,1,0:T(8,128)}, f32[2,16,128]{2,1,0:T(8,128)}, f32[16,2,128]...) custom-call(f32[64]{0:T(128)} %compare_select_fusion.5.refs_0_, ...), custom_call_target="tpu_custom_call" | custom-call | flops 2621440 | bytes 1572864 | tf_op jit(solution)/shard_map/pallas_call | solution.py:229
  (163 shorter events, 41.9 us)
Async XLA Ops:
  4.0 21.5 %collective-permute-start.4 = (f32[16,16,4]{2,1,0:T(8,128)S(1)}, f32[16,16,4]{2,1,0:T(8,128)S(1)}, u32[]{:S(2)}, u32[]{:S(2)}) collective-permute-start(f32[16,16,4]{2,1,0:T(8,128)S(1)} %copy.20), channel_id=1, source_target_pairs={{0,1},{1,2},{2,3},{4,5},{5,6},{6,7},{8,9},{9,10},{10,11},{12,13},{... | collective-permute-start | bytes 12296 | tf_op jit(solution)/shard_map/ppermute | solution.py:18
  8.3 20.8 %collective-permute-start.5 = (f32[16,16,4]{2,1,0:T(8,128)S(1)}, f32[16,16,4]{2,1,0:T(8,128)S(1)}, u32[]{:S(2)}, u32[]{:S(2)}) collective-permute-start(f32[16,16,4]{2,1,0:T(8,128)S(1)} %copy.23), channel_id=1, source_target_pairs={{1,0},{2,1},{3,2},{5,4},{6,5},{7,6},{9,8},{10,9},{11,10},{13,12},{... | collective-permute-start | bytes 12296 | tf_op jit(solution)/shard_map/ppermute | solution.py:23
  10.5 27.0 %collective-permute-start.2 = (f32[16,10,128]{2,1,0:T(8,128)S(1)}, f32[16,10,128]{2,1,0:T(8,128)S(1)}, u32[]{:S(2)}, u32[]{:S(2)}) collective-permute-start(f32[16,10,128]{2,1,0:T(8,128)S(1)} %pad_maximum_fusion), channel_id=1, source_target_pairs={{0,4},{4,8},{8,12},{12,16},{16,20},{20,24},{24,28},{1,5},{5,9},{9,... | collective-permute-start | bytes 245768 | tf_op jit(solution)/shard_map/ppermute | solution.py:18
  12.4 25.0 %collective-permute-start.3 = (f32[16,10,128]{2,1,0:T(8,128)S(1)}, f32[16,10,128]{2,1,0:T(8,128)S(1)}, u32[]{:S(2)}, u32[]{:S(2)}) collective-permute-start(f32[16,10,128]{2,1,0:T(8,128)S(1)} %pad_maximum_fusion.1), channel_id=1, source_target_pairs={{4,0},{8,4},{12,8},{16,12},{20,16},{24,20},{28,24},{5,1},{9,5},{13... | collective-permute-start | bytes 245768 | tf_op jit(solution)/shard_map/ppermute | solution.py:23
  16.8 12.4 %collective-permute-start = (f32[4,16,128]{2,1,0:T(8,128)S(1)}, f32[4,16,128]{2,1,0:T(8,128)S(1)}, u32[]{:S(2)}, u32[]{:S(2)}) collective-permute-start(f32[4,16,128]{2,1,0:T(8,128)S(1)} %pad_maximum_fusion.2), channel_id=1, source_target_pairs={{0,32},{32,64},{64,96},{96,128},{128,160},{160,192},{192,224},{1,3... | collective-permute-start | bytes 98312 | tf_op jit(solution)/shard_map/ppermute | solution.py:18
  25.5 11.9 %collective-permute-start.1 = (f32[4,16,128]{2,1,0:T(8,128)S(1)}, f32[4,16,128]{2,1,0:T(8,128)S(1)}, u32[]{:S(2)}, u32[]{:S(2)}) collective-permute-start(f32[4,16,128]{2,1,0:T(8,128)S(1)} %pad_maximum_fusion.3), channel_id=1, source_target_pairs={{32,0},{64,32},{96,64},{128,96},{160,128},{192,160},{224,192},{33,... | collective-permute-start | bytes 98312 | tf_op jit(solution)/shard_map/ppermute | solution.py:23
  42.2 13.4 %collective-permute-start.10 = (f32[16,16,4]{2,1,0:T(8,128)}, f32[16,16,4]{2,1,0:T(8,128)S(1)}, u32[]{:S(2)}, u32[]{:S(2)}) collective-permute-start(f32[16,16,4]{2,1,0:T(8,128)} %get-tuple-element.47), channel_id=1, source_target_pairs={{0,1},{1,2},{2,3},{4,5},{5,6},{6,7},{8,9},{9,10},{10,11},{12,13},{... | collective-permute-start | bytes 12296 | tf_op jit(solution)/shard_map/ppermute | solution.py:18
  45.0 14.5 %collective-permute-start.11 = (f32[16,16,4]{2,1,0:T(8,128)}, f32[16,16,4]{2,1,0:T(8,128)S(1)}, u32[]{:S(2)}, u32[]{:S(2)}) collective-permute-start(f32[16,16,4]{2,1,0:T(8,128)} %get-tuple-element.48), channel_id=1, source_target_pairs={{1,0},{2,1},{3,2},{5,4},{6,5},{7,6},{9,8},{10,9},{11,10},{13,12},{... | collective-permute-start | bytes 12296 | tf_op jit(solution)/shard_map/ppermute | solution.py:23
  48.0 19.4 %collective-permute-start.8 = (f32[16,8,128]{2,1,0:T(8,128)}, f32[16,8,128]{2,1,0:T(8,128)S(1)}, u32[]{:S(2)}, u32[]{:S(2)}) collective-permute-start(f32[16,8,128]{2,1,0:T(8,128)} %get-tuple-element.45), channel_id=1, source_target_pairs={{0,4},{4,8},{8,12},{12,16},{16,20},{20,24},{24,28},{1,5},{5,9},{9,... | collective-permute-start | bytes 196616 | tf_op jit(solution)/shard_map/ppermute | solution.py:18
  50.0 17.5 %collective-permute-start.9 = (f32[16,8,128]{2,1,0:T(8,128)}, f32[16,8,128]{2,1,0:T(8,128)S(1)}, u32[]{:S(2)}, u32[]{:S(2)}) collective-permute-start(f32[16,8,128]{2,1,0:T(8,128)} %get-tuple-element.46), channel_id=1, source_target_pairs={{4,0},{8,4},{12,8},{16,12},{20,16},{24,20},{28,24},{5,1},{9,5},{13... | collective-permute-start | bytes 196616 | tf_op jit(solution)/shard_map/ppermute | solution.py:23
  55.6 11.9 %collective-permute-start.7 = (f32[2,16,128]{2,1,0:T(8,128)}, f32[2,16,128]{2,1,0:T(8,128)S(1)}, u32[]{:S(2)}, u32[]{:S(2)}) collective-permute-start(f32[2,16,128]{2,1,0:T(8,128)} %get-tuple-element.44), channel_id=1, source_target_pairs={{32,0},{64,32},{96,64},{128,96},{160,128},{192,160},{224,192},{33,... | collective-permute-start | bytes 49160 | tf_op jit(solution)/shard_map/ppermute | solution.py:23
  71.6 15.2 %collective-permute-start.16 = (f32[16,16,4]{2,1,0:T(8,128)}, f32[16,16,4]{2,1,0:T(8,128)S(1)}, u32[]{:S(2)}, u32[]{:S(2)}) collective-permute-start(f32[16,16,4]{2,1,0:T(8,128)} %get-tuple-element.60), channel_id=1, source_target_pairs={{0,1},{1,2},{2,3},{4,5},{5,6},{6,7},{8,9},{9,10},{10,11},{12,13},{... | collective-permute-start | bytes 12296 | tf_op jit(solution)/shard_map/ppermute | solution.py:18
  76.2 14.5 %collective-permute-start.17 = (f32[16,16,4]{2,1,0:T(8,128)S(1)}, f32[16,16,4]{2,1,0:T(8,128)S(1)}, u32[]{:S(2)}, u32[]{:S(2)}) collective-permute-start(f32[16,16,4]{2,1,0:T(8,128)S(1)} %copy-done.33), channel_id=1, source_target_pairs={{1,0},{2,1},{3,2},{5,4},{6,5},{7,6},{9,8},{10,9},{11,10},{13,12},{... | collective-permute-start | bytes 12296 | tf_op jit(solution)/shard_map/ppermute | solution.py:23
  79.2 19.2 %collective-permute-start.14 = (f32[16,8,128]{2,1,0:T(8,128)S(1)}, f32[16,8,128]{2,1,0:T(8,128)S(1)}, u32[]{:S(2)}, u32[]{:S(2)}) collective-permute-start(f32[16,8,128]{2,1,0:T(8,128)S(1)} %copy-done.36), channel_id=1, source_target_pairs={{0,4},{4,8},{8,12},{12,16},{16,20},{20,24},{24,28},{1,5},{5,9},{9,... | collective-permute-start | bytes 196616 | tf_op jit(solution)/shard_map/ppermute | solution.py:18
  81.2 17.3 %collective-permute-start.15 = (f32[16,8,128]{2,1,0:T(8,128)S(1)}, f32[16,8,128]{2,1,0:T(8,128)S(1)}, u32[]{:S(2)}, u32[]{:S(2)}) collective-permute-start(f32[16,8,128]{2,1,0:T(8,128)S(1)} %copy-done.35), channel_id=1, source_target_pairs={{4,0},{8,4},{12,8},{16,12},{20,16},{24,20},{28,24},{5,1},{9,5},{13... | collective-permute-start | bytes 196616 | tf_op jit(solution)/shard_map/ppermute | solution.py:23
  86.8 11.6 %collective-permute-start.13 = (f32[2,16,128]{2,1,0:T(8,128)S(1)}, f32[2,16,128]{2,1,0:T(8,128)S(1)}, u32[]{:S(2)}, u32[]{:S(2)}) collective-permute-start(f32[2,16,128]{2,1,0:T(8,128)S(1)} %copy-done.39), channel_id=1, source_target_pairs={{32,0},{64,32},{96,64},{128,96},{160,128},{192,160},{224,192},{33,... | collective-permute-start | bytes 49160 | tf_op jit(solution)/shard_map/ppermute | solution.py:23
  105.3 17.1 %all-to-all-start = ((f32[64,1,128]{2,1,0:T(1,128)}), f32[64,1,128]{2,1,0:T(1,128)S(1)}, u32[]{:S(2)}, u32[]{:S(2)}) async-start(f32[64,1,128]{2,1,0:T(1,128)} %bitcast.9), calls=%async_computation | async-start | bytes 65536 | tf_op jit(solution)/shard_map/all_to_all | solution.py:33
  112.9 18.1 %collective-permute-start.22 = (f32[16,16,4]{2,1,0:T(8,128)S(1)}, f32[16,16,4]{2,1,0:T(8,128)S(1)}, u32[]{:S(2)}, u32[]{:S(2)}) collective-permute-start(f32[16,16,4]{2,1,0:T(8,128)S(1)} %copy-done.32), channel_id=1, source_target_pairs={{0,1},{1,2},{2,3},{4,5},{5,6},{6,7},{8,9},{9,10},{10,11},{12,13},{... | collective-permute-start | bytes 12296 | tf_op jit(solution)/shard_map/ppermute | solution.py:18
  125.5 11.0 %collective-permute-start.25 = (f32[128]{0:T(128)S(1)}, f32[128]{0:T(128)S(1)}, u32[]{:S(2)}, u32[]{:S(2)}) collective-permute-start(f32[128]{0:T(128)S(1)} %reduce_sum.9), channel_id=1, source_target_pairs={{1,0},{2,3},{5,4},{6,7},{9,8},{10,11},{13,12},{14,15},{17,16},{18,... | collective-permute-start | bytes 1544 | tf_op jit(solution)/shard_map/ppermute | solution.py:352
  126.8 13.8 %collective-permute-start.26 = (f32[128]{0:T(128)S(1)}, f32[128]{0:T(128)S(1)}, u32[]{:S(2)}, u32[]{:S(2)}) collective-permute-start(f32[128]{0:T(128)S(1)} %reduce_sum.9), channel_id=1, source_target_pairs={{2,0},{1,3},{6,4},{5,7},{10,8},{9,11},{14,12},{13,15},{18,16},{17,... | collective-permute-start | bytes 1544 | tf_op jit(solution)/shard_map/ppermute | solution.py:353
  128.1 15.0 %collective-permute-start.23 = (f32[16,16,4]{2,1,0:T(8,128)S(1)}, f32[16,16,4]{2,1,0:T(8,128)S(1)}, u32[]{:S(2)}, u32[]{:S(2)}) collective-permute-start(f32[16,16,4]{2,1,0:T(8,128)S(1)} %copy-done.31), channel_id=1, source_target_pairs={{1,0},{2,1},{3,2},{5,4},{6,5},{7,6},{9,8},{10,9},{11,10},{13,12},{... | collective-permute-start | bytes 12296 | tf_op jit(solution)/shard_map/ppermute | solution.py:23
  130.9 21.3 %collective-permute-start.20 = (f32[16,8,128]{2,1,0:T(8,128)}, f32[16,8,128]{2,1,0:T(8,128)S(1)}, u32[]{:S(2)}, u32[]{:S(2)}) collective-permute-start(f32[16,8,128]{2,1,0:T(8,128)} %get-tuple-element.69), channel_id=1, source_target_pairs={{0,4},{4,8},{8,12},{12,16},{16,20},{20,24},{24,28},{1,5},{5,9},{9,... | collective-permute-start | bytes 196616 | tf_op jit(solution)/shard_map/ppermute | solution.py:18
  132.9 19.4 %collective-permute-start.21 = (f32[16,8,128]{2,1,0:T(8,128)S(1)}, f32[16,8,128]{2,1,0:T(8,128)S(1)}, u32[]{:S(2)}, u32[]{:S(2)}) collective-permute-start(f32[16,8,128]{2,1,0:T(8,128)S(1)} %copy-done.34), channel_id=1, source_target_pairs={{4,0},{8,4},{12,8},{16,12},{20,16},{24,20},{28,24},{5,1},{9,5},{13... | collective-permute-start | bytes 196616 | tf_op jit(solution)/shard_map/ppermute | solution.py:23
  140.6 11.6 %collective-permute-start.19 = (f32[2,16,128]{2,1,0:T(8,128)S(1)}, f32[2,16,128]{2,1,0:T(8,128)S(1)}, u32[]{:S(2)}, u32[]{:S(2)}) collective-permute-start(f32[2,16,128]{2,1,0:T(8,128)S(1)} %copy-done.37), channel_id=1, source_target_pairs={{32,0},{64,32},{96,64},{128,96},{160,128},{192,160},{224,192},{33,... | collective-permute-start | bytes 49160 | tf_op jit(solution)/shard_map/ppermute | solution.py:23
  (46 other events, 379.3 us)

commit v13 on v11

--- a/solution.py
+++ b/solution.py
@@ -349,6 +349,7 @@
         sends = outs[5:11]
         if instant == 0:
             media_halo = outs[11:13]
+    owner_sums = owner_sums + 0.0 * pres[0, 0, 0]
     ocean_plane = first_crust // Z - 1
     crust_plane = first_crust // Z
     spread_out = lax.ppermute(

time: 155 us -> 162 us (1.045)
  waiting for transfers between devices: 33.6 us -> 39.1 us
    ppermute x1, waiting for transfers between devices: 0.01 us -> 4.13 us  [local(): lax.ppermute(owner_sums, 'gz', [(ocean_plane, ocean_plane - 1), (crust_pl...]
    ppermute x12, waiting for transfers between devices: 29.6 us -> 32.1 us  [shifted_down(): return lax.ppermute(x, axis, [(i + 1, i) for i in range(count - 1)])]
  transfers between devices with their start and end apart: 26 -> 26, of which waited for: 6 -> 6; matrix products, arithmetic and copies ran while one was open for 5% -> 6% of each run, Pallas kernels for 2% -> 2%
where the time goes in v13:
time: 162 us; the launch traced here: 161 us
  starting transfers between devices  88.1 us (54%)
  waiting for transfers between devices  39.1 us (24%)
  local copies, waits for them, and re-layouts  13.9 us (9%)
  Pallas kernels  13.6 us (8%)
  other arithmetic  2.77 us (2%)
  between operations  2.06 us (1%)
    ppermute x12, starting transfers between devices, shifted_up(): return lax.ppermute(x, axis, [(i, i + 1) for i in range(count - 1)])  55.7 us
    ppermute x12, waiting for transfers between devices, shifted_down(): return lax.ppermute(x, axis, [(i + 1, i) for i in range(count - 1)])  32.1 us
    ppermute x12, starting transfers between devices, shifted_down(): return lax.ppermute(x, axis, [(i + 1, i) for i in range(count - 1)])  19.3 us
    pallas_call x4, Pallas kernels, run_step(): pl.pallas_call(functools.partial(step_kernel, instant, first), out_shape=...  13.6 us
    all_to_all x1, starting transfers between devices, summed_on_arrival(): parts = lax.all_to_all(in_blocks(x, dim, size), axis, 0, 0, tiled=True)  11.9 us
    unnamed x73, local copies, waits for them, and re-layouts  6.91 us
    ppermute x1, waiting for transfers between devices, local(): lax.ppermute(owner_sums, 'gz', [(ocean_plane, ocean_plane - 1), (crust_pl...  4.13 us
  transfers between devices with their start and end apart: 26, of which 6 were waited for; matrix products, arithmetic and copies ran while one was open for 6% of the time, Pallas kernels for 2%

profile of v13, /device:TPU:24, one launch (start us, length us, event | category | flops | bytes accessed | tf_op | source)
XLA Modules:
  0.0 160.7 jit_solution(13195719721878385103)
XLA Ops:
  4.0 3.8 %collective-permute-start.4 = (f32[16,16,4]{2,1,0:T(8,128)S(1)}, f32[16,16,4]{2,1,0:T(8,128)S(1)}, u32[]{:S(2)}, u32[]{:S(2)}) collective-permute-start(f32[16,16,4]{2,1,0:T(8,128)S(1)} %copy.20), channel_id=1, source_target_pairs={{0,1},{1,2},{2,3},{4,5},{5,6},{6,7},{8,9},{9,10},{10,11},{12,13},{... | collective-permute-start | bytes 12296 | tf_op jit(solution)/shard_map/ppermute | solution.py:18
  13.3 7.8 %collective-permute-start = (f32[4,16,128]{2,1,0:T(8,128)S(1)}, f32[4,16,128]{2,1,0:T(8,128)S(1)}, u32[]{:S(2)}, u32[]{:S(2)}) collective-permute-start(f32[4,16,128]{2,1,0:T(8,128)S(1)} %pad_maximum_fusion.2), channel_id=1, source_target_pairs={{0,32},{32,64},{64,96},{96,128},{128,160},{160,192},{192,224},{1,3... | collective-permute-start | bytes 98312 | tf_op jit(solution)/shard_map/ppermute | solution.py:18
  22.8 1.9 %collective-permute-start.1 = (f32[4,16,128]{2,1,0:T(8,128)S(1)}, f32[4,16,128]{2,1,0:T(8,128)S(1)}, u32[]{:S(2)}, u32[]{:S(2)}) collective-permute-start(f32[4,16,128]{2,1,0:T(8,128)S(1)} %pad_maximum_fusion.3), channel_id=1, source_target_pairs={{32,0},{64,32},{96,64},{128,96},{160,128},{192,160},{224,192},{33,... | collective-permute-start | bytes 98312 | tf_op jit(solution)/shard_map/ppermute | solution.py:23
  26.5 8.2 %collective-permute-done.1.refs_8_ = f32[4,16,128]{2,1,0:T(8,128)S(1)} collective-permute-done((f32[4,16,128]{2,1,0:T(8,128)S(1)}, f32[4,16,128]{2,1,0:T(8,128)S(1)}, u32[]{:S(2)}, u32[]{:S(2)}) %collective-permute-start.1) | collective-permute-done | bytes 32800 | tf_op jit(solution)/shard_map/ppermute | solution.py:23
  36.0 3.4 %shard_map.121 = (f32[16,16,128]{2,1,0:T(8,128)}, f32[3,16,16,128]{3,2,1,0:T(8,128)}, f32[16,16,1]{2,1,0:T(8,128)}, f32[2,16,128]{2,1,0:T(8,128)}, f32[16,2,128]...) custom-call(f32[64]{0:T(128)} %compare_select_fusion.5.refs_0_, ...), custom_call_target="tpu_custom_call" | custom-call | flops 2621440 | bytes 1572864 | tf_op jit(solution)/shard_map/pallas_call | solution.py:226
  39.4 3.2 %collective-permute-start.8 = (f32[16,8,128]{2,1,0:T(8,128)}, f32[16,8,128]{2,1,0:T(8,128)S(1)}, u32[]{:S(2)}, u32[]{:S(2)}) collective-permute-start(f32[16,8,128]{2,1,0:T(8,128)} %get-tuple-element.45), channel_id=1, source_target_pairs={{0,4},{4,8},{8,12},{12,16},{16,20},{20,24},{24,28},{1,5},{5,9},{9,... | collective-permute-start | bytes 196616 | tf_op jit(solution)/shard_map/ppermute | solution.py:18
  43.8 2.6 %collective-permute-start.6 = (f32[2,16,128]{2,1,0:T(8,128)}, f32[2,16,128]{2,1,0:T(8,128)S(1)}, u32[]{:S(2)}, u32[]{:S(2)}) collective-permute-start(f32[2,16,128]{2,1,0:T(8,128)} %get-tuple-element.43), channel_id=1, source_target_pairs={{0,32},{32,64},{64,96},{96,128},{128,160},{160,192},{192,224},{1,3... | collective-permute-start | bytes 49160 | tf_op jit(solution)/shard_map/ppermute | solution.py:18
  46.5 3.2 %collective-permute-start.7 = (f32[2,16,128]{2,1,0:T(8,128)}, f32[2,16,128]{2,1,0:T(8,128)S(1)}, u32[]{:S(2)}, u32[]{:S(2)}) collective-permute-start(f32[2,16,128]{2,1,0:T(8,128)} %get-tuple-element.44), channel_id=1, source_target_pairs={{32,0},{64,32},{96,64},{128,96},{160,128},{192,160},{224,192},{33,... | collective-permute-start | bytes 49160 | tf_op jit(solution)/shard_map/ppermute | solution.py:23
  49.7 4.6 %collective-permute-start.10 = (f32[16,16,4]{2,1,0:T(8,128)}, f32[16,16,4]{2,1,0:T(8,128)S(1)}, u32[]{:S(2)}, u32[]{:S(2)}) collective-permute-start(f32[16,16,4]{2,1,0:T(8,128)} %get-tuple-element.47), channel_id=1, source_target_pairs={{0,1},{1,2},{2,3},{4,5},{5,6},{6,7},{8,9},{9,10},{10,11},{12,13},{... | collective-permute-start | bytes 12296 | tf_op jit(solution)/shard_map/ppermute | solution.py:18
  54.2 2.8 %collective-permute-done.10.refs_12_ = f32[16,16,4]{2,1,0:T(8,128)S(1)} collective-permute-done((f32[16,16,4]{2,1,0:T(8,128)}, f32[16,16,4]{2,1,0:T(8,128)S(1)}, u32[]{:S(2)}, u32[]{:S(2)}) %collective-permute-start.10) | collective-permute-done | bytes 4128 | tf_op jit(solution)/shard_map/ppermute | solution.py:18
  58.3 6.1 %collective-permute-done.11.refs_13_ = f32[16,16,4]{2,1,0:T(8,128)S(1)} collective-permute-done((f32[16,16,4]{2,1,0:T(8,128)}, f32[16,16,4]{2,1,0:T(8,128)S(1)}, u32[]{:S(2)}, u32[]{:S(2)}) %collective-permute-start.11) | collective-permute-done | bytes 4128 | tf_op jit(solution)/shard_map/ppermute | solution.py:23
  65.2 3.4 %shard_map.122 = (f32[16,16,128]{2,1,0:T(8,128)}, f32[3,16,16,128]{3,2,1,0:T(8,128)}, f32[16,16,1]{2,1,0:T(8,128)}, f32[2,16,128]{2,1,0:T(8,128)}, f32[16,2,128]...) custom-call(f32[64]{0:T(128)} %compare_select_fusion.5.refs_0_, ...), custom_call_target="tpu_custom_call" | custom-call | flops 2621440 | bytes 1572864 | tf_op jit(solution)/shard_map/pallas_call | solution.py:226
  68.6 4.2 %collective-permute-start.16 = (f32[16,16,4]{2,1,0:T(8,128)}, f32[16,16,4]{2,1,0:T(8,128)S(1)}, u32[]{:S(2)}, u32[]{:S(2)}) collective-permute-start(f32[16,16,4]{2,1,0:T(8,128)} %get-tuple-element.60), channel_id=1, source_target_pairs={{0,1},{1,2},{2,3},{4,5},{5,6},{6,7},{8,9},{9,10},{10,11},{12,13},{... | collective-permute-start | bytes 12296 | tf_op jit(solution)/shard_map/ppermute | solution.py:18
  74.1 2.6 %collective-permute-start.14 = (f32[16,8,128]{2,1,0:T(8,128)}, f32[16,8,128]{2,1,0:T(8,128)S(1)}, u32[]{:S(2)}, u32[]{:S(2)}) collective-permute-start(f32[16,8,128]{2,1,0:T(8,128)} %get-tuple-element.58), channel_id=1, source_target_pairs={{0,4},{4,8},{8,12},{12,16},{16,20},{20,24},{24,28},{1,5},{5,9},{9,... | collective-permute-start | bytes 196616 | tf_op jit(solution)/shard_map/ppermute | solution.py:18
  78.0 8.7 %collective-permute-start.12 = (f32[2,16,128]{2,1,0:T(8,128)}, f32[2,16,128]{2,1,0:T(8,128)S(1)}, u32[]{:S(2)}, u32[]{:S(2)}) collective-permute-start(f32[2,16,128]{2,1,0:T(8,128)} %get-tuple-element.56), channel_id=1, source_target_pairs={{0,32},{32,64},{64,96},{96,128},{128,160},{160,192},{192,224},{1,3... | collective-permute-start | bytes 49160 | tf_op jit(solution)/shard_map/ppermute | solution.py:18
  90.4 8.1 %collective-permute-done.13.refs_9_ = f32[2,16,128]{2,1,0:T(8,128)S(1)} collective-permute-done((f32[2,16,128]{2,1,0:T(8,128)}, f32[2,16,128]{2,1,0:T(8,128)S(1)}, u32[]{:S(2)}, u32[]{:S(2)}) %collective-permute-start.13) | collective-permute-done | bytes 16416 | tf_op jit(solution)/shard_map/ppermute | solution.py:23
  99.2 3.4 %shard_map.123 = (f32[16,16,128]{2,1,0:T(8,128)}, f32[3,16,16,128]{3,2,1,0:T(8,128)}, f32[16,16,1]{2,1,0:T(8,128)}, f32[2,16,128]{2,1,0:T(8,128)}, f32[16,2,128]...) custom-call(f32[64]{0:T(128)} %compare_select_fusion.5.refs_0_, ...), custom_call_target="tpu_custom_call" | custom-call | flops 2621440 | bytes 1572864 | tf_op jit(solution)/shard_map/pallas_call | solution.py:226
  102.6 4.4 %collective-permute-start.22 = (f32[16,16,4]{2,1,0:T(8,128)}, f32[16,16,4]{2,1,0:T(8,128)S(1)}, u32[]{:S(2)}, u32[]{:S(2)}) collective-permute-start(f32[16,16,4]{2,1,0:T(8,128)} %get-tuple-element.71), channel_id=1, source_target_pairs={{0,1},{1,2},{2,3},{4,5},{5,6},{6,7},{8,9},{9,10},{10,11},{12,13},{... | collective-permute-start | bytes 12296 | tf_op jit(solution)/shard_map/ppermute | solution.py:18
  108.4 5.1 %collective-permute-start.20 = (f32[16,8,128]{2,1,0:T(8,128)}, f32[16,8,128]{2,1,0:T(8,128)S(1)}, u32[]{:S(2)}, u32[]{:S(2)}) collective-permute-start(f32[16,8,128]{2,1,0:T(8,128)} %get-tuple-element.69), channel_id=1, source_target_pairs={{0,4},{4,8},{8,12},{12,16},{16,20},{20,24},{24,28},{1,5},{5,9},{9,... | collective-permute-start | bytes 196616 | tf_op jit(solution)/shard_map/ppermute | solution.py:18
  117.8 11.9 %all-to-all-start = ((f32[64,1,128]{2,1,0:T(1,128)}), f32[64,1,128]{2,1,0:T(1,128)S(1)}, u32[]{:S(2)}, u32[]{:S(2)}) async-start(f32[64,1,128]{2,1,0:T(1,128)} %bitcast.9), calls=%async_computation | async-start | bytes 65536 | tf_op jit(solution)/shard_map/all_to_all | solution.py:33
  129.6 7.3 %collective-permute-start.18 = (f32[2,16,128]{2,1,0:T(8,128)S(1)}, f32[2,16,128]{2,1,0:T(8,128)S(1)}, u32[]{:S(2)}, u32[]{:S(2)}) collective-permute-start(f32[2,16,128]{2,1,0:T(8,128)S(1)} %copy-done.32), channel_id=1, source_target_pairs={{0,32},{32,64},{64,96},{96,128},{128,160},{160,192},{192,224},{1,3... | collective-permute-start | bytes 49160 | tf_op jit(solution)/shard_map/ppermute | solution.py:18
  138.9 9.7 %collective-permute-done.19.refs_9_ = f32[2,16,128]{2,1,0:T(8,128)S(1)} collective-permute-done((f32[2,16,128]{2,1,0:T(8,128)S(1)}, f32[2,16,128]{2,1,0:T(8,128)S(1)}, u32[]{:S(2)}, u32[]{:S(2)}) %collective-permute-start.19) | collective-permute-done | bytes 16416 | tf_op jit(solution)/shard_map/ppermute | solution.py:23
  149.3 3.4 %shard_map.124 = (f32[16,16,128]{2,1,0:T(8,128)}, f32[3,16,16,128]{3,2,1,0:T(8,128)}, f32[16,16,1]{2,1,0:T(8,128)}, f32[2,16,128]{2,1,0:T(8,128)}, f32[16,2,128]...) custom-call(f32[64]{0:T(128)} %compare_select_fusion.5.refs_0_, ...), custom_call_target="tpu_custom_call" | custom-call | flops 2621440 | bytes 1572864 | tf_op jit(solution)/shard_map/pallas_call | solution.py:226
  155.9 4.1 %collective-permute-done.24 = f32[128]{0:T(128)S(1)} collective-permute-done((f32[128]{0:T(128)S(1)}, f32[128]{0:T(128)S(1)}, u32[]{:S(2)}, u32[]{:S(2)}) %collective-permute-start.24) | collective-permute-done | bytes 544 | tf_op jit(solution)/shard_map/ppermute | solution.py:355
  (145 shorter events, 34.8 us)
Async XLA Ops:
  4.0 18.8 %collective-permute-start.4 = (f32[16,16,4]{2,1,0:T(8,128)S(1)}, f32[16,16,4]{2,1,0:T(8,128)S(1)}, u32[]{:S(2)}, u32[]{:S(2)}) collective-permute-start(f32[16,16,4]{2,1,0:T(8,128)S(1)} %copy.20), channel_id=1, source_target_pairs={{0,1},{1,2},{2,3},{4,5},{5,6},{6,7},{8,9},{9,10},{10,11},{12,13},{... | collective-permute-start | bytes 12296 | tf_op jit(solution)/shard_map/ppermute | solution.py:18
  8.3 18.1 %collective-permute-start.5 = (f32[16,16,4]{2,1,0:T(8,128)S(1)}, f32[16,16,4]{2,1,0:T(8,128)S(1)}, u32[]{:S(2)}, u32[]{:S(2)}) collective-permute-start(f32[16,16,4]{2,1,0:T(8,128)S(1)} %copy.23), channel_id=1, source_target_pairs={{1,0},{2,1},{3,2},{5,4},{6,5},{7,6},{9,8},{10,9},{11,10},{13,12},{... | collective-permute-start | bytes 12296 | tf_op jit(solution)/shard_map/ppermute | solution.py:23
  9.7 24.9 %collective-permute-start.2 = (f32[16,10,128]{2,1,0:T(8,128)S(1)}, f32[16,10,128]{2,1,0:T(8,128)S(1)}, u32[]{:S(2)}, u32[]{:S(2)}) collective-permute-start(f32[16,10,128]{2,1,0:T(8,128)S(1)} %pad_maximum_fusion), channel_id=1, source_target_pairs={{0,4},{4,8},{8,12},{12,16},{16,20},{20,24},{24,28},{1,5},{5,9},{9,... | collective-permute-start | bytes 245768 | tf_op jit(solution)/shard_map/ppermute | solution.py:18
  11.2 23.4 %collective-permute-start.3 = (f32[16,10,128]{2,1,0:T(8,128)S(1)}, f32[16,10,128]{2,1,0:T(8,128)S(1)}, u32[]{:S(2)}, u32[]{:S(2)}) collective-permute-start(f32[16,10,128]{2,1,0:T(8,128)S(1)} %pad_maximum_fusion.1), channel_id=1, source_target_pairs={{4,0},{8,4},{12,8},{16,12},{20,16},{24,20},{28,24},{5,1},{9,5},{13... | collective-permute-start | bytes 245768 | tf_op jit(solution)/shard_map/ppermute | solution.py:23
  13.3 13.2 %collective-permute-start = (f32[4,16,128]{2,1,0:T(8,128)S(1)}, f32[4,16,128]{2,1,0:T(8,128)S(1)}, u32[]{:S(2)}, u32[]{:S(2)}) collective-permute-start(f32[4,16,128]{2,1,0:T(8,128)S(1)} %pad_maximum_fusion.2), channel_id=1, source_target_pairs={{0,32},{32,64},{64,96},{96,128},{128,160},{160,192},{192,224},{1,3... | collective-permute-start | bytes 98312 | tf_op jit(solution)/shard_map/ppermute | solution.py:18
  22.8 11.8 %collective-permute-start.1 = (f32[4,16,128]{2,1,0:T(8,128)S(1)}, f32[4,16,128]{2,1,0:T(8,128)S(1)}, u32[]{:S(2)}, u32[]{:S(2)}) collective-permute-start(f32[4,16,128]{2,1,0:T(8,128)S(1)} %pad_maximum_fusion.3), channel_id=1, source_target_pairs={{32,0},{64,32},{96,64},{128,96},{160,128},{192,160},{224,192},{33,... | collective-permute-start | bytes 98312 | tf_op jit(solution)/shard_map/ppermute | solution.py:23
  39.4 25.1 %collective-permute-start.8 = (f32[16,8,128]{2,1,0:T(8,128)}, f32[16,8,128]{2,1,0:T(8,128)S(1)}, u32[]{:S(2)}, u32[]{:S(2)}) collective-permute-start(f32[16,8,128]{2,1,0:T(8,128)} %get-tuple-element.45), channel_id=1, source_target_pairs={{0,4},{4,8},{8,12},{12,16},{16,20},{20,24},{24,28},{1,5},{5,9},{9,... | collective-permute-start | bytes 196616 | tf_op jit(solution)/shard_map/ppermute | solution.py:18
  42.5 22.0 %collective-permute-start.9 = (f32[16,8,128]{2,1,0:T(8,128)}, f32[16,8,128]{2,1,0:T(8,128)S(1)}, u32[]{:S(2)}, u32[]{:S(2)}) collective-permute-start(f32[16,8,128]{2,1,0:T(8,128)} %get-tuple-element.46), channel_id=1, source_target_pairs={{4,0},{8,4},{12,8},{16,12},{20,16},{24,20},{28,24},{5,1},{9,5},{13... | collective-permute-start | bytes 196616 | tf_op jit(solution)/shard_map/ppermute | solution.py:23
  43.8 20.6 %collective-permute-start.6 = (f32[2,16,128]{2,1,0:T(8,128)}, f32[2,16,128]{2,1,0:T(8,128)S(1)}, u32[]{:S(2)}, u32[]{:S(2)}) collective-permute-start(f32[2,16,128]{2,1,0:T(8,128)} %get-tuple-element.43), channel_id=1, source_target_pairs={{0,32},{32,64},{64,96},{96,128},{128,160},{160,192},{192,224},{1,3... | collective-permute-start | bytes 49160 | tf_op jit(solution)/shard_map/ppermute | solution.py:18
  46.5 18.0 %collective-permute-start.7 = (f32[2,16,128]{2,1,0:T(8,128)}, f32[2,16,128]{2,1,0:T(8,128)S(1)}, u32[]{:S(2)}, u32[]{:S(2)}) collective-permute-start(f32[2,16,128]{2,1,0:T(8,128)} %get-tuple-element.44), channel_id=1, source_target_pairs={{32,0},{64,32},{96,64},{128,96},{160,128},{192,160},{224,192},{33,... | collective-permute-start | bytes 49160 | tf_op jit(solution)/shard_map/ppermute | solution.py:23
  57.1 7.4 %collective-permute-start.11 = (f32[16,16,4]{2,1,0:T(8,128)}, f32[16,16,4]{2,1,0:T(8,128)S(1)}, u32[]{:S(2)}, u32[]{:S(2)}) collective-permute-start(f32[16,16,4]{2,1,0:T(8,128)} %get-tuple-element.48), channel_id=1, source_target_pairs={{1,0},{2,1},{3,2},{5,4},{6,5},{7,6},{9,8},{10,9},{11,10},{13,12},{... | collective-permute-start | bytes 12296 | tf_op jit(solution)/shard_map/ppermute | solution.py:23
  68.6 18.1 %collective-permute-start.16 = (f32[16,16,4]{2,1,0:T(8,128)}, f32[16,16,4]{2,1,0:T(8,128)S(1)}, u32[]{:S(2)}, u32[]{:S(2)}) collective-permute-start(f32[16,16,4]{2,1,0:T(8,128)} %get-tuple-element.60), channel_id=1, source_target_pairs={{0,1},{1,2},{2,3},{4,5},{5,6},{6,7},{8,9},{9,10},{10,11},{12,13},{... | collective-permute-start | bytes 12296 | tf_op jit(solution)/shard_map/ppermute | solution.py:18
  72.8 17.6 %collective-permute-start.17 = (f32[16,16,4]{2,1,0:T(8,128)}, f32[16,16,4]{2,1,0:T(8,128)S(1)}, u32[]{:S(2)}, u32[]{:S(2)}) collective-permute-start(f32[16,16,4]{2,1,0:T(8,128)} %get-tuple-element.61), channel_id=1, source_target_pairs={{1,0},{2,1},{3,2},{5,4},{6,5},{7,6},{9,8},{10,9},{11,10},{13,12},{... | collective-permute-start | bytes 12296 | tf_op jit(solution)/shard_map/ppermute | solution.py:23
  74.1 24.4 %collective-permute-start.14 = (f32[16,8,128]{2,1,0:T(8,128)}, f32[16,8,128]{2,1,0:T(8,128)S(1)}, u32[]{:S(2)}, u32[]{:S(2)}) collective-permute-start(f32[16,8,128]{2,1,0:T(8,128)} %get-tuple-element.58), channel_id=1, source_target_pairs={{0,4},{4,8},{8,12},{12,16},{16,20},{20,24},{24,28},{1,5},{5,9},{9,... | collective-permute-start | bytes 196616 | tf_op jit(solution)/shard_map/ppermute | solution.py:18
  76.7 21.9 %collective-permute-start.15 = (f32[16,8,128]{2,1,0:T(8,128)}, f32[16,8,128]{2,1,0:T(8,128)S(1)}, u32[]{:S(2)}, u32[]{:S(2)}) collective-permute-start(f32[16,8,128]{2,1,0:T(8,128)} %get-tuple-element.59), channel_id=1, source_target_pairs={{4,0},{8,4},{12,8},{16,12},{20,16},{24,20},{28,24},{5,1},{9,5},{13... | collective-permute-start | bytes 196616 | tf_op jit(solution)/shard_map/ppermute | solution.py:23
  78.0 12.4 %collective-permute-start.12 = (f32[2,16,128]{2,1,0:T(8,128)}, f32[2,16,128]{2,1,0:T(8,128)S(1)}, u32[]{:S(2)}, u32[]{:S(2)}) collective-permute-start(f32[2,16,128]{2,1,0:T(8,128)} %get-tuple-element.56), channel_id=1, source_target_pairs={{0,32},{32,64},{64,96},{96,128},{128,160},{160,192},{192,224},{1,3... | collective-permute-start | bytes 49160 | tf_op jit(solution)/shard_map/ppermute | solution.py:18
  86.7 11.9 %collective-permute-start.13 = (f32[2,16,128]{2,1,0:T(8,128)}, f32[2,16,128]{2,1,0:T(8,128)S(1)}, u32[]{:S(2)}, u32[]{:S(2)}) collective-permute-start(f32[2,16,128]{2,1,0:T(8,128)} %get-tuple-element.57), channel_id=1, source_target_pairs={{32,0},{64,32},{96,64},{128,96},{160,128},{192,160},{224,192},{33,... | collective-permute-start | bytes 49160 | tf_op jit(solution)/shard_map/ppermute | solution.py:23
  102.6 12.1 %collective-permute-start.22 = (f32[16,16,4]{2,1,0:T(8,128)}, f32[16,16,4]{2,1,0:T(8,128)S(1)}, u32[]{:S(2)}, u32[]{:S(2)}) collective-permute-start(f32[16,16,4]{2,1,0:T(8,128)} %get-tuple-element.71), channel_id=1, source_target_pairs={{0,1},{1,2},{2,3},{4,5},{5,6},{6,7},{8,9},{9,10},{10,11},{12,13},{... | collective-permute-start | bytes 12296 | tf_op jit(solution)/shard_map/ppermute | solution.py:18
  107.0 7.7 %collective-permute-start.23 = (f32[16,16,4]{2,1,0:T(8,128)}, f32[16,16,4]{2,1,0:T(8,128)S(1)}, u32[]{:S(2)}, u32[]{:S(2)}) collective-permute-start(f32[16,16,4]{2,1,0:T(8,128)} %get-tuple-element.72), channel_id=1, source_target_pairs={{1,0},{2,1},{3,2},{5,4},{6,5},{7,6},{9,8},{10,9},{11,10},{13,12},{... | collective-permute-start | bytes 12296 | tf_op jit(solution)/shard_map/ppermute | solution.py:23
  108.4 40.3 %collective-permute-start.20 = (f32[16,8,128]{2,1,0:T(8,128)}, f32[16,8,128]{2,1,0:T(8,128)S(1)}, u32[]{:S(2)}, u32[]{:S(2)}) collective-permute-start(f32[16,8,128]{2,1,0:T(8,128)} %get-tuple-element.69), channel_id=1, source_target_pairs={{0,4},{4,8},{8,12},{12,16},{16,20},{20,24},{24,28},{1,5},{5,9},{9,... | collective-permute-start | bytes 196616 | tf_op jit(solution)/shard_map/ppermute | solution.py:18
  113.4 35.2 %collective-permute-start.21 = (f32[16,8,128]{2,1,0:T(8,128)}, f32[16,8,128]{2,1,0:T(8,128)S(1)}, u32[]{:S(2)}, u32[]{:S(2)}) collective-permute-start(f32[16,8,128]{2,1,0:T(8,128)} %get-tuple-element.70), channel_id=1, source_target_pairs={{4,0},{8,4},{12,8},{16,12},{20,16},{24,20},{28,24},{5,1},{9,5},{13... | collective-permute-start | bytes 196616 | tf_op jit(solution)/shard_map/ppermute | solution.py:23
  117.8 36.8 %all-to-all-start = ((f32[64,1,128]{2,1,0:T(1,128)}), f32[64,1,128]{2,1,0:T(1,128)S(1)}, u32[]{:S(2)}, u32[]{:S(2)}) async-start(f32[64,1,128]{2,1,0:T(1,128)} %bitcast.9), calls=%async_computation | async-start | bytes 65536 | tf_op jit(solution)/shard_map/all_to_all | solution.py:33
  129.6 9.3 %collective-permute-start.18 = (f32[2,16,128]{2,1,0:T(8,128)S(1)}, f32[2,16,128]{2,1,0:T(8,128)S(1)}, u32[]{:S(2)}, u32[]{:S(2)}) collective-permute-start(f32[2,16,128]{2,1,0:T(8,128)S(1)} %copy-done.32), channel_id=1, source_target_pairs={{0,32},{32,64},{64,96},{96,128},{128,160},{160,192},{192,224},{1,3... | collective-permute-start | bytes 49160 | tf_op jit(solution)/shard_map/ppermute | solution.py:18
  137.0 11.6 %collective-permute-start.19 = (f32[2,16,128]{2,1,0:T(8,128)S(1)}, f32[2,16,128]{2,1,0:T(8,128)S(1)}, u32[]{:S(2)}, u32[]{:S(2)}) collective-permute-start(f32[2,16,128]{2,1,0:T(8,128)S(1)} %copy-done.31), channel_id=1, source_target_pairs={{32,0},{64,32},{96,64},{128,96},{160,128},{192,160},{224,192},{33,... | collective-permute-start | bytes 49160 | tf_op jit(solution)/shard_map/ppermute | solution.py:23
  (36 other events, 209.7 us)

commit v14 on v10

--- a/solution.py
+++ b/solution.py
@@ -240,7 +240,7 @@
     ).astype(jnp.float32)
     weighted = jnp.where(owner_hot, sea_values[None, :], 0.0)
     partial_slip = jnp.dot(weighted, within_hot, precision=lax.Precision.HIGHEST).reshape(-1)
-    return summed_on_arrival(partial_slip, ("gx", "gy"), 0)
+    return summed_on_arrival(partial_slip, ("gx", "gy", "gz"), 0)
 
 
 def local(
@@ -332,7 +332,8 @@
                 ocean * (sends[4][:, :, 1:2] + halos[5][:, :, 0:1])
                 + crust * (halos[4][:, :, 1:2] + sends[5][:, :, 0:1])
             )
-            owner_sums = seafloor_sums(sf_last[:, :, 0], node_weight, node_patch, patch_slot)
+            sf_last = jnp.where(depth_index == first_crust // Z, sf_last, 0.0)
+            slip_grad = seafloor_sums(sf_last[:, :, 0], node_weight, node_patch, patch_slot)
         if instant == 0:
             operands = common + (pres, vel, inv_density, bulk, src_all) + halos
         else:
@@ -343,15 +344,6 @@
         sends = outs[6:12]
         if instant == 0:
             media_halo = outs[12:15]
-    ocean_plane = first_crust // Z - 1
-    crust_plane = first_crust // Z
-    spread_out = lax.ppermute(
-        owner_sums, "gz", [(ocean_plane, ocean_plane - 1), (crust_plane, crust_plane + 1)]
-    )
-    inner = (depth_index == ocean_plane) | (depth_index == crust_plane)
-    owner_sums = jnp.where(inner, owner_sums, spread_out)
-    piece = owner_sums.shape[0] // tiles_z
-    slip_grad = lax.dynamic_slice_in_dim(owner_sums, depth_index * piece, piece)
     return (pres, vel, slip_grad)
 
 

time: 155 us -> 158 us (1.019)
  starting transfers between devices: 88.1 us -> 89.9 us
    ppermute x12, waiting for transfers between devices: 29.6 us -> 32.1 us  [shifted_down(): return lax.ppermute(x, axis, [(i + 1, i) for i in range(count - 1)])]
    all_to_all x1, starting transfers between devices: 11.8 us -> 14.1 us  [summed_on_arrival(): parts = lax.all_to_all(in_blocks(x, dim, size), axis, 0, 0, tiled=True)]
  transfers between devices with their start and end apart: 26 -> 25, of which waited for: 6 -> 5; matrix products, arithmetic and copies ran while one was open for 5% -> 5% of each run, Pallas kernels for 2% -> 2%
where the time goes in v14:
time: 158 us; the launch traced here: 157 us
  starting transfers between devices  89.9 us (57%)
  waiting for transfers between devices  35 us (22%)
  Pallas kernels  13.6 us (9%)
  local copies, waits for them, and re-layouts  12.8 us (8%)
  other arithmetic  3.5 us (2%)
    ppermute x12, starting transfers between devices, shifted_up(): return lax.ppermute(x, axis, [(i, i + 1) for i in range(count - 1)])  56.5 us
    ppermute x12, waiting for transfers between devices, shifted_down(): return lax.ppermute(x, axis, [(i + 1, i) for i in range(count - 1)])  32.1 us
    ppermute x12, starting transfers between devices, shifted_down(): return lax.ppermute(x, axis, [(i + 1, i) for i in range(count - 1)])  19.3 us
    all_to_all x1, starting transfers between devices, summed_on_arrival(): parts = lax.all_to_all(in_blocks(x, dim, size), axis, 0, 0, tiled=True)  14.1 us
    pallas_call x4, Pallas kernels, run_step(): pl.pallas_call(functools.partial(step_kernel, instant, first), out_shape=...  13.6 us
    unnamed x73, local copies, waits for them, and re-layouts  6.84 us
  transfers between devices with their start and end apart: 25, of which 5 were waited for; matrix products, arithmetic and copies ran while one was open for 5% of the time, Pallas kernels for 2%

profile of v14, /device:TPU:24, one launch (start us, length us, event | category | flops | bytes accessed | tf_op | source)
XLA Modules:
  0.0 156.7 jit_solution(15985364313737350031)
XLA Ops:
  4.0 3.8 %collective-permute-start.4 = (f32[16,16,4]{2,1,0:T(8,128)S(1)}, f32[16,16,4]{2,1,0:T(8,128)S(1)}, u32[]{:S(2)}, u32[]{:S(2)}) collective-permute-start(f32[16,16,4]{2,1,0:T(8,128)S(1)} %copy.20), channel_id=1, source_target_pairs={{0,1},{1,2},{2,3},{4,5},{5,6},{6,7},{8,9},{9,10},{10,11},{12,13},{... | collective-permute-start | bytes 12296 | tf_op jit(solution)/shard_map/ppermute | solution.py:18
  13.3 7.8 %collective-permute-start = (f32[4,16,128]{2,1,0:T(8,128)S(1)}, f32[4,16,128]{2,1,0:T(8,128)S(1)}, u32[]{:S(2)}, u32[]{:S(2)}) collective-permute-start(f32[4,16,128]{2,1,0:T(8,128)S(1)} %pad_maximum_fusion.2), channel_id=1, source_target_pairs={{0,32},{32,64},{64,96},{96,128},{128,160},{160,192},{192,224},{1,3... | collective-permute-start | bytes 98312 | tf_op jit(solution)/shard_map/ppermute | solution.py:18
  22.9 1.9 %collective-permute-start.1 = (f32[4,16,128]{2,1,0:T(8,128)S(1)}, f32[4,16,128]{2,1,0:T(8,128)S(1)}, u32[]{:S(2)}, u32[]{:S(2)}) collective-permute-start(f32[4,16,128]{2,1,0:T(8,128)S(1)} %pad_maximum_fusion.3), channel_id=1, source_target_pairs={{32,0},{64,32},{96,64},{128,96},{160,128},{192,160},{224,192},{33,... | collective-permute-start | bytes 98312 | tf_op jit(solution)/shard_map/ppermute | solution.py:23
  26.5 8.2 %collective-permute-done.1.refs_8_ = f32[4,16,128]{2,1,0:T(8,128)S(1)} collective-permute-done((f32[4,16,128]{2,1,0:T(8,128)S(1)}, f32[4,16,128]{2,1,0:T(8,128)S(1)}, u32[]{:S(2)}, u32[]{:S(2)}) %collective-permute-start.1) | collective-permute-done | bytes 32800 | tf_op jit(solution)/shard_map/ppermute | solution.py:23
  36.0 3.6 %shard_map.121 = (f32[16,16,128]{2,1,0:T(8,128)}, f32[3,16,16,128]{3,2,1,0:T(8,128)}, f32[16,16,1]{2,1,0:T(8,128)}, f32[2,16,128]{2,1,0:T(8,128)}, f32[16,2,128]...) custom-call(f32[64]{0:T(128)} %compare_select_fusion.5.refs_0_, ...), custom_call_target="tpu_custom_call" | custom-call | flops 2621440 | bytes 1572864 | tf_op jit(solution)/shard_map/pallas_call | solution.py:221
  39.6 3.2 %collective-permute-start.8 = (f32[16,8,128]{2,1,0:T(8,128)}, f32[16,8,128]{2,1,0:T(8,128)S(1)}, u32[]{:S(2)}, u32[]{:S(2)}) collective-permute-start(f32[16,8,128]{2,1,0:T(8,128)} %get-tuple-element.49), channel_id=1, source_target_pairs={{0,4},{4,8},{8,12},{12,16},{16,20},{20,24},{24,28},{1,5},{5,9},{9,... | collective-permute-start | bytes 196616 | tf_op jit(solution)/shard_map/ppermute | solution.py:18
  44.1 2.7 %collective-permute-start.6 = (f32[2,16,128]{2,1,0:T(8,128)}, f32[2,16,128]{2,1,0:T(8,128)S(1)}, u32[]{:S(2)}, u32[]{:S(2)}) collective-permute-start(f32[2,16,128]{2,1,0:T(8,128)} %get-tuple-element.47), channel_id=1, source_target_pairs={{0,32},{32,64},{64,96},{96,128},{128,160},{160,192},{192,224},{1,3... | collective-permute-start | bytes 49160 | tf_op jit(solution)/shard_map/ppermute | solution.py:18
  46.7 3.2 %collective-permute-start.7 = (f32[2,16,128]{2,1,0:T(8,128)}, f32[2,16,128]{2,1,0:T(8,128)S(1)}, u32[]{:S(2)}, u32[]{:S(2)}) collective-permute-start(f32[2,16,128]{2,1,0:T(8,128)} %get-tuple-element.48), channel_id=1, source_target_pairs={{32,0},{64,32},{96,64},{128,96},{160,128},{192,160},{224,192},{33,... | collective-permute-start | bytes 49160 | tf_op jit(solution)/shard_map/ppermute | solution.py:23
  49.9 4.6 %collective-permute-start.10 = (f32[16,16,2]{2,1,0:T(8,128)}, f32[16,16,2]{2,1,0:T(8,128)S(1)}, u32[]{:S(2)}, u32[]{:S(2)}) collective-permute-start(f32[16,16,2]{2,1,0:T(8,128)} %get-tuple-element.51), channel_id=1, source_target_pairs={{0,1},{1,2},{2,3},{4,5},{5,6},{6,7},{8,9},{9,10},{10,11},{12,13},{... | collective-permute-start | bytes 6152 | tf_op jit(solution)/shard_map/ppermute | solution.py:18
  54.5 2.8 %collective-permute-done.10.refs_12_ = f32[16,16,2]{2,1,0:T(8,128)S(1)} collective-permute-done((f32[16,16,2]{2,1,0:T(8,128)}, f32[16,16,2]{2,1,0:T(8,128)S(1)}, u32[]{:S(2)}, u32[]{:S(2)}) %collective-permute-start.10) | collective-permute-done | bytes 2080 | tf_op jit(solution)/shard_map/ppermute | solution.py:18
  58.6 6.1 %collective-permute-done.11.refs_13_ = f32[16,16,2]{2,1,0:T(8,128)S(1)} collective-permute-done((f32[16,16,2]{2,1,0:T(8,128)}, f32[16,16,2]{2,1,0:T(8,128)S(1)}, u32[]{:S(2)}, u32[]{:S(2)}) %collective-permute-start.11) | collective-permute-done | bytes 2080 | tf_op jit(solution)/shard_map/ppermute | solution.py:23
  65.4 3.3 %shard_map.122 = (f32[16,16,128]{2,1,0:T(8,128)}, f32[3,16,16,128]{3,2,1,0:T(8,128)}, f32[16,16,1]{2,1,0:T(8,128)}, f32[2,16,128]{2,1,0:T(8,128)}, f32[16,2,128]...) custom-call(f32[64]{0:T(128)} %compare_select_fusion.5.refs_0_, ...), custom_call_target="tpu_custom_call" | custom-call | flops 2621440 | bytes 1572864 | tf_op jit(solution)/shard_map/pallas_call | solution.py:221
  68.8 4.2 %collective-permute-start.16 = (f32[16,16,2]{2,1,0:T(8,128)}, f32[16,16,2]{2,1,0:T(8,128)S(1)}, u32[]{:S(2)}, u32[]{:S(2)}) collective-permute-start(f32[16,16,2]{2,1,0:T(8,128)} %get-tuple-element.66), channel_id=1, source_target_pairs={{0,1},{1,2},{2,3},{4,5},{5,6},{6,7},{8,9},{9,10},{10,11},{12,13},{... | collective-permute-start | bytes 6152 | tf_op jit(solution)/shard_map/ppermute | solution.py:18
  74.3 2.6 %collective-permute-start.14 = (f32[16,8,128]{2,1,0:T(8,128)}, f32[16,8,128]{2,1,0:T(8,128)S(1)}, u32[]{:S(2)}, u32[]{:S(2)}) collective-permute-start(f32[16,8,128]{2,1,0:T(8,128)} %get-tuple-element.64), channel_id=1, source_target_pairs={{0,4},{4,8},{8,12},{12,16},{16,20},{20,24},{24,28},{1,5},{5,9},{9,... | collective-permute-start | bytes 196616 | tf_op jit(solution)/shard_map/ppermute | solution.py:18
  78.2 8.7 %collective-permute-start.12 = (f32[2,16,128]{2,1,0:T(8,128)}, f32[2,16,128]{2,1,0:T(8,128)S(1)}, u32[]{:S(2)}, u32[]{:S(2)}) collective-permute-start(f32[2,16,128]{2,1,0:T(8,128)} %get-tuple-element.62), channel_id=1, source_target_pairs={{0,32},{32,64},{64,96},{96,128},{128,160},{160,192},{192,224},{1,3... | collective-permute-start | bytes 49160 | tf_op jit(solution)/shard_map/ppermute | solution.py:18
  90.6 8.1 %collective-permute-done.13.refs_9_ = f32[2,16,128]{2,1,0:T(8,128)S(1)} collective-permute-done((f32[2,16,128]{2,1,0:T(8,128)}, f32[2,16,128]{2,1,0:T(8,128)S(1)}, u32[]{:S(2)}, u32[]{:S(2)}) %collective-permute-start.13) | collective-permute-done | bytes 16416 | tf_op jit(solution)/shard_map/ppermute | solution.py:23
  99.4 3.3 %shard_map.123 = (f32[16,16,128]{2,1,0:T(8,128)}, f32[3,16,16,128]{3,2,1,0:T(8,128)}, f32[16,16,1]{2,1,0:T(8,128)}, f32[2,16,128]{2,1,0:T(8,128)}, f32[16,2,128]...) custom-call(f32[64]{0:T(128)} %compare_select_fusion.5.refs_0_, ...), custom_call_target="tpu_custom_call" | custom-call | flops 2621440 | bytes 1572864 | tf_op jit(solution)/shard_map/pallas_call | solution.py:221
  102.7 4.5 %collective-permute-start.22 = (f32[16,16,2]{2,1,0:T(8,128)}, f32[16,16,2]{2,1,0:T(8,128)S(1)}, u32[]{:S(2)}, u32[]{:S(2)}) collective-permute-start(f32[16,16,2]{2,1,0:T(8,128)} %get-tuple-element.78), channel_id=1, source_target_pairs={{0,1},{1,2},{2,3},{4,5},{5,6},{6,7},{8,9},{9,10},{10,11},{12,13},{... | collective-permute-start | bytes 6152 | tf_op jit(solution)/shard_map/ppermute | solution.py:18
  108.5 5.0 %collective-permute-start.20 = (f32[16,8,128]{2,1,0:T(8,128)}, f32[16,8,128]{2,1,0:T(8,128)S(1)}, u32[]{:S(2)}, u32[]{:S(2)}) collective-permute-start(f32[16,8,128]{2,1,0:T(8,128)} %get-tuple-element.76), channel_id=1, source_target_pairs={{0,4},{4,8},{8,12},{12,16},{16,20},{20,24},{24,28},{1,5},{5,9},{9,... | collective-permute-start | bytes 196616 | tf_op jit(solution)/shard_map/ppermute | solution.py:18
  118.0 14.1 %all-to-all-start = ((f32[256,1,32]{2,1,0:T(1,128)}), f32[256,1,32]{2,1,0:T(1,128)S(1)}, u32[]{:S(2)}, u32[]{:S(2)}) async-start(f32[256,1,32]{2,1,0:T(1,128)} %bitcast.8), calls=%async_computation | async-start | bytes 262144 | tf_op jit(solution)/shard_map/all_to_all | solution.py:33
  132.1 8.2 %collective-permute-start.18 = (f32[2,16,128]{2,1,0:T(8,128)S(1)}, f32[2,16,128]{2,1,0:T(8,128)S(1)}, u32[]{:S(2)}, u32[]{:S(2)}) collective-permute-start(f32[2,16,128]{2,1,0:T(8,128)S(1)} %copy-done.32), channel_id=1, source_target_pairs={{0,32},{32,64},{64,96},{96,128},{128,160},{160,192},{192,224},{1,3... | collective-permute-start | bytes 49160 | tf_op jit(solution)/shard_map/ppermute | solution.py:18
  140.3 1.9 %collective-permute-start.19 = (f32[2,16,128]{2,1,0:T(8,128)S(1)}, f32[2,16,128]{2,1,0:T(8,128)S(1)}, u32[]{:S(2)}, u32[]{:S(2)}) collective-permute-start(f32[2,16,128]{2,1,0:T(8,128)S(1)} %copy-done.31), channel_id=1, source_target_pairs={{32,0},{64,32},{96,64},{128,96},{160,128},{192,160},{224,192},{33,... | collective-permute-start | bytes 49160 | tf_op jit(solution)/shard_map/ppermute | solution.py:23
  142.2 9.7 %collective-permute-done.19.refs_9_ = f32[2,16,128]{2,1,0:T(8,128)S(1)} collective-permute-done((f32[2,16,128]{2,1,0:T(8,128)S(1)}, f32[2,16,128]{2,1,0:T(8,128)S(1)}, u32[]{:S(2)}, u32[]{:S(2)}) %collective-permute-start.19) | collective-permute-done | bytes 16416 | tf_op jit(solution)/shard_map/ppermute | solution.py:23
  152.6 3.3 %shard_map.124 = (f32[16,16,128]{2,1,0:T(8,128)}, f32[3,16,16,128]{3,2,1,0:T(8,128)}, f32[16,16,1]{2,1,0:T(8,128)}, f32[2,16,128]{2,1,0:T(8,128)}, f32[16,2,128]...) custom-call(f32[64]{0:T(128)} %compare_select_fusion.5.refs_0_, ...), custom_call_target="tpu_custom_call" | custom-call | flops 2621440 | bytes 1572864 | tf_op jit(solution)/shard_map/pallas_call | solution.py:221
  (140 shorter events, 30.6 us)
Async XLA Ops:
  4.0 18.9 %collective-permute-start.4 = (f32[16,16,4]{2,1,0:T(8,128)S(1)}, f32[16,16,4]{2,1,0:T(8,128)S(1)}, u32[]{:S(2)}, u32[]{:S(2)}) collective-permute-start(f32[16,16,4]{2,1,0:T(8,128)S(1)} %copy.20), channel_id=1, source_target_pairs={{0,1},{1,2},{2,3},{4,5},{5,6},{6,7},{8,9},{9,10},{10,11},{12,13},{... | collective-permute-start | bytes 12296 | tf_op jit(solution)/shard_map/ppermute | solution.py:18
  8.3 18.1 %collective-permute-start.5 = (f32[16,16,4]{2,1,0:T(8,128)S(1)}, f32[16,16,4]{2,1,0:T(8,128)S(1)}, u32[]{:S(2)}, u32[]{:S(2)}) collective-permute-start(f32[16,16,4]{2,1,0:T(8,128)S(1)} %copy.23), channel_id=1, source_target_pairs={{1,0},{2,1},{3,2},{5,4},{6,5},{7,6},{9,8},{10,9},{11,10},{13,12},{... | collective-permute-start | bytes 12296 | tf_op jit(solution)/shard_map/ppermute | solution.py:23
  9.7 25.0 %collective-permute-start.2 = (f32[16,10,128]{2,1,0:T(8,128)S(1)}, f32[16,10,128]{2,1,0:T(8,128)S(1)}, u32[]{:S(2)}, u32[]{:S(2)}) collective-permute-start(f32[16,10,128]{2,1,0:T(8,128)S(1)} %pad_maximum_fusion), channel_id=1, source_target_pairs={{0,4},{4,8},{8,12},{12,16},{16,20},{20,24},{24,28},{1,5},{5,9},{9,... | collective-permute-start | bytes 245768 | tf_op jit(solution)/shard_map/ppermute | solution.py:18
  11.2 23.5 %collective-permute-start.3 = (f32[16,10,128]{2,1,0:T(8,128)S(1)}, f32[16,10,128]{2,1,0:T(8,128)S(1)}, u32[]{:S(2)}, u32[]{:S(2)}) collective-permute-start(f32[16,10,128]{2,1,0:T(8,128)S(1)} %pad_maximum_fusion.1), channel_id=1, source_target_pairs={{4,0},{8,4},{12,8},{16,12},{20,16},{24,20},{28,24},{5,1},{9,5},{13... | collective-permute-start | bytes 245768 | tf_op jit(solution)/shard_map/ppermute | solution.py:23
  13.3 13.2 %collective-permute-start = (f32[4,16,128]{2,1,0:T(8,128)S(1)}, f32[4,16,128]{2,1,0:T(8,128)S(1)}, u32[]{:S(2)}, u32[]{:S(2)}) collective-permute-start(f32[4,16,128]{2,1,0:T(8,128)S(1)} %pad_maximum_fusion.2), channel_id=1, source_target_pairs={{0,32},{32,64},{64,96},{96,128},{128,160},{160,192},{192,224},{1,3... | collective-permute-start | bytes 98312 | tf_op jit(solution)/shard_map/ppermute | solution.py:18
  22.9 11.8 %collective-permute-start.1 = (f32[4,16,128]{2,1,0:T(8,128)S(1)}, f32[4,16,128]{2,1,0:T(8,128)S(1)}, u32[]{:S(2)}, u32[]{:S(2)}) collective-permute-start(f32[4,16,128]{2,1,0:T(8,128)S(1)} %pad_maximum_fusion.3), channel_id=1, source_target_pairs={{32,0},{64,32},{96,64},{128,96},{160,128},{192,160},{224,192},{33,... | collective-permute-start | bytes 98312 | tf_op jit(solution)/shard_map/ppermute | solution.py:23
  39.6 25.1 %collective-permute-start.8 = (f32[16,8,128]{2,1,0:T(8,128)}, f32[16,8,128]{2,1,0:T(8,128)S(1)}, u32[]{:S(2)}, u32[]{:S(2)}) collective-permute-start(f32[16,8,128]{2,1,0:T(8,128)} %get-tuple-element.49), channel_id=1, source_target_pairs={{0,4},{4,8},{8,12},{12,16},{16,20},{20,24},{24,28},{1,5},{5,9},{9,... | collective-permute-start | bytes 196616 | tf_op jit(solution)/shard_map/ppermute | solution.py:18
  42.8 22.0 %collective-permute-start.9 = (f32[16,8,128]{2,1,0:T(8,128)}, f32[16,8,128]{2,1,0:T(8,128)S(1)}, u32[]{:S(2)}, u32[]{:S(2)}) collective-permute-start(f32[16,8,128]{2,1,0:T(8,128)} %get-tuple-element.50), channel_id=1, source_target_pairs={{4,0},{8,4},{12,8},{16,12},{20,16},{24,20},{28,24},{5,1},{9,5},{13... | collective-permute-start | bytes 196616 | tf_op jit(solution)/shard_map/ppermute | solution.py:23
  44.1 20.6 %collective-permute-start.6 = (f32[2,16,128]{2,1,0:T(8,128)}, f32[2,16,128]{2,1,0:T(8,128)S(1)}, u32[]{:S(2)}, u32[]{:S(2)}) collective-permute-start(f32[2,16,128]{2,1,0:T(8,128)} %get-tuple-element.47), channel_id=1, source_target_pairs={{0,32},{32,64},{64,96},{96,128},{128,160},{160,192},{192,224},{1,3... | collective-permute-start | bytes 49160 | tf_op jit(solution)/shard_map/ppermute | solution.py:18
  46.7 18.0 %collective-permute-start.7 = (f32[2,16,128]{2,1,0:T(8,128)}, f32[2,16,128]{2,1,0:T(8,128)S(1)}, u32[]{:S(2)}, u32[]{:S(2)}) collective-permute-start(f32[2,16,128]{2,1,0:T(8,128)} %get-tuple-element.48), channel_id=1, source_target_pairs={{32,0},{64,32},{96,64},{128,96},{160,128},{192,160},{224,192},{33,... | collective-permute-start | bytes 49160 | tf_op jit(solution)/shard_map/ppermute | solution.py:23
  57.3 7.4 %collective-permute-start.11 = (f32[16,16,2]{2,1,0:T(8,128)}, f32[16,16,2]{2,1,0:T(8,128)S(1)}, u32[]{:S(2)}, u32[]{:S(2)}) collective-permute-start(f32[16,16,2]{2,1,0:T(8,128)} %get-tuple-element.52), channel_id=1, source_target_pairs={{1,0},{2,1},{3,2},{5,4},{6,5},{7,6},{9,8},{10,9},{11,10},{13,12},{... | collective-permute-start | bytes 6152 | tf_op jit(solution)/shard_map/ppermute | solution.py:23
  68.8 18.1 %collective-permute-start.16 = (f32[16,16,2]{2,1,0:T(8,128)}, f32[16,16,2]{2,1,0:T(8,128)S(1)}, u32[]{:S(2)}, u32[]{:S(2)}) collective-permute-start(f32[16,16,2]{2,1,0:T(8,128)} %get-tuple-element.66), channel_id=1, source_target_pairs={{0,1},{1,2},{2,3},{4,5},{5,6},{6,7},{8,9},{9,10},{10,11},{12,13},{... | collective-permute-start | bytes 6152 | tf_op jit(solution)/shard_map/ppermute | solution.py:18
  73.0 17.6 %collective-permute-start.17 = (f32[16,16,2]{2,1,0:T(8,128)}, f32[16,16,2]{2,1,0:T(8,128)S(1)}, u32[]{:S(2)}, u32[]{:S(2)}) collective-permute-start(f32[16,16,2]{2,1,0:T(8,128)} %get-tuple-element.67), channel_id=1, source_target_pairs={{1,0},{2,1},{3,2},{5,4},{6,5},{7,6},{9,8},{10,9},{11,10},{13,12},{... | collective-permute-start | bytes 6152 | tf_op jit(solution)/shard_map/ppermute | solution.py:23
  74.3 24.4 %collective-permute-start.14 = (f32[16,8,128]{2,1,0:T(8,128)}, f32[16,8,128]{2,1,0:T(8,128)S(1)}, u32[]{:S(2)}, u32[]{:S(2)}) collective-permute-start(f32[16,8,128]{2,1,0:T(8,128)} %get-tuple-element.64), channel_id=1, source_target_pairs={{0,4},{4,8},{8,12},{12,16},{16,20},{20,24},{24,28},{1,5},{5,9},{9,... | collective-permute-start | bytes 196616 | tf_op jit(solution)/shard_map/ppermute | solution.py:18
  76.9 21.9 %collective-permute-start.15 = (f32[16,8,128]{2,1,0:T(8,128)}, f32[16,8,128]{2,1,0:T(8,128)S(1)}, u32[]{:S(2)}, u32[]{:S(2)}) collective-permute-start(f32[16,8,128]{2,1,0:T(8,128)} %get-tuple-element.65), channel_id=1, source_target_pairs={{4,0},{8,4},{12,8},{16,12},{20,16},{24,20},{28,24},{5,1},{9,5},{13... | collective-permute-start | bytes 196616 | tf_op jit(solution)/shard_map/ppermute | solution.py:23
  78.2 12.4 %collective-permute-start.12 = (f32[2,16,128]{2,1,0:T(8,128)}, f32[2,16,128]{2,1,0:T(8,128)S(1)}, u32[]{:S(2)}, u32[]{:S(2)}) collective-permute-start(f32[2,16,128]{2,1,0:T(8,128)} %get-tuple-element.62), channel_id=1, source_target_pairs={{0,32},{32,64},{64,96},{96,128},{128,160},{160,192},{192,224},{1,3... | collective-permute-start | bytes 49160 | tf_op jit(solution)/shard_map/ppermute | solution.py:18
  86.9 11.9 %collective-permute-start.13 = (f32[2,16,128]{2,1,0:T(8,128)}, f32[2,16,128]{2,1,0:T(8,128)S(1)}, u32[]{:S(2)}, u32[]{:S(2)}) collective-permute-start(f32[2,16,128]{2,1,0:T(8,128)} %get-tuple-element.63), channel_id=1, source_target_pairs={{32,0},{64,32},{96,64},{128,96},{160,128},{192,160},{224,192},{33,... | collective-permute-start | bytes 49160 | tf_op jit(solution)/shard_map/ppermute | solution.py:23
  102.7 12.1 %collective-permute-start.22 = (f32[16,16,2]{2,1,0:T(8,128)}, f32[16,16,2]{2,1,0:T(8,128)S(1)}, u32[]{:S(2)}, u32[]{:S(2)}) collective-permute-start(f32[16,16,2]{2,1,0:T(8,128)} %get-tuple-element.78), channel_id=1, source_target_pairs={{0,1},{1,2},{2,3},{4,5},{5,6},{6,7},{8,9},{9,10},{10,11},{12,13},{... | collective-permute-start | bytes 6152 | tf_op jit(solution)/shard_map/ppermute | solution.py:18
  107.2 7.6 %collective-permute-start.23 = (f32[16,16,2]{2,1,0:T(8,128)}, f32[16,16,2]{2,1,0:T(8,128)S(1)}, u32[]{:S(2)}, u32[]{:S(2)}) collective-permute-start(f32[16,16,2]{2,1,0:T(8,128)} %get-tuple-element.79), channel_id=1, source_target_pairs={{1,0},{2,1},{3,2},{5,4},{6,5},{7,6},{9,8},{10,9},{11,10},{13,12},{... | collective-permute-start | bytes 6152 | tf_op jit(solution)/shard_map/ppermute | solution.py:23
  108.5 43.4 %collective-permute-start.20 = (f32[16,8,128]{2,1,0:T(8,128)}, f32[16,8,128]{2,1,0:T(8,128)S(1)}, u32[]{:S(2)}, u32[]{:S(2)}) collective-permute-start(f32[16,8,128]{2,1,0:T(8,128)} %get-tuple-element.76), channel_id=1, source_target_pairs={{0,4},{4,8},{8,12},{12,16},{16,20},{20,24},{24,28},{1,5},{5,9},{9,... | collective-permute-start | bytes 196616 | tf_op jit(solution)/shard_map/ppermute | solution.py:18
  113.5 38.5 %collective-permute-start.21 = (f32[16,8,128]{2,1,0:T(8,128)}, f32[16,8,128]{2,1,0:T(8,128)S(1)}, u32[]{:S(2)}, u32[]{:S(2)}) collective-permute-start(f32[16,8,128]{2,1,0:T(8,128)} %get-tuple-element.77), channel_id=1, source_target_pairs={{4,0},{8,4},{12,8},{16,12},{20,16},{24,20},{28,24},{5,1},{9,5},{13... | collective-permute-start | bytes 196616 | tf_op jit(solution)/shard_map/ppermute | solution.py:23
  118.0 37.9 %all-to-all-start = ((f32[256,1,32]{2,1,0:T(1,128)}), f32[256,1,32]{2,1,0:T(1,128)S(1)}, u32[]{:S(2)}, u32[]{:S(2)}) async-start(f32[256,1,32]{2,1,0:T(1,128)} %bitcast.8), calls=%async_computation | async-start | bytes 262144 | tf_op jit(solution)/shard_map/all_to_all | solution.py:33
  132.1 10.1 %collective-permute-start.18 = (f32[2,16,128]{2,1,0:T(8,128)S(1)}, f32[2,16,128]{2,1,0:T(8,128)S(1)}, u32[]{:S(2)}, u32[]{:S(2)}) collective-permute-start(f32[2,16,128]{2,1,0:T(8,128)S(1)} %copy-done.32), channel_id=1, source_target_pairs={{0,32},{32,64},{64,96},{96,128},{128,160},{160,192},{192,224},{1,3... | collective-permute-start | bytes 49160 | tf_op jit(solution)/shard_map/ppermute | solution.py:18
  140.3 11.6 %collective-permute-start.19 = (f32[2,16,128]{2,1,0:T(8,128)S(1)}, f32[2,16,128]{2,1,0:T(8,128)S(1)}, u32[]{:S(2)}, u32[]{:S(2)}) collective-permute-start(f32[2,16,128]{2,1,0:T(8,128)S(1)} %copy-done.31), channel_id=1, source_target_pairs={{32,0},{64,32},{96,64},{128,96},{160,128},{192,160},{224,192},{33,... | collective-permute-start | bytes 49160 | tf_op jit(solution)/shard_map/ppermute | solution.py:23
  (35 other events, 209.7 us)

commit v15 on v10

--- a/solution.py
+++ b/solution.py
@@ -103,7 +103,7 @@
     yh = yh_ref[...]
     zl = zl_ref[...]
     zh = zh_ref[...]
-    pxl2, pxl1 = xl[0:1], xl[1:2]
+    pxl2, pxl1 = (xl[0:1], xl[1:2]) if first else (xl[-2:-1], xl[-1:])
     pxh1, pxh2 = xh[0:1], xh[1:2]
     yl2, yl1 = pick(yl, 1, rows - 2), pick(yl, 1, rows - 1)
     yh1, yh2 = pick(yh, 1, 0), pick(yh, 1, 1)
@@ -185,8 +185,8 @@
     new_p = jnp.where(zi == 0, new_p + jnp.broadcast_to(src_ref[instant], full), new_p)
     po_ref[...] = new_p
 
-    sxu_ref[...] = new_p[X - 2 :]
-    sxd_ref[...] = new_p[0:2]
+    sxu_ref[...] = new_p[X - sxu_ref.shape[0] :]
+    sxd_ref[...] = new_p[0 : sxd_ref.shape[0]]
     syu_ref[...] = new_p[:, Y - rows :]
     syd_ref[...] = new_p[:, 0:rows]
     zshape = szu_ref.shape
@@ -198,6 +198,7 @@
     pres = operands[2]
     X, Y, Z = pres.shape
     first = instant == 0
+    planes = rows if instant < ITERS - 2 else 2
     f32 = jnp.float32
     shapes = [
         jax.ShapeDtypeStruct((X, Y, Z), f32),
@@ -206,8 +207,8 @@
         jax.ShapeDtypeStruct((2, Y, Z), f32),
         jax.ShapeDtypeStruct((X, 2, Z), f32),
         jax.ShapeDtypeStruct((X, Y, 2), f32),
-        jax.ShapeDtypeStruct((2, Y, Z), f32),
-        jax.ShapeDtypeStruct((2, Y, Z), f32),
+        jax.ShapeDtypeStruct((planes, Y, Z), f32),
+        jax.ShapeDtypeStruct((planes, Y, Z), f32),
         jax.ShapeDtypeStruct((X, rows, Z), f32),
         jax.ShapeDtypeStruct((X, rows, Z), f32),
         jax.ShapeDtypeStruct((X, Y, 2), f32),

time: 155 us -> 153 us (0.987)
    ppermute x12, starting transfers between devices: 55.7 us -> 53.3 us  [shifted_up(): return lax.ppermute(x, axis, [(i, i + 1) for i in range(count - 1)])]
  transfers between devices with their start and end apart: 26 -> 26, of which waited for: 6 -> 7; matrix products, arithmetic and copies ran while one was open for 5% -> 5% of each run, Pallas kernels for 2% -> 2%
where the time goes in v15:
time: 153 us; the launch traced here: 152 us
  starting transfers between devices  87 us (57%)
  waiting for transfers between devices  33.7 us (22%)
  Pallas kernels  13.6 us (9%)
  local copies, waits for them, and re-layouts  12.8 us (8%)
  other arithmetic  2.71 us (2%)
    ppermute x12, starting transfers between devices, shifted_up(): return lax.ppermute(x, axis, [(i, i + 1) for i in range(count - 1)])  53.3 us
    ppermute x12, waiting for transfers between devices, shifted_down(): return lax.ppermute(x, axis, [(i + 1, i) for i in range(count - 1)])  29.7 us
    ppermute x12, starting transfers between devices, shifted_down(): return lax.ppermute(x, axis, [(i + 1, i) for i in range(count - 1)])  20 us
    pallas_call x4, Pallas kernels, run_step(): pl.pallas_call(functools.partial(step_kernel, instant, first), out_shape=...  13.6 us
    all_to_all x1, starting transfers between devices, summed_on_arrival(): parts = lax.all_to_all(in_blocks(x, dim, size), axis, 0, 0, tiled=True)  12.5 us
    unnamed x73, local copies, waits for them, and re-layouts  6.93 us
  transfers between devices with their start and end apart: 26, of which 7 were waited for; matrix products, arithmetic and copies ran while one was open for 5% of the time, Pallas kernels for 2%

profile of v15, /device:TPU:24, one launch (start us, length us, event | category | flops | bytes accessed | tf_op | source)
XLA Modules:
  0.0 152.3 jit_solution(1059985771422845974)
XLA Ops:
  4.0 3.8 %collective-permute-start.4 = (f32[16,16,4]{2,1,0:T(8,128)S(1)}, f32[16,16,4]{2,1,0:T(8,128)S(1)}, u32[]{:S(2)}, u32[]{:S(2)}) collective-permute-start(f32[16,16,4]{2,1,0:T(8,128)S(1)} %copy.20), channel_id=1, source_target_pairs={{0,1},{1,2},{2,3},{4,5},{5,6},{6,7},{8,9},{9,10},{10,11},{12,13},{... | collective-permute-start | bytes 12296 | tf_op jit(solution)/shard_map/ppermute | solution.py:18
  13.3 7.8 %collective-permute-start = (f32[4,16,128]{2,1,0:T(8,128)S(1)}, f32[4,16,128]{2,1,0:T(8,128)S(1)}, u32[]{:S(2)}, u32[]{:S(2)}) collective-permute-start(f32[4,16,128]{2,1,0:T(8,128)S(1)} %pad_maximum_fusion.2), channel_id=1, source_target_pairs={{0,32},{32,64},{64,96},{96,128},{128,160},{160,192},{192,224},{1,3... | collective-permute-start | bytes 98312 | tf_op jit(solution)/shard_map/ppermute | solution.py:18
  22.8 1.9 %collective-permute-start.1 = (f32[4,16,128]{2,1,0:T(8,128)S(1)}, f32[4,16,128]{2,1,0:T(8,128)S(1)}, u32[]{:S(2)}, u32[]{:S(2)}) collective-permute-start(f32[4,16,128]{2,1,0:T(8,128)S(1)} %pad_maximum_fusion.3), channel_id=1, source_target_pairs={{32,0},{64,32},{96,64},{128,96},{160,128},{192,160},{224,192},{33,... | collective-permute-start | bytes 98312 | tf_op jit(solution)/shard_map/ppermute | solution.py:23
  26.5 8.2 %collective-permute-done.1.refs_8_ = f32[4,16,128]{2,1,0:T(8,128)S(1)} collective-permute-done((f32[4,16,128]{2,1,0:T(8,128)S(1)}, f32[4,16,128]{2,1,0:T(8,128)S(1)}, u32[]{:S(2)}, u32[]{:S(2)}) %collective-permute-start.1) | collective-permute-done | bytes 32800 | tf_op jit(solution)/shard_map/ppermute | solution.py:23
  36.0 3.6 %shard_map.121 = (f32[16,16,128]{2,1,0:T(8,128)}, f32[3,16,16,128]{3,2,1,0:T(8,128)}, f32[16,16,1]{2,1,0:T(8,128)}, f32[2,16,128]{2,1,0:T(8,128)}, f32[16,2,128]...) custom-call(f32[64]{0:T(128)} %compare_select_fusion.5.refs_0_, ...), custom_call_target="tpu_custom_call" | custom-call | flops 2621440 | bytes 1572864 | tf_op jit(solution)/shard_map/pallas_call | solution.py:222
  41.5 3.9 %collective-permute-start.7 = (f32[8,16,128]{2,1,0:T(8,128)}, f32[8,16,128]{2,1,0:T(8,128)S(1)}, u32[]{:S(2)}, u32[]{:S(2)}) collective-permute-start(f32[8,16,128]{2,1,0:T(8,128)} %get-tuple-element.48), channel_id=1, source_target_pairs={{32,0},{64,32},{96,64},{128,96},{160,128},{192,160},{224,192},{33,... | collective-permute-start | bytes 196616 | tf_op jit(solution)/shard_map/ppermute | solution.py:23
  45.5 2.6 %collective-permute-start.8 = (f32[16,8,128]{2,1,0:T(8,128)}, f32[16,8,128]{2,1,0:T(8,128)S(1)}, u32[]{:S(2)}, u32[]{:S(2)}) collective-permute-start(f32[16,8,128]{2,1,0:T(8,128)} %get-tuple-element.49), channel_id=1, source_target_pairs={{0,4},{4,8},{8,12},{12,16},{16,20},{20,24},{24,28},{1,5},{5,9},{9,... | collective-permute-start | bytes 196616 | tf_op jit(solution)/shard_map/ppermute | solution.py:18
  49.4 4.6 %collective-permute-start.10 = (f32[16,16,2]{2,1,0:T(8,128)}, f32[16,16,2]{2,1,0:T(8,128)S(1)}, u32[]{:S(2)}, u32[]{:S(2)}) collective-permute-start(f32[16,16,2]{2,1,0:T(8,128)} %get-tuple-element.51), channel_id=1, source_target_pairs={{0,1},{1,2},{2,3},{4,5},{5,6},{6,7},{8,9},{9,10},{10,11},{12,13},{... | collective-permute-start | bytes 6152 | tf_op jit(solution)/shard_map/ppermute | solution.py:18
  53.9 2.8 %collective-permute-done.10.refs_12_ = f32[16,16,2]{2,1,0:T(8,128)S(1)} collective-permute-done((f32[16,16,2]{2,1,0:T(8,128)}, f32[16,16,2]{2,1,0:T(8,128)S(1)}, u32[]{:S(2)}, u32[]{:S(2)}) %collective-permute-start.10) | collective-permute-done | bytes 2080 | tf_op jit(solution)/shard_map/ppermute | solution.py:18
  58.0 6.1 %collective-permute-done.11.refs_13_ = f32[16,16,2]{2,1,0:T(8,128)S(1)} collective-permute-done((f32[16,16,2]{2,1,0:T(8,128)}, f32[16,16,2]{2,1,0:T(8,128)S(1)}, u32[]{:S(2)}, u32[]{:S(2)}) %collective-permute-start.11) | collective-permute-done | bytes 2080 | tf_op jit(solution)/shard_map/ppermute | solution.py:23
  64.9 3.4 %shard_map.122 = (f32[16,16,128]{2,1,0:T(8,128)}, f32[3,16,16,128]{3,2,1,0:T(8,128)}, f32[16,16,1]{2,1,0:T(8,128)}, f32[2,16,128]{2,1,0:T(8,128)}, f32[16,2,128]...) custom-call(f32[64]{0:T(128)} %compare_select_fusion.5.refs_0_, ...), custom_call_target="tpu_custom_call" | custom-call | flops 2621440 | bytes 1572864 | tf_op jit(solution)/shard_map/pallas_call | solution.py:222
  68.3 3.9 %collective-permute-start.16 = (f32[16,16,2]{2,1,0:T(8,128)}, f32[16,16,2]{2,1,0:T(8,128)S(1)}, u32[]{:S(2)}, u32[]{:S(2)}) collective-permute-start(f32[16,16,2]{2,1,0:T(8,128)} %get-tuple-element.66), channel_id=1, source_target_pairs={{0,1},{1,2},{2,3},{4,5},{5,6},{6,7},{8,9},{9,10},{10,11},{12,13},{... | collective-permute-start | bytes 6152 | tf_op jit(solution)/shard_map/ppermute | solution.py:18
  73.5 8.7 %collective-permute-start.12 = (f32[8,16,128]{2,1,0:T(8,128)}, f32[8,16,128]{2,1,0:T(8,128)S(1)}, u32[]{:S(2)}, u32[]{:S(2)}) collective-permute-start(f32[8,16,128]{2,1,0:T(8,128)} %get-tuple-element.62), channel_id=1, source_target_pairs={{0,32},{32,64},{64,96},{96,128},{128,160},{160,192},{192,224},{1,3... | collective-permute-start | bytes 196616 | tf_op jit(solution)/shard_map/ppermute | solution.py:18
  84.1 2.7 %collective-permute-start.14 = (f32[16,8,128]{2,1,0:T(8,128)}, f32[16,8,128]{2,1,0:T(8,128)S(1)}, u32[]{:S(2)}, u32[]{:S(2)}) collective-permute-start(f32[16,8,128]{2,1,0:T(8,128)} %get-tuple-element.64), channel_id=1, source_target_pairs={{0,4},{4,8},{8,12},{12,16},{16,20},{20,24},{24,28},{1,5},{5,9},{9,... | collective-permute-start | bytes 196616 | tf_op jit(solution)/shard_map/ppermute | solution.py:18
  89.9 5.2 %collective-permute-done.13.refs_9_ = f32[8,16,128]{2,1,0:T(8,128)S(1)} collective-permute-done((f32[8,16,128]{2,1,0:T(8,128)}, f32[8,16,128]{2,1,0:T(8,128)S(1)}, u32[]{:S(2)}, u32[]{:S(2)}) %collective-permute-start.13) | collective-permute-done | bytes 65568 | tf_op jit(solution)/shard_map/ppermute | solution.py:23
  95.8 3.3 %shard_map.123 = (f32[16,16,128]{2,1,0:T(8,128)}, f32[3,16,16,128]{3,2,1,0:T(8,128)}, f32[16,16,1]{2,1,0:T(8,128)}, f32[2,16,128]{2,1,0:T(8,128)}, f32[16,2,128]...) custom-call(f32[64]{0:T(128)} %compare_select_fusion.5.refs_0_, ...), custom_call_target="tpu_custom_call" | custom-call | flops 2621440 | bytes 1572864 | tf_op jit(solution)/shard_map/pallas_call | solution.py:222
  99.2 5.8 %collective-permute-start.22 = (f32[16,16,2]{2,1,0:T(8,128)}, f32[16,16,2]{2,1,0:T(8,128)S(1)}, u32[]{:S(2)}, u32[]{:S(2)}) collective-permute-start(f32[16,16,2]{2,1,0:T(8,128)} %get-tuple-element.78), channel_id=1, source_target_pairs={{0,1},{1,2},{2,3},{4,5},{5,6},{6,7},{8,9},{9,10},{10,11},{12,13},{... | collective-permute-start | bytes 6152 | tf_op jit(solution)/shard_map/ppermute | solution.py:18
  106.3 2.7 %collective-permute-start.20 = (f32[16,8,128]{2,1,0:T(8,128)}, f32[16,8,128]{2,1,0:T(8,128)S(1)}, u32[]{:S(2)}, u32[]{:S(2)}) collective-permute-start(f32[16,8,128]{2,1,0:T(8,128)} %get-tuple-element.76), channel_id=1, source_target_pairs={{0,4},{4,8},{8,12},{12,16},{16,20},{20,24},{24,28},{1,5},{5,9},{9,... | collective-permute-start | bytes 196616 | tf_op jit(solution)/shard_map/ppermute | solution.py:18
  110.3 2.9 %collective-permute-done.23.refs_13_ = f32[16,16,2]{2,1,0:T(8,128)S(1)} collective-permute-done((f32[16,16,2]{2,1,0:T(8,128)}, f32[16,16,2]{2,1,0:T(8,128)S(1)}, u32[]{:S(2)}, u32[]{:S(2)}) %collective-permute-start.23) | collective-permute-done | bytes 2080 | tf_op jit(solution)/shard_map/ppermute | solution.py:23
  116.2 12.5 %all-to-all-start = ((f32[64,1,128]{2,1,0:T(1,128)}), f32[64,1,128]{2,1,0:T(1,128)S(1)}, u32[]{:S(2)}, u32[]{:S(2)}) async-start(f32[64,1,128]{2,1,0:T(1,128)} %bitcast.9), calls=%async_computation | async-start | bytes 65536 | tf_op jit(solution)/shard_map/all_to_all | solution.py:33
  128.7 7.3 %collective-permute-start.18 = (f32[2,16,128]{2,1,0:T(8,128)S(1)}, f32[2,16,128]{2,1,0:T(8,128)S(1)}, u32[]{:S(2)}, u32[]{:S(2)}) collective-permute-start(f32[2,16,128]{2,1,0:T(8,128)S(1)} %copy-done.32), channel_id=1, source_target_pairs={{0,32},{32,64},{64,96},{96,128},{128,160},{160,192},{192,224},{1,3... | collective-permute-start | bytes 49160 | tf_op jit(solution)/shard_map/ppermute | solution.py:18
  136.1 1.9 %collective-permute-start.19 = (f32[2,16,128]{2,1,0:T(8,128)S(1)}, f32[2,16,128]{2,1,0:T(8,128)S(1)}, u32[]{:S(2)}, u32[]{:S(2)}) collective-permute-start(f32[2,16,128]{2,1,0:T(8,128)S(1)} %copy-done.31), channel_id=1, source_target_pairs={{32,0},{64,32},{96,64},{128,96},{160,128},{192,160},{224,192},{33,... | collective-permute-start | bytes 49160 | tf_op jit(solution)/shard_map/ppermute | solution.py:23
  140.5 7.2 %collective-permute-done.19.refs_9_ = f32[2,16,128]{2,1,0:T(8,128)S(1)} collective-permute-done((f32[2,16,128]{2,1,0:T(8,128)S(1)}, f32[2,16,128]{2,1,0:T(8,128)S(1)}, u32[]{:S(2)}, u32[]{:S(2)}) %collective-permute-start.19) | collective-permute-done | bytes 16416 | tf_op jit(solution)/shard_map/ppermute | solution.py:23
  148.4 3.3 %shard_map.124 = (f32[16,16,128]{2,1,0:T(8,128)}, f32[3,16,16,128]{3,2,1,0:T(8,128)}, f32[16,16,1]{2,1,0:T(8,128)}, f32[2,16,128]{2,1,0:T(8,128)}, f32[16,2,128]...) custom-call(f32[64]{0:T(128)} %compare_select_fusion.5.refs_0_, ...), custom_call_target="tpu_custom_call" | custom-call | flops 2621440 | bytes 1572864 | tf_op jit(solution)/shard_map/pallas_call | solution.py:222
  (143 shorter events, 34.6 us)
Async XLA Ops:
  4.0 18.8 %collective-permute-start.4 = (f32[16,16,4]{2,1,0:T(8,128)S(1)}, f32[16,16,4]{2,1,0:T(8,128)S(1)}, u32[]{:S(2)}, u32[]{:S(2)}) collective-permute-start(f32[16,16,4]{2,1,0:T(8,128)S(1)} %copy.20), channel_id=1, source_target_pairs={{0,1},{1,2},{2,3},{4,5},{5,6},{6,7},{8,9},{9,10},{10,11},{12,13},{... | collective-permute-start | bytes 12296 | tf_op jit(solution)/shard_map/ppermute | solution.py:18
  8.3 18.1 %collective-permute-start.5 = (f32[16,16,4]{2,1,0:T(8,128)S(1)}, f32[16,16,4]{2,1,0:T(8,128)S(1)}, u32[]{:S(2)}, u32[]{:S(2)}) collective-permute-start(f32[16,16,4]{2,1,0:T(8,128)S(1)} %copy.23), channel_id=1, source_target_pairs={{1,0},{2,1},{3,2},{5,4},{6,5},{7,6},{9,8},{10,9},{11,10},{13,12},{... | collective-permute-start | bytes 12296 | tf_op jit(solution)/shard_map/ppermute | solution.py:23
  9.7 24.9 %collective-permute-start.2 = (f32[16,10,128]{2,1,0:T(8,128)S(1)}, f32[16,10,128]{2,1,0:T(8,128)S(1)}, u32[]{:S(2)}, u32[]{:S(2)}) collective-permute-start(f32[16,10,128]{2,1,0:T(8,128)S(1)} %pad_maximum_fusion), channel_id=1, source_target_pairs={{0,4},{4,8},{8,12},{12,16},{16,20},{20,24},{24,28},{1,5},{5,9},{9,... | collective-permute-start | bytes 245768 | tf_op jit(solution)/shard_map/ppermute | solution.py:18
  11.2 23.4 %collective-permute-start.3 = (f32[16,10,128]{2,1,0:T(8,128)S(1)}, f32[16,10,128]{2,1,0:T(8,128)S(1)}, u32[]{:S(2)}, u32[]{:S(2)}) collective-permute-start(f32[16,10,128]{2,1,0:T(8,128)S(1)} %pad_maximum_fusion.1), channel_id=1, source_target_pairs={{4,0},{8,4},{12,8},{16,12},{20,16},{24,20},{28,24},{5,1},{9,5},{13... | collective-permute-start | bytes 245768 | tf_op jit(solution)/shard_map/ppermute | solution.py:23
  13.3 13.2 %collective-permute-start = (f32[4,16,128]{2,1,0:T(8,128)S(1)}, f32[4,16,128]{2,1,0:T(8,128)S(1)}, u32[]{:S(2)}, u32[]{:S(2)}) collective-permute-start(f32[4,16,128]{2,1,0:T(8,128)S(1)} %pad_maximum_fusion.2), channel_id=1, source_target_pairs={{0,32},{32,64},{64,96},{96,128},{128,160},{160,192},{192,224},{1,3... | collective-permute-start | bytes 98312 | tf_op jit(solution)/shard_map/ppermute | solution.py:18
  22.8 11.8 %collective-permute-start.1 = (f32[4,16,128]{2,1,0:T(8,128)S(1)}, f32[4,16,128]{2,1,0:T(8,128)S(1)}, u32[]{:S(2)}, u32[]{:S(2)}) collective-permute-start(f32[4,16,128]{2,1,0:T(8,128)S(1)} %pad_maximum_fusion.3), channel_id=1, source_target_pairs={{32,0},{64,32},{96,64},{128,96},{160,128},{192,160},{224,192},{33,... | collective-permute-start | bytes 98312 | tf_op jit(solution)/shard_map/ppermute | solution.py:23
  39.6 24.5 %collective-permute-start.6 = (f32[8,16,128]{2,1,0:T(8,128)}, f32[8,16,128]{2,1,0:T(8,128)S(1)}, u32[]{:S(2)}, u32[]{:S(2)}) collective-permute-start(f32[8,16,128]{2,1,0:T(8,128)} %get-tuple-element.47), channel_id=1, source_target_pairs={{0,32},{32,64},{64,96},{96,128},{128,160},{160,192},{192,224},{1,3... | collective-permute-start | bytes 196616 | tf_op jit(solution)/shard_map/ppermute | solution.py:18
  41.5 22.6 %collective-permute-start.7 = (f32[8,16,128]{2,1,0:T(8,128)}, f32[8,16,128]{2,1,0:T(8,128)S(1)}, u32[]{:S(2)}, u32[]{:S(2)}) collective-permute-start(f32[8,16,128]{2,1,0:T(8,128)} %get-tuple-element.48), channel_id=1, source_target_pairs={{32,0},{64,32},{96,64},{128,96},{160,128},{192,160},{224,192},{33,... | collective-permute-start | bytes 196616 | tf_op jit(solution)/shard_map/ppermute | solution.py:23
  45.5 18.7 %collective-permute-start.8 = (f32[16,8,128]{2,1,0:T(8,128)}, f32[16,8,128]{2,1,0:T(8,128)S(1)}, u32[]{:S(2)}, u32[]{:S(2)}) collective-permute-start(f32[16,8,128]{2,1,0:T(8,128)} %get-tuple-element.49), channel_id=1, source_target_pairs={{0,4},{4,8},{8,12},{12,16},{16,20},{20,24},{24,28},{1,5},{5,9},{9,... | collective-permute-start | bytes 196616 | tf_op jit(solution)/shard_map/ppermute | solution.py:18
  48.1 16.1 %collective-permute-start.9 = (f32[16,8,128]{2,1,0:T(8,128)}, f32[16,8,128]{2,1,0:T(8,128)S(1)}, u32[]{:S(2)}, u32[]{:S(2)}) collective-permute-start(f32[16,8,128]{2,1,0:T(8,128)} %get-tuple-element.50), channel_id=1, source_target_pairs={{4,0},{8,4},{12,8},{16,12},{20,16},{24,20},{28,24},{5,1},{9,5},{13... | collective-permute-start | bytes 196616 | tf_op jit(solution)/shard_map/ppermute | solution.py:23
  68.3 18.5 %collective-permute-start.16 = (f32[16,16,2]{2,1,0:T(8,128)}, f32[16,16,2]{2,1,0:T(8,128)S(1)}, u32[]{:S(2)}, u32[]{:S(2)}) collective-permute-start(f32[16,16,2]{2,1,0:T(8,128)} %get-tuple-element.66), channel_id=1, source_target_pairs={{0,1},{1,2},{2,3},{4,5},{5,6},{6,7},{8,9},{9,10},{10,11},{12,13},{... | collective-permute-start | bytes 6152 | tf_op jit(solution)/shard_map/ppermute | solution.py:18
  72.2 17.7 %collective-permute-start.17 = (f32[16,16,2]{2,1,0:T(8,128)}, f32[16,16,2]{2,1,0:T(8,128)S(1)}, u32[]{:S(2)}, u32[]{:S(2)}) collective-permute-start(f32[16,16,2]{2,1,0:T(8,128)} %get-tuple-element.67), channel_id=1, source_target_pairs={{1,0},{2,1},{3,2},{5,4},{6,5},{7,6},{9,8},{10,9},{11,10},{13,12},{... | collective-permute-start | bytes 6152 | tf_op jit(solution)/shard_map/ppermute | solution.py:23
  73.5 16.4 %collective-permute-start.12 = (f32[8,16,128]{2,1,0:T(8,128)}, f32[8,16,128]{2,1,0:T(8,128)S(1)}, u32[]{:S(2)}, u32[]{:S(2)}) collective-permute-start(f32[8,16,128]{2,1,0:T(8,128)} %get-tuple-element.62), channel_id=1, source_target_pairs={{0,32},{32,64},{64,96},{96,128},{128,160},{160,192},{192,224},{1,3... | collective-permute-start | bytes 196616 | tf_op jit(solution)/shard_map/ppermute | solution.py:18
  82.2 13.0 %collective-permute-start.13 = (f32[8,16,128]{2,1,0:T(8,128)}, f32[8,16,128]{2,1,0:T(8,128)S(1)}, u32[]{:S(2)}, u32[]{:S(2)}) collective-permute-start(f32[8,16,128]{2,1,0:T(8,128)} %get-tuple-element.63), channel_id=1, source_target_pairs={{32,0},{64,32},{96,64},{128,96},{160,128},{192,160},{224,192},{33,... | collective-permute-start | bytes 196616 | tf_op jit(solution)/shard_map/ppermute | solution.py:23
  84.1 11.1 %collective-permute-start.14 = (f32[16,8,128]{2,1,0:T(8,128)}, f32[16,8,128]{2,1,0:T(8,128)S(1)}, u32[]{:S(2)}, u32[]{:S(2)}) collective-permute-start(f32[16,8,128]{2,1,0:T(8,128)} %get-tuple-element.64), channel_id=1, source_target_pairs={{0,4},{4,8},{8,12},{12,16},{16,20},{20,24},{24,28},{1,5},{5,9},{9,... | collective-permute-start | bytes 196616 | tf_op jit(solution)/shard_map/ppermute | solution.py:18
  86.8 8.4 %collective-permute-start.15 = (f32[16,8,128]{2,1,0:T(8,128)}, f32[16,8,128]{2,1,0:T(8,128)S(1)}, u32[]{:S(2)}, u32[]{:S(2)}) collective-permute-start(f32[16,8,128]{2,1,0:T(8,128)} %get-tuple-element.65), channel_id=1, source_target_pairs={{4,0},{8,4},{12,8},{16,12},{20,16},{24,20},{28,24},{5,1},{9,5},{13... | collective-permute-start | bytes 196616 | tf_op jit(solution)/shard_map/ppermute | solution.py:23
  99.2 11.1 %collective-permute-start.22 = (f32[16,16,2]{2,1,0:T(8,128)}, f32[16,16,2]{2,1,0:T(8,128)S(1)}, u32[]{:S(2)}, u32[]{:S(2)}) collective-permute-start(f32[16,16,2]{2,1,0:T(8,128)} %get-tuple-element.78), channel_id=1, source_target_pairs={{0,1},{1,2},{2,3},{4,5},{5,6},{6,7},{8,9},{9,10},{10,11},{12,13},{... | collective-permute-start | bytes 6152 | tf_op jit(solution)/shard_map/ppermute | solution.py:18
  105.0 8.3 %collective-permute-start.23 = (f32[16,16,2]{2,1,0:T(8,128)}, f32[16,16,2]{2,1,0:T(8,128)S(1)}, u32[]{:S(2)}, u32[]{:S(2)}) collective-permute-start(f32[16,16,2]{2,1,0:T(8,128)} %get-tuple-element.79), channel_id=1, source_target_pairs={{1,0},{2,1},{3,2},{5,4},{6,5},{7,6},{9,8},{10,9},{11,10},{13,12},{... | collective-permute-start | bytes 6152 | tf_op jit(solution)/shard_map/ppermute | solution.py:23
  106.3 41.4 %collective-permute-start.20 = (f32[16,8,128]{2,1,0:T(8,128)}, f32[16,8,128]{2,1,0:T(8,128)S(1)}, u32[]{:S(2)}, u32[]{:S(2)}) collective-permute-start(f32[16,8,128]{2,1,0:T(8,128)} %get-tuple-element.76), channel_id=1, source_target_pairs={{0,4},{4,8},{8,12},{12,16},{16,20},{20,24},{24,28},{1,5},{5,9},{9,... | collective-permute-start | bytes 196616 | tf_op jit(solution)/shard_map/ppermute | solution.py:18
  109.0 38.7 %collective-permute-start.21 = (f32[16,8,128]{2,1,0:T(8,128)}, f32[16,8,128]{2,1,0:T(8,128)S(1)}, u32[]{:S(2)}, u32[]{:S(2)}) collective-permute-start(f32[16,8,128]{2,1,0:T(8,128)} %get-tuple-element.77), channel_id=1, source_target_pairs={{4,0},{8,4},{12,8},{16,12},{20,16},{24,20},{28,24},{5,1},{9,5},{13... | collective-permute-start | bytes 196616 | tf_op jit(solution)/shard_map/ppermute | solution.py:23
  116.2 22.9 %all-to-all-start = ((f32[64,1,128]{2,1,0:T(1,128)}), f32[64,1,128]{2,1,0:T(1,128)S(1)}, u32[]{:S(2)}, u32[]{:S(2)}) async-start(f32[64,1,128]{2,1,0:T(1,128)} %bitcast.9), calls=%async_computation | async-start | bytes 65536 | tf_op jit(solution)/shard_map/all_to_all | solution.py:33
  128.7 11.8 %collective-permute-start.18 = (f32[2,16,128]{2,1,0:T(8,128)S(1)}, f32[2,16,128]{2,1,0:T(8,128)S(1)}, u32[]{:S(2)}, u32[]{:S(2)}) collective-permute-start(f32[2,16,128]{2,1,0:T(8,128)S(1)} %copy-done.32), channel_id=1, source_target_pairs={{0,32},{32,64},{64,96},{96,128},{128,160},{160,192},{192,224},{1,3... | collective-permute-start | bytes 49160 | tf_op jit(solution)/shard_map/ppermute | solution.py:18
  136.1 11.6 %collective-permute-start.19 = (f32[2,16,128]{2,1,0:T(8,128)S(1)}, f32[2,16,128]{2,1,0:T(8,128)S(1)}, u32[]{:S(2)}, u32[]{:S(2)}) collective-permute-start(f32[2,16,128]{2,1,0:T(8,128)S(1)} %copy-done.31), channel_id=1, source_target_pairs={{32,0},{64,32},{96,64},{128,96},{160,128},{192,160},{224,192},{33,... | collective-permute-start | bytes 49160 | tf_op jit(solution)/shard_map/ppermute | solution.py:23
  139.2 12.5 %collective-permute-start.24 = (f32[128]{0:T(128)S(1)}, f32[128]{0:T(128)S(1)}, u32[]{:S(2)}, u32[]{:S(2)}) collective-permute-start(f32[128]{0:T(128)S(1)} %reduce_sum.9), channel_id=1, source_target_pairs={{1,0},{2,3},{5,4},{6,7},{9,8},{10,11},{13,12},{14,15},{17,16},{18,... | collective-permute-start | bytes 1544 | tf_op jit(solution)/shard_map/ppermute | solution.py:349
  (36 other events, 206.2 us)

commit v16 on v15

--- a/solution.py
+++ b/solution.py
@@ -198,7 +198,7 @@
     pres = operands[2]
     X, Y, Z = pres.shape
     first = instant == 0
-    planes = rows if instant < ITERS - 2 else 2
+    planes = (rows if instant == 0 else X) if instant < ITERS - 2 else 2
     f32 = jnp.float32
     shapes = [
         jax.ShapeDtypeStruct((X, Y, Z), f32),

time: 153 us -> 154 us (level)
  waiting for transfers between devices: 33.7 us -> 30.2 us
  starting transfers between devices: 87 us -> 90.5 us
    ppermute x12, waiting for transfers between devices: 29.7 us -> 26.1 us  [shifted_down(): return lax.ppermute(x, axis, [(i + 1, i) for i in range(count - 1)])]
    all_to_all x1, starting transfers between devices: 12.5 us -> 15.4 us  [summed_on_arrival(): parts = lax.all_to_all(in_blocks(x, dim, size), axis, 0, 0, tiled=True)]
  transfers between devices with their start and end apart: 26 -> 26, of which waited for: 7 -> 8; matrix products, arithmetic and copies ran while one was open for 5% -> 5% of each run, Pallas kernels for 2% -> 2%
where the time goes in v16:
time: 154 us; the launch traced here: 153 us
  starting transfers between devices  90.5 us (59%)
  waiting for transfers between devices  30.2 us (20%)
  Pallas kernels  13.7 us (9%)
  local copies, waits for them, and re-layouts  12.8 us (8%)
  other arithmetic  2.77 us (2%)
    ppermute x12, starting transfers between devices, shifted_up(): return lax.ppermute(x, axis, [(i, i + 1) for i in range(count - 1)])  53.9 us
    ppermute x12, waiting for transfers between devices, shifted_down(): return lax.ppermute(x, axis, [(i + 1, i) for i in range(count - 1)])  26.1 us
    ppermute x12, starting transfers between devices, shifted_down(): return lax.ppermute(x, axis, [(i + 1, i) for i in range(count - 1)])  20 us
    all_to_all x1, starting transfers between devices, summed_on_arrival(): parts = lax.all_to_all(in_blocks(x, dim, size), axis, 0, 0, tiled=True)  15.4 us
    pallas_call x4, Pallas kernels, run_step(): pl.pallas_call(functools.partial(step_kernel, instant, first), out_shape=...  13.7 us
    unnamed x73, local copies, waits for them, and re-layouts  6.97 us
  transfers between devices with their start and end apart: 26, of which 8 were waited for; matrix products, arithmetic and copies ran while one was open for 5% of the time, Pallas kernels for 2%

profile of v16, /device:TPU:24, one launch (start us, length us, event | category | flops | bytes accessed | tf_op | source)
XLA Modules:
  0.0 152.5 jit_solution(3335571599232472899)
XLA Ops:
  4.0 3.8 %collective-permute-start.4 = (f32[16,16,4]{2,1,0:T(8,128)S(1)}, f32[16,16,4]{2,1,0:T(8,128)S(1)}, u32[]{:S(2)}, u32[]{:S(2)}) collective-permute-start(f32[16,16,4]{2,1,0:T(8,128)S(1)} %copy.20), channel_id=1, source_target_pairs={{0,1},{1,2},{2,3},{4,5},{5,6},{6,7},{8,9},{9,10},{10,11},{12,13},{... | collective-permute-start | bytes 12296 | tf_op jit(solution)/shard_map/ppermute | solution.py:18
  13.3 7.8 %collective-permute-start = (f32[4,16,128]{2,1,0:T(8,128)S(1)}, f32[4,16,128]{2,1,0:T(8,128)S(1)}, u32[]{:S(2)}, u32[]{:S(2)}) collective-permute-start(f32[4,16,128]{2,1,0:T(8,128)S(1)} %pad_maximum_fusion.2), channel_id=1, source_target_pairs={{0,32},{32,64},{64,96},{96,128},{128,160},{160,192},{192,224},{1,3... | collective-permute-start | bytes 98312 | tf_op jit(solution)/shard_map/ppermute | solution.py:18
  22.8 1.9 %collective-permute-start.1 = (f32[4,16,128]{2,1,0:T(8,128)S(1)}, f32[4,16,128]{2,1,0:T(8,128)S(1)}, u32[]{:S(2)}, u32[]{:S(2)}) collective-permute-start(f32[4,16,128]{2,1,0:T(8,128)S(1)} %pad_maximum_fusion.3), channel_id=1, source_target_pairs={{32,0},{64,32},{96,64},{128,96},{160,128},{192,160},{224,192},{33,... | collective-permute-start | bytes 98312 | tf_op jit(solution)/shard_map/ppermute | solution.py:23
  26.5 8.2 %collective-permute-done.1.refs_8_ = f32[4,16,128]{2,1,0:T(8,128)S(1)} collective-permute-done((f32[4,16,128]{2,1,0:T(8,128)S(1)}, f32[4,16,128]{2,1,0:T(8,128)S(1)}, u32[]{:S(2)}, u32[]{:S(2)}) %collective-permute-start.1) | collective-permute-done | bytes 32800 | tf_op jit(solution)/shard_map/ppermute | solution.py:23
  36.0 3.6 %shard_map.121 = (f32[16,16,128]{2,1,0:T(8,128)}, f32[3,16,16,128]{3,2,1,0:T(8,128)}, f32[16,16,1]{2,1,0:T(8,128)}, f32[2,16,128]{2,1,0:T(8,128)}, f32[16,2,128]...) custom-call(f32[64]{0:T(128)} %compare_select_fusion.5.refs_0_, ...), custom_call_target="tpu_custom_call" | custom-call | flops 2621440 | bytes 1572864 | tf_op jit(solution)/shard_map/pallas_call | solution.py:222
  39.6 1.9 %collective-permute-start.6 = (f32[8,16,128]{2,1,0:T(8,128)}, f32[8,16,128]{2,1,0:T(8,128)S(1)}, u32[]{:S(2)}, u32[]{:S(2)}) collective-permute-start(f32[8,16,128]{2,1,0:T(8,128)} %get-tuple-element.47), channel_id=1, source_target_pairs={{0,32},{32,64},{64,96},{96,128},{128,160},{160,192},{192,224},{1,3... | collective-permute-start | bytes 196616 | tf_op jit(solution)/shard_map/ppermute | solution.py:18
  41.5 3.9 %collective-permute-start.7 = (f32[8,16,128]{2,1,0:T(8,128)}, f32[8,16,128]{2,1,0:T(8,128)S(1)}, u32[]{:S(2)}, u32[]{:S(2)}) collective-permute-start(f32[8,16,128]{2,1,0:T(8,128)} %get-tuple-element.48), channel_id=1, source_target_pairs={{32,0},{64,32},{96,64},{128,96},{160,128},{192,160},{224,192},{33,... | collective-permute-start | bytes 196616 | tf_op jit(solution)/shard_map/ppermute | solution.py:23
  45.5 2.6 %collective-permute-start.8 = (f32[16,8,128]{2,1,0:T(8,128)}, f32[16,8,128]{2,1,0:T(8,128)S(1)}, u32[]{:S(2)}, u32[]{:S(2)}) collective-permute-start(f32[16,8,128]{2,1,0:T(8,128)} %get-tuple-element.49), channel_id=1, source_target_pairs={{0,4},{4,8},{8,12},{12,16},{16,20},{20,24},{24,28},{1,5},{5,9},{9,... | collective-permute-start | bytes 196616 | tf_op jit(solution)/shard_map/ppermute | solution.py:18
  49.4 4.6 %collective-permute-start.10 = (f32[16,16,2]{2,1,0:T(8,128)}, f32[16,16,2]{2,1,0:T(8,128)S(1)}, u32[]{:S(2)}, u32[]{:S(2)}) collective-permute-start(f32[16,16,2]{2,1,0:T(8,128)} %get-tuple-element.51), channel_id=1, source_target_pairs={{0,1},{1,2},{2,3},{4,5},{5,6},{6,7},{8,9},{9,10},{10,11},{12,13},{... | collective-permute-start | bytes 6152 | tf_op jit(solution)/shard_map/ppermute | solution.py:18
  53.9 2.8 %collective-permute-done.10.refs_12_ = f32[16,16,2]{2,1,0:T(8,128)S(1)} collective-permute-done((f32[16,16,2]{2,1,0:T(8,128)}, f32[16,16,2]{2,1,0:T(8,128)S(1)}, u32[]{:S(2)}, u32[]{:S(2)}) %collective-permute-start.10) | collective-permute-done | bytes 2080 | tf_op jit(solution)/shard_map/ppermute | solution.py:18
  58.0 6.1 %collective-permute-done.11.refs_13_ = f32[16,16,2]{2,1,0:T(8,128)S(1)} collective-permute-done((f32[16,16,2]{2,1,0:T(8,128)}, f32[16,16,2]{2,1,0:T(8,128)S(1)}, u32[]{:S(2)}, u32[]{:S(2)}) %collective-permute-start.11) | collective-permute-done | bytes 2080 | tf_op jit(solution)/shard_map/ppermute | solution.py:23
  64.9 3.4 %shard_map.122 = (f32[16,16,128]{2,1,0:T(8,128)}, f32[3,16,16,128]{3,2,1,0:T(8,128)}, f32[16,16,1]{2,1,0:T(8,128)}, f32[2,16,128]{2,1,0:T(8,128)}, f32[16,2,128]...) custom-call(f32[64]{0:T(128)} %compare_select_fusion.5.refs_0_, ...), custom_call_target="tpu_custom_call" | custom-call | flops 2621440 | bytes 1572864 | tf_op jit(solution)/shard_map/pallas_call | solution.py:222
  68.3 8.7 %collective-permute-start.12 = (f32[16,16,128]{2,1,0:T(8,128)}, f32[16,16,128]{2,1,0:T(8,128)S(1)}, u32[]{:S(2)}, u32[]{:S(2)}) collective-permute-start(f32[16,16,128]{2,1,0:T(8,128)} %get-tuple-element.62), channel_id=1, source_target_pairs={{0,32},{32,64},{64,96},{96,128},{128,160},{160,192},{192,224},{1,3... | collective-permute-start | bytes 393224 | tf_op jit(solution)/shard_map/ppermute | solution.py:18
  78.9 3.9 %collective-permute-start.16 = (f32[16,16,2]{2,1,0:T(8,128)}, f32[16,16,2]{2,1,0:T(8,128)S(1)}, u32[]{:S(2)}, u32[]{:S(2)}) collective-permute-start(f32[16,16,2]{2,1,0:T(8,128)} %get-tuple-element.66), channel_id=1, source_target_pairs={{0,1},{1,2},{2,3},{4,5},{5,6},{6,7},{8,9},{9,10},{10,11},{12,13},{... | collective-permute-start | bytes 6152 | tf_op jit(solution)/shard_map/ppermute | solution.py:18
  84.2 2.7 %collective-permute-start.14 = (f32[16,8,128]{2,1,0:T(8,128)}, f32[16,8,128]{2,1,0:T(8,128)S(1)}, u32[]{:S(2)}, u32[]{:S(2)}) collective-permute-start(f32[16,8,128]{2,1,0:T(8,128)} %get-tuple-element.64), channel_id=1, source_target_pairs={{0,4},{4,8},{8,12},{12,16},{16,20},{20,24},{24,28},{1,5},{5,9},{9,... | collective-permute-start | bytes 196616 | tf_op jit(solution)/shard_map/ppermute | solution.py:18
  91.2 3.5 %collective-permute-done.15.refs_11_ = f32[16,8,128]{2,1,0:T(8,128)S(1)} collective-permute-done((f32[16,8,128]{2,1,0:T(8,128)}, f32[16,8,128]{2,1,0:T(8,128)S(1)}, u32[]{:S(2)}, u32[]{:S(2)}) %collective-permute-start.15) | collective-permute-done | bytes 65568 | tf_op jit(solution)/shard_map/ppermute | solution.py:23
  95.4 3.4 %shard_map.123 = (f32[16,16,128]{2,1,0:T(8,128)}, f32[3,16,16,128]{3,2,1,0:T(8,128)}, f32[16,16,1]{2,1,0:T(8,128)}, f32[2,16,128]{2,1,0:T(8,128)}, f32[16,2,128]...) custom-call(f32[64]{0:T(128)} %compare_select_fusion.5.refs_0_, ...), custom_call_target="tpu_custom_call" | custom-call | flops 2621440 | bytes 1572864 | tf_op jit(solution)/shard_map/pallas_call | solution.py:222
  98.8 4.6 %collective-permute-start.22 = (f32[16,16,2]{2,1,0:T(8,128)}, f32[16,16,2]{2,1,0:T(8,128)S(1)}, u32[]{:S(2)}, u32[]{:S(2)}) collective-permute-start(f32[16,16,2]{2,1,0:T(8,128)} %get-tuple-element.78), channel_id=1, source_target_pairs={{0,1},{1,2},{2,3},{4,5},{5,6},{6,7},{8,9},{9,10},{10,11},{12,13},{... | collective-permute-start | bytes 6152 | tf_op jit(solution)/shard_map/ppermute | solution.py:18
  104.6 4.6 %collective-permute-start.20 = (f32[16,8,128]{2,1,0:T(8,128)}, f32[16,8,128]{2,1,0:T(8,128)S(1)}, u32[]{:S(2)}, u32[]{:S(2)}) collective-permute-start(f32[16,8,128]{2,1,0:T(8,128)} %get-tuple-element.76), channel_id=1, source_target_pairs={{0,4},{4,8},{8,12},{12,16},{16,20},{20,24},{24,28},{1,5},{5,9},{9,... | collective-permute-start | bytes 196616 | tf_op jit(solution)/shard_map/ppermute | solution.py:18
  113.5 15.4 %all-to-all-start = ((f32[64,1,128]{2,1,0:T(1,128)}), f32[64,1,128]{2,1,0:T(1,128)S(1)}, u32[]{:S(2)}, u32[]{:S(2)}) async-start(f32[64,1,128]{2,1,0:T(1,128)} %bitcast.9), calls=%async_computation | async-start | bytes 65536 | tf_op jit(solution)/shard_map/all_to_all | solution.py:33
  128.9 7.3 %collective-permute-start.18 = (f32[2,16,128]{2,1,0:T(8,128)S(1)}, f32[2,16,128]{2,1,0:T(8,128)S(1)}, u32[]{:S(2)}, u32[]{:S(2)}) collective-permute-start(f32[2,16,128]{2,1,0:T(8,128)S(1)} %copy-done.32), channel_id=1, source_target_pairs={{0,32},{32,64},{64,96},{96,128},{128,160},{160,192},{192,224},{1,3... | collective-permute-start | bytes 49160 | tf_op jit(solution)/shard_map/ppermute | solution.py:18
  136.3 1.9 %collective-permute-start.19 = (f32[2,16,128]{2,1,0:T(8,128)S(1)}, f32[2,16,128]{2,1,0:T(8,128)S(1)}, u32[]{:S(2)}, u32[]{:S(2)}) collective-permute-start(f32[2,16,128]{2,1,0:T(8,128)S(1)} %copy-done.31), channel_id=1, source_target_pairs={{32,0},{64,32},{96,64},{128,96},{160,128},{192,160},{224,192},{33,... | collective-permute-start | bytes 49160 | tf_op jit(solution)/shard_map/ppermute | solution.py:23
  140.7 7.2 %collective-permute-done.19.refs_9_ = f32[2,16,128]{2,1,0:T(8,128)S(1)} collective-permute-done((f32[2,16,128]{2,1,0:T(8,128)S(1)}, f32[2,16,128]{2,1,0:T(8,128)S(1)}, u32[]{:S(2)}, u32[]{:S(2)}) %collective-permute-start.19) | collective-permute-done | bytes 16416 | tf_op jit(solution)/shard_map/ppermute | solution.py:23
  148.6 3.3 %shard_map.124 = (f32[16,16,128]{2,1,0:T(8,128)}, f32[3,16,16,128]{3,2,1,0:T(8,128)}, f32[16,16,1]{2,1,0:T(8,128)}, f32[2,16,128]{2,1,0:T(8,128)}, f32[16,2,128]...) custom-call(f32[64]{0:T(128)} %compare_select_fusion.5.refs_0_, ...), custom_call_target="tpu_custom_call" | custom-call | flops 2621440 | bytes 1572864 | tf_op jit(solution)/shard_map/pallas_call | solution.py:222
  (143 shorter events, 34.1 us)
Async XLA Ops:
  4.0 18.8 %collective-permute-start.4 = (f32[16,16,4]{2,1,0:T(8,128)S(1)}, f32[16,16,4]{2,1,0:T(8,128)S(1)}, u32[]{:S(2)}, u32[]{:S(2)}) collective-permute-start(f32[16,16,4]{2,1,0:T(8,128)S(1)} %copy.20), channel_id=1, source_target_pairs={{0,1},{1,2},{2,3},{4,5},{5,6},{6,7},{8,9},{9,10},{10,11},{12,13},{... | collective-permute-start | bytes 12296 | tf_op jit(solution)/shard_map/ppermute | solution.py:18
  8.3 18.1 %collective-permute-start.5 = (f32[16,16,4]{2,1,0:T(8,128)S(1)}, f32[16,16,4]{2,1,0:T(8,128)S(1)}, u32[]{:S(2)}, u32[]{:S(2)}) collective-permute-start(f32[16,16,4]{2,1,0:T(8,128)S(1)} %copy.23), channel_id=1, source_target_pairs={{1,0},{2,1},{3,2},{5,4},{6,5},{7,6},{9,8},{10,9},{11,10},{13,12},{... | collective-permute-start | bytes 12296 | tf_op jit(solution)/shard_map/ppermute | solution.py:23
  9.7 24.9 %collective-permute-start.2 = (f32[16,10,128]{2,1,0:T(8,128)S(1)}, f32[16,10,128]{2,1,0:T(8,128)S(1)}, u32[]{:S(2)}, u32[]{:S(2)}) collective-permute-start(f32[16,10,128]{2,1,0:T(8,128)S(1)} %pad_maximum_fusion), channel_id=1, source_target_pairs={{0,4},{4,8},{8,12},{12,16},{16,20},{20,24},{24,28},{1,5},{5,9},{9,... | collective-permute-start | bytes 245768 | tf_op jit(solution)/shard_map/ppermute | solution.py:18
  11.2 23.4 %collective-permute-start.3 = (f32[16,10,128]{2,1,0:T(8,128)S(1)}, f32[16,10,128]{2,1,0:T(8,128)S(1)}, u32[]{:S(2)}, u32[]{:S(2)}) collective-permute-start(f32[16,10,128]{2,1,0:T(8,128)S(1)} %pad_maximum_fusion.1), channel_id=1, source_target_pairs={{4,0},{8,4},{12,8},{16,12},{20,16},{24,20},{28,24},{5,1},{9,5},{13... | collective-permute-start | bytes 245768 | tf_op jit(solution)/shard_map/ppermute | solution.py:23
  13.3 13.2 %collective-permute-start = (f32[4,16,128]{2,1,0:T(8,128)S(1)}, f32[4,16,128]{2,1,0:T(8,128)S(1)}, u32[]{:S(2)}, u32[]{:S(2)}) collective-permute-start(f32[4,16,128]{2,1,0:T(8,128)S(1)} %pad_maximum_fusion.2), channel_id=1, source_target_pairs={{0,32},{32,64},{64,96},{96,128},{128,160},{160,192},{192,224},{1,3... | collective-permute-start | bytes 98312 | tf_op jit(solution)/shard_map/ppermute | solution.py:18
  22.8 11.8 %collective-permute-start.1 = (f32[4,16,128]{2,1,0:T(8,128)S(1)}, f32[4,16,128]{2,1,0:T(8,128)S(1)}, u32[]{:S(2)}, u32[]{:S(2)}) collective-permute-start(f32[4,16,128]{2,1,0:T(8,128)S(1)} %pad_maximum_fusion.3), channel_id=1, source_target_pairs={{32,0},{64,32},{96,64},{128,96},{160,128},{192,160},{224,192},{33,... | collective-permute-start | bytes 98312 | tf_op jit(solution)/shard_map/ppermute | solution.py:23
  39.6 24.5 %collective-permute-start.6 = (f32[8,16,128]{2,1,0:T(8,128)}, f32[8,16,128]{2,1,0:T(8,128)S(1)}, u32[]{:S(2)}, u32[]{:S(2)}) collective-permute-start(f32[8,16,128]{2,1,0:T(8,128)} %get-tuple-element.47), channel_id=1, source_target_pairs={{0,32},{32,64},{64,96},{96,128},{128,160},{160,192},{192,224},{1,3... | collective-permute-start | bytes 196616 | tf_op jit(solution)/shard_map/ppermute | solution.py:18
  41.5 22.6 %collective-permute-start.7 = (f32[8,16,128]{2,1,0:T(8,128)}, f32[8,16,128]{2,1,0:T(8,128)S(1)}, u32[]{:S(2)}, u32[]{:S(2)}) collective-permute-start(f32[8,16,128]{2,1,0:T(8,128)} %get-tuple-element.48), channel_id=1, source_target_pairs={{32,0},{64,32},{96,64},{128,96},{160,128},{192,160},{224,192},{33,... | collective-permute-start | bytes 196616 | tf_op jit(solution)/shard_map/ppermute | solution.py:23
  45.5 18.7 %collective-permute-start.8 = (f32[16,8,128]{2,1,0:T(8,128)}, f32[16,8,128]{2,1,0:T(8,128)S(1)}, u32[]{:S(2)}, u32[]{:S(2)}) collective-permute-start(f32[16,8,128]{2,1,0:T(8,128)} %get-tuple-element.49), channel_id=1, source_target_pairs={{0,4},{4,8},{8,12},{12,16},{16,20},{20,24},{24,28},{1,5},{5,9},{9,... | collective-permute-start | bytes 196616 | tf_op jit(solution)/shard_map/ppermute | solution.py:18
  48.1 16.1 %collective-permute-start.9 = (f32[16,8,128]{2,1,0:T(8,128)}, f32[16,8,128]{2,1,0:T(8,128)S(1)}, u32[]{:S(2)}, u32[]{:S(2)}) collective-permute-start(f32[16,8,128]{2,1,0:T(8,128)} %get-tuple-element.50), channel_id=1, source_target_pairs={{4,0},{8,4},{12,8},{16,12},{20,16},{24,20},{28,24},{5,1},{9,5},{13... | collective-permute-start | bytes 196616 | tf_op jit(solution)/shard_map/ppermute | solution.py:23
  49.4 7.4 %collective-permute-start.10 = (f32[16,16,2]{2,1,0:T(8,128)}, f32[16,16,2]{2,1,0:T(8,128)S(1)}, u32[]{:S(2)}, u32[]{:S(2)}) collective-permute-start(f32[16,16,2]{2,1,0:T(8,128)} %get-tuple-element.51), channel_id=1, source_target_pairs={{0,1},{1,2},{2,3},{4,5},{5,6},{6,7},{8,9},{9,10},{10,11},{12,13},{... | collective-permute-start | bytes 6152 | tf_op jit(solution)/shard_map/ppermute | solution.py:18
  56.8 7.4 %collective-permute-start.11 = (f32[16,16,2]{2,1,0:T(8,128)}, f32[16,16,2]{2,1,0:T(8,128)S(1)}, u32[]{:S(2)}, u32[]{:S(2)}) collective-permute-start(f32[16,16,2]{2,1,0:T(8,128)} %get-tuple-element.52), channel_id=1, source_target_pairs={{1,0},{2,1},{3,2},{5,4},{6,5},{7,6},{9,8},{10,9},{11,10},{13,12},{... | collective-permute-start | bytes 6152 | tf_op jit(solution)/shard_map/ppermute | solution.py:23
  68.3 26.3 %collective-permute-start.12 = (f32[16,16,128]{2,1,0:T(8,128)}, f32[16,16,128]{2,1,0:T(8,128)S(1)}, u32[]{:S(2)}, u32[]{:S(2)}) collective-permute-start(f32[16,16,128]{2,1,0:T(8,128)} %get-tuple-element.62), channel_id=1, source_target_pairs={{0,32},{32,64},{64,96},{96,128},{128,160},{160,192},{192,224},{1,3... | collective-permute-start | bytes 393224 | tf_op jit(solution)/shard_map/ppermute | solution.py:18
  77.0 17.7 %collective-permute-start.13 = (f32[16,16,128]{2,1,0:T(8,128)}, f32[16,16,128]{2,1,0:T(8,128)S(1)}, u32[]{:S(2)}, u32[]{:S(2)}) collective-permute-start(f32[16,16,128]{2,1,0:T(8,128)} %get-tuple-element.63), channel_id=1, source_target_pairs={{32,0},{64,32},{96,64},{128,96},{160,128},{192,160},{224,192},{33,... | collective-permute-start | bytes 393224 | tf_op jit(solution)/shard_map/ppermute | solution.py:23
  78.9 8.0 %collective-permute-start.16 = (f32[16,16,2]{2,1,0:T(8,128)}, f32[16,16,2]{2,1,0:T(8,128)S(1)}, u32[]{:S(2)}, u32[]{:S(2)}) collective-permute-start(f32[16,16,2]{2,1,0:T(8,128)} %get-tuple-element.66), channel_id=1, source_target_pairs={{0,1},{1,2},{2,3},{4,5},{5,6},{6,7},{8,9},{9,10},{10,11},{12,13},{... | collective-permute-start | bytes 6152 | tf_op jit(solution)/shard_map/ppermute | solution.py:18
  82.9 8.3 %collective-permute-start.17 = (f32[16,16,2]{2,1,0:T(8,128)}, f32[16,16,2]{2,1,0:T(8,128)S(1)}, u32[]{:S(2)}, u32[]{:S(2)}) collective-permute-start(f32[16,16,2]{2,1,0:T(8,128)} %get-tuple-element.67), channel_id=1, source_target_pairs={{1,0},{2,1},{3,2},{5,4},{6,5},{7,6},{9,8},{10,9},{11,10},{13,12},{... | collective-permute-start | bytes 6152 | tf_op jit(solution)/shard_map/ppermute | solution.py:23
  87.0 7.7 %collective-permute-start.15 = (f32[16,8,128]{2,1,0:T(8,128)}, f32[16,8,128]{2,1,0:T(8,128)S(1)}, u32[]{:S(2)}, u32[]{:S(2)}) collective-permute-start(f32[16,8,128]{2,1,0:T(8,128)} %get-tuple-element.65), channel_id=1, source_target_pairs={{4,0},{8,4},{12,8},{16,12},{20,16},{24,20},{28,24},{5,1},{9,5},{13... | collective-permute-start | bytes 196616 | tf_op jit(solution)/shard_map/ppermute | solution.py:23
  98.8 11.8 %collective-permute-start.22 = (f32[16,16,2]{2,1,0:T(8,128)}, f32[16,16,2]{2,1,0:T(8,128)S(1)}, u32[]{:S(2)}, u32[]{:S(2)}) collective-permute-start(f32[16,16,2]{2,1,0:T(8,128)} %get-tuple-element.78), channel_id=1, source_target_pairs={{0,1},{1,2},{2,3},{4,5},{5,6},{6,7},{8,9},{9,10},{10,11},{12,13},{... | collective-permute-start | bytes 6152 | tf_op jit(solution)/shard_map/ppermute | solution.py:18
  104.6 43.3 %collective-permute-start.20 = (f32[16,8,128]{2,1,0:T(8,128)}, f32[16,8,128]{2,1,0:T(8,128)S(1)}, u32[]{:S(2)}, u32[]{:S(2)}) collective-permute-start(f32[16,8,128]{2,1,0:T(8,128)} %get-tuple-element.76), channel_id=1, source_target_pairs={{0,4},{4,8},{8,12},{12,16},{16,20},{20,24},{24,28},{1,5},{5,9},{9,... | collective-permute-start | bytes 196616 | tf_op jit(solution)/shard_map/ppermute | solution.py:18
  109.2 38.7 %collective-permute-start.21 = (f32[16,8,128]{2,1,0:T(8,128)}, f32[16,8,128]{2,1,0:T(8,128)S(1)}, u32[]{:S(2)}, u32[]{:S(2)}) collective-permute-start(f32[16,8,128]{2,1,0:T(8,128)} %get-tuple-element.77), channel_id=1, source_target_pairs={{4,0},{8,4},{12,8},{16,12},{20,16},{24,20},{28,24},{5,1},{9,5},{13... | collective-permute-start | bytes 196616 | tf_op jit(solution)/shard_map/ppermute | solution.py:23
  113.5 25.8 %all-to-all-start = ((f32[64,1,128]{2,1,0:T(1,128)}), f32[64,1,128]{2,1,0:T(1,128)S(1)}, u32[]{:S(2)}, u32[]{:S(2)}) async-start(f32[64,1,128]{2,1,0:T(1,128)} %bitcast.9), calls=%async_computation | async-start | bytes 65536 | tf_op jit(solution)/shard_map/all_to_all | solution.py:33
  128.9 11.8 %collective-permute-start.18 = (f32[2,16,128]{2,1,0:T(8,128)S(1)}, f32[2,16,128]{2,1,0:T(8,128)S(1)}, u32[]{:S(2)}, u32[]{:S(2)}) collective-permute-start(f32[2,16,128]{2,1,0:T(8,128)S(1)} %copy-done.32), channel_id=1, source_target_pairs={{0,32},{32,64},{64,96},{96,128},{128,160},{160,192},{192,224},{1,3... | collective-permute-start | bytes 49160 | tf_op jit(solution)/shard_map/ppermute | solution.py:18
  136.3 11.6 %collective-permute-start.19 = (f32[2,16,128]{2,1,0:T(8,128)S(1)}, f32[2,16,128]{2,1,0:T(8,128)S(1)}, u32[]{:S(2)}, u32[]{:S(2)}) collective-permute-start(f32[2,16,128]{2,1,0:T(8,128)S(1)} %copy-done.31), channel_id=1, source_target_pairs={{32,0},{64,32},{96,64},{128,96},{160,128},{192,160},{224,192},{33,... | collective-permute-start | bytes 49160 | tf_op jit(solution)/shard_map/ppermute | solution.py:23
  139.4 12.5 %collective-permute-start.24 = (f32[128]{0:T(128)S(1)}, f32[128]{0:T(128)S(1)}, u32[]{:S(2)}, u32[]{:S(2)}) collective-permute-start(f32[128]{0:T(128)S(1)} %reduce_sum.9), channel_id=1, source_target_pairs={{1,0},{2,3},{5,4},{6,7},{9,8},{10,11},{13,12},{14,15},{17,16},{18,... | collective-permute-start | bytes 1544 | tf_op jit(solution)/shard_map/ppermute | solution.py:349
  (36 other events, 207.1 us)

commit v17 on v16

--- a/solution.py
+++ b/solution.py
@@ -296,8 +296,9 @@
     src_all = (time_step * sources * top_flag)[..., None]
 
     v0, v1, v2 = velocity[0], velocity[1], velocity[2]
-    x_up = jnp.concatenate([pressure[X - 2 :], v0[X - 1 :], inv_density[X - 1 :]], axis=0)
-    x_dn = jnp.concatenate([pressure[:2], v0[:1], inv_density[:1]], axis=0)
+    filler = jnp.zeros((X - 4, Y, Z), jnp.float32)
+    x_up = jnp.concatenate([pressure[X - 2 :], v0[X - 1 :], inv_density[X - 1 :], filler], axis=0)
+    x_dn = jnp.concatenate([pressure[:2], v0[:1], inv_density[:1], filler], axis=0)
     y_up = jnp.concatenate(
         [pressure[:, Y - rows :], v1[:, Y - 1 :], inv_density[:, Y - 1 :]], axis=1
     )

time: 154 us -> 158 us (1.026)
  starting transfers between devices: 90.5 us -> 96.6 us
  waiting for transfers between devices: 30.2 us -> 27.9 us
    ppermute x12, starting transfers between devices: 53.9 us -> 62 us  [shifted_up(): return lax.ppermute(x, axis, [(i, i + 1) for i in range(count - 1)])]
    ppermute x12, waiting for transfers between devices: 26.1 us -> 23.4 us  [shifted_down(): return lax.ppermute(x, axis, [(i + 1, i) for i in range(count - 1)])]
    ppermute x12, starting transfers between devices: 20 us -> 18 us  [shifted_down(): return lax.ppermute(x, axis, [(i + 1, i) for i in range(count - 1)])]
  transfers between devices with their start and end apart: 26 -> 26, of which waited for: 8 -> 8; matrix products, arithmetic and copies ran while one was open for 5% -> 6% of each run, Pallas kernels for 2% -> 2%
where the time goes in v17:
time: 158 us; the launch traced here: 156 us
  starting transfers between devices  96.6 us (61%)
  waiting for transfers between devices  27.9 us (18%)
  Pallas kernels  13.8 us (9%)
  local copies, waits for them, and re-layouts  12.8 us (8%)
  other arithmetic  2.83 us (2%)
    ppermute x12, starting transfers between devices, shifted_up(): return lax.ppermute(x, axis, [(i, i + 1) for i in range(count - 1)])  62 us
    ppermute x12, waiting for transfers between devices, shifted_down(): return lax.ppermute(x, axis, [(i + 1, i) for i in range(count - 1)])  23.4 us
    ppermute x12, starting transfers between devices, shifted_down(): return lax.ppermute(x, axis, [(i + 1, i) for i in range(count - 1)])  18 us
    all_to_all x1, starting transfers between devices, summed_on_arrival(): parts = lax.all_to_all(in_blocks(x, dim, size), axis, 0, 0, tiled=True)  15.4 us
    pallas_call x4, Pallas kernels, run_step(): pl.pallas_call(functools.partial(step_kernel, instant, first), out_shape=...  13.8 us
    unnamed x73, local copies, waits for them, and re-layouts  6.85 us
    ppermute x12, waiting for transfers between devices, shifted_up(): return lax.ppermute(x, axis, [(i, i + 1) for i in range(count - 1)])  3.33 us
  transfers between devices with their start and end apart: 26, of which 8 were waited for; matrix products, arithmetic and copies ran while one was open for 6% of the time, Pallas kernels for 2%

profile of v17, /device:TPU:24, one launch (start us, length us, event | category | flops | bytes accessed | tf_op | source)
XLA Modules:
  0.0 156.4 jit_solution(8389267475059650763)
XLA Ops:
  6.7 8.8 %collective-permute-start = (f32[16,16,128]{2,1,0:T(8,128)S(1)}, f32[16,16,128]{2,1,0:T(8,128)S(1)}, u32[]{:S(2)}, u32[]{:S(2)}) collective-permute-start(f32[16,16,128]{2,1,0:T(8,128)S(1)} %get-tuple-element.108), channel_id=1, source_target_pairs={{0,32},{32,64},{64,96},{96,128},{128,160},{160,192},{192,224},{1,3... | collective-permute-start | bytes 393224 | tf_op jit(solution)/shard_map/ppermute | solution.py:18
  15.4 1.9 %collective-permute-start.1 = (f32[16,16,128]{2,1,0:T(8,128)S(1)}, f32[16,16,128]{2,1,0:T(8,128)S(1)}, u32[]{:S(2)}, u32[]{:S(2)}) collective-permute-start(f32[16,16,128]{2,1,0:T(8,128)S(1)} %get-tuple-element.107), channel_id=1, source_target_pairs={{32,0},{64,32},{96,64},{128,96},{160,128},{192,160},{224,192},{33,... | collective-permute-start | bytes 393224 | tf_op jit(solution)/shard_map/ppermute | solution.py:23
  18.6 2.9 %collective-permute-start.4 = (f32[16,16,4]{2,1,0:T(8,128)S(1)}, f32[16,16,4]{2,1,0:T(8,128)S(1)}, u32[]{:S(2)}, u32[]{:S(2)}) collective-permute-start(f32[16,16,4]{2,1,0:T(8,128)S(1)} %copy.20), channel_id=1, source_target_pairs={{0,1},{1,2},{2,3},{4,5},{5,6},{6,7},{8,9},{9,10},{10,11},{12,13},{... | collective-permute-start | bytes 12296 | tf_op jit(solution)/shard_map/ppermute | solution.py:18
  27.2 5.5 %collective-permute-done.5.refs_12_ = f32[16,16,4]{2,1,0:T(8,128)S(1)} collective-permute-done((f32[16,16,4]{2,1,0:T(8,128)S(1)}, f32[16,16,4]{2,1,0:T(8,128)S(1)}, u32[]{:S(2)}, u32[]{:S(2)}) %collective-permute-start.5) | collective-permute-done | bytes 4128 | tf_op jit(solution)/shard_map/ppermute | solution.py:23
  34.1 3.7 %shard_map.121 = (f32[16,16,128]{2,1,0:T(8,128)}, f32[3,16,16,128]{3,2,1,0:T(8,128)}, f32[16,16,1]{2,1,0:T(8,128)}, f32[2,16,128]{2,1,0:T(8,128)}, f32[16,2,128]...) custom-call(f32[64]{0:T(128)} %compare_select_fusion.5.refs_0_, ...), custom_call_target="tpu_custom_call" | custom-call | flops 2621440 | bytes 1572864 | tf_op jit(solution)/shard_map/pallas_call | solution.py:222
  37.8 10.5 %collective-permute-start.6 = (f32[8,16,128]{2,1,0:T(8,128)}, f32[8,16,128]{2,1,0:T(8,128)S(1)}, u32[]{:S(2)}, u32[]{:S(2)}) collective-permute-start(f32[8,16,128]{2,1,0:T(8,128)} %get-tuple-element.47), channel_id=1, source_target_pairs={{0,32},{32,64},{64,96},{96,128},{128,160},{160,192},{192,224},{1,3... | collective-permute-start | bytes 196616 | tf_op jit(solution)/shard_map/ppermute | solution.py:18
  48.3 1.9 %collective-permute-start.7 = (f32[8,16,128]{2,1,0:T(8,128)}, f32[8,16,128]{2,1,0:T(8,128)S(1)}, u32[]{:S(2)}, u32[]{:S(2)}) collective-permute-start(f32[8,16,128]{2,1,0:T(8,128)} %get-tuple-element.48), channel_id=1, source_target_pairs={{32,0},{64,32},{96,64},{128,96},{160,128},{192,160},{224,192},{33,... | collective-permute-start | bytes 196616 | tf_op jit(solution)/shard_map/ppermute | solution.py:23
  53.3 3.4 %collective-permute-start.10 = (f32[16,16,2]{2,1,0:T(8,128)}, f32[16,16,2]{2,1,0:T(8,128)S(1)}, u32[]{:S(2)}, u32[]{:S(2)}) collective-permute-start(f32[16,16,2]{2,1,0:T(8,128)} %get-tuple-element.51), channel_id=1, source_target_pairs={{0,1},{1,2},{2,3},{4,5},{5,6},{6,7},{8,9},{9,10},{10,11},{12,13},{... | collective-permute-start | bytes 6152 | tf_op jit(solution)/shard_map/ppermute | solution.py:18
  56.7 2.8 %collective-permute-done.10.refs_12_ = f32[16,16,2]{2,1,0:T(8,128)S(1)} collective-permute-done((f32[16,16,2]{2,1,0:T(8,128)}, f32[16,16,2]{2,1,0:T(8,128)S(1)}, u32[]{:S(2)}, u32[]{:S(2)}) %collective-permute-start.10) | collective-permute-done | bytes 2080 | tf_op jit(solution)/shard_map/ppermute | solution.py:18
  60.8 6.1 %collective-permute-done.11.refs_13_ = f32[16,16,2]{2,1,0:T(8,128)S(1)} collective-permute-done((f32[16,16,2]{2,1,0:T(8,128)}, f32[16,16,2]{2,1,0:T(8,128)S(1)}, u32[]{:S(2)}, u32[]{:S(2)}) %collective-permute-start.11) | collective-permute-done | bytes 2080 | tf_op jit(solution)/shard_map/ppermute | solution.py:23
  67.6 3.4 %shard_map.122 = (f32[16,16,128]{2,1,0:T(8,128)}, f32[3,16,16,128]{3,2,1,0:T(8,128)}, f32[16,16,1]{2,1,0:T(8,128)}, f32[2,16,128]{2,1,0:T(8,128)}, f32[16,2,128]...) custom-call(f32[64]{0:T(128)} %compare_select_fusion.5.refs_0_, ...), custom_call_target="tpu_custom_call" | custom-call | flops 2621440 | bytes 1572864 | tf_op jit(solution)/shard_map/pallas_call | solution.py:222
  71.0 9.8 %collective-permute-start.12 = (f32[16,16,128]{2,1,0:T(8,128)}, f32[16,16,128]{2,1,0:T(8,128)S(1)}, u32[]{:S(2)}, u32[]{:S(2)}) collective-permute-start(f32[16,16,128]{2,1,0:T(8,128)} %get-tuple-element.62), channel_id=1, source_target_pairs={{0,32},{32,64},{64,96},{96,128},{128,160},{160,192},{192,224},{1,3... | collective-permute-start | bytes 393224 | tf_op jit(solution)/shard_map/ppermute | solution.py:18
  80.8 1.9 %collective-permute-start.13 = (f32[16,16,128]{2,1,0:T(8,128)}, f32[16,16,128]{2,1,0:T(8,128)S(1)}, u32[]{:S(2)}, u32[]{:S(2)}) collective-permute-start(f32[16,16,128]{2,1,0:T(8,128)} %get-tuple-element.63), channel_id=1, source_target_pairs={{32,0},{64,32},{96,64},{128,96},{160,128},{192,160},{224,192},{33,... | collective-permute-start | bytes 393224 | tf_op jit(solution)/shard_map/ppermute | solution.py:23
  82.8 3.9 %collective-permute-start.16 = (f32[16,16,2]{2,1,0:T(8,128)}, f32[16,16,2]{2,1,0:T(8,128)S(1)}, u32[]{:S(2)}, u32[]{:S(2)}) collective-permute-start(f32[16,16,2]{2,1,0:T(8,128)} %get-tuple-element.66), channel_id=1, source_target_pairs={{0,1},{1,2},{2,3},{4,5},{5,6},{6,7},{8,9},{9,10},{10,11},{12,13},{... | collective-permute-start | bytes 6152 | tf_op jit(solution)/shard_map/ppermute | solution.py:18
  88.0 2.8 %collective-permute-start.14 = (f32[16,8,128]{2,1,0:T(8,128)}, f32[16,8,128]{2,1,0:T(8,128)S(1)}, u32[]{:S(2)}, u32[]{:S(2)}) collective-permute-start(f32[16,8,128]{2,1,0:T(8,128)} %get-tuple-element.64), channel_id=1, source_target_pairs={{0,4},{4,8},{8,12},{12,16},{16,20},{20,24},{24,28},{1,5},{5,9},{9,... | collective-permute-start | bytes 196616 | tf_op jit(solution)/shard_map/ppermute | solution.py:18
  95.1 3.5 %collective-permute-done.15.refs_11_ = f32[16,8,128]{2,1,0:T(8,128)S(1)} collective-permute-done((f32[16,8,128]{2,1,0:T(8,128)}, f32[16,8,128]{2,1,0:T(8,128)S(1)}, u32[]{:S(2)}, u32[]{:S(2)}) %collective-permute-start.15) | collective-permute-done | bytes 65568 | tf_op jit(solution)/shard_map/ppermute | solution.py:23
  99.3 3.4 %shard_map.123 = (f32[16,16,128]{2,1,0:T(8,128)}, f32[3,16,16,128]{3,2,1,0:T(8,128)}, f32[16,16,1]{2,1,0:T(8,128)}, f32[2,16,128]{2,1,0:T(8,128)}, f32[16,2,128]...) custom-call(f32[64]{0:T(128)} %compare_select_fusion.5.refs_0_, ...), custom_call_target="tpu_custom_call" | custom-call | flops 2621440 | bytes 1572864 | tf_op jit(solution)/shard_map/pallas_call | solution.py:222
  102.7 4.6 %collective-permute-start.22 = (f32[16,16,2]{2,1,0:T(8,128)}, f32[16,16,2]{2,1,0:T(8,128)S(1)}, u32[]{:S(2)}, u32[]{:S(2)}) collective-permute-start(f32[16,16,2]{2,1,0:T(8,128)} %get-tuple-element.78), channel_id=1, source_target_pairs={{0,1},{1,2},{2,3},{4,5},{5,6},{6,7},{8,9},{9,10},{10,11},{12,13},{... | collective-permute-start | bytes 6152 | tf_op jit(solution)/shard_map/ppermute | solution.py:18
  108.6 4.6 %collective-permute-start.20 = (f32[16,8,128]{2,1,0:T(8,128)}, f32[16,8,128]{2,1,0:T(8,128)S(1)}, u32[]{:S(2)}, u32[]{:S(2)}) collective-permute-start(f32[16,8,128]{2,1,0:T(8,128)} %get-tuple-element.76), channel_id=1, source_target_pairs={{0,4},{4,8},{8,12},{12,16},{16,20},{20,24},{24,28},{1,5},{5,9},{9,... | collective-permute-start | bytes 196616 | tf_op jit(solution)/shard_map/ppermute | solution.py:18
  117.5 15.4 %all-to-all-start = ((f32[64,1,128]{2,1,0:T(1,128)}), f32[64,1,128]{2,1,0:T(1,128)S(1)}, u32[]{:S(2)}, u32[]{:S(2)}) async-start(f32[64,1,128]{2,1,0:T(1,128)} %bitcast.9), calls=%async_computation | async-start | bytes 65536 | tf_op jit(solution)/shard_map/all_to_all | solution.py:33
  132.8 7.3 %collective-permute-start.18 = (f32[2,16,128]{2,1,0:T(8,128)S(1)}, f32[2,16,128]{2,1,0:T(8,128)S(1)}, u32[]{:S(2)}, u32[]{:S(2)}) collective-permute-start(f32[2,16,128]{2,1,0:T(8,128)S(1)} %copy-done.32), channel_id=1, source_target_pairs={{0,32},{32,64},{64,96},{96,128},{128,160},{160,192},{192,224},{1,3... | collective-permute-start | bytes 49160 | tf_op jit(solution)/shard_map/ppermute | solution.py:18
  140.2 1.9 %collective-permute-start.19 = (f32[2,16,128]{2,1,0:T(8,128)S(1)}, f32[2,16,128]{2,1,0:T(8,128)S(1)}, u32[]{:S(2)}, u32[]{:S(2)}) collective-permute-start(f32[2,16,128]{2,1,0:T(8,128)S(1)} %copy-done.31), channel_id=1, source_target_pairs={{32,0},{64,32},{96,64},{128,96},{160,128},{192,160},{224,192},{33,... | collective-permute-start | bytes 49160 | tf_op jit(solution)/shard_map/ppermute | solution.py:23
  144.7 7.2 %collective-permute-done.19.refs_9_ = f32[2,16,128]{2,1,0:T(8,128)S(1)} collective-permute-done((f32[2,16,128]{2,1,0:T(8,128)S(1)}, f32[2,16,128]{2,1,0:T(8,128)S(1)}, u32[]{:S(2)}, u32[]{:S(2)}) %collective-permute-start.19) | collective-permute-done | bytes 16416 | tf_op jit(solution)/shard_map/ppermute | solution.py:23
  152.5 3.3 %shard_map.124 = (f32[16,16,128]{2,1,0:T(8,128)}, f32[3,16,16,128]{3,2,1,0:T(8,128)}, f32[16,16,1]{2,1,0:T(8,128)}, f32[2,16,128]{2,1,0:T(8,128)}, f32[16,2,128]...) custom-call(f32[64]{0:T(128)} %compare_select_fusion.5.refs_0_, ...), custom_call_target="tpu_custom_call" | custom-call | flops 2621440 | bytes 1572864 | tf_op jit(solution)/shard_map/pallas_call | solution.py:222
  (143 shorter events, 34.7 us)
Async XLA Ops:
  2.7 30.0 %collective-permute-start.2 = (f32[16,10,128]{2,1,0:T(8,128)S(1)}, f32[16,10,128]{2,1,0:T(8,128)S(1)}, u32[]{:S(2)}, u32[]{:S(2)}) collective-permute-start(f32[16,10,128]{2,1,0:T(8,128)S(1)} %pad_maximum_fusion), channel_id=1, source_target_pairs={{0,4},{4,8},{8,12},{12,16},{16,20},{20,24},{24,28},{1,5},{5,9},{9,... | collective-permute-start | bytes 245768 | tf_op jit(solution)/shard_map/ppermute | solution.py:18
  4.4 28.2 %collective-permute-start.3 = (f32[16,10,128]{2,1,0:T(8,128)S(1)}, f32[16,10,128]{2,1,0:T(8,128)S(1)}, u32[]{:S(2)}, u32[]{:S(2)}) collective-permute-start(f32[16,10,128]{2,1,0:T(8,128)S(1)} %pad_maximum_fusion.1), channel_id=1, source_target_pairs={{4,0},{8,4},{12,8},{16,12},{20,16},{24,20},{28,24},{5,1},{9,5},{13... | collective-permute-start | bytes 245768 | tf_op jit(solution)/shard_map/ppermute | solution.py:23
  6.7 26.0 %collective-permute-start = (f32[16,16,128]{2,1,0:T(8,128)S(1)}, f32[16,16,128]{2,1,0:T(8,128)S(1)}, u32[]{:S(2)}, u32[]{:S(2)}) collective-permute-start(f32[16,16,128]{2,1,0:T(8,128)S(1)} %get-tuple-element.108), channel_id=1, source_target_pairs={{0,32},{32,64},{64,96},{96,128},{128,160},{160,192},{192,224},{1,3... | collective-permute-start | bytes 393224 | tf_op jit(solution)/shard_map/ppermute | solution.py:18
  15.4 17.3 %collective-permute-start.1 = (f32[16,16,128]{2,1,0:T(8,128)S(1)}, f32[16,16,128]{2,1,0:T(8,128)S(1)}, u32[]{:S(2)}, u32[]{:S(2)}) collective-permute-start(f32[16,16,128]{2,1,0:T(8,128)S(1)} %get-tuple-element.107), channel_id=1, source_target_pairs={{32,0},{64,32},{96,64},{128,96},{160,128},{192,160},{224,192},{33,... | collective-permute-start | bytes 393224 | tf_op jit(solution)/shard_map/ppermute | solution.py:23
  24.2 8.4 %collective-permute-start.5 = (f32[16,16,4]{2,1,0:T(8,128)S(1)}, f32[16,16,4]{2,1,0:T(8,128)S(1)}, u32[]{:S(2)}, u32[]{:S(2)}) collective-permute-start(f32[16,16,4]{2,1,0:T(8,128)S(1)} %copy.23), channel_id=1, source_target_pairs={{1,0},{2,1},{3,2},{5,4},{6,5},{7,6},{9,8},{10,9},{11,10},{13,12},{... | collective-permute-start | bytes 12296 | tf_op jit(solution)/shard_map/ppermute | solution.py:23
  37.8 29.1 %collective-permute-start.6 = (f32[8,16,128]{2,1,0:T(8,128)}, f32[8,16,128]{2,1,0:T(8,128)S(1)}, u32[]{:S(2)}, u32[]{:S(2)}) collective-permute-start(f32[8,16,128]{2,1,0:T(8,128)} %get-tuple-element.47), channel_id=1, source_target_pairs={{0,32},{32,64},{64,96},{96,128},{128,160},{160,192},{192,224},{1,3... | collective-permute-start | bytes 196616 | tf_op jit(solution)/shard_map/ppermute | solution.py:18
  48.3 18.5 %collective-permute-start.7 = (f32[8,16,128]{2,1,0:T(8,128)}, f32[8,16,128]{2,1,0:T(8,128)S(1)}, u32[]{:S(2)}, u32[]{:S(2)}) collective-permute-start(f32[8,16,128]{2,1,0:T(8,128)} %get-tuple-element.48), channel_id=1, source_target_pairs={{32,0},{64,32},{96,64},{128,96},{160,128},{192,160},{224,192},{33,... | collective-permute-start | bytes 196616 | tf_op jit(solution)/shard_map/ppermute | solution.py:23
  50.2 16.6 %collective-permute-start.8 = (f32[16,8,128]{2,1,0:T(8,128)}, f32[16,8,128]{2,1,0:T(8,128)S(1)}, u32[]{:S(2)}, u32[]{:S(2)}) collective-permute-start(f32[16,8,128]{2,1,0:T(8,128)} %get-tuple-element.49), channel_id=1, source_target_pairs={{0,4},{4,8},{8,12},{12,16},{16,20},{20,24},{24,28},{1,5},{5,9},{9,... | collective-permute-start | bytes 196616 | tf_op jit(solution)/shard_map/ppermute | solution.py:18
  52.0 14.9 %collective-permute-start.9 = (f32[16,8,128]{2,1,0:T(8,128)}, f32[16,8,128]{2,1,0:T(8,128)S(1)}, u32[]{:S(2)}, u32[]{:S(2)}) collective-permute-start(f32[16,8,128]{2,1,0:T(8,128)} %get-tuple-element.50), channel_id=1, source_target_pairs={{4,0},{8,4},{12,8},{16,12},{20,16},{24,20},{28,24},{5,1},{9,5},{13... | collective-permute-start | bytes 196616 | tf_op jit(solution)/shard_map/ppermute | solution.py:23
  59.5 7.4 %collective-permute-start.11 = (f32[16,16,2]{2,1,0:T(8,128)}, f32[16,16,2]{2,1,0:T(8,128)S(1)}, u32[]{:S(2)}, u32[]{:S(2)}) collective-permute-start(f32[16,16,2]{2,1,0:T(8,128)} %get-tuple-element.52), channel_id=1, source_target_pairs={{1,0},{2,1},{3,2},{5,4},{6,5},{7,6},{9,8},{10,9},{11,10},{13,12},{... | collective-permute-start | bytes 6152 | tf_op jit(solution)/shard_map/ppermute | solution.py:23
  71.0 27.6 %collective-permute-start.12 = (f32[16,16,128]{2,1,0:T(8,128)}, f32[16,16,128]{2,1,0:T(8,128)S(1)}, u32[]{:S(2)}, u32[]{:S(2)}) collective-permute-start(f32[16,16,128]{2,1,0:T(8,128)} %get-tuple-element.62), channel_id=1, source_target_pairs={{0,32},{32,64},{64,96},{96,128},{128,160},{160,192},{192,224},{1,3... | collective-permute-start | bytes 393224 | tf_op jit(solution)/shard_map/ppermute | solution.py:18
  80.8 17.7 %collective-permute-start.13 = (f32[16,16,128]{2,1,0:T(8,128)}, f32[16,16,128]{2,1,0:T(8,128)S(1)}, u32[]{:S(2)}, u32[]{:S(2)}) collective-permute-start(f32[16,16,128]{2,1,0:T(8,128)} %get-tuple-element.63), channel_id=1, source_target_pairs={{32,0},{64,32},{96,64},{128,96},{160,128},{192,160},{224,192},{33,... | collective-permute-start | bytes 393224 | tf_op jit(solution)/shard_map/ppermute | solution.py:23
  82.8 8.0 %collective-permute-start.16 = (f32[16,16,2]{2,1,0:T(8,128)}, f32[16,16,2]{2,1,0:T(8,128)S(1)}, u32[]{:S(2)}, u32[]{:S(2)}) collective-permute-start(f32[16,16,2]{2,1,0:T(8,128)} %get-tuple-element.66), channel_id=1, source_target_pairs={{0,1},{1,2},{2,3},{4,5},{5,6},{6,7},{8,9},{9,10},{10,11},{12,13},{... | collective-permute-start | bytes 6152 | tf_op jit(solution)/shard_map/ppermute | solution.py:18
  86.7 8.4 %collective-permute-start.17 = (f32[16,16,2]{2,1,0:T(8,128)}, f32[16,16,2]{2,1,0:T(8,128)S(1)}, u32[]{:S(2)}, u32[]{:S(2)}) collective-permute-start(f32[16,16,2]{2,1,0:T(8,128)} %get-tuple-element.67), channel_id=1, source_target_pairs={{1,0},{2,1},{3,2},{5,4},{6,5},{7,6},{9,8},{10,9},{11,10},{13,12},{... | collective-permute-start | bytes 6152 | tf_op jit(solution)/shard_map/ppermute | solution.py:23
  88.0 7.1 %collective-permute-start.14 = (f32[16,8,128]{2,1,0:T(8,128)}, f32[16,8,128]{2,1,0:T(8,128)S(1)}, u32[]{:S(2)}, u32[]{:S(2)}) collective-permute-start(f32[16,8,128]{2,1,0:T(8,128)} %get-tuple-element.64), channel_id=1, source_target_pairs={{0,4},{4,8},{8,12},{12,16},{16,20},{20,24},{24,28},{1,5},{5,9},{9,... | collective-permute-start | bytes 196616 | tf_op jit(solution)/shard_map/ppermute | solution.py:18
  90.8 7.8 %collective-permute-start.15 = (f32[16,8,128]{2,1,0:T(8,128)}, f32[16,8,128]{2,1,0:T(8,128)S(1)}, u32[]{:S(2)}, u32[]{:S(2)}) collective-permute-start(f32[16,8,128]{2,1,0:T(8,128)} %get-tuple-element.65), channel_id=1, source_target_pairs={{4,0},{8,4},{12,8},{16,12},{20,16},{24,20},{28,24},{5,1},{9,5},{13... | collective-permute-start | bytes 196616 | tf_op jit(solution)/shard_map/ppermute | solution.py:23
  102.7 11.8 %collective-permute-start.22 = (f32[16,16,2]{2,1,0:T(8,128)}, f32[16,16,2]{2,1,0:T(8,128)S(1)}, u32[]{:S(2)}, u32[]{:S(2)}) collective-permute-start(f32[16,16,2]{2,1,0:T(8,128)} %get-tuple-element.78), channel_id=1, source_target_pairs={{0,1},{1,2},{2,3},{4,5},{5,6},{6,7},{8,9},{9,10},{10,11},{12,13},{... | collective-permute-start | bytes 6152 | tf_op jit(solution)/shard_map/ppermute | solution.py:18
  107.2 7.2 %collective-permute-start.23 = (f32[16,16,2]{2,1,0:T(8,128)}, f32[16,16,2]{2,1,0:T(8,128)S(1)}, u32[]{:S(2)}, u32[]{:S(2)}) collective-permute-start(f32[16,16,2]{2,1,0:T(8,128)} %get-tuple-element.79), channel_id=1, source_target_pairs={{1,0},{2,1},{3,2},{5,4},{6,5},{7,6},{9,8},{10,9},{11,10},{13,12},{... | collective-permute-start | bytes 6152 | tf_op jit(solution)/shard_map/ppermute | solution.py:23
  108.6 43.3 %collective-permute-start.20 = (f32[16,8,128]{2,1,0:T(8,128)}, f32[16,8,128]{2,1,0:T(8,128)S(1)}, u32[]{:S(2)}, u32[]{:S(2)}) collective-permute-start(f32[16,8,128]{2,1,0:T(8,128)} %get-tuple-element.76), channel_id=1, source_target_pairs={{0,4},{4,8},{8,12},{12,16},{16,20},{20,24},{24,28},{1,5},{5,9},{9,... | collective-permute-start | bytes 196616 | tf_op jit(solution)/shard_map/ppermute | solution.py:18
  113.1 38.7 %collective-permute-start.21 = (f32[16,8,128]{2,1,0:T(8,128)}, f32[16,8,128]{2,1,0:T(8,128)S(1)}, u32[]{:S(2)}, u32[]{:S(2)}) collective-permute-start(f32[16,8,128]{2,1,0:T(8,128)} %get-tuple-element.77), channel_id=1, source_target_pairs={{4,0},{8,4},{12,8},{16,12},{20,16},{24,20},{28,24},{5,1},{9,5},{13... | collective-permute-start | bytes 196616 | tf_op jit(solution)/shard_map/ppermute | solution.py:23
  117.5 25.8 %all-to-all-start = ((f32[64,1,128]{2,1,0:T(1,128)}), f32[64,1,128]{2,1,0:T(1,128)S(1)}, u32[]{:S(2)}, u32[]{:S(2)}) async-start(f32[64,1,128]{2,1,0:T(1,128)} %bitcast.9), calls=%async_computation | async-start | bytes 65536 | tf_op jit(solution)/shard_map/all_to_all | solution.py:33
  132.8 11.8 %collective-permute-start.18 = (f32[2,16,128]{2,1,0:T(8,128)S(1)}, f32[2,16,128]{2,1,0:T(8,128)S(1)}, u32[]{:S(2)}, u32[]{:S(2)}) collective-permute-start(f32[2,16,128]{2,1,0:T(8,128)S(1)} %copy-done.32), channel_id=1, source_target_pairs={{0,32},{32,64},{64,96},{96,128},{128,160},{160,192},{192,224},{1,3... | collective-permute-start | bytes 49160 | tf_op jit(solution)/shard_map/ppermute | solution.py:18
  140.2 11.6 %collective-permute-start.19 = (f32[2,16,128]{2,1,0:T(8,128)S(1)}, f32[2,16,128]{2,1,0:T(8,128)S(1)}, u32[]{:S(2)}, u32[]{:S(2)}) collective-permute-start(f32[2,16,128]{2,1,0:T(8,128)S(1)} %copy-done.31), channel_id=1, source_target_pairs={{32,0},{64,32},{96,64},{128,96},{160,128},{192,160},{224,192},{33,... | collective-permute-start | bytes 49160 | tf_op jit(solution)/shard_map/ppermute | solution.py:23
  143.3 12.5 %collective-permute-start.24 = (f32[128]{0:T(128)S(1)}, f32[128]{0:T(128)S(1)}, u32[]{:S(2)}, u32[]{:S(2)}) collective-permute-start(f32[128]{0:T(128)S(1)} %reduce_sum.9), channel_id=1, source_target_pairs={{1,0},{2,3},{5,4},{6,7},{9,8},{10,11},{13,12},{14,15},{17,16},{18,... | collective-permute-start | bytes 1544 | tf_op jit(solution)/shard_map/ppermute | solution.py:350
  (36 other events, 193.3 us)
